TPU v7x, 1024 devices: a whole 4x8x16 slice. The times are simulated.
1024 devices in a mesh: half: 2 (over x_hi), gx: 16 (over z), gy: 32 (over y, x_lo, core).
Axes of the slice: x: 4 (x_hi: 2, x_lo: 2; x = x_hi * 2 + x_lo), y: 8, z: 16, core: 2. Of those that a mesh axis runs over, the one named last changes fastest.
Arguments:
- state: float32 [2, 20, 32, 512, 128], P('half', None, 'gx', 'gy'), may hold values from -4 to 4
- levels: int32 [4, 32, 512], P(None, 'gx', 'gy'), may hold values from 0 to 128
- old_flux: float32 [2, 32, 512, 128], P(None, 'gx', 'gy'), may hold values from -4 to 4
- eco_prey: int32 [19], replicated, may hold values from 0 to 18
- eco_rate: float32 [19], replicated, may hold values from 0.3 to 3
Outputs:
- state_next: float32 [2, 20, 32, 512, 128], P('half', None, 'gx', 'gy')
All inputs are finite; a program needn't handle non-finite values.
Results may differ from a plain program's by a relative error of at most 0.00013.
Values sent between devices are 32-bit elements; how exact they have to be, the bound alone decides.
No kernel may reach another device: no remote copies, remote signals or barrier semaphores. Data moves between devices by JAX's collectives and lax.ppermute only.
A program may use at most 32 MiB of HBM per device.

v0:
```python
import jax
import jax.numpy as jnp
from jax import lax
from jax.sharding import PartitionSpec as P

NSUB = 4


DT = 0.1
NU = 1.0
CORIOLIS = 0.5
DRAG = 0.1
MORTALITY = 0.1
HEATING = 2.0
SURFACE = 8.0


def extended_2(shard, sides, width):
    for axis, dim in sides:
        peers, length = (lax.axis_size(axis), shard.shape[dim])
        up = [(i, (i + 1) % peers) for i in range(peers - 1)]
        down = [(j, i) for i, j in up]
        last = lax.slice_in_dim(shard, length - width, length, axis=dim)
        leading = lax.slice_in_dim(shard, 0, width, axis=dim)
        before = lax.ppermute(last, axis, up)
        after = lax.ppermute(leading, axis, down)
        shard = jnp.concatenate([before, shard, after], axis=dim)
    return shard


def from_behind(shard, axis, by):
    peers = lax.axis_size(axis)
    pairs = [(i, i + by) for i in range(peers) if 0 <= i + by < peers]
    return lax.ppermute(shard, axis, pairs)


def to_fine(coarse):
    fields = coarse.shape[0] // 4
    size_x, size_y, depth = (coarse.shape[1], coarse.shape[2], coarse.shape[3])
    split = coarse.reshape(fields, 2, 2, size_x, size_y, depth).transpose(0, 3, 1, 4, 2, 5)
    return split.reshape(fields, 2 * size_x, 2 * size_y, depth)


def to_coarse(fine_cells):
    fields, fine_x, fine_y, depth = fine_cells.shape
    split = fine_cells.reshape(fields, fine_x // 2, 2, fine_y // 2, 2, depth).transpose(
        0, 2, 4, 1, 3, 5
    )
    return split.reshape(fields * 4, fine_x // 2, fine_y // 2, depth)


def fine_levels(levels):
    size_x, size_y = (levels.shape[1], levels.shape[2])
    return (
        levels.reshape(2, 2, size_x, size_y).transpose(2, 0, 3, 1).reshape(2 * size_x, 2 * size_y)
    )


def wet_of(levels, depth):
    shape = levels.shape + (depth,)
    return (lax.broadcasted_iota(jnp.int32, shape, len(shape) - 1) < levels[..., None]).astype(
        jnp.float32
    )


def trim_margin(values, margin, keep):
    cut = margin - keep
    if cut == 0:
        return values
    return values[..., cut : values.shape[-3] - cut, cut : values.shape[-2] - cut, :]


def ocean_substep(fields, wet_mask, heating):
    centre = fields[:, 1:-1, 1:-1]
    to_east = fields[:, 2:, 1:-1]
    to_west = fields[:, :-2, 1:-1]
    to_north = fields[:, 1:-1, 2:]
    to_south = fields[:, 1:-1, :-2]
    speed_east = centre[0]
    speed_north = centre[1]
    advect = speed_east * (to_east - to_west) * 0.5 + speed_north * (to_north - to_south) * 0.5
    spread = to_east + to_west + to_north + to_south - 4.0 * centre
    zeroes = jnp.zeros_like(speed_east)
    forcing = jnp.stack(
        [
            CORIOLIS * speed_north - DRAG * speed_east,
            -CORIOLIS * speed_east - DRAG * speed_north,
            zeroes + heating,
            zeroes,
            zeroes + 1.0,
        ]
    )
    return wet_mask * (centre + DT * (NU * spread - advect + forcing))


def tracer_substep(fields, wet_mask, volume_flux, onehot, eco_rate):
    species = eco_rate.shape[0]
    centre = fields[:, 1:-1, 1:-1]
    to_east = fields[:, 2:, 1:-1]
    to_west = fields[:, :-2, 1:-1]
    to_north = fields[:, 1:-1, 2:]
    to_south = fields[:, 1:-1, :-2]
    advect = (
        volume_flux[0] * (to_east - to_west) * 0.5 + volume_flux[1] * (to_north - to_south) * 0.5
    )
    spread = to_east + to_west + to_north + to_south - 4.0 * centre
    living = centre[:species]
    prey_values = jnp.einsum("ts,sxyk->txyk", onehot, living, precision=lax.Precision.HIGHEST)
    growth = eco_rate[:, None, None, None] * living * jnp.tanh(prey_values) - MORTALITY * living
    reaction = jnp.concatenate([growth, jnp.zeros_like(centre[species:])], axis=0)
    return wet_mask * (centre + DT * (NU * spread - advect + reaction))


def coarse_mean(fine_cells):
    coarse = to_coarse(fine_cells)
    return (
        coarse.reshape(
            fine_cells.shape[0], 4, coarse.shape[1], coarse.shape[2], coarse.shape[3]
        ).sum(axis=1)
        * 0.25
    )


def absorption(tracer, wet_mask, above_table):
    attenuation = wet_mask * (0.03 + 0.05 * jax.nn.softplus(tracer[0]))
    overhead = jnp.einsum("xyk,kl->xyl", attenuation, above_table, precision=lax.Precision.HIGHEST)
    return SURFACE * jnp.exp(-overhead) * (1.0 - jnp.exp(-attenuation))


def advance(
    is_ocean,
    extended,
    wide,
    steps,
    wet_fine,
    fine_margin,
    wet_coarse,
    coarse_margin,
    volume_flux,
    flux_margin,
    heating,
    running,
    onehot,
    eco_rate,
):

    def ocean_part():
        fine_cells = trim_margin(to_fine(extended), 2 * wide, steps)
        summed = running
        remain = steps - 1
        fine_cells = ocean_substep(fine_cells, trim_margin(wet_fine, fine_margin, remain), heating)
        summed = summed + coarse_mean(trim_margin(fine_cells[0:2], remain, 0))
        return (to_coarse(fine_cells), summed)

    def tracer_part():
        tracer = trim_margin(extended, wide, steps)
        remain = steps - 1
        tracer = tracer_substep(
            tracer,
            trim_margin(wet_coarse, coarse_margin, remain),
            trim_margin(volume_flux, flux_margin, remain),
            onehot,
            eco_rate,
        )
        return (tracer, running)

    return lax.cond(is_ocean, ocean_part, tracer_part)


def rim_single(own_block):
    return extended_2(own_block, (("gx", 1), ("gy", 2)), 1)


def body(state, levels, old_flux, eco_prey, eco_rate):
    depth = state.shape[-1]
    size_x, size_y = (state.shape[2], state.shape[3])
    species = eco_rate.shape[0]
    is_ocean = lax.axis_index("half") == 0
    onehot = (eco_prey[:, None] == lax.broadcasted_iota(jnp.int32, (species, species), 1)).astype(
        jnp.float32
    )
    above_table = (
        lax.broadcasted_iota(jnp.int32, (depth, depth), 0)
        < lax.broadcasted_iota(jnp.int32, (depth, depth), 1)
    ).astype(jnp.float32)
    wet_channels = wet_of(levels, depth)
    wet_fine = wet_of(fine_levels(levels), depth)
    wet_coarse = wet_of(jnp.max(levels, axis=0), depth)
    own_block = state[0]
    channels = own_block.shape[0]
    own_block = lax.cond(
        is_ocean,
        lambda: (
            own_block.reshape(channels // 4, 4, size_x, size_y, depth) * wet_channels[None]
        ).reshape(channels, size_x, size_y, depth),
        lambda: own_block * wet_coarse,
    )
    running = jnp.zeros((2, size_x, size_y, depth), jnp.float32)
    for substep in range(NSUB):
        extended = rim_single(own_block)
        own_block, running = advance(
            is_ocean,
            extended,
            1,
            1,
            wet_fine,
            0,
            wet_coarse,
            0,
            old_flux,
            0,
            0.0,
            running,
            onehot,
            eco_rate,
        )
    new_flux = running / NSUB
    absorbed = lax.cond(
        is_ocean,
        lambda: jnp.zeros((size_x, size_y, depth), jnp.float32),
        lambda: absorption(own_block, wet_coarse, above_table),
    )
    flux_arrived = from_behind(new_flux, "half", 1)
    light_arrived = from_behind(absorbed[None], "half", -1)
    heating = HEATING * to_fine(jnp.broadcast_to(light_arrived, (4, size_x, size_y, depth)))[0]
    extended = rim_single(own_block)
    own_block, running = advance(
        is_ocean,
        extended,
        1,
        1,
        wet_fine,
        0,
        wet_coarse,
        0,
        flux_arrived,
        0,
        heating,
        running,
        onehot,
        eco_rate,
    )
    return own_block[None]


def solution(mesh):
    placed = (
        P("half", None, "gx", "gy", None),
        P(None, "gx", "gy"),
        P(None, "gx", "gy", None),
        P(),
        P(),
    )
    return jax.shard_map(
        body,
        mesh=mesh,
        in_specs=placed,
        out_specs=P("half", None, "gx", "gy", None),
        check_vma=False,
    )
```

profile of v0, /device:TPU:100, one launch (start us, length us, event | category | flops | bytes accessed | tf_op | source)
XLA Modules:
  0.0 130.6 jit_solution(8946349282116501513)
XLA Ops:
  0.0 0.8 fusion.51
  1.0 1.0 bitcast_multiply_fusion
  2.0 4.3 %collective-permute-start = (f32[20,1,16,128]{3,2,1,0:T(8,128)S(1)}, f32[20,1,16,128]{3,2,1,0:T(8,128)S(1)}, u32[]{:S(2)}, u32[]{:S(2)}) collective-permute-start(f32[20,1,16,128]{3,2,1,0:T(8,128)S(1)} %get-tuple-element.463), channel_id=1, source_target_pairs={{0,32},{32,64},{64,96},{96,128},{128,160},{160,192},{192,224},{224... | collective-permute-start | bytes 491528 | tf_op jit(solution)/shard_map/ppermute | solution.py:25
  6.3 1.9 %collective-permute-start.1 = (f32[20,1,16,128]{3,2,1,0:T(8,128)S(1)}, f32[20,1,16,128]{3,2,1,0:T(8,128)S(1)}, u32[]{:S(2)}, u32[]{:S(2)}) collective-permute-start(f32[20,1,16,128]{3,2,1,0:T(8,128)S(1)} %get-tuple-element.464), channel_id=1, source_target_pairs={{32,0},{64,32},{96,64},{128,96},{160,128},{192,160},{224,192},{256... | collective-permute-start | bytes 491528 | tf_op jit(solution)/shard_map/ppermute | solution.py:26
  8.6 1.3 %collective-permute-done = f32[20,1,16,128]{3,2,1,0:T(8,128)S(1)} collective-permute-done((f32[20,1,16,128]{3,2,1,0:T(8,128)S(1)}, f32[20,1,16,128]{3,2,1,0:T(8,128)S(1)}, u32[]{:S(2)}, u32[]{:S(2)}) %collective-permute-start) | collective-permute-done | bytes 163872 | tf_op jit(solution)/shard_map/ppermute | solution.py:25
  9.9 4.6 %collective-permute-done.1 = f32[20,1,16,128]{3,2,1,0:T(8,128)S(1)} collective-permute-done((f32[20,1,16,128]{3,2,1,0:T(8,128)S(1)}, f32[20,1,16,128]{3,2,1,0:T(8,128)S(1)}, u32[]{:S(2)}, u32[]{:S(2)}) %collective-permute-start.1) | collective-permute-done | bytes 163872 | tf_op jit(solution)/shard_map/ppermute | solution.py:26
  14.7 1.9 %collective-permute-start.2 = (f32[20,4,1,128]{3,2,1,0:T(1,128)S(1)}, f32[20,4,1,128]{3,2,1,0:T(1,128)S(1)}, u32[]{:S(2)}, u32[]{:S(2)}) collective-permute-start(f32[20,4,1,128]{3,2,1,0:T(1,128)S(1)} %get-tuple-element.453), channel_id=1, source_target_pairs={{0,1},{1,2},{2,3},{3,4},{4,5},{5,6},{6,7},{7,8},{8,9},{9,10},{10,1... | collective-permute-start | bytes 122888 | tf_op jit(solution)/shard_map/ppermute | solution.py:25
  16.6 5.8 %collective-permute-start.3 = (f32[20,4,1,128]{3,2,1,0:T(1,128)S(1)}, f32[20,4,1,128]{3,2,1,0:T(1,128)S(1)}, u32[]{:S(2)}, u32[]{:S(2)}) collective-permute-start(f32[20,4,1,128]{3,2,1,0:T(1,128)S(1)} %get-tuple-element.454), channel_id=1, source_target_pairs={{1,0},{2,1},{3,2},{4,3},{5,4},{6,5},{7,6},{8,7},{9,8},{10,9},{11,1... | collective-permute-start | bytes 122888 | tf_op jit(solution)/shard_map/ppermute | solution.py:26
  22.4 1.6 %collective-permute-done.3 = f32[20,4,1,128]{3,2,1,0:T(1,128)S(1)} collective-permute-done((f32[20,4,1,128]{3,2,1,0:T(1,128)S(1)}, f32[20,4,1,128]{3,2,1,0:T(1,128)S(1)}, u32[]{:S(2)}, u32[]{:S(2)}) %collective-permute-start.3) | collective-permute-done | bytes 40992 | tf_op jit(solution)/shard_map/ppermute | solution.py:26
  24.2 0.6 copy-done.3
  24.8 2.0 %conditional.8 = (f32[20,2,16,128]{3,2,1,0:T(8,128)S(1)}, f32[2,2,16,128]{3,1,2,0:T(2,128)S(1)}) conditional(s32[]{:T(128)} %convert_element_type.24, (f32[2,16,128]{2,1,0:T(8,128)S(1)}, f32[20,4,16,128]{3,2,1,0:T(8,128)S(1)}, f32[20,4,18,128]{3,2,1,0:T(8,128)S(1)}, f32[20,2,16,128]{3,2,1,0:T(8,128)S(1)}, f32[2,2,16,128]{3,2,1,0:T(8,128)S(1)}, ...), branch_computations={%region_3.0_spmd, %region_4.0_spmd} | conditional | flops 19365888 | bytes 7631380 | solution.py:167
  25.0 0.5 fusion.1
  25.5 0.4 copy.123
  26.0 0.4 copy.122
  26.4 0.3 add_multiply_fusion
  26.9 5.5 %collective-permute-start.4 = (f32[20,1,16,128]{3,2,1,0:T(8,128)S(1)}, f32[20,1,16,128]{3,2,1,0:T(8,128)S(1)}, u32[]{:S(2)}, u32[]{:S(2)}) collective-permute-start(f32[20,1,16,128]{3,2,1,0:T(8,128)S(1)} %get-tuple-element.462), channel_id=1, source_target_pairs={{0,32},{32,64},{64,96},{96,128},{128,160},{160,192},{192,224},{224... | collective-permute-start | bytes 491528 | tf_op jit(solution)/shard_map/ppermute | solution.py:25
  32.4 1.9 %collective-permute-start.5 = (f32[20,1,16,128]{3,2,1,0:T(8,128)S(1)}, f32[20,1,16,128]{3,2,1,0:T(8,128)S(1)}, u32[]{:S(2)}, u32[]{:S(2)}) collective-permute-start(f32[20,1,16,128]{3,2,1,0:T(8,128)S(1)} %get-tuple-element.461), channel_id=1, source_target_pairs={{32,0},{64,32},{96,64},{128,96},{160,128},{192,160},{224,192},{256... | collective-permute-start | bytes 491528 | tf_op jit(solution)/shard_map/ppermute | solution.py:26
  34.3 0.9 collective-permute-done.4
  35.2 5.3 %collective-permute-done.5 = f32[20,1,16,128]{3,2,1,0:T(8,128)S(1)} collective-permute-done((f32[20,1,16,128]{3,2,1,0:T(8,128)S(1)}, f32[20,1,16,128]{3,2,1,0:T(8,128)S(1)}, u32[]{:S(2)}, u32[]{:S(2)}) %collective-permute-start.5) | collective-permute-done | bytes 163872 | tf_op jit(solution)/shard_map/ppermute | solution.py:26
  40.6 1.9 %collective-permute-start.6 = (f32[20,4,1,128]{3,2,1,0:T(1,128)S(1)}, f32[20,4,1,128]{3,2,1,0:T(1,128)S(1)}, u32[]{:S(2)}, u32[]{:S(2)}) collective-permute-start(f32[20,4,1,128]{3,2,1,0:T(1,128)S(1)} %get-tuple-element.451), channel_id=1, source_target_pairs={{0,1},{1,2},{2,3},{3,4},{4,5},{5,6},{6,7},{7,8},{8,9},{9,10},{10,1... | collective-permute-start | bytes 122888 | tf_op jit(solution)/shard_map/ppermute | solution.py:25
  42.5 5.8 %collective-permute-start.7 = (f32[20,4,1,128]{3,2,1,0:T(1,128)S(1)}, f32[20,4,1,128]{3,2,1,0:T(1,128)S(1)}, u32[]{:S(2)}, u32[]{:S(2)}) collective-permute-start(f32[20,4,1,128]{3,2,1,0:T(1,128)S(1)} %get-tuple-element.452), channel_id=1, source_target_pairs={{1,0},{2,1},{3,2},{4,3},{5,4},{6,5},{7,6},{8,7},{9,8},{10,9},{11,1... | collective-permute-start | bytes 122888 | tf_op jit(solution)/shard_map/ppermute | solution.py:26
  48.3 1.6 %collective-permute-done.7 = f32[20,4,1,128]{3,2,1,0:T(1,128)S(1)} collective-permute-done((f32[20,4,1,128]{3,2,1,0:T(1,128)S(1)}, f32[20,4,1,128]{3,2,1,0:T(1,128)S(1)}, u32[]{:S(2)}, u32[]{:S(2)}) %collective-permute-start.7) | collective-permute-done | bytes 40992 | tf_op jit(solution)/shard_map/ppermute | solution.py:26
  50.1 2.0 %conditional.9 = (f32[20,2,16,128]{3,2,1,0:T(8,128)S(1)}, f32[2,2,16,128]{3,1,2,0:T(2,128)S(1)}) conditional(s32[]{:T(128)} %convert_element_type.24, (f32[2,16,128]{2,1,0:T(8,128)S(1)}, f32[20,4,16,128]{3,2,1,0:T(8,128)S(1)}, f32[20,4,18,128]{3,2,1,0:T(8,128)S(1)}, f32[20,2,16,128]{3,2,1,0:T(8,128)S(1)}, f32[2,2,16,128]{3,2,1,0:T(8,128)S(1)}, ...), branch_computations={%region_6.0_spmd, %region_7.0_spmd} | conditional | flops 19365888 | bytes 7598608 | solution.py:167
  50.3 0.5 fusion.8
  50.8 0.4 copy.126
  51.3 0.4 copy.125
  52.1 3.9 %collective-permute-start.8 = (f32[20,1,16,128]{3,2,1,0:T(8,128)S(1)}, f32[20,1,16,128]{3,2,1,0:T(8,128)S(1)}, u32[]{:S(2)}, u32[]{:S(2)}) collective-permute-start(f32[20,1,16,128]{3,2,1,0:T(8,128)S(1)} %get-tuple-element.460), channel_id=1, source_target_pairs={{0,32},{32,64},{64,96},{96,128},{128,160},{160,192},{192,224},{224... | collective-permute-start | bytes 491528 | tf_op jit(solution)/shard_map/ppermute | solution.py:25
  56.0 1.9 %collective-permute-start.9 = (f32[20,1,16,128]{3,2,1,0:T(8,128)S(1)}, f32[20,1,16,128]{3,2,1,0:T(8,128)S(1)}, u32[]{:S(2)}, u32[]{:S(2)}) collective-permute-start(f32[20,1,16,128]{3,2,1,0:T(8,128)S(1)} %get-tuple-element.459), channel_id=1, source_target_pairs={{32,0},{64,32},{96,64},{128,96},{160,128},{192,160},{224,192},{256... | collective-permute-start | bytes 491528 | tf_op jit(solution)/shard_map/ppermute | solution.py:26
  58.0 1.3 %collective-permute-done.8 = f32[20,1,16,128]{3,2,1,0:T(8,128)S(1)} collective-permute-done((f32[20,1,16,128]{3,2,1,0:T(8,128)S(1)}, f32[20,1,16,128]{3,2,1,0:T(8,128)S(1)}, u32[]{:S(2)}, u32[]{:S(2)}) %collective-permute-start.8) | collective-permute-done | bytes 163872 | tf_op jit(solution)/shard_map/ppermute | solution.py:25
  59.4 4.9 %collective-permute-done.9 = f32[20,1,16,128]{3,2,1,0:T(8,128)S(1)} collective-permute-done((f32[20,1,16,128]{3,2,1,0:T(8,128)S(1)}, f32[20,1,16,128]{3,2,1,0:T(8,128)S(1)}, u32[]{:S(2)}, u32[]{:S(2)}) %collective-permute-start.9) | collective-permute-done | bytes 163872 | tf_op jit(solution)/shard_map/ppermute | solution.py:26
  64.3 1.9 %collective-permute-start.10 = (f32[20,4,1,128]{3,2,1,0:T(1,128)S(1)}, f32[20,4,1,128]{3,2,1,0:T(1,128)S(1)}, u32[]{:S(2)}, u32[]{:S(2)}) collective-permute-start(f32[20,4,1,128]{3,2,1,0:T(1,128)S(1)} %get-tuple-element.449), channel_id=1, source_target_pairs={{0,1},{1,2},{2,3},{3,4},{4,5},{5,6},{6,7},{7,8},{8,9},{9,10},{10,1... | collective-permute-start | bytes 122888 | tf_op jit(solution)/shard_map/ppermute | solution.py:25
  66.3 5.8 %collective-permute-start.11 = (f32[20,4,1,128]{3,2,1,0:T(1,128)S(1)}, f32[20,4,1,128]{3,2,1,0:T(1,128)S(1)}, u32[]{:S(2)}, u32[]{:S(2)}) collective-permute-start(f32[20,4,1,128]{3,2,1,0:T(1,128)S(1)} %get-tuple-element.450), channel_id=1, source_target_pairs={{1,0},{2,1},{3,2},{4,3},{5,4},{6,5},{7,6},{8,7},{9,8},{10,9},{11,1... | collective-permute-start | bytes 122888 | tf_op jit(solution)/shard_map/ppermute | solution.py:26
  72.0 1.6 %collective-permute-done.11 = f32[20,4,1,128]{3,2,1,0:T(1,128)S(1)} collective-permute-done((f32[20,4,1,128]{3,2,1,0:T(1,128)S(1)}, f32[20,4,1,128]{3,2,1,0:T(1,128)S(1)}, u32[]{:S(2)}, u32[]{:S(2)}) %collective-permute-start.11) | collective-permute-done | bytes 40992 | tf_op jit(solution)/shard_map/ppermute | solution.py:26
  73.8 2.2 %conditional.10 = (f32[20,2,16,128]{3,2,1,0:T(8,128)S(1)}, f32[2,2,16,128]{3,1,2,0:T(2,128)S(1)}) conditional(s32[]{:T(128)} %convert_element_type.24, (f32[2,16,128]{2,1,0:T(8,128)S(1)}, f32[20,4,16,128]{3,2,1,0:T(8,128)S(1)}, f32[20,4,18,128]{3,2,1,0:T(8,128)S(1)}, f32[20,2,16,128]{3,2,1,0:T(8,128)S(1)}, f32[2,2,16,128]{3,2,1,0:T(8,128)S(1)}, ...), branch_computations={%region_9.0_spmd, %region_10.0_spmd} | conditional | flops 19365888 | bytes 7598608 | solution.py:167
  74.1 0.5 fusion.15
  74.6 0.4 copy.129
  75.0 0.4 copy.128
  75.4 0.3 add_multiply_fusion.2
  76.1 4.6 %collective-permute-start.12 = (f32[20,1,16,128]{3,2,1,0:T(8,128)S(1)}, f32[20,1,16,128]{3,2,1,0:T(8,128)S(1)}, u32[]{:S(2)}, u32[]{:S(2)}) collective-permute-start(f32[20,1,16,128]{3,2,1,0:T(8,128)S(1)} %get-tuple-element.458), channel_id=1, source_target_pairs={{0,32},{32,64},{64,96},{96,128},{128,160},{160,192},{192,224},{224... | collective-permute-start | bytes 491528 | tf_op jit(solution)/shard_map/ppermute | solution.py:25
  80.7 1.9 %collective-permute-start.13 = (f32[20,1,16,128]{3,2,1,0:T(8,128)S(1)}, f32[20,1,16,128]{3,2,1,0:T(8,128)S(1)}, u32[]{:S(2)}, u32[]{:S(2)}) collective-permute-start(f32[20,1,16,128]{3,2,1,0:T(8,128)S(1)} %get-tuple-element.457), channel_id=1, source_target_pairs={{32,0},{64,32},{96,64},{128,96},{160,128},{192,160},{224,192},{256... | collective-permute-start | bytes 491528 | tf_op jit(solution)/shard_map/ppermute | solution.py:26
  82.6 0.9 collective-permute-done.12
  83.6 5.6 %collective-permute-done.13 = f32[20,1,16,128]{3,2,1,0:T(8,128)S(1)} collective-permute-done((f32[20,1,16,128]{3,2,1,0:T(8,128)S(1)}, f32[20,1,16,128]{3,2,1,0:T(8,128)S(1)}, u32[]{:S(2)}, u32[]{:S(2)}) %collective-permute-start.13) | collective-permute-done | bytes 163872 | tf_op jit(solution)/shard_map/ppermute | solution.py:26
  89.2 1.9 %collective-permute-start.14 = (f32[20,4,1,128]{3,2,1,0:T(1,128)S(1)}, f32[20,4,1,128]{3,2,1,0:T(1,128)S(1)}, u32[]{:S(2)}, u32[]{:S(2)}) collective-permute-start(f32[20,4,1,128]{3,2,1,0:T(1,128)S(1)} %get-tuple-element.447), channel_id=1, source_target_pairs={{0,1},{1,2},{2,3},{3,4},{4,5},{5,6},{6,7},{7,8},{8,9},{9,10},{10,1... | collective-permute-start | bytes 122888 | tf_op jit(solution)/shard_map/ppermute | solution.py:25
  91.1 5.8 %collective-permute-start.15 = (f32[20,4,1,128]{3,2,1,0:T(1,128)S(1)}, f32[20,4,1,128]{3,2,1,0:T(1,128)S(1)}, u32[]{:S(2)}, u32[]{:S(2)}) collective-permute-start(f32[20,4,1,128]{3,2,1,0:T(1,128)S(1)} %get-tuple-element.448), channel_id=1, source_target_pairs={{1,0},{2,1},{3,2},{4,3},{5,4},{6,5},{7,6},{8,7},{9,8},{10,9},{11,1... | collective-permute-start | bytes 122888 | tf_op jit(solution)/shard_map/ppermute | solution.py:26
  96.9 1.6 %collective-permute-done.15 = f32[20,4,1,128]{3,2,1,0:T(1,128)S(1)} collective-permute-done((f32[20,4,1,128]{3,2,1,0:T(1,128)S(1)}, f32[20,4,1,128]{3,2,1,0:T(1,128)S(1)}, u32[]{:S(2)}, u32[]{:S(2)}) %collective-permute-start.15) | collective-permute-done | bytes 40992 | tf_op jit(solution)/shard_map/ppermute | solution.py:26
  98.7 2.0 %conditional.11 = (f32[20,2,16,128]{3,2,1,0:T(8,128)S(1)}, f32[2,2,16,128]{3,1,2,0:T(2,128)S(1)}) conditional(s32[]{:T(128)} %convert_element_type.24, (f32[2,16,128]{2,1,0:T(8,128)S(1)}, f32[20,4,16,128]{3,2,1,0:T(8,128)S(1)}, f32[20,4,18,128]{3,2,1,0:T(8,128)S(1)}, f32[20,2,16,128]{3,2,1,0:T(8,128)S(1)}, f32[2,2,16,128]{3,2,1,0:T(8,128)S(1)}, ...), branch_computations={%region_12.0_spmd, %region_13.0_spmd} | conditional | flops 19365888 | bytes 7598608 | solution.py:167
  98.9 0.5 fusion.22
  99.5 0.4 copy.132
  99.9 0.4 copy.131
  100.3 0.3 add_multiply_fusion.3
  100.7 3.9 %collective-permute-start.16 = (f32[20,1,16,128]{3,2,1,0:T(8,128)S(1)}, f32[20,1,16,128]{3,2,1,0:T(8,128)S(1)}, u32[]{:S(2)}, u32[]{:S(2)}) collective-permute-start(f32[20,1,16,128]{3,2,1,0:T(8,128)S(1)} %get-tuple-element.456), channel_id=1, source_target_pairs={{0,32},{32,64},{64,96},{96,128},{128,160},{160,192},{192,224},{224... | collective-permute-start | bytes 491528 | tf_op jit(solution)/shard_map/ppermute | solution.py:25
  104.7 1.9 %collective-permute-start.17 = (f32[20,1,16,128]{3,2,1,0:T(8,128)S(1)}, f32[20,1,16,128]{3,2,1,0:T(8,128)S(1)}, u32[]{:S(2)}, u32[]{:S(2)}) collective-permute-start(f32[20,1,16,128]{3,2,1,0:T(8,128)S(1)} %get-tuple-element.455), channel_id=1, source_target_pairs={{32,0},{64,32},{96,64},{128,96},{160,128},{192,160},{224,192},{256... | collective-permute-start | bytes 491528 | tf_op jit(solution)/shard_map/ppermute | solution.py:26
  106.9 1.3 collective-permute-start.21
  108.2 4.6 %collective-permute-done.17 = f32[20,1,16,128]{3,2,1,0:T(8,128)S(1)} collective-permute-done((f32[20,1,16,128]{3,2,1,0:T(8,128)S(1)}, f32[20,1,16,128]{3,2,1,0:T(8,128)S(1)}, u32[]{:S(2)}, u32[]{:S(2)}) %collective-permute-start.17) | collective-permute-done | bytes 163872 | tf_op jit(solution)/shard_map/ppermute | solution.py:26
  112.9 1.9 %collective-permute-start.18 = (f32[20,4,1,128]{3,2,1,0:T(1,128)S(1)}, f32[20,4,1,128]{3,2,1,0:T(1,128)S(1)}, u32[]{:S(2)}, u32[]{:S(2)}) collective-permute-start(f32[20,4,1,128]{3,2,1,0:T(1,128)S(1)} %get-tuple-element.445), channel_id=1, source_target_pairs={{0,1},{1,2},{2,3},{3,4},{4,5},{5,6},{6,7},{7,8},{8,9},{9,10},{10,1... | collective-permute-start | bytes 122888 | tf_op jit(solution)/shard_map/ppermute | solution.py:25
  114.8 5.8 %collective-permute-start.19 = (f32[20,4,1,128]{3,2,1,0:T(1,128)S(1)}, f32[20,4,1,128]{3,2,1,0:T(1,128)S(1)}, u32[]{:S(2)}, u32[]{:S(2)}) collective-permute-start(f32[20,4,1,128]{3,2,1,0:T(1,128)S(1)} %get-tuple-element.446), channel_id=1, source_target_pairs={{1,0},{2,1},{3,2},{4,3},{5,4},{6,5},{7,6},{8,7},{9,8},{10,9},{11,1... | collective-permute-start | bytes 122888 | tf_op jit(solution)/shard_map/ppermute | solution.py:26
  120.6 1.3 collective-permute-start.20
  121.9 0.3 collective-permute-done.19
  122.4 5.5 %collective-permute-done.20 = f32[2,2,16,128]{3,2,1,0:T(8,128)S(1)} collective-permute-done((f32[2,2,16,128]{3,2,1,0:T(8,128)S(1)}, f32[2,2,16,128]{3,2,1,0:T(8,128)S(1)}, u32[]{:S(2)}, u32[]{:S(2)}) %collective-permute-start.20) | collective-permute-done | bytes 32800 | tf_op jit(solution)/shard_map/ppermute | solution.py:34
  127.9 2.0 %conditional.13 = (f32[1,20,2,16,128]{4,3,2,1,0:T(8,128)S(1)}) conditional(s32[]{:T(128)} %convert_element_type.24, (f32[2,16,128]{2,1,0:T(8,128)S(1)}, f32[20,4,16,128]{3,2,1,0:T(8,128)S(1)}, f32[20,4,18,128]{3,2,1,0:T(8,128)S(1)}, f32[20,2,16,128]{3,2,1,0:T(8,128)S(1)}, f32[2,2,16,128]{3,2,1,0:T(8,128)S(1)}, /*index=5*/f32[19]{0:T(128)S(1)}, ...), branch_computations={%region_17.18_spmd, %region_18.19_spmd} | conditional | flops 19365888 | bytes 7598600 | solution.py:167
  128.1 0.5 fusion.48
  128.7 0.4 copy.137
  129.1 0.4 copy.136
  129.9 0.7 copy-done.1
  (74 shorter events, 4.4 us)
Async XLA Ops:
  0.0 0.8 copy-start.2
  2.0 7.8 %collective-permute-start = (f32[20,1,16,128]{3,2,1,0:T(8,128)S(1)}, f32[20,1,16,128]{3,2,1,0:T(8,128)S(1)}, u32[]{:S(2)}, u32[]{:S(2)}) collective-permute-start(f32[20,1,16,128]{3,2,1,0:T(8,128)S(1)} %get-tuple-element.463), channel_id=1, source_target_pairs={{0,32},{32,64},{64,96},{96,128},{128,160},{160,192},{192,224},{224... | collective-permute-start | bytes 491528 | tf_op jit(solution)/shard_map/ppermute | solution.py:25
  6.3 8.2 %collective-permute-start.1 = (f32[20,1,16,128]{3,2,1,0:T(8,128)S(1)}, f32[20,1,16,128]{3,2,1,0:T(8,128)S(1)}, u32[]{:S(2)}, u32[]{:S(2)}) collective-permute-start(f32[20,1,16,128]{3,2,1,0:T(8,128)S(1)} %get-tuple-element.464), channel_id=1, source_target_pairs={{32,0},{64,32},{96,64},{128,96},{160,128},{192,160},{224,192},{256... | collective-permute-start | bytes 491528 | tf_op jit(solution)/shard_map/ppermute | solution.py:26
  14.7 7.7 %copy-start.4 = (s32[19]{0:T(128)S(1)}, s32[19]{0:T(128)}, u32[]{:S(2)}) copy-start(s32[19]{0:T(128)} %param.22) | copy-start | bytes 232
  14.7 7.8 %collective-permute-start.2 = (f32[20,4,1,128]{3,2,1,0:T(1,128)S(1)}, f32[20,4,1,128]{3,2,1,0:T(1,128)S(1)}, u32[]{:S(2)}, u32[]{:S(2)}) collective-permute-start(f32[20,4,1,128]{3,2,1,0:T(1,128)S(1)} %get-tuple-element.453), channel_id=1, source_target_pairs={{0,1},{1,2},{2,3},{3,4},{4,5},{5,6},{6,7},{7,8},{8,9},{9,10},{10,1... | collective-permute-start | bytes 122888 | tf_op jit(solution)/shard_map/ppermute | solution.py:25
  16.6 7.4 %collective-permute-start.3 = (f32[20,4,1,128]{3,2,1,0:T(1,128)S(1)}, f32[20,4,1,128]{3,2,1,0:T(1,128)S(1)}, u32[]{:S(2)}, u32[]{:S(2)}) collective-permute-start(f32[20,4,1,128]{3,2,1,0:T(1,128)S(1)} %get-tuple-element.454), channel_id=1, source_target_pairs={{1,0},{2,1},{3,2},{4,3},{5,4},{6,5},{7,6},{8,7},{9,8},{10,9},{11,1... | collective-permute-start | bytes 122888 | tf_op jit(solution)/shard_map/ppermute | solution.py:26
  22.4 1.7 %copy-start = (f32[2,2,16,128]{3,2,1,0:T(8,128)S(1)}, f32[2,2,16,128]{3,2,1,0:T(8,128)}, u32[]{:S(2)}) copy-start(f32[2,2,16,128]{3,2,1,0:T(8,128)} %param.21) | copy-start | bytes 98308
  24.2 0.7 copy-start.3
  26.9 8.3 %collective-permute-start.4 = (f32[20,1,16,128]{3,2,1,0:T(8,128)S(1)}, f32[20,1,16,128]{3,2,1,0:T(8,128)S(1)}, u32[]{:S(2)}, u32[]{:S(2)}) collective-permute-start(f32[20,1,16,128]{3,2,1,0:T(8,128)S(1)} %get-tuple-element.462), channel_id=1, source_target_pairs={{0,32},{32,64},{64,96},{96,128},{128,160},{160,192},{192,224},{224... | collective-permute-start | bytes 491528 | tf_op jit(solution)/shard_map/ppermute | solution.py:25
  32.4 8.1 %collective-permute-start.5 = (f32[20,1,16,128]{3,2,1,0:T(8,128)S(1)}, f32[20,1,16,128]{3,2,1,0:T(8,128)S(1)}, u32[]{:S(2)}, u32[]{:S(2)}) collective-permute-start(f32[20,1,16,128]{3,2,1,0:T(8,128)S(1)} %get-tuple-element.461), channel_id=1, source_target_pairs={{32,0},{64,32},{96,64},{128,96},{160,128},{192,160},{224,192},{256... | collective-permute-start | bytes 491528 | tf_op jit(solution)/shard_map/ppermute | solution.py:26
  40.6 7.7 %collective-permute-start.6 = (f32[20,4,1,128]{3,2,1,0:T(1,128)S(1)}, f32[20,4,1,128]{3,2,1,0:T(1,128)S(1)}, u32[]{:S(2)}, u32[]{:S(2)}) collective-permute-start(f32[20,4,1,128]{3,2,1,0:T(1,128)S(1)} %get-tuple-element.451), channel_id=1, source_target_pairs={{0,1},{1,2},{2,3},{3,4},{4,5},{5,6},{6,7},{7,8},{8,9},{9,10},{10,1... | collective-permute-start | bytes 122888 | tf_op jit(solution)/shard_map/ppermute | solution.py:25
  42.5 7.4 %collective-permute-start.7 = (f32[20,4,1,128]{3,2,1,0:T(1,128)S(1)}, f32[20,4,1,128]{3,2,1,0:T(1,128)S(1)}, u32[]{:S(2)}, u32[]{:S(2)}) collective-permute-start(f32[20,4,1,128]{3,2,1,0:T(1,128)S(1)} %get-tuple-element.452), channel_id=1, source_target_pairs={{1,0},{2,1},{3,2},{4,3},{5,4},{6,5},{7,6},{8,7},{9,8},{10,9},{11,1... | collective-permute-start | bytes 122888 | tf_op jit(solution)/shard_map/ppermute | solution.py:26
  52.1 7.2 %collective-permute-start.8 = (f32[20,1,16,128]{3,2,1,0:T(8,128)S(1)}, f32[20,1,16,128]{3,2,1,0:T(8,128)S(1)}, u32[]{:S(2)}, u32[]{:S(2)}) collective-permute-start(f32[20,1,16,128]{3,2,1,0:T(8,128)S(1)} %get-tuple-element.460), channel_id=1, source_target_pairs={{0,32},{32,64},{64,96},{96,128},{128,160},{160,192},{192,224},{224... | collective-permute-start | bytes 491528 | tf_op jit(solution)/shard_map/ppermute | solution.py:25
  56.0 8.2 %collective-permute-start.9 = (f32[20,1,16,128]{3,2,1,0:T(8,128)S(1)}, f32[20,1,16,128]{3,2,1,0:T(8,128)S(1)}, u32[]{:S(2)}, u32[]{:S(2)}) collective-permute-start(f32[20,1,16,128]{3,2,1,0:T(8,128)S(1)} %get-tuple-element.459), channel_id=1, source_target_pairs={{32,0},{64,32},{96,64},{128,96},{160,128},{192,160},{224,192},{256... | collective-permute-start | bytes 491528 | tf_op jit(solution)/shard_map/ppermute | solution.py:26
  64.3 7.7 %collective-permute-start.10 = (f32[20,4,1,128]{3,2,1,0:T(1,128)S(1)}, f32[20,4,1,128]{3,2,1,0:T(1,128)S(1)}, u32[]{:S(2)}, u32[]{:S(2)}) collective-permute-start(f32[20,4,1,128]{3,2,1,0:T(1,128)S(1)} %get-tuple-element.449), channel_id=1, source_target_pairs={{0,1},{1,2},{2,3},{3,4},{4,5},{5,6},{6,7},{7,8},{8,9},{9,10},{10,1... | collective-permute-start | bytes 122888 | tf_op jit(solution)/shard_map/ppermute | solution.py:25
  66.3 7.4 %collective-permute-start.11 = (f32[20,4,1,128]{3,2,1,0:T(1,128)S(1)}, f32[20,4,1,128]{3,2,1,0:T(1,128)S(1)}, u32[]{:S(2)}, u32[]{:S(2)}) collective-permute-start(f32[20,4,1,128]{3,2,1,0:T(1,128)S(1)} %get-tuple-element.450), channel_id=1, source_target_pairs={{1,0},{2,1},{3,2},{4,3},{5,4},{6,5},{7,6},{8,7},{9,8},{10,9},{11,1... | collective-permute-start | bytes 122888 | tf_op jit(solution)/shard_map/ppermute | solution.py:26
  76.1 7.5 %collective-permute-start.12 = (f32[20,1,16,128]{3,2,1,0:T(8,128)S(1)}, f32[20,1,16,128]{3,2,1,0:T(8,128)S(1)}, u32[]{:S(2)}, u32[]{:S(2)}) collective-permute-start(f32[20,1,16,128]{3,2,1,0:T(8,128)S(1)} %get-tuple-element.458), channel_id=1, source_target_pairs={{0,32},{32,64},{64,96},{96,128},{128,160},{160,192},{192,224},{224... | collective-permute-start | bytes 491528 | tf_op jit(solution)/shard_map/ppermute | solution.py:25
  80.7 8.4 %collective-permute-start.13 = (f32[20,1,16,128]{3,2,1,0:T(8,128)S(1)}, f32[20,1,16,128]{3,2,1,0:T(8,128)S(1)}, u32[]{:S(2)}, u32[]{:S(2)}) collective-permute-start(f32[20,1,16,128]{3,2,1,0:T(8,128)S(1)} %get-tuple-element.457), channel_id=1, source_target_pairs={{32,0},{64,32},{96,64},{128,96},{160,128},{192,160},{224,192},{256... | collective-permute-start | bytes 491528 | tf_op jit(solution)/shard_map/ppermute | solution.py:26
  89.2 7.7 %collective-permute-start.14 = (f32[20,4,1,128]{3,2,1,0:T(1,128)S(1)}, f32[20,4,1,128]{3,2,1,0:T(1,128)S(1)}, u32[]{:S(2)}, u32[]{:S(2)}) collective-permute-start(f32[20,4,1,128]{3,2,1,0:T(1,128)S(1)} %get-tuple-element.447), channel_id=1, source_target_pairs={{0,1},{1,2},{2,3},{3,4},{4,5},{5,6},{6,7},{7,8},{8,9},{9,10},{10,1... | collective-permute-start | bytes 122888 | tf_op jit(solution)/shard_map/ppermute | solution.py:25
  91.1 7.4 %collective-permute-start.15 = (f32[20,4,1,128]{3,2,1,0:T(1,128)S(1)}, f32[20,4,1,128]{3,2,1,0:T(1,128)S(1)}, u32[]{:S(2)}, u32[]{:S(2)}) collective-permute-start(f32[20,4,1,128]{3,2,1,0:T(1,128)S(1)} %get-tuple-element.448), channel_id=1, source_target_pairs={{1,0},{2,1},{3,2},{4,3},{5,4},{6,5},{7,6},{8,7},{9,8},{10,9},{11,1... | collective-permute-start | bytes 122888 | tf_op jit(solution)/shard_map/ppermute | solution.py:26
  100.7 7.4 %collective-permute-start.16 = (f32[20,1,16,128]{3,2,1,0:T(8,128)S(1)}, f32[20,1,16,128]{3,2,1,0:T(8,128)S(1)}, u32[]{:S(2)}, u32[]{:S(2)}) collective-permute-start(f32[20,1,16,128]{3,2,1,0:T(8,128)S(1)} %get-tuple-element.456), channel_id=1, source_target_pairs={{0,32},{32,64},{64,96},{96,128},{128,160},{160,192},{192,224},{224... | collective-permute-start | bytes 491528 | tf_op jit(solution)/shard_map/ppermute | solution.py:25
  104.7 8.1 %collective-permute-start.17 = (f32[20,1,16,128]{3,2,1,0:T(8,128)S(1)}, f32[20,1,16,128]{3,2,1,0:T(8,128)S(1)}, u32[]{:S(2)}, u32[]{:S(2)}) collective-permute-start(f32[20,1,16,128]{3,2,1,0:T(8,128)S(1)} %get-tuple-element.455), channel_id=1, source_target_pairs={{32,0},{64,32},{96,64},{128,96},{160,128},{192,160},{224,192},{256... | collective-permute-start | bytes 491528 | tf_op jit(solution)/shard_map/ppermute | solution.py:26
  106.9 15.6 %collective-permute-start.21 = (f32[1,2,16,128]{3,1,2,0:T(2,128)S(1)}, f32[1,2,16,128]{3,1,2,0:T(2,128)S(1)}, u32[]{:S(2)}, u32[]{:S(2)}) collective-permute-start(f32[1,2,16,128]{3,1,2,0:T(2,128)S(1)} %bitcast.185), channel_id=1, source_target_pairs={{512,0},{513,1},{514,2},{515,3},{516,4},{517,5},{518,6},{519,7},{5... | collective-permute-start | bytes 49160 | tf_op jit(solution)/shard_map/ppermute | solution.py:34
  112.9 9.0 %collective-permute-start.18 = (f32[20,4,1,128]{3,2,1,0:T(1,128)S(1)}, f32[20,4,1,128]{3,2,1,0:T(1,128)S(1)}, u32[]{:S(2)}, u32[]{:S(2)}) collective-permute-start(f32[20,4,1,128]{3,2,1,0:T(1,128)S(1)} %get-tuple-element.445), channel_id=1, source_target_pairs={{0,1},{1,2},{2,3},{3,4},{4,5},{5,6},{6,7},{7,8},{8,9},{9,10},{10,1... | collective-permute-start | bytes 122888 | tf_op jit(solution)/shard_map/ppermute | solution.py:25
  114.8 7.4 %collective-permute-start.19 = (f32[20,4,1,128]{3,2,1,0:T(1,128)S(1)}, f32[20,4,1,128]{3,2,1,0:T(1,128)S(1)}, u32[]{:S(2)}, u32[]{:S(2)}) collective-permute-start(f32[20,4,1,128]{3,2,1,0:T(1,128)S(1)} %get-tuple-element.446), channel_id=1, source_target_pairs={{1,0},{2,1},{3,2},{4,3},{5,4},{6,5},{7,6},{8,7},{9,8},{10,9},{11,1... | collective-permute-start | bytes 122888 | tf_op jit(solution)/shard_map/ppermute | solution.py:26
  120.6 7.3 %collective-permute-start.20 = (f32[2,2,16,128]{3,2,1,0:T(8,128)S(1)}, f32[2,2,16,128]{3,2,1,0:T(8,128)S(1)}, u32[]{:S(2)}, u32[]{:S(2)}) collective-permute-start(f32[2,2,16,128]{3,2,1,0:T(8,128)S(1)} %copy_multiply_fusion), channel_id=1, source_target_pairs={{0,512},{1,513},{2,514},{3,515},{4,516},{5,517},{6,518},{7,519},{8... | collective-permute-start | bytes 98312 | tf_op jit(solution)/shard_map/ppermute | solution.py:34
  129.9 0.7 copy-start.1
where the time goes:
time: 131 us
  starting transfers between devices  72.8 us (56%)
  waiting for transfers between devices  41.7 us (32%)
  local copies, waits for them, and re-layouts  7.7 us (6%)
  other arithmetic  4.59 us (4%)
  matrix products  2.7 us (2%)
    ppermute x10, starting transfers between devices, extended_2(): after = lax.ppermute(leading, axis, down)  38.4 us
    ppermute x10, starting transfers between devices, extended_2(): before = lax.ppermute(last, axis, up)  31.9 us
    ppermute x10, waiting for transfers between devices, extended_2(): after = lax.ppermute(leading, axis, down)  31.8 us
    ppermute x2, waiting for transfers between devices, from_behind(): return lax.ppermute(shard, axis, pairs)  5.5 us
    another operation x19, local copies, waits for them, and re-layouts  5.39 us
    ppermute x10, waiting for transfers between devices, extended_2(): before = lax.ppermute(last, axis, up)  4.45 us
  transfers between devices with their start and end apart: 22, of which 15 were waited for; matrix products, arithmetic and copies ran while one was open for 1% of the time, Pallas kernels for 0%

commit v1 on v0

--- a/solution.py
+++ b/solution.py
@@ -16,16 +16,21 @@
 
 
 def extended_2(shard, sides, width):
+    pieces = []
     for axis, dim in sides:
         peers, length = (lax.axis_size(axis), shard.shape[dim])
         up = [(i, (i + 1) % peers) for i in range(peers - 1)]
         down = [(j, i) for i, j in up]
         last = lax.slice_in_dim(shard, length - width, length, axis=dim)
         leading = lax.slice_in_dim(shard, 0, width, axis=dim)
-        before = lax.ppermute(last, axis, up)
-        after = lax.ppermute(leading, axis, down)
-        shard = jnp.concatenate([before, shard, after], axis=dim)
-    return shard
+        pieces.append((dim, lax.ppermute(last, axis, up), lax.ppermute(leading, axis, down)))
+    (dx, xb, xa), (dy, yb, ya) = pieces
+    out = jnp.concatenate([xb, shard, xa], axis=dx)
+    pad = [(0, 0)] * shard.ndim
+    pad[dx] = (width, width)
+    yb = jnp.pad(yb, pad)
+    ya = jnp.pad(ya, pad)
+    return jnp.concatenate([yb, out, ya], axis=dy)
 
 
 def from_behind(shard, axis, by):
@@ -220,8 +225,10 @@
         lambda: jnp.zeros((size_x, size_y, depth), jnp.float32),
         lambda: absorption(own_block, wet_coarse, above_table),
     )
-    flux_arrived = from_behind(new_flux, "half", 1)
-    light_arrived = from_behind(absorbed[None], "half", -1)
+    outgoing = jnp.where(is_ocean, new_flux, jnp.broadcast_to(absorbed[None], new_flux.shape))
+    arrived = lax.ppermute(outgoing, "half", [(0, 1), (1, 0)])
+    flux_arrived = arrived
+    light_arrived = arrived[0:1]
     heating = HEATING * to_fine(jnp.broadcast_to(light_arrived, (4, size_x, size_y, depth)))[0]
     extended = rim_single(own_block)
     own_block, running = advance(

time: 131 us -> 105 us (0.80)
  the two profiles are of different devices: /device:TPU:100 before, /device:TPU:219 now
where the time goes in v1:
time: 105 us; the launch traced here: 104 us
  starting transfers between devices  65.3 us (62%)
  waiting for transfers between devices  24.5 us (23%)
  local copies, waits for them, and re-layouts  7.21 us (7%)
  other arithmetic  5.63 us (5%)
    ppermute x10, starting transfers between devices, extended_2(): lax.ppermute(last, axis, up)  39.6 us
    ppermute x10, waiting for transfers between devices, extended_2(): lax.ppermute(leading, axis, down)  24.5 us
    ppermute x10, starting transfers between devices, extended_2(): lax.ppermute(leading, axis, down)  19.8 us
    ppermute x1, starting transfers between devices, body(): arrived = lax.ppermute(outgoing, 'half', [(0, 1), (1, 0)])  5.98 us
    reshape x5, local copies, waits for them, and re-layouts, to_fine(): coarse.reshape(fields, 2, 2, size_x, size_y, depth)  2.85 us
    unnamed x18, local copies, waits for them, and re-layouts  2.79 us
    mul x5, other arithmetic, ocean_substep(): return wet_mask * (centre + DT * (NU * spread - advect + forcing))  2.5 us
  transfers between devices with their start and end apart: 21, of which 9 were waited for; matrix products, arithmetic and copies ran while one was open for 1% of the time, Pallas kernels for 0%

profile of v1, /device:TPU:219, one launch (start us, length us, event | category | flops | bytes accessed | tf_op | source)
XLA Modules:
  0.0 103.8 jit_solution(2738446270880965492)
XLA Ops:
  0.0 0.7 copy-done.2
  0.7 0.1 fusion.51
  0.9 1.0 bitcast_multiply_fusion
  2.0 5.2 %collective-permute-start = (f32[20,1,16,128]{3,2,1,0:T(8,128)S(1)}, f32[20,1,16,128]{3,2,1,0:T(8,128)S(1)}, u32[]{:S(2)}, u32[]{:S(2)}) collective-permute-start(f32[20,1,16,128]{3,2,1,0:T(8,128)S(1)} %get-tuple-element.464), channel_id=1, source_target_pairs={{0,32},{32,64},{64,96},{96,128},{128,160},{160,192},{192,224},{224... | collective-permute-start | bytes 491528 | tf_op jit(solution)/shard_map/ppermute | solution.py:26
  7.2 1.9 %collective-permute-start.1 = (f32[20,1,16,128]{3,2,1,0:T(8,128)S(1)}, f32[20,1,16,128]{3,2,1,0:T(8,128)S(1)}, u32[]{:S(2)}, u32[]{:S(2)}) collective-permute-start(f32[20,1,16,128]{3,2,1,0:T(8,128)S(1)} %get-tuple-element.465), channel_id=1, source_target_pairs={{32,0},{64,32},{96,64},{128,96},{160,128},{192,160},{224,192},{256... | collective-permute-start | bytes 491528 | tf_op jit(solution)/shard_map/ppermute | solution.py:26
  9.1 5.2 %collective-permute-start.2 = (f32[20,2,1,128]{3,2,1,0:T(1,128)S(1)}, f32[20,2,1,128]{3,2,1,0:T(1,128)S(1)}, u32[]{:S(2)}, u32[]{:S(2)}) collective-permute-start(f32[20,2,1,128]{3,2,1,0:T(1,128)S(1)} %get-tuple-element.462), channel_id=1, source_target_pairs={{0,1},{1,2},{2,3},{3,4},{4,5},{5,6},{6,7},{7,8},{8,9},{9,10},{10,1... | collective-permute-start | bytes 61448 | tf_op jit(solution)/shard_map/ppermute | solution.py:26
  14.4 1.9 %collective-permute-start.3 = (f32[20,2,1,128]{3,2,1,0:T(1,128)S(1)}, f32[20,2,1,128]{3,2,1,0:T(1,128)S(1)}, u32[]{:S(2)}, u32[]{:S(2)}) collective-permute-start(f32[20,2,1,128]{3,2,1,0:T(1,128)S(1)} %get-tuple-element.463), channel_id=1, source_target_pairs={{1,0},{2,1},{3,2},{4,3},{5,4},{6,5},{7,6},{8,7},{9,8},{10,9},{11,1... | collective-permute-start | bytes 61448 | tf_op jit(solution)/shard_map/ppermute | solution.py:26
  16.3 0.1 copy.148
  16.4 0.1 reshape.128
  16.5 0.1 fusion.52
  16.6 0.5 copy-done.4
  17.3 4.3 %collective-permute-done.3 = f32[20,2,1,128]{3,2,1,0:T(1,128)S(1)} collective-permute-done((f32[20,2,1,128]{3,2,1,0:T(1,128)S(1)}, f32[20,2,1,128]{3,2,1,0:T(1,128)S(1)}, u32[]{:S(2)}, u32[]{:S(2)}) %collective-permute-start.3) | collective-permute-done | bytes 20512 | tf_op jit(solution)/shard_map/ppermute | solution.py:26
  21.6 0.2 select_maximum_fusion.8
  21.8 0.7 copy-done
  22.5 1.5 %conditional.8 = (f32[20,2,16,128]{3,2,1,0:T(8,128)S(1)}, f32[2,2,16,128]{3,1,2,0:T(2,128)S(1)}) conditional(s32[]{:T(128)} %convert_element_type.35, (f32[2,16,128]{2,1,0:T(8,128)S(1)}, f32[20,4,16,128]{3,2,1,0:T(8,128)S(1)}, f32[20,4,18,128]{3,2,1,0:T(8,128)S(1)}, f32[20,2,16,128]{3,2,1,0:T(8,128)S(1)}, f32[2,2,16,128]{3,2,1,0:T(8,128)S(1)}, ...), branch_computations={%region_3.4_spmd, %region_4.6_spmd} | conditional | flops 19365888 | bytes 7631380 | solution.py:172
  22.5 0.6 copy.105
  23.2 0.1 pad.48.clone
  23.3 0.5 fusion.6
  23.9 0.1 reduce_sum.32
  24.1 4.9 %collective-permute-start.4 = (f32[20,1,16,128]{3,2,1,0:T(8,128)S(1)}, f32[20,1,16,128]{3,2,1,0:T(8,128)S(1)}, u32[]{:S(2)}, u32[]{:S(2)}) collective-permute-start(f32[20,1,16,128]{3,2,1,0:T(8,128)S(1)} %get-tuple-element.461), channel_id=1, source_target_pairs={{0,32},{32,64},{64,96},{96,128},{128,160},{160,192},{192,224},{224... | collective-permute-start | bytes 491528 | tf_op jit(solution)/shard_map/ppermute | solution.py:26
  29.0 1.9 %collective-permute-start.5 = (f32[20,1,16,128]{3,2,1,0:T(8,128)S(1)}, f32[20,1,16,128]{3,2,1,0:T(8,128)S(1)}, u32[]{:S(2)}, u32[]{:S(2)}) collective-permute-start(f32[20,1,16,128]{3,2,1,0:T(8,128)S(1)} %get-tuple-element.460), channel_id=1, source_target_pairs={{32,0},{64,32},{96,64},{128,96},{160,128},{192,160},{224,192},{256... | collective-permute-start | bytes 491528 | tf_op jit(solution)/shard_map/ppermute | solution.py:26
  30.9 2.2 %collective-permute-start.6 = (f32[20,2,1,128]{3,2,1,0:T(1,128)S(1)}, f32[20,2,1,128]{3,2,1,0:T(1,128)S(1)}, u32[]{:S(2)}, u32[]{:S(2)}) collective-permute-start(f32[20,2,1,128]{3,2,1,0:T(1,128)S(1)} %get-tuple-element.458), channel_id=1, source_target_pairs={{0,1},{1,2},{2,3},{3,4},{4,5},{5,6},{6,7},{7,8},{8,9},{9,10},{10,1... | collective-permute-start | bytes 61448 | tf_op jit(solution)/shard_map/ppermute | solution.py:26
  33.1 2.1 %collective-permute-start.7 = (f32[20,2,1,128]{3,2,1,0:T(1,128)S(1)}, f32[20,2,1,128]{3,2,1,0:T(1,128)S(1)}, u32[]{:S(2)}, u32[]{:S(2)}) collective-permute-start(f32[20,2,1,128]{3,2,1,0:T(1,128)S(1)} %get-tuple-element.459), channel_id=1, source_target_pairs={{1,0},{2,1},{3,2},{4,3},{5,4},{6,5},{7,6},{8,7},{9,8},{10,9},{11,1... | collective-permute-start | bytes 61448 | tf_op jit(solution)/shard_map/ppermute | solution.py:26
  35.3 0.9 collective-permute-done.5
  36.3 4.1 %collective-permute-done.7 = f32[20,2,1,128]{3,2,1,0:T(1,128)S(1)} collective-permute-done((f32[20,2,1,128]{3,2,1,0:T(1,128)S(1)}, f32[20,2,1,128]{3,2,1,0:T(1,128)S(1)}, u32[]{:S(2)}, u32[]{:S(2)}) %collective-permute-start.7) | collective-permute-done | bytes 20512 | tf_op jit(solution)/shard_map/ppermute | solution.py:26
  40.3 0.2 select_maximum_fusion.6
  40.5 1.6 %conditional.9 = (f32[20,2,16,128]{3,2,1,0:T(8,128)S(1)}, f32[2,2,16,128]{3,1,2,0:T(2,128)S(1)}) conditional(s32[]{:T(128)} %convert_element_type.35, (f32[2,16,128]{2,1,0:T(8,128)S(1)}, f32[20,4,16,128]{3,2,1,0:T(8,128)S(1)}, f32[20,4,18,128]{3,2,1,0:T(8,128)S(1)}, f32[20,2,16,128]{3,2,1,0:T(8,128)S(1)}, f32[2,2,16,128]{3,2,1,0:T(8,128)S(1)}, ...), branch_computations={%region_6.7_spmd, %region_7.9_spmd} | conditional | flops 19365888 | bytes 7598608 | solution.py:172
  40.5 0.6 copy.109
  41.3 0.5 fusion.13
  41.9 0.1 reduce_sum.33
  42.1 4.9 %collective-permute-start.8 = (f32[20,1,16,128]{3,2,1,0:T(8,128)S(1)}, f32[20,1,16,128]{3,2,1,0:T(8,128)S(1)}, u32[]{:S(2)}, u32[]{:S(2)}) collective-permute-start(f32[20,1,16,128]{3,2,1,0:T(8,128)S(1)} %get-tuple-element.457), channel_id=1, source_target_pairs={{0,32},{32,64},{64,96},{96,128},{128,160},{160,192},{192,224},{224... | collective-permute-start | bytes 491528 | tf_op jit(solution)/shard_map/ppermute | solution.py:26
  47.0 1.9 %collective-permute-start.9 = (f32[20,1,16,128]{3,2,1,0:T(8,128)S(1)}, f32[20,1,16,128]{3,2,1,0:T(8,128)S(1)}, u32[]{:S(2)}, u32[]{:S(2)}) collective-permute-start(f32[20,1,16,128]{3,2,1,0:T(8,128)S(1)} %get-tuple-element.456), channel_id=1, source_target_pairs={{32,0},{64,32},{96,64},{128,96},{160,128},{192,160},{224,192},{256... | collective-permute-start | bytes 491528 | tf_op jit(solution)/shard_map/ppermute | solution.py:26
  48.9 2.2 %collective-permute-start.10 = (f32[20,2,1,128]{3,2,1,0:T(1,128)S(1)}, f32[20,2,1,128]{3,2,1,0:T(1,128)S(1)}, u32[]{:S(2)}, u32[]{:S(2)}) collective-permute-start(f32[20,2,1,128]{3,2,1,0:T(1,128)S(1)} %get-tuple-element.454), channel_id=1, source_target_pairs={{0,1},{1,2},{2,3},{3,4},{4,5},{5,6},{6,7},{7,8},{8,9},{9,10},{10,1... | collective-permute-start | bytes 61448 | tf_op jit(solution)/shard_map/ppermute | solution.py:26
  51.2 2.1 %collective-permute-start.11 = (f32[20,2,1,128]{3,2,1,0:T(1,128)S(1)}, f32[20,2,1,128]{3,2,1,0:T(1,128)S(1)}, u32[]{:S(2)}, u32[]{:S(2)}) collective-permute-start(f32[20,2,1,128]{3,2,1,0:T(1,128)S(1)} %get-tuple-element.455), channel_id=1, source_target_pairs={{1,0},{2,1},{3,2},{4,3},{5,4},{6,5},{7,6},{8,7},{9,8},{10,9},{11,1... | collective-permute-start | bytes 61448 | tf_op jit(solution)/shard_map/ppermute | solution.py:26
  53.3 0.9 collective-permute-done.9
  54.3 4.1 %collective-permute-done.11 = f32[20,2,1,128]{3,2,1,0:T(1,128)S(1)} collective-permute-done((f32[20,2,1,128]{3,2,1,0:T(1,128)S(1)}, f32[20,2,1,128]{3,2,1,0:T(1,128)S(1)}, u32[]{:S(2)}, u32[]{:S(2)}) %collective-permute-start.11) | collective-permute-done | bytes 20512 | tf_op jit(solution)/shard_map/ppermute | solution.py:26
  58.4 0.2 select_maximum_fusion.4
  58.5 1.8 %conditional.10 = (f32[20,2,16,128]{3,2,1,0:T(8,128)S(1)}, f32[2,2,16,128]{3,1,2,0:T(2,128)S(1)}) conditional(s32[]{:T(128)} %convert_element_type.35, (f32[2,16,128]{2,1,0:T(8,128)S(1)}, f32[20,4,16,128]{3,2,1,0:T(8,128)S(1)}, f32[20,4,18,128]{3,2,1,0:T(8,128)S(1)}, f32[20,2,16,128]{3,2,1,0:T(8,128)S(1)}, f32[2,2,16,128]{3,2,1,0:T(8,128)S(1)}, ...), branch_computations={%region_9.10_spmd, %region_10.12_spmd} | conditional | flops 19365888 | bytes 7598608 | solution.py:172
  58.7 0.6 copy.113
  59.5 0.5 fusion.20
  60.1 0.1 reduce_sum.34
  60.3 4.9 %collective-permute-start.12 = (f32[20,1,16,128]{3,2,1,0:T(8,128)S(1)}, f32[20,1,16,128]{3,2,1,0:T(8,128)S(1)}, u32[]{:S(2)}, u32[]{:S(2)}) collective-permute-start(f32[20,1,16,128]{3,2,1,0:T(8,128)S(1)} %get-tuple-element.453), channel_id=1, source_target_pairs={{0,32},{32,64},{64,96},{96,128},{128,160},{160,192},{192,224},{224... | collective-permute-start | bytes 491528 | tf_op jit(solution)/shard_map/ppermute | solution.py:26
  65.2 1.9 %collective-permute-start.13 = (f32[20,1,16,128]{3,2,1,0:T(8,128)S(1)}, f32[20,1,16,128]{3,2,1,0:T(8,128)S(1)}, u32[]{:S(2)}, u32[]{:S(2)}) collective-permute-start(f32[20,1,16,128]{3,2,1,0:T(8,128)S(1)} %get-tuple-element.452), channel_id=1, source_target_pairs={{32,0},{64,32},{96,64},{128,96},{160,128},{192,160},{224,192},{256... | collective-permute-start | bytes 491528 | tf_op jit(solution)/shard_map/ppermute | solution.py:26
  67.1 2.2 %collective-permute-start.14 = (f32[20,2,1,128]{3,2,1,0:T(1,128)S(1)}, f32[20,2,1,128]{3,2,1,0:T(1,128)S(1)}, u32[]{:S(2)}, u32[]{:S(2)}) collective-permute-start(f32[20,2,1,128]{3,2,1,0:T(1,128)S(1)} %get-tuple-element.450), channel_id=1, source_target_pairs={{0,1},{1,2},{2,3},{3,4},{4,5},{5,6},{6,7},{7,8},{8,9},{9,10},{10,1... | collective-permute-start | bytes 61448 | tf_op jit(solution)/shard_map/ppermute | solution.py:26
  69.4 2.1 %collective-permute-start.15 = (f32[20,2,1,128]{3,2,1,0:T(1,128)S(1)}, f32[20,2,1,128]{3,2,1,0:T(1,128)S(1)}, u32[]{:S(2)}, u32[]{:S(2)}) collective-permute-start(f32[20,2,1,128]{3,2,1,0:T(1,128)S(1)} %get-tuple-element.451), channel_id=1, source_target_pairs={{1,0},{2,1},{3,2},{4,3},{5,4},{6,5},{7,6},{8,7},{9,8},{10,9},{11,1... | collective-permute-start | bytes 61448 | tf_op jit(solution)/shard_map/ppermute | solution.py:26
  71.5 0.9 collective-permute-done.13
  72.5 4.1 %collective-permute-done.15 = f32[20,2,1,128]{3,2,1,0:T(1,128)S(1)} collective-permute-done((f32[20,2,1,128]{3,2,1,0:T(1,128)S(1)}, f32[20,2,1,128]{3,2,1,0:T(1,128)S(1)}, u32[]{:S(2)}, u32[]{:S(2)}) %collective-permute-start.15) | collective-permute-done | bytes 20512 | tf_op jit(solution)/shard_map/ppermute | solution.py:26
  76.6 0.2 select_maximum_fusion.2
  76.7 1.6 %conditional.11 = (f32[20,2,16,128]{3,2,1,0:T(8,128)S(1)}, f32[2,2,16,128]{3,1,2,0:T(2,128)S(1)}) conditional(s32[]{:T(128)} %convert_element_type.35, (f32[2,16,128]{2,1,0:T(8,128)S(1)}, f32[20,4,16,128]{3,2,1,0:T(8,128)S(1)}, f32[20,4,18,128]{3,2,1,0:T(8,128)S(1)}, f32[20,2,16,128]{3,2,1,0:T(8,128)S(1)}, f32[2,2,16,128]{3,2,1,0:T(8,128)S(1)}, ...), branch_computations={%region_12.13_spmd, %region_13.15_spmd} | conditional | flops 19365888 | bytes 7598608 | solution.py:172
  76.7 0.6 copy.117
  77.6 0.5 fusion.27
  78.2 0.1 reduce_sum.35
  78.4 6.0 %collective-permute-start.20 = (f32[2,2,16,128]{3,1,2,0:T(2,128)S(1)}, f32[2,2,16,128]{3,1,2,0:T(2,128)S(1)}, u32[]{:S(2)}, u32[]{:S(2)}) collective-permute-start(f32[2,2,16,128]{3,1,2,0:T(2,128)S(1)} %multiply_select_fusion), channel_id=1, source_target_pairs={{0,512},{512,0},{1,513},{513,1},{2,514},{514,2},{3,515},{515,3},{4... | collective-permute-start | bytes 98312 | tf_op jit(solution)/shard_map/ppermute | solution.py:229
  84.4 4.9 %collective-permute-start.16 = (f32[20,1,16,128]{3,2,1,0:T(8,128)S(1)}, f32[20,1,16,128]{3,2,1,0:T(8,128)S(1)}, u32[]{:S(2)}, u32[]{:S(2)}) collective-permute-start(f32[20,1,16,128]{3,2,1,0:T(8,128)S(1)} %get-tuple-element.449), channel_id=1, source_target_pairs={{0,32},{32,64},{64,96},{96,128},{128,160},{160,192},{192,224},{224... | collective-permute-start | bytes 491528 | tf_op jit(solution)/shard_map/ppermute | solution.py:26
  89.3 1.9 %collective-permute-start.17 = (f32[20,1,16,128]{3,2,1,0:T(8,128)S(1)}, f32[20,1,16,128]{3,2,1,0:T(8,128)S(1)}, u32[]{:S(2)}, u32[]{:S(2)}) collective-permute-start(f32[20,1,16,128]{3,2,1,0:T(8,128)S(1)} %get-tuple-element.448), channel_id=1, source_target_pairs={{32,0},{64,32},{96,64},{128,96},{160,128},{192,160},{224,192},{256... | collective-permute-start | bytes 491528 | tf_op jit(solution)/shard_map/ppermute | solution.py:26
  91.2 3.1 %collective-permute-start.18 = (f32[20,2,1,128]{3,2,1,0:T(1,128)S(1)}, f32[20,2,1,128]{3,2,1,0:T(1,128)S(1)}, u32[]{:S(2)}, u32[]{:S(2)}) collective-permute-start(f32[20,2,1,128]{3,2,1,0:T(1,128)S(1)} %get-tuple-element.446), channel_id=1, source_target_pairs={{0,1},{1,2},{2,3},{3,4},{4,5},{5,6},{6,7},{7,8},{8,9},{9,10},{10,1... | collective-permute-start | bytes 61448 | tf_op jit(solution)/shard_map/ppermute | solution.py:26
  94.3 1.9 %collective-permute-start.19 = (f32[20,2,1,128]{3,2,1,0:T(1,128)S(1)}, f32[20,2,1,128]{3,2,1,0:T(1,128)S(1)}, u32[]{:S(2)}, u32[]{:S(2)}) collective-permute-start(f32[20,2,1,128]{3,2,1,0:T(1,128)S(1)} %get-tuple-element.447), channel_id=1, source_target_pairs={{1,0},{2,1},{3,2},{4,3},{5,4},{6,5},{7,6},{8,7},{9,8},{10,9},{11,1... | collective-permute-start | bytes 61448 | tf_op jit(solution)/shard_map/ppermute | solution.py:26
  96.3 0.2 collective-permute-done.17
  96.6 5.0 %collective-permute-done.19 = f32[20,2,1,128]{3,2,1,0:T(1,128)S(1)} collective-permute-done((f32[20,2,1,128]{3,2,1,0:T(1,128)S(1)}, f32[20,2,1,128]{3,2,1,0:T(1,128)S(1)}, u32[]{:S(2)}, u32[]{:S(2)}) %collective-permute-start.19) | collective-permute-done | bytes 20512 | tf_op jit(solution)/shard_map/ppermute | solution.py:26
  101.5 0.2 select_maximum_fusion
  101.7 1.4 %conditional.13 = (f32[1,20,2,16,128]{4,3,2,1,0:T(8,128)S(1)}) conditional(s32[]{:T(128)} %convert_element_type.35, (f32[2,16,128]{2,1,0:T(8,128)S(1)}, f32[20,4,16,128]{3,2,1,0:T(8,128)S(1)}, f32[20,4,18,128]{3,2,1,0:T(8,128)S(1)}, f32[20,2,16,128]{3,2,1,0:T(8,128)S(1)}, f32[2,2,16,128]{3,1,2,0:T(2,128)S(1)}, /*index=5*/f32[19]{0:T(128)S(1)}, ...), branch_computations={%region_17.18_spmd, %region_18.19_spmd} | conditional | flops 19365888 | bytes 7664136 | solution.py:172
  101.7 0.6 copy.121
  102.5 0.5 add_multiply_fusion.4
  103.1 0.7 copy-done.1
  (91 shorter events, 2.3 us)
Async XLA Ops:
  0.0 0.7 copy-start.2
  2.0 19.6 %collective-permute-start = (f32[20,1,16,128]{3,2,1,0:T(8,128)S(1)}, f32[20,1,16,128]{3,2,1,0:T(8,128)S(1)}, u32[]{:S(2)}, u32[]{:S(2)}) collective-permute-start(f32[20,1,16,128]{3,2,1,0:T(8,128)S(1)} %get-tuple-element.464), channel_id=1, source_target_pairs={{0,32},{32,64},{64,96},{96,128},{128,160},{160,192},{192,224},{224... | collective-permute-start | bytes 491528 | tf_op jit(solution)/shard_map/ppermute | solution.py:26
  7.2 14.4 %collective-permute-start.1 = (f32[20,1,16,128]{3,2,1,0:T(8,128)S(1)}, f32[20,1,16,128]{3,2,1,0:T(8,128)S(1)}, u32[]{:S(2)}, u32[]{:S(2)}) collective-permute-start(f32[20,1,16,128]{3,2,1,0:T(8,128)S(1)} %get-tuple-element.465), channel_id=1, source_target_pairs={{32,0},{64,32},{96,64},{128,96},{160,128},{192,160},{224,192},{256... | collective-permute-start | bytes 491528 | tf_op jit(solution)/shard_map/ppermute | solution.py:26
  9.1 8.1 %collective-permute-start.2 = (f32[20,2,1,128]{3,2,1,0:T(1,128)S(1)}, f32[20,2,1,128]{3,2,1,0:T(1,128)S(1)}, u32[]{:S(2)}, u32[]{:S(2)}) collective-permute-start(f32[20,2,1,128]{3,2,1,0:T(1,128)S(1)} %get-tuple-element.462), channel_id=1, source_target_pairs={{0,1},{1,2},{2,3},{3,4},{4,5},{5,6},{6,7},{7,8},{8,9},{9,10},{10,1... | collective-permute-start | bytes 61448 | tf_op jit(solution)/shard_map/ppermute | solution.py:26
  14.4 7.2 %collective-permute-start.3 = (f32[20,2,1,128]{3,2,1,0:T(1,128)S(1)}, f32[20,2,1,128]{3,2,1,0:T(1,128)S(1)}, u32[]{:S(2)}, u32[]{:S(2)}) collective-permute-start(f32[20,2,1,128]{3,2,1,0:T(1,128)S(1)} %get-tuple-element.463), channel_id=1, source_target_pairs={{1,0},{2,1},{3,2},{4,3},{5,4},{6,5},{7,6},{8,7},{9,8},{10,9},{11,1... | collective-permute-start | bytes 61448 | tf_op jit(solution)/shard_map/ppermute | solution.py:26
  16.5 0.7 copy-start.4
  21.8 0.8 copy-start
  21.8 0.8 copy-start.3
  24.1 11.2 %collective-permute-start.4 = (f32[20,1,16,128]{3,2,1,0:T(8,128)S(1)}, f32[20,1,16,128]{3,2,1,0:T(8,128)S(1)}, u32[]{:S(2)}, u32[]{:S(2)}) collective-permute-start(f32[20,1,16,128]{3,2,1,0:T(8,128)S(1)} %get-tuple-element.461), channel_id=1, source_target_pairs={{0,32},{32,64},{64,96},{96,128},{128,160},{160,192},{192,224},{224... | collective-permute-start | bytes 491528 | tf_op jit(solution)/shard_map/ppermute | solution.py:26
  29.0 7.3 %collective-permute-start.5 = (f32[20,1,16,128]{3,2,1,0:T(8,128)S(1)}, f32[20,1,16,128]{3,2,1,0:T(8,128)S(1)}, u32[]{:S(2)}, u32[]{:S(2)}) collective-permute-start(f32[20,1,16,128]{3,2,1,0:T(8,128)S(1)} %get-tuple-element.460), channel_id=1, source_target_pairs={{32,0},{64,32},{96,64},{128,96},{160,128},{192,160},{224,192},{256... | collective-permute-start | bytes 491528 | tf_op jit(solution)/shard_map/ppermute | solution.py:26
  30.9 5.3 %collective-permute-start.6 = (f32[20,2,1,128]{3,2,1,0:T(1,128)S(1)}, f32[20,2,1,128]{3,2,1,0:T(1,128)S(1)}, u32[]{:S(2)}, u32[]{:S(2)}) collective-permute-start(f32[20,2,1,128]{3,2,1,0:T(1,128)S(1)} %get-tuple-element.458), channel_id=1, source_target_pairs={{0,1},{1,2},{2,3},{3,4},{4,5},{5,6},{6,7},{7,8},{8,9},{9,10},{10,1... | collective-permute-start | bytes 61448 | tf_op jit(solution)/shard_map/ppermute | solution.py:26
  33.1 7.2 %collective-permute-start.7 = (f32[20,2,1,128]{3,2,1,0:T(1,128)S(1)}, f32[20,2,1,128]{3,2,1,0:T(1,128)S(1)}, u32[]{:S(2)}, u32[]{:S(2)}) collective-permute-start(f32[20,2,1,128]{3,2,1,0:T(1,128)S(1)} %get-tuple-element.459), channel_id=1, source_target_pairs={{1,0},{2,1},{3,2},{4,3},{5,4},{6,5},{7,6},{8,7},{9,8},{10,9},{11,1... | collective-permute-start | bytes 61448 | tf_op jit(solution)/shard_map/ppermute | solution.py:26
  42.1 11.2 %collective-permute-start.8 = (f32[20,1,16,128]{3,2,1,0:T(8,128)S(1)}, f32[20,1,16,128]{3,2,1,0:T(8,128)S(1)}, u32[]{:S(2)}, u32[]{:S(2)}) collective-permute-start(f32[20,1,16,128]{3,2,1,0:T(8,128)S(1)} %get-tuple-element.457), channel_id=1, source_target_pairs={{0,32},{32,64},{64,96},{96,128},{128,160},{160,192},{192,224},{224... | collective-permute-start | bytes 491528 | tf_op jit(solution)/shard_map/ppermute | solution.py:26
  47.0 7.3 %collective-permute-start.9 = (f32[20,1,16,128]{3,2,1,0:T(8,128)S(1)}, f32[20,1,16,128]{3,2,1,0:T(8,128)S(1)}, u32[]{:S(2)}, u32[]{:S(2)}) collective-permute-start(f32[20,1,16,128]{3,2,1,0:T(8,128)S(1)} %get-tuple-element.456), channel_id=1, source_target_pairs={{32,0},{64,32},{96,64},{128,96},{160,128},{192,160},{224,192},{256... | collective-permute-start | bytes 491528 | tf_op jit(solution)/shard_map/ppermute | solution.py:26
  48.9 5.3 %collective-permute-start.10 = (f32[20,2,1,128]{3,2,1,0:T(1,128)S(1)}, f32[20,2,1,128]{3,2,1,0:T(1,128)S(1)}, u32[]{:S(2)}, u32[]{:S(2)}) collective-permute-start(f32[20,2,1,128]{3,2,1,0:T(1,128)S(1)} %get-tuple-element.454), channel_id=1, source_target_pairs={{0,1},{1,2},{2,3},{3,4},{4,5},{5,6},{6,7},{7,8},{8,9},{9,10},{10,1... | collective-permute-start | bytes 61448 | tf_op jit(solution)/shard_map/ppermute | solution.py:26
  51.2 7.2 %collective-permute-start.11 = (f32[20,2,1,128]{3,2,1,0:T(1,128)S(1)}, f32[20,2,1,128]{3,2,1,0:T(1,128)S(1)}, u32[]{:S(2)}, u32[]{:S(2)}) collective-permute-start(f32[20,2,1,128]{3,2,1,0:T(1,128)S(1)} %get-tuple-element.455), channel_id=1, source_target_pairs={{1,0},{2,1},{3,2},{4,3},{5,4},{6,5},{7,6},{8,7},{9,8},{10,9},{11,1... | collective-permute-start | bytes 61448 | tf_op jit(solution)/shard_map/ppermute | solution.py:26
  60.3 11.2 %collective-permute-start.12 = (f32[20,1,16,128]{3,2,1,0:T(8,128)S(1)}, f32[20,1,16,128]{3,2,1,0:T(8,128)S(1)}, u32[]{:S(2)}, u32[]{:S(2)}) collective-permute-start(f32[20,1,16,128]{3,2,1,0:T(8,128)S(1)} %get-tuple-element.453), channel_id=1, source_target_pairs={{0,32},{32,64},{64,96},{96,128},{128,160},{160,192},{192,224},{224... | collective-permute-start | bytes 491528 | tf_op jit(solution)/shard_map/ppermute | solution.py:26
  65.2 7.3 %collective-permute-start.13 = (f32[20,1,16,128]{3,2,1,0:T(8,128)S(1)}, f32[20,1,16,128]{3,2,1,0:T(8,128)S(1)}, u32[]{:S(2)}, u32[]{:S(2)}) collective-permute-start(f32[20,1,16,128]{3,2,1,0:T(8,128)S(1)} %get-tuple-element.452), channel_id=1, source_target_pairs={{32,0},{64,32},{96,64},{128,96},{160,128},{192,160},{224,192},{256... | collective-permute-start | bytes 491528 | tf_op jit(solution)/shard_map/ppermute | solution.py:26
  67.1 5.3 %collective-permute-start.14 = (f32[20,2,1,128]{3,2,1,0:T(1,128)S(1)}, f32[20,2,1,128]{3,2,1,0:T(1,128)S(1)}, u32[]{:S(2)}, u32[]{:S(2)}) collective-permute-start(f32[20,2,1,128]{3,2,1,0:T(1,128)S(1)} %get-tuple-element.450), channel_id=1, source_target_pairs={{0,1},{1,2},{2,3},{3,4},{4,5},{5,6},{6,7},{7,8},{8,9},{9,10},{10,1... | collective-permute-start | bytes 61448 | tf_op jit(solution)/shard_map/ppermute | solution.py:26
  69.4 7.2 %collective-permute-start.15 = (f32[20,2,1,128]{3,2,1,0:T(1,128)S(1)}, f32[20,2,1,128]{3,2,1,0:T(1,128)S(1)}, u32[]{:S(2)}, u32[]{:S(2)}) collective-permute-start(f32[20,2,1,128]{3,2,1,0:T(1,128)S(1)} %get-tuple-element.451), channel_id=1, source_target_pairs={{1,0},{2,1},{3,2},{4,3},{5,4},{6,5},{7,6},{8,7},{9,8},{10,9},{11,1... | collective-permute-start | bytes 61448 | tf_op jit(solution)/shard_map/ppermute | solution.py:26
  78.4 23.3 %collective-permute-start.20 = (f32[2,2,16,128]{3,1,2,0:T(2,128)S(1)}, f32[2,2,16,128]{3,1,2,0:T(2,128)S(1)}, u32[]{:S(2)}, u32[]{:S(2)}) collective-permute-start(f32[2,2,16,128]{3,1,2,0:T(2,128)S(1)} %multiply_select_fusion), channel_id=1, source_target_pairs={{0,512},{512,0},{1,513},{513,1},{2,514},{514,2},{3,515},{515,3},{4... | collective-permute-start | bytes 98312 | tf_op jit(solution)/shard_map/ppermute | solution.py:229
  84.4 11.9 %collective-permute-start.16 = (f32[20,1,16,128]{3,2,1,0:T(8,128)S(1)}, f32[20,1,16,128]{3,2,1,0:T(8,128)S(1)}, u32[]{:S(2)}, u32[]{:S(2)}) collective-permute-start(f32[20,1,16,128]{3,2,1,0:T(8,128)S(1)} %get-tuple-element.449), channel_id=1, source_target_pairs={{0,32},{32,64},{64,96},{96,128},{128,160},{160,192},{192,224},{224... | collective-permute-start | bytes 491528 | tf_op jit(solution)/shard_map/ppermute | solution.py:26
  89.3 7.3 %collective-permute-start.17 = (f32[20,1,16,128]{3,2,1,0:T(8,128)S(1)}, f32[20,1,16,128]{3,2,1,0:T(8,128)S(1)}, u32[]{:S(2)}, u32[]{:S(2)}) collective-permute-start(f32[20,1,16,128]{3,2,1,0:T(8,128)S(1)} %get-tuple-element.448), channel_id=1, source_target_pairs={{32,0},{64,32},{96,64},{128,96},{160,128},{192,160},{224,192},{256... | collective-permute-start | bytes 491528 | tf_op jit(solution)/shard_map/ppermute | solution.py:26
  91.2 5.3 %collective-permute-start.18 = (f32[20,2,1,128]{3,2,1,0:T(1,128)S(1)}, f32[20,2,1,128]{3,2,1,0:T(1,128)S(1)}, u32[]{:S(2)}, u32[]{:S(2)}) collective-permute-start(f32[20,2,1,128]{3,2,1,0:T(1,128)S(1)} %get-tuple-element.446), channel_id=1, source_target_pairs={{0,1},{1,2},{2,3},{3,4},{4,5},{5,6},{6,7},{7,8},{8,9},{9,10},{10,1... | collective-permute-start | bytes 61448 | tf_op jit(solution)/shard_map/ppermute | solution.py:26
  94.3 7.2 %collective-permute-start.19 = (f32[20,2,1,128]{3,2,1,0:T(1,128)S(1)}, f32[20,2,1,128]{3,2,1,0:T(1,128)S(1)}, u32[]{:S(2)}, u32[]{:S(2)}) collective-permute-start(f32[20,2,1,128]{3,2,1,0:T(1,128)S(1)} %get-tuple-element.447), channel_id=1, source_target_pairs={{1,0},{2,1},{3,2},{4,3},{5,4},{6,5},{7,6},{8,7},{9,8},{10,9},{11,1... | collective-permute-start | bytes 61448 | tf_op jit(solution)/shard_map/ppermute | solution.py:26
  103.1 0.7 copy-start.1

commit v2 on v0

--- a/solution.py
+++ b/solution.py
@@ -15,23 +15,35 @@
 SURFACE = 8.0
 
 
-def extended_2(shard, sides, width):
-    for axis, dim in sides:
-        peers, length = (lax.axis_size(axis), shard.shape[dim])
-        up = [(i, (i + 1) % peers) for i in range(peers - 1)]
-        down = [(j, i) for i, j in up]
-        last = lax.slice_in_dim(shard, length - width, length, axis=dim)
-        leading = lax.slice_in_dim(shard, 0, width, axis=dim)
-        before = lax.ppermute(last, axis, up)
-        after = lax.ppermute(leading, axis, down)
-        shard = jnp.concatenate([before, shard, after], axis=dim)
-    return shard
-
-
-def from_behind(shard, axis, by):
+def shifts(axis):
     peers = lax.axis_size(axis)
-    pairs = [(i, i + by) for i in range(peers) if 0 <= i + by < peers]
-    return lax.ppermute(shard, axis, pairs)
+    up = [(i, i + 1) for i in range(peers - 1)]
+    down = [(j, i) for i, j in up]
+    return up, down
+
+
+def halo_wide(block):
+    up, down = shifts("gx")
+    before = lax.ppermute(block, "gx", up)
+    after = lax.ppermute(block, "gx", down)
+    wide = jnp.concatenate([before, block, after], axis=1)
+    rows = block.shape[1]
+    up, down = shifts("gy")
+    below = lax.ppermute(wide[:, :, -rows:], "gy", up)
+    above = lax.ppermute(wide[:, :, :rows], "gy", down)
+    return jnp.concatenate([below, wide, above], axis=2)
+
+
+def halo_one(block):
+    up, down = shifts("gx")
+    xb = lax.ppermute(block[:, -1:], "gx", up)
+    xa = lax.ppermute(block[:, :1], "gx", down)
+    up, down = shifts("gy")
+    yb = lax.ppermute(block[:, :, -1:], "gy", up)
+    ya = lax.ppermute(block[:, :, :1], "gy", down)
+    wide = jnp.concatenate([xb, block, xa], axis=1)
+    pad = ((0, 0), (1, 1), (0, 0), (0, 0))
+    return jnp.concatenate([jnp.pad(yb, pad), wide, jnp.pad(ya, pad)], axis=2)
 
 
 def to_fine(coarse):
@@ -63,8 +75,15 @@
     )
 
 
-def trim_margin(values, margin, keep):
-    cut = margin - keep
+def wet_of_float(levels, depth):
+    shape = levels.shape + (depth,)
+    return (
+        lax.broadcasted_iota(jnp.int32, shape, len(shape) - 1).astype(jnp.float32)
+        < levels[..., None]
+    ).astype(jnp.float32)
+
+
+def trim(values, cut):
     if cut == 0:
         return values
     return values[..., cut : values.shape[-3] - cut, cut : values.shape[-2] - cut, :]
@@ -127,54 +146,11 @@
     return SURFACE * jnp.exp(-overhead) * (1.0 - jnp.exp(-attenuation))
 
 
-def advance(
-    is_ocean,
-    extended,
-    wide,
-    steps,
-    wet_fine,
-    fine_margin,
-    wet_coarse,
-    coarse_margin,
-    volume_flux,
-    flux_margin,
-    heating,
-    running,
-    onehot,
-    eco_rate,
-):
-
-    def ocean_part():
-        fine_cells = trim_margin(to_fine(extended), 2 * wide, steps)
-        summed = running
-        remain = steps - 1
-        fine_cells = ocean_substep(fine_cells, trim_margin(wet_fine, fine_margin, remain), heating)
-        summed = summed + coarse_mean(trim_margin(fine_cells[0:2], remain, 0))
-        return (to_coarse(fine_cells), summed)
-
-    def tracer_part():
-        tracer = trim_margin(extended, wide, steps)
-        remain = steps - 1
-        tracer = tracer_substep(
-            tracer,
-            trim_margin(wet_coarse, coarse_margin, remain),
-            trim_margin(volume_flux, flux_margin, remain),
-            onehot,
-            eco_rate,
-        )
-        return (tracer, running)
-
-    return lax.cond(is_ocean, ocean_part, tracer_part)
-
-
-def rim_single(own_block):
-    return extended_2(own_block, (("gx", 1), ("gy", 2)), 1)
-
-
 def body(state, levels, old_flux, eco_prey, eco_rate):
     depth = state.shape[-1]
     size_x, size_y = (state.shape[2], state.shape[3])
     species = eco_rate.shape[0]
+    channels = state.shape[1]
     is_ocean = lax.axis_index("half") == 0
     onehot = (eco_prey[:, None] == lax.broadcasted_iota(jnp.int32, (species, species), 1)).astype(
         jnp.float32
@@ -187,7 +163,6 @@
     wet_fine = wet_of(fine_levels(levels), depth)
     wet_coarse = wet_of(jnp.max(levels, axis=0), depth)
     own_block = state[0]
-    channels = own_block.shape[0]
     own_block = lax.cond(
         is_ocean,
         lambda: (
@@ -195,52 +170,73 @@
         ).reshape(channels, size_x, size_y, depth),
         lambda: own_block * wet_coarse,
     )
-    running = jnp.zeros((2, size_x, size_y, depth), jnp.float32)
-    for substep in range(NSUB):
-        extended = rim_single(own_block)
-        own_block, running = advance(
-            is_ocean,
-            extended,
-            1,
-            1,
-            wet_fine,
-            0,
-            wet_coarse,
-            0,
-            old_flux,
-            0,
-            0.0,
-            running,
-            onehot,
-            eco_rate,
-        )
-    new_flux = running / NSUB
-    absorbed = lax.cond(
-        is_ocean,
-        lambda: jnp.zeros((size_x, size_y, depth), jnp.float32),
-        lambda: absorption(own_block, wet_coarse, above_table),
-    )
-    flux_arrived = from_behind(new_flux, "half", 1)
-    light_arrived = from_behind(absorbed[None], "half", -1)
-    heating = HEATING * to_fine(jnp.broadcast_to(light_arrived, (4, size_x, size_y, depth)))[0]
-    extended = rim_single(own_block)
-    own_block, running = advance(
-        is_ocean,
-        extended,
-        1,
-        1,
-        wet_fine,
-        0,
-        wet_coarse,
-        0,
-        flux_arrived,
-        0,
-        heating,
-        running,
-        onehot,
-        eco_rate,
-    )
-    return own_block[None]
+    level_lanes = jnp.pad(
+        levels.astype(jnp.float32).transpose(1, 2, 0), ((0, 0), (0, 0), (0, depth - 4))
+    )[None]
+    packed = jnp.concatenate([own_block, old_flux, level_lanes], axis=0)
+    ext1 = halo_wide(packed)
+    margin = (ext1.shape[1] - size_x) // 2
+    state_ext = ext1[:channels]
+    flux_ext = ext1[channels : channels + 2]
+    levels_ext = ext1[channels + 2, :, :, 0:4].transpose(2, 0, 1)
+    wet_coarse_ext = wet_of_float(jnp.max(levels_ext, axis=0), depth)
+    wet_fine_ext = wet_of_float(fine_levels(levels_ext), depth)
+
+    def ocean_a():
+        fine = to_fine(state_ext)
+        reach = 2 * margin
+        running = jnp.zeros((2, size_x, size_y, depth), jnp.float32)
+        for substep in range(NSUB):
+            fine = ocean_substep(fine, trim(wet_fine_ext, substep + 1), 0.0)
+            left = reach - substep - 1
+            running = running + coarse_mean(trim(fine[0:2], left))
+        return to_coarse(fine), running
+
+    def tracer_a():
+        tracer = state_ext
+        for substep in range(margin):
+            tracer = tracer_substep(
+                tracer,
+                trim(wet_coarse_ext, substep + 1),
+                trim(flux_ext, substep + 1),
+                onehot,
+                eco_rate,
+            )
+        return tracer, jnp.zeros((2, size_x, size_y, depth), jnp.float32)
+
+    block_a, running = lax.cond(is_ocean, ocean_a, tracer_a)
+    ext2 = halo_wide(block_a)
+
+    def ocean_b():
+        return block_a, running / NSUB
+
+    def tracer_b():
+        tracer = ext2
+        for substep in range(margin):
+            tracer = tracer_substep(
+                tracer,
+                trim(wet_coarse_ext, substep + 1),
+                trim(flux_ext, substep + 1),
+                onehot,
+                eco_rate,
+            )
+        absorbed = absorption(tracer, wet_coarse, above_table)
+        return tracer, jnp.broadcast_to(absorbed[None], (2, size_x, size_y, depth))
+
+    block_b, outgoing = lax.cond(is_ocean, ocean_b, tracer_b)
+    ext3 = halo_one(block_b)
+    arrived = lax.ppermute(outgoing, "half", [(0, 1), (1, 0)])
+
+    def ocean_c():
+        fine = trim(to_fine(ext3), 1)
+        light = arrived[0:1]
+        heating = HEATING * to_fine(jnp.broadcast_to(light, (4, size_x, size_y, depth)))[0]
+        return to_coarse(ocean_substep(fine, wet_fine, heating))
+
+    def tracer_c():
+        return tracer_substep(ext3, wet_coarse, arrived, onehot, eco_rate)
+
+    return lax.cond(is_ocean, ocean_c, tracer_c)[None]
 
 
 def solution(mesh):

time: 131 us -> 98.6 us (0.75)
  the two profiles are of different devices: /device:TPU:100 before, /device:TPU:228 now
where the time goes in v2:
time: 98.6 us; the launch traced here: 97.8 us
  starting transfers between devices  45.2 us (46%)
  waiting for transfers between devices  31.5 us (32%)
  other arithmetic  8.18 us (8%)
  local copies, waits for them, and re-layouts  7.82 us (8%)
  matrix products  4.43 us (4%)
    ppermute x2, waiting for transfers between devices, halo_wide(): before = lax.ppermute(block, 'gx', up)  12.7 us
    ppermute x2, starting transfers between devices, halo_wide(): above = lax.ppermute(wide[:, :, :rows], 'gy', down)  11.5 us
    ppermute x2, starting transfers between devices, halo_wide(): before = lax.ppermute(block, 'gx', up)  9.19 us
    ppermute x2, waiting for transfers between devices, halo_wide(): after = lax.ppermute(block, 'gx', down)  8.92 us
    ppermute x1, starting transfers between devices, halo_one(): ya = lax.ppermute(block[:, :, :1], 'gy', down)  5.75 us
    ppermute x1, starting transfers between devices, halo_one(): xb = lax.ppermute(block[:, -1:], 'gx', up)  4.92 us
    ppermute x1, waiting for transfers between devices, body(): arrived = lax.ppermute(outgoing, 'half', [(0, 1), (1, 0)])  4.9 us
    ppermute x2, starting transfers between devices, halo_wide(): after = lax.ppermute(block, 'gx', down)  4.05 us
  transfers between devices with their start and end apart: 13, of which 9 were waited for; matrix products, arithmetic and copies ran while one was open for 2% of the time, Pallas kernels for 0%

profile of v2, /device:TPU:228, one launch (start us, length us, event | category | flops | bytes accessed | tf_op | source)
XLA Modules:
  0.0 97.8 jit_solution(3630984359525000172)
XLA Ops:
  0.0 0.8 fusion.54
  0.8 0.7 fusion.59
  1.5 0.7 reduce_max.18
  2.2 0.7 fusion.57
  2.9 1.0 %conditional.4 = (f32[20,2,16,128]{3,2,1,0:T(8,128)S(1)}) conditional(s32[]{:T(128)} %convert_element_type.43, (f32[1,20,2,16,128]{4,3,2,1,0:T(8,128)}, f32[2,16,128]{2,1,0:T(8,128)}) %tuple.35, (f32[1,20,2,16,128]{4,3,2,1,0:T(8,128)}, f32[4,2,16,128]{3,2,1,0:T(8,128)S(1)}) %tuple.36), branch_computations={%region_1.0_spmd, %region_2.0_spmd} | conditional | flops 81920 | bytes 720904 | solution.py:166
  2.9 1.0 %bitcast_multiply_fusion = f32[20,2,16,128]{3,2,1,0:T(8,128)S(1)} fusion(f32[1,20,2,16,128]{4,3,2,1,0:T(8,128)} %get-tuple-element.73, f32[2,16,128]{2,1,0:T(8,128)} %get-tuple-element.74), kind=kLoop, calls=%fused_computation | loop fusion | flops 81920 | bytes 671744 | tf_op jit(solution)/shard_map/cond/branch_0_fun/mul | solution.py:171
  4.0 5.5 %collective-permute-start = (f32[23,2,16,128]{3,2,1,0:T(8,128)S(1)}, f32[23,2,16,128]{3,2,1,0:T(8,128)S(1)}, u32[]{:S(2)}, u32[]{:S(2)}) collective-permute-start(f32[23,2,16,128]{3,2,1,0:T(8,128)S(1)} %pad_maximum_fusion.2), channel_id=1, source_target_pairs={{0,32},{32,64},{64,96},{96,128},{128,160},{160,192},{192,224},{224... | collective-permute-start | bytes 1130504 | tf_op jit(solution)/shard_map/ppermute | solution.py:27
  9.5 1.9 %collective-permute-start.1 = (f32[23,2,16,128]{3,2,1,0:T(8,128)S(1)}, f32[23,2,16,128]{3,2,1,0:T(8,128)S(1)}, u32[]{:S(2)}, u32[]{:S(2)}) collective-permute-start(f32[23,2,16,128]{3,2,1,0:T(8,128)S(1)} %pad_maximum_fusion.2), channel_id=1, source_target_pairs={{32,0},{64,32},{96,64},{128,96},{160,128},{192,160},{224,192},{256... | collective-permute-start | bytes 1130504 | tf_op jit(solution)/shard_map/ppermute | solution.py:28
  11.4 6.1 %collective-permute-done = f32[23,2,16,128]{3,2,1,0:T(8,128)S(1)} collective-permute-done((f32[23,2,16,128]{3,2,1,0:T(8,128)S(1)}, f32[23,2,16,128]{3,2,1,0:T(8,128)S(1)}, u32[]{:S(2)}, u32[]{:S(2)}) %collective-permute-start) | collective-permute-done | bytes 376864 | tf_op jit(solution)/shard_map/ppermute | solution.py:27
  17.5 5.3 %collective-permute-done.1 = f32[23,2,16,128]{3,2,1,0:T(8,128)S(1)} collective-permute-done((f32[23,2,16,128]{3,2,1,0:T(8,128)S(1)}, f32[23,2,16,128]{3,2,1,0:T(8,128)S(1)}, u32[]{:S(2)}, u32[]{:S(2)}) %collective-permute-start.1) | collective-permute-done | bytes 376864 | tf_op jit(solution)/shard_map/ppermute | solution.py:28
  22.8 0.1 pad_maximum_fusion.8
  22.9 1.9 %collective-permute-start.2 = (f32[23,6,2,128]{3,2,1,0:T(2,128)S(1)}, f32[23,6,2,128]{3,2,1,0:T(2,128)S(1)}, u32[]{:S(2)}, u32[]{:S(2)}) collective-permute-start(f32[23,6,2,128]{3,2,1,0:T(2,128)S(1)} %get-tuple-element.226), channel_id=1, source_target_pairs={{0,1},{1,2},{2,3},{3,4},{4,5},{5,6},{6,7},{7,8},{8,9},{9,10},{10,1... | collective-permute-start | bytes 423944 | tf_op jit(solution)/shard_map/ppermute | solution.py:32
  24.9 5.8 %collective-permute-start.3 = (f32[23,6,2,128]{3,2,1,0:T(2,128)S(1)}, f32[23,6,2,128]{3,2,1,0:T(2,128)S(1)}, u32[]{:S(2)}, u32[]{:S(2)}) collective-permute-start(f32[23,6,2,128]{3,2,1,0:T(2,128)S(1)} %get-tuple-element.227), channel_id=1, source_target_pairs={{1,0},{2,1},{3,2},{4,3},{5,4},{6,5},{7,6},{8,7},{9,8},{10,9},{11,1... | collective-permute-start | bytes 423944 | tf_op jit(solution)/shard_map/ppermute | solution.py:33
  30.6 0.1 fusion.58
  30.7 0.8 collective-permute-done.2
  31.5 1.8 %collective-permute-done.3 = f32[23,6,2,128]{3,2,1,0:T(2,128)S(1)} collective-permute-done((f32[23,6,2,128]{3,2,1,0:T(2,128)S(1)}, f32[23,6,2,128]{3,2,1,0:T(2,128)S(1)}, u32[]{:S(2)}, u32[]{:S(2)}) %collective-permute-start.3) | collective-permute-done | bytes 141344 | tf_op jit(solution)/shard_map/ppermute | solution.py:33
  33.2 0.3 pad_maximum_fusion
  33.5 1.2 %copy-done = f32[23,6,20,128]{3,2,1,0:T(8,128)} copy-done((f32[23,6,20,128]{3,2,1,0:T(8,128)}, f32[23,6,20,128]{3,2,1,0:T(8,128)S(1)}, u32[]{:S(2)}) %copy-start) | copy-done | bytes 1413144
  34.7 0.1 fusion.60
  34.8 0.1 copy.83
  35.0 0.2 copy.84
  35.1 0.1 lt.53
  35.2 0.1 compare_convert_fusion
  35.4 0.1 compare_convert_fusion.1
  35.5 0.7 slice-done
  36.2 5.2 %conditional.5 = (f32[20,2,16,128]{3,0,2,1:T(8,128)}, (f32[2,2,16,128]{3,2,1,0:T(8,128)S(1)}, f32[20,2,16,128]{3,2,1,0:T(8,128)})) conditional(s32[]{:T(128)} %convert_element_type.43, (f32[6,20,128]{2,1,0:T(8,128)S(1)}, f32[20,6,20,128]{3,2,1,0:T(8,128)S(1)}, f32[2,6,20,128]{3,2,1,0:T(8,128)S(1)}, f32[19]{0:T(128)S(1)}, ...), branch_computations={%region_4.5_spmd.clone, %region_5.10_spmd.clone} | conditional | flops 62939136 | bytes 27652376 | solution.py:207
  36.2 0.4 copy.109
  36.6 1.0 %fusion.34 = f32[19,4,18,128]{3,0,2,1:T(8,128)S(1)} fusion(f32[20,6,20,128]{3,0,2,1:T(8,128)S(1)} %copy.109, f32[19]{0:T(128)S(1)} %get-tuple-element.185, f32[19,19]{1,0:T(8,128)S(1)} %get-tuple-element.186), kind=kOutput, calls=%fused_computation.60 | convolution fusion | flops 40624128 | bytes 2482688 | tf_op jit(solution)/shard_map/cond/branch_0_fun/ts,sxyk->txyk/dot_general | solution.py:127
  37.6 0.5 add_multiply_fusion.3
  38.1 0.5 fusion.37
  38.7 1.0 add_multiply_fusion.4
  39.6 1.8 %copy.108 = f32[20,2,16,128]{3,2,1,0:T(8,128)} copy(f32[20,2,16,128]{3,0,2,1:T(8,128)} %add_multiply_fusion.4) | data formatting | bytes 655360 | tf_op jit(solution)/shard_map
  41.4 3.7 %collective-permute-start.4 = (f32[20,2,16,128]{3,0,2,1:T(8,128)}, f32[20,2,16,128]{3,0,2,1:T(8,128)S(1)}, u32[]{:S(2)}, u32[]{:S(2)}) collective-permute-start(f32[20,2,16,128]{3,0,2,1:T(8,128)} %get-tuple-element.180), channel_id=1, source_target_pairs={{0,32},{32,64},{64,96},{96,128},{128,160},{160,192},{192,224},{224... | collective-permute-start | bytes 983048 | tf_op jit(solution)/shard_map/ppermute | solution.py:27
  45.1 2.1 %collective-permute-start.5 = (f32[20,2,16,128]{3,0,2,1:T(8,128)}, f32[20,2,16,128]{3,0,2,1:T(8,128)S(1)}, u32[]{:S(2)}, u32[]{:S(2)}) collective-permute-start(f32[20,2,16,128]{3,0,2,1:T(8,128)} %get-tuple-element.180), channel_id=1, source_target_pairs={{32,0},{64,32},{96,64},{128,96},{160,128},{192,160},{224,192},{256... | collective-permute-start | bytes 983048 | tf_op jit(solution)/shard_map/ppermute | solution.py:28
  47.3 0.1 copy.104
  47.4 0.1 reshape.95
  47.5 6.6 %collective-permute-done.4 = f32[20,2,16,128]{3,0,2,1:T(8,128)S(1)} collective-permute-done((f32[20,2,16,128]{3,0,2,1:T(8,128)}, f32[20,2,16,128]{3,0,2,1:T(8,128)S(1)}, u32[]{:S(2)}, u32[]{:S(2)}) %collective-permute-start.4) | collective-permute-done | bytes 327712 | tf_op jit(solution)/shard_map/ppermute | solution.py:27
  54.1 1.0 %constant_dynamic-update-slice_fusion.2 = f32[20,6,16,128]{3,0,2,1:T(8,128)S(1)} fusion(f32[20,6,16,128]{3,0,2,1:T(8,128)S(1)} %constant_dynamic-update-slice_fusion.3, f32[20,2,16,128]{3,0,2,1:T(8,128)} %get-tuple-element.180), kind=kLoop, calls=%fused_computation.134 | loop fusion | bytes 720896
  55.2 3.6 %collective-permute-done.5 = f32[20,2,16,128]{3,0,2,1:T(8,128)S(1)} collective-permute-done((f32[20,2,16,128]{3,0,2,1:T(8,128)}, f32[20,2,16,128]{3,0,2,1:T(8,128)S(1)}, u32[]{:S(2)}, u32[]{:S(2)}) %collective-permute-start.5) | collective-permute-done | bytes 327712 | tf_op jit(solution)/shard_map/ppermute | solution.py:28
  58.8 1.9 %collective-permute-start.6 = (f32[20,6,2,128]{3,0,2,1:T(8,128)S(1)}, f32[20,6,2,128]{3,0,2,1:T(8,128)S(1)}, u32[]{:S(2)}, u32[]{:S(2)}) collective-permute-start(f32[20,6,2,128]{3,0,2,1:T(8,128)S(1)} %get-tuple-element.224), channel_id=1, source_target_pairs={{0,1},{1,2},{2,3},{3,4},{4,5},{5,6},{6,7},{7,8},{8,9},{9,10},{10,1... | collective-permute-start | bytes 368648 | tf_op jit(solution)/shard_map/ppermute | solution.py:32
  60.7 5.8 %collective-permute-start.7 = (f32[20,6,2,128]{3,0,2,1:T(8,128)S(1)}, f32[20,6,2,128]{3,0,2,1:T(8,128)S(1)}, u32[]{:S(2)}, u32[]{:S(2)}) collective-permute-start(f32[20,6,2,128]{3,0,2,1:T(8,128)S(1)} %get-tuple-element.225), channel_id=1, source_target_pairs={{1,0},{2,1},{3,2},{4,3},{5,4},{6,5},{7,6},{8,7},{9,8},{10,9},{11,1... | collective-permute-start | bytes 368648 | tf_op jit(solution)/shard_map/ppermute | solution.py:33
  66.5 0.1 fusion.56
  66.6 0.8 collective-permute-done.6
  67.5 1.7 %collective-permute-done.7 = f32[20,6,2,128]{3,0,2,1:T(8,128)S(1)} collective-permute-done((f32[20,6,2,128]{3,0,2,1:T(8,128)S(1)}, f32[20,6,2,128]{3,0,2,1:T(8,128)S(1)}, u32[]{:S(2)}, u32[]{:S(2)}) %collective-permute-start.7) | collective-permute-done | bytes 122912 | tf_op jit(solution)/shard_map/ppermute | solution.py:33
  69.1 0.1 pad_maximum_fusion.1
  69.3 3.3 %conditional.6 = (f32[20,2,16,128]{3,0,2,1:T(8,128)S(1)}, f32[2,2,16,128]{3,2,1,0:T(8,128)S(1)}) conditional(s32[]{:T(128)} %convert_element_type.43, (f32[6,20,128]{2,1,0:T(8,128)S(1)}, f32[20,6,20,128]{3,0,2,1:T(8,128)S(1)}, f32[2,6,20,128]{3,2,1,0:T(8,128)S(1)}, f32[19]{0:T(128)S(1)}, f32[19,19]{1,0:T(8,128)S(1)}, ...), branch_computations={%region_10.11_spmd, %region_11.12_spmd} | conditional | flops 69324800 | bytes 11670544 | solution.py:226
  69.3 1.0 fusion.1
  70.3 0.5 add_multiply_fusion
  70.8 0.5 fusion.4
  71.3 0.2 add_multiply_fusion.1
  71.6 1.0 %fusion.7 = f32[2,16,128]{2,1,0:T(8,128)S(1)} fusion(f32[128,128]{1,0:T(8,128)S(1)} %get-tuple-element.90, f32[2,16,128]{2,1,0:T(8,128)} %get-tuple-element.89, f32[2,16,128]{2,1,0:T(8,128)S(1)} %bitcast.166), kind=kOutput, calls=%fused_computation.12 | convolution fusion | flops 6385664 | bytes 114688 | tf_op jit(solution)/shard_map/cond/branch_0_fun/xyk,kl->xyl/dot_general | solution.py:145
  72.7 4.9 %collective-permute-start.8 = (f32[20,1,16,128]{3,2,1,0:T(8,128)S(1)}, f32[20,1,16,128]{3,2,1,0:T(8,128)S(1)}, u32[]{:S(2)}, u32[]{:S(2)}) collective-permute-start(f32[20,1,16,128]{3,2,1,0:T(8,128)S(1)} %get-tuple-element.231), channel_id=1, source_target_pairs={{0,32},{32,64},{64,96},{96,128},{128,160},{160,192},{192,224},{224... | collective-permute-start | bytes 491528 | tf_op jit(solution)/shard_map/ppermute | solution.py:39
  77.6 1.9 %collective-permute-start.9 = (f32[20,1,16,128]{3,2,1,0:T(8,128)S(1)}, f32[20,1,16,128]{3,2,1,0:T(8,128)S(1)}, u32[]{:S(2)}, u32[]{:S(2)}) collective-permute-start(f32[20,1,16,128]{3,2,1,0:T(8,128)S(1)} %get-tuple-element.230), channel_id=1, source_target_pairs={{32,0},{64,32},{96,64},{128,96},{160,128},{192,160},{224,192},{256... | collective-permute-start | bytes 491528 | tf_op jit(solution)/shard_map/ppermute | solution.py:40
  79.6 1.9 %collective-permute-start.10 = (f32[20,2,1,128]{3,2,1,0:T(1,128)S(1)}, f32[20,2,1,128]{3,2,1,0:T(1,128)S(1)}, u32[]{:S(2)}, u32[]{:S(2)}) collective-permute-start(f32[20,2,1,128]{3,2,1,0:T(1,128)S(1)} %copy.93), channel_id=1, source_target_pairs={{0,1},{1,2},{2,3},{3,4},{4,5},{5,6},{6,7},{7,8},{8,9},{9,10},{10,1... | collective-permute-start | bytes 61448 | tf_op jit(solution)/shard_map/ppermute | solution.py:42
  81.6 5.8 %collective-permute-start.11 = (f32[20,2,1,128]{3,2,1,0:T(1,128)S(1)}, f32[20,2,1,128]{3,2,1,0:T(1,128)S(1)}, u32[]{:S(2)}, u32[]{:S(2)}) collective-permute-start(f32[20,2,1,128]{3,2,1,0:T(1,128)S(1)} %copy.94), channel_id=1, source_target_pairs={{1,0},{2,1},{3,2},{4,3},{5,4},{6,5},{7,6},{8,7},{9,8},{10,9},{11,1... | collective-permute-start | bytes 61448 | tf_op jit(solution)/shard_map/ppermute | solution.py:43
  87.3 2.1 %collective-permute-start.12 = (f32[2,2,16,128]{3,1,2,0:T(2,128)S(1)}, f32[2,2,16,128]{3,1,2,0:T(2,128)S(1)}, u32[]{:S(2)}, u32[]{:S(2)}) collective-permute-start(f32[2,2,16,128]{3,1,2,0:T(2,128)S(1)} %copy.95), channel_id=1, source_target_pairs={{0,512},{512,0},{1,513},{513,1},{2,514},{514,2},{3,515},{515,3},{4... | collective-permute-start | bytes 98312 | tf_op jit(solution)/shard_map/ppermute | solution.py:228
  89.6 0.2 select_maximum_fusion
  89.8 4.9 %collective-permute-done.12 = f32[2,2,16,128]{3,1,2,0:T(2,128)S(1)} collective-permute-done((f32[2,2,16,128]{3,1,2,0:T(2,128)S(1)}, f32[2,2,16,128]{3,1,2,0:T(2,128)S(1)}, u32[]{:S(2)}, u32[]{:S(2)}) %collective-permute-start.12) | collective-permute-done | bytes 32800 | tf_op jit(solution)/shard_map/ppermute | solution.py:228
  94.7 2.4 %conditional.7 = (f32[1,20,2,16,128]{4,3,2,1,0:T(8,128)S(1)}) conditional(s32[]{:T(128)} %convert_element_type.43, (f32[2,16,128]{2,1,0:T(8,128)}, f32[20,4,16,128]{3,2,1,0:T(8,128)S(1)}, f32[20,4,18,128]{3,2,1,0:T(8,128)S(1)}, f32[20,2,16,128]{3,0,2,1:T(8,128)S(1)}, f32[2,2,16,128]{3,1,2,0:T(2,128)S(1)}, /*index=5*/f32[19]{0:T(128)S(1)}, ...), branch_computations={%region_12.13_spmd, %region_13.14_spmd} | conditional | flops 19365888 | bytes 7008776 | solution.py:239
  94.7 0.5 fusion.30
  95.2 0.4 copy.99
  95.6 0.4 copy.98
  96.0 0.9 multiply_bitcast_fusion
  97.1 0.7 copy-done.2
  (53 shorter events, 0.7 us)
Async XLA Ops:
  0.0 4.0 %copy-start.1 = (f32[2,2,16,128]{3,2,1,0:T(8,128)S(1)}, f32[2,2,16,128]{3,2,1,0:T(8,128)}, u32[]{:S(2)}) copy-start(f32[2,2,16,128]{3,2,1,0:T(8,128)} %param.15) | copy-start | bytes 98308
  2.9 27.7 %copy-start.8 = (s32[19]{0:T(128)S(1)}, s32[19]{0:T(128)}, u32[]{:S(2)}) copy-start(s32[19]{0:T(128)} %param.16) | copy-start | bytes 232
  4.0 13.5 %collective-permute-start = (f32[23,2,16,128]{3,2,1,0:T(8,128)S(1)}, f32[23,2,16,128]{3,2,1,0:T(8,128)S(1)}, u32[]{:S(2)}, u32[]{:S(2)}) collective-permute-start(f32[23,2,16,128]{3,2,1,0:T(8,128)S(1)} %pad_maximum_fusion.2), channel_id=1, source_target_pairs={{0,32},{32,64},{64,96},{96,128},{128,160},{160,192},{192,224},{224... | collective-permute-start | bytes 1130504 | tf_op jit(solution)/shard_map/ppermute | solution.py:27
  9.5 13.3 %collective-permute-start.1 = (f32[23,2,16,128]{3,2,1,0:T(8,128)S(1)}, f32[23,2,16,128]{3,2,1,0:T(8,128)S(1)}, u32[]{:S(2)}, u32[]{:S(2)}) collective-permute-start(f32[23,2,16,128]{3,2,1,0:T(8,128)S(1)} %pad_maximum_fusion.2), channel_id=1, source_target_pairs={{32,0},{64,32},{96,64},{128,96},{160,128},{192,160},{224,192},{256... | collective-permute-start | bytes 1130504 | tf_op jit(solution)/shard_map/ppermute | solution.py:28
  22.9 8.5 %collective-permute-start.2 = (f32[23,6,2,128]{3,2,1,0:T(2,128)S(1)}, f32[23,6,2,128]{3,2,1,0:T(2,128)S(1)}, u32[]{:S(2)}, u32[]{:S(2)}) collective-permute-start(f32[23,6,2,128]{3,2,1,0:T(2,128)S(1)} %get-tuple-element.226), channel_id=1, source_target_pairs={{0,1},{1,2},{2,3},{3,4},{4,5},{5,6},{6,7},{7,8},{8,9},{9,10},{10,1... | collective-permute-start | bytes 423944 | tf_op jit(solution)/shard_map/ppermute | solution.py:32
  24.9 8.4 %collective-permute-start.3 = (f32[23,6,2,128]{3,2,1,0:T(2,128)S(1)}, f32[23,6,2,128]{3,2,1,0:T(2,128)S(1)}, u32[]{:S(2)}, u32[]{:S(2)}) collective-permute-start(f32[23,6,2,128]{3,2,1,0:T(2,128)S(1)} %get-tuple-element.227), channel_id=1, source_target_pairs={{1,0},{2,1},{3,2},{4,3},{5,4},{6,5},{7,6},{8,7},{9,8},{10,9},{11,1... | collective-permute-start | bytes 423944 | tf_op jit(solution)/shard_map/ppermute | solution.py:33
  33.5 1.2 %copy-start = (f32[23,6,20,128]{3,2,1,0:T(8,128)}, f32[23,6,20,128]{3,2,1,0:T(8,128)S(1)}, u32[]{:S(2)}) copy-start(f32[23,6,20,128]{3,2,1,0:T(8,128)S(1)} %pad_maximum_fusion) | copy-start | bytes 4239364
  34.8 1.4 %slice-start = ((f32[23,6,20,128]{3,2,1,0:T(8,128)}), f32[20,6,20,128]{3,2,1,0:T(8,128)S(1)}, s32[]{:S(2)}) async-start(f32[23,6,20,128]{3,2,1,0:T(8,128)} %copy-done), calls=%async_computation | async-start | bytes 2949120 | tf_op jit(solution)/shard_map/slice | solution.py:179
  34.8 1.4 %copy-start.6 = (f32[19]{0:T(128)S(1)}, f32[19]{0:T(128)}, u32[]{:S(2)}) copy-start(f32[19]{0:T(128)} %param.17) | copy-start | bytes 232
  36.2 11.1 %copy-start.5 = (s32[4,2,16]{2,1,0:T(2,128)S(1)}, s32[4,2,16]{2,1,0:T(2,128)}, u32[]{:S(2)}) copy-start(s32[4,2,16]{2,1,0:T(2,128)} %param.14) | copy-start | bytes 1540
  41.4 5.8 %copy-start.3 = (f32[2,2,16,128]{3,2,1,0:T(8,128)}, f32[2,2,16,128]{3,2,1,0:T(8,128)S(1)}, u32[]{:S(2)}) copy-start(f32[2,2,16,128]{3,2,1,0:T(8,128)S(1)} %get-tuple-element.266) | copy-start | bytes 98308
  41.4 12.7 %collective-permute-start.4 = (f32[20,2,16,128]{3,0,2,1:T(8,128)}, f32[20,2,16,128]{3,0,2,1:T(8,128)S(1)}, u32[]{:S(2)}, u32[]{:S(2)}) collective-permute-start(f32[20,2,16,128]{3,0,2,1:T(8,128)} %get-tuple-element.180), channel_id=1, source_target_pairs={{0,32},{32,64},{64,96},{96,128},{128,160},{160,192},{192,224},{224... | collective-permute-start | bytes 983048 | tf_op jit(solution)/shard_map/ppermute | solution.py:27
  45.1 13.6 %collective-permute-start.5 = (f32[20,2,16,128]{3,0,2,1:T(8,128)}, f32[20,2,16,128]{3,0,2,1:T(8,128)S(1)}, u32[]{:S(2)}, u32[]{:S(2)}) collective-permute-start(f32[20,2,16,128]{3,0,2,1:T(8,128)} %get-tuple-element.180), channel_id=1, source_target_pairs={{32,0},{64,32},{96,64},{128,96},{160,128},{192,160},{224,192},{256... | collective-permute-start | bytes 983048 | tf_op jit(solution)/shard_map/ppermute | solution.py:28
  58.8 8.7 %collective-permute-start.6 = (f32[20,6,2,128]{3,0,2,1:T(8,128)S(1)}, f32[20,6,2,128]{3,0,2,1:T(8,128)S(1)}, u32[]{:S(2)}, u32[]{:S(2)}) collective-permute-start(f32[20,6,2,128]{3,0,2,1:T(8,128)S(1)} %get-tuple-element.224), channel_id=1, source_target_pairs={{0,1},{1,2},{2,3},{3,4},{4,5},{5,6},{6,7},{7,8},{8,9},{9,10},{10,1... | collective-permute-start | bytes 368648 | tf_op jit(solution)/shard_map/ppermute | solution.py:32
  60.7 8.4 %collective-permute-start.7 = (f32[20,6,2,128]{3,0,2,1:T(8,128)S(1)}, f32[20,6,2,128]{3,0,2,1:T(8,128)S(1)}, u32[]{:S(2)}, u32[]{:S(2)}) collective-permute-start(f32[20,6,2,128]{3,0,2,1:T(8,128)S(1)} %get-tuple-element.225), channel_id=1, source_target_pairs={{1,0},{2,1},{3,2},{4,3},{5,4},{6,5},{7,6},{8,7},{9,8},{10,9},{11,1... | collective-permute-start | bytes 368648 | tf_op jit(solution)/shard_map/ppermute | solution.py:33
  66.6 2.6 %copy-start.4 = (f32[2,2,16,128]{3,2,1,0:T(8,128)S(1)}, f32[2,2,16,128]{3,2,1,0:T(8,128)}, u32[]{:S(2)}) copy-start(f32[2,2,16,128]{3,2,1,0:T(8,128)} %copy-done.3) | copy-start | bytes 98308
  66.6 2.6 %copy-start.7 = (f32[19]{0:T(128)S(1)}, f32[19]{0:T(128)}, u32[]{:S(2)}) copy-start(f32[19]{0:T(128)} %param.17) | copy-start | bytes 232
  72.7 16.8 %collective-permute-start.8 = (f32[20,1,16,128]{3,2,1,0:T(8,128)S(1)}, f32[20,1,16,128]{3,2,1,0:T(8,128)S(1)}, u32[]{:S(2)}, u32[]{:S(2)}) collective-permute-start(f32[20,1,16,128]{3,2,1,0:T(8,128)S(1)} %get-tuple-element.231), channel_id=1, source_target_pairs={{0,32},{32,64},{64,96},{96,128},{128,160},{160,192},{192,224},{224... | collective-permute-start | bytes 491528 | tf_op jit(solution)/shard_map/ppermute | solution.py:39
  77.6 11.9 %collective-permute-start.9 = (f32[20,1,16,128]{3,2,1,0:T(8,128)S(1)}, f32[20,1,16,128]{3,2,1,0:T(8,128)S(1)}, u32[]{:S(2)}, u32[]{:S(2)}) collective-permute-start(f32[20,1,16,128]{3,2,1,0:T(8,128)S(1)} %get-tuple-element.230), channel_id=1, source_target_pairs={{32,0},{64,32},{96,64},{128,96},{160,128},{192,160},{224,192},{256... | collective-permute-start | bytes 491528 | tf_op jit(solution)/shard_map/ppermute | solution.py:40
  79.6 10.0 %collective-permute-start.10 = (f32[20,2,1,128]{3,2,1,0:T(1,128)S(1)}, f32[20,2,1,128]{3,2,1,0:T(1,128)S(1)}, u32[]{:S(2)}, u32[]{:S(2)}) collective-permute-start(f32[20,2,1,128]{3,2,1,0:T(1,128)S(1)} %copy.93), channel_id=1, source_target_pairs={{0,1},{1,2},{2,3},{3,4},{4,5},{5,6},{6,7},{7,8},{8,9},{9,10},{10,1... | collective-permute-start | bytes 61448 | tf_op jit(solution)/shard_map/ppermute | solution.py:42
  81.6 8.0 %collective-permute-start.11 = (f32[20,2,1,128]{3,2,1,0:T(1,128)S(1)}, f32[20,2,1,128]{3,2,1,0:T(1,128)S(1)}, u32[]{:S(2)}, u32[]{:S(2)}) collective-permute-start(f32[20,2,1,128]{3,2,1,0:T(1,128)S(1)} %copy.94), channel_id=1, source_target_pairs={{1,0},{2,1},{3,2},{4,3},{5,4},{6,5},{7,6},{8,7},{9,8},{10,9},{11,1... | collective-permute-start | bytes 61448 | tf_op jit(solution)/shard_map/ppermute | solution.py:43
  87.3 7.3 %collective-permute-start.12 = (f32[2,2,16,128]{3,1,2,0:T(2,128)S(1)}, f32[2,2,16,128]{3,1,2,0:T(2,128)S(1)}, u32[]{:S(2)}, u32[]{:S(2)}) collective-permute-start(f32[2,2,16,128]{3,1,2,0:T(2,128)S(1)} %copy.95), channel_id=1, source_target_pairs={{0,512},{512,0},{1,513},{513,1},{2,514},{514,2},{3,515},{515,3},{4... | collective-permute-start | bytes 98312 | tf_op jit(solution)/shard_map/ppermute | solution.py:228
  97.1 0.7 copy-start.2

commit v3 on v2

--- a/solution.py
+++ b/solution.py
@@ -31,6 +31,22 @@
     up, down = shifts("gy")
     below = lax.ppermute(wide[:, :, -rows:], "gy", up)
     above = lax.ppermute(wide[:, :, :rows], "gy", down)
+    return jnp.concatenate([below, wide, above], axis=2)
+
+
+def halo_three(block):
+    up, down = shifts("gx")
+    peers = lax.axis_size("gx")
+    up2 = [(i, i + 2) for i in range(peers - 2)]
+    down2 = [(j, i) for i, j in up2]
+    b1 = lax.ppermute(block, "gx", up)
+    a1 = lax.ppermute(block, "gx", down)
+    b2 = lax.ppermute(block[:, -1:], "gx", up2)
+    a2 = lax.ppermute(block[:, :1], "gx", down2)
+    wide = jnp.concatenate([b2, b1, block, a1, a2], axis=1)
+    up, down = shifts("gy")
+    below = lax.ppermute(wide[:, :, -3:], "gy", up)
+    above = lax.ppermute(wide[:, :, :3], "gy", down)
     return jnp.concatenate([below, wide, above], axis=2)
 
 
@@ -152,6 +168,12 @@
     species = eco_rate.shape[0]
     channels = state.shape[1]
     is_ocean = lax.axis_index("half") == 0
+    level_lanes = jnp.pad(
+        levels.astype(jnp.float32).transpose(1, 2, 0), ((0, 0), (0, 0), (0, depth - 4))
+    )[None]
+    packed = jnp.concatenate([state[0], old_flux, level_lanes], axis=0)
+    ext1 = halo_wide(packed)
+    margin = (ext1.shape[1] - size_x) // 2
     onehot = (eco_prey[:, None] == lax.broadcasted_iota(jnp.int32, (species, species), 1)).astype(
         jnp.float32
     )
@@ -159,41 +181,26 @@
         lax.broadcasted_iota(jnp.int32, (depth, depth), 0)
         < lax.broadcasted_iota(jnp.int32, (depth, depth), 1)
     ).astype(jnp.float32)
-    wet_channels = wet_of(levels, depth)
     wet_fine = wet_of(fine_levels(levels), depth)
     wet_coarse = wet_of(jnp.max(levels, axis=0), depth)
-    own_block = state[0]
-    own_block = lax.cond(
-        is_ocean,
-        lambda: (
-            own_block.reshape(channels // 4, 4, size_x, size_y, depth) * wet_channels[None]
-        ).reshape(channels, size_x, size_y, depth),
-        lambda: own_block * wet_coarse,
-    )
-    level_lanes = jnp.pad(
-        levels.astype(jnp.float32).transpose(1, 2, 0), ((0, 0), (0, 0), (0, depth - 4))
-    )[None]
-    packed = jnp.concatenate([own_block, old_flux, level_lanes], axis=0)
-    ext1 = halo_wide(packed)
-    margin = (ext1.shape[1] - size_x) // 2
-    state_ext = ext1[:channels]
+    raw_ext = ext1[:channels]
     flux_ext = ext1[channels : channels + 2]
     levels_ext = ext1[channels + 2, :, :, 0:4].transpose(2, 0, 1)
     wet_coarse_ext = wet_of_float(jnp.max(levels_ext, axis=0), depth)
     wet_fine_ext = wet_of_float(fine_levels(levels_ext), depth)
+    zeros_flux = jnp.zeros((2, size_x, size_y, depth), jnp.float32)
 
     def ocean_a():
-        fine = to_fine(state_ext)
+        fine = to_fine(raw_ext) * wet_fine_ext[None]
         reach = 2 * margin
-        running = jnp.zeros((2, size_x, size_y, depth), jnp.float32)
-        for substep in range(NSUB):
+        running = zeros_flux
+        for substep in range(2):
             fine = ocean_substep(fine, trim(wet_fine_ext, substep + 1), 0.0)
-            left = reach - substep - 1
-            running = running + coarse_mean(trim(fine[0:2], left))
-        return to_coarse(fine), running
+            running = running + coarse_mean(trim(fine[0:2], reach - substep - 1))
+        return to_coarse(trim(fine, reach - 2)), running
 
     def tracer_a():
-        tracer = state_ext
+        tracer = raw_ext * wet_coarse_ext[None]
         for substep in range(margin):
             tracer = tracer_substep(
                 tracer,
@@ -202,39 +209,46 @@
                 onehot,
                 eco_rate,
             )
-        return tracer, jnp.zeros((2, size_x, size_y, depth), jnp.float32)
+        return tracer, zeros_flux
 
     block_a, running = lax.cond(is_ocean, ocean_a, tracer_a)
-    ext2 = halo_wide(block_a)
+    ext2 = halo_three(block_a)
+    reach2 = (ext2.shape[1] - size_x) // 2
+    tracer_shape = (channels, size_x + 2, size_y + 2, depth)
+    ocean_shape = (channels // 4, 2 * size_x + 2, 2 * size_y + 2, depth)
 
     def ocean_b():
-        return block_a, running / NSUB
+        fine = trim(to_fine(ext2), 2 * reach2 - 3)
+        summed = running
+        for substep in range(2):
+            fine = ocean_substep(fine, trim(wet_fine_ext, 2 * margin - 2 + substep), 0.0)
+            summed = summed + coarse_mean(trim(fine[0:2], 2 - substep))
+        return jnp.zeros(tracer_shape, jnp.float32), fine, summed / NSUB
 
     def tracer_b():
         tracer = ext2
-        for substep in range(margin):
+        for substep in range(2):
             tracer = tracer_substep(
                 tracer,
-                trim(wet_coarse_ext, substep + 1),
-                trim(flux_ext, substep + 1),
+                trim(wet_coarse_ext, substep),
+                trim(flux_ext, substep),
                 onehot,
                 eco_rate,
             )
-        absorbed = absorption(tracer, wet_coarse, above_table)
-        return tracer, jnp.broadcast_to(absorbed[None], (2, size_x, size_y, depth))
-
-    block_b, outgoing = lax.cond(is_ocean, ocean_b, tracer_b)
-    ext3 = halo_one(block_b)
+        absorbed = absorption(trim(tracer, 1), wet_coarse, above_table)
+        outgoing = jnp.broadcast_to(absorbed[None], (2, size_x, size_y, depth))
+        return tracer, jnp.zeros(ocean_shape, jnp.float32), outgoing
+
+    tracer_b4, ocean_b4, outgoing = lax.cond(is_ocean, ocean_b, tracer_b)
     arrived = lax.ppermute(outgoing, "half", [(0, 1), (1, 0)])
 
     def ocean_c():
-        fine = trim(to_fine(ext3), 1)
         light = arrived[0:1]
         heating = HEATING * to_fine(jnp.broadcast_to(light, (4, size_x, size_y, depth)))[0]
-        return to_coarse(ocean_substep(fine, wet_fine, heating))
+        return to_coarse(ocean_substep(ocean_b4, wet_fine, heating))
 
     def tracer_c():
-        return tracer_substep(ext3, wet_coarse, arrived, onehot, eco_rate)
+        return tracer_substep(tracer_b4, wet_coarse, arrived, onehot, eco_rate)
 
     return lax.cond(is_ocean, ocean_c, tracer_c)[None]
 

time: 98.6 us -> 103 us (1.045)
  the two profiles are of different devices: /device:TPU:228 before, /device:TPU:155 now
where the time goes in v3:
time: 103 us; the launch traced here: 102 us
  starting transfers between devices  44.1 us (43%)
  waiting for transfers between devices  35.3 us (34%)
  other arithmetic  13.6 us (13%)
  local copies, waits for them, and re-layouts  8.5 us (8%)
    ppermute x1, starting transfers between devices, body(): arrived = lax.ppermute(outgoing, 'half', [(0, 1), (1, 0)])  8.79 us
    ppermute x1, waiting for transfers between devices, halo_three(): a2 = lax.ppermute(block[:, :1], 'gx', down2)  7.13 us
    ppermute x1, waiting for transfers between devices, halo_wide(): above = lax.ppermute(wide[:, :, :rows], 'gy', down)  6.48 us
    ppermute x1, waiting for transfers between devices, halo_three(): above = lax.ppermute(wide[:, :, :3], 'gy', down)  6.46 us
    ppermute x1, waiting for transfers between devices, halo_wide(): after = lax.ppermute(block, 'gx', down)  5.86 us
    ppermute x1, starting transfers between devices, halo_wide(): below = lax.ppermute(wide[:, :, -rows:], 'gy', up)  5.82 us
    ppermute x1, starting transfers between devices, halo_three(): b2 = lax.ppermute(block[:, -1:], 'gx', up2)  5.81 us
    ppermute x1, waiting for transfers between devices, halo_wide(): before = lax.ppermute(block, 'gx', up)  5.59 us
  transfers between devices with their start and end apart: 11, of which 8 were waited for; matrix products, arithmetic and copies ran while one was open for 1% of the time, Pallas kernels for 0%

profile of v3, /device:TPU:155, one launch (start us, length us, event | category | flops | bytes accessed | tf_op | source)
XLA Modules:
  0.0 102.2 jit_solution(11601126034041277140)
XLA Ops:
  0.0 0.7 fusion.59
  0.8 1.0 %pad_maximum_fusion.2 = f32[23,2,16,128]{3,2,1,0:T(8,128)S(1)} fusion(f32[1,2,16,128]{3,2,1,0:T(8,128)S(1)} %copy.86, f32[2,2,16,128]{3,2,1,0:T(8,128)} %param.13, f32[20,2,16,128]{3,2,1,0:T(8,128)} %bitcast.136), kind=kLoop, calls=%fused_computation.111 | loop fusion | flops 188416 | bytes 753664 | tf_op jit(solution)/shard_map/concatenate | solution.py:174
  1.9 4.0 %collective-permute-start = (f32[23,2,16,128]{3,2,1,0:T(8,128)S(1)}, f32[23,2,16,128]{3,2,1,0:T(8,128)S(1)}, u32[]{:S(2)}, u32[]{:S(2)}) collective-permute-start(f32[23,2,16,128]{3,2,1,0:T(8,128)S(1)} %pad_maximum_fusion.2), channel_id=1, source_target_pairs={{0,32},{32,64},{64,96},{96,128},{128,160},{160,192},{192,224},{224... | collective-permute-start | bytes 1130504 | tf_op jit(solution)/shard_map/ppermute | solution.py:27
  5.9 1.9 %collective-permute-start.1 = (f32[23,2,16,128]{3,2,1,0:T(8,128)S(1)}, f32[23,2,16,128]{3,2,1,0:T(8,128)S(1)}, u32[]{:S(2)}, u32[]{:S(2)}) collective-permute-start(f32[23,2,16,128]{3,2,1,0:T(8,128)S(1)} %pad_maximum_fusion.2), channel_id=1, source_target_pairs={{32,0},{64,32},{96,64},{128,96},{160,128},{192,160},{224,192},{256... | collective-permute-start | bytes 1130504 | tf_op jit(solution)/shard_map/ppermute | solution.py:28
  7.8 5.6 %collective-permute-done = f32[23,2,16,128]{3,2,1,0:T(8,128)S(1)} collective-permute-done((f32[23,2,16,128]{3,2,1,0:T(8,128)S(1)}, f32[23,2,16,128]{3,2,1,0:T(8,128)S(1)}, u32[]{:S(2)}, u32[]{:S(2)}) %collective-permute-start) | collective-permute-done | bytes 376864 | tf_op jit(solution)/shard_map/ppermute | solution.py:27
  13.4 5.9 %collective-permute-done.1 = f32[23,2,16,128]{3,2,1,0:T(8,128)S(1)} collective-permute-done((f32[23,2,16,128]{3,2,1,0:T(8,128)S(1)}, f32[23,2,16,128]{3,2,1,0:T(8,128)S(1)}, u32[]{:S(2)}, u32[]{:S(2)}) %collective-permute-start.1) | collective-permute-done | bytes 376864 | tf_op jit(solution)/shard_map/ppermute | solution.py:28
  19.3 1.1 %pad_maximum_fusion.8 = (f32[23,6,2,128]{3,2,1,0:T(2,128)S(1)}, f32[23,6,2,128]{3,2,1,0:T(2,128)S(1)}) fusion(f32[23,2,16,128]{3,2,1,0:T(8,128)S(1)} %collective-permute-done.1, f32[23,2,16,128]{3,2,1,0:T(8,128)S(1)} %collective-permute-done, f32[1,2,16,128]{3,2,1,0:T(8,128)S(1)} %copy.86, f32[2,2,16,128]{3,2,1,0:T(8,128)} %param.13, ...), kind=kLoop, calls=%fused_computation.118 | loop fusion | flops 282624 | bytes 1413120 | tf_op jit(solution)/shard_map/slice | solution.py:32
  20.4 5.8 %collective-permute-start.2 = (f32[23,6,2,128]{3,2,1,0:T(2,128)S(1)}, f32[23,6,2,128]{3,2,1,0:T(2,128)S(1)}, u32[]{:S(2)}, u32[]{:S(2)}) collective-permute-start(f32[23,6,2,128]{3,2,1,0:T(2,128)S(1)} %get-tuple-element.229), channel_id=1, source_target_pairs={{0,1},{1,2},{2,3},{3,4},{4,5},{5,6},{6,7},{7,8},{8,9},{9,10},{10,1... | collective-permute-start | bytes 423944 | tf_op jit(solution)/shard_map/ppermute | solution.py:32
  26.2 1.9 %collective-permute-start.3 = (f32[23,6,2,128]{3,2,1,0:T(2,128)S(1)}, f32[23,6,2,128]{3,2,1,0:T(2,128)S(1)}, u32[]{:S(2)}, u32[]{:S(2)}) collective-permute-start(f32[23,6,2,128]{3,2,1,0:T(2,128)S(1)} %get-tuple-element.230), channel_id=1, source_target_pairs={{1,0},{2,1},{3,2},{4,3},{5,4},{6,5},{7,6},{8,7},{9,8},{10,9},{11,1... | collective-permute-start | bytes 423944 | tf_op jit(solution)/shard_map/ppermute | solution.py:33
  28.2 6.5 %collective-permute-done.3 = f32[23,6,2,128]{3,2,1,0:T(2,128)S(1)} collective-permute-done((f32[23,6,2,128]{3,2,1,0:T(2,128)S(1)}, f32[23,6,2,128]{3,2,1,0:T(2,128)S(1)}, u32[]{:S(2)}, u32[]{:S(2)}) %collective-permute-start.3) | collective-permute-done | bytes 141344 | tf_op jit(solution)/shard_map/ppermute | solution.py:33
  34.7 0.3 pad_maximum_fusion.1
  35.0 1.2 %copy-done = f32[23,6,20,128]{3,2,1,0:T(8,128)} copy-done((f32[23,6,20,128]{3,2,1,0:T(8,128)}, f32[23,6,20,128]{3,2,1,0:T(8,128)S(1)}, u32[]{:S(2)}) %copy-start) | copy-done | bytes 1413144
  36.2 0.1 fusion.60
  36.3 0.1 copy.87
  36.5 0.2 copy.103
  36.7 0.1 reshape.91
  36.8 0.1 compare_convert_fusion
  36.9 0.1 compare_convert_fusion.1
  37.0 0.7 pad_maximum_fusion.3
  37.7 2.8 %conditional.3 = (f32[20,2,16,128]{3,2,1,0:T(8,128)S(1)}, f32[2,2,16,128]{3,2,1,0:T(8,128)S(1)}) conditional(s32[]{:T(128)} %convert_element_type.36, (f32[6,20,128]{2,1,0:T(8,128)S(1)}, f32[20,6,20,128]{3,2,1,0:T(8,128)S(1)}, f32[2,6,20,128]{3,2,1,0:T(8,128)}, f32[19]{0:T(128)S(1)}, f32[19,19]{1,0:T(8,128)S(1)}) %tuple.101, ...), branch_computations={%region_1.2_spmd, %region_2.5_spmd} | conditional | flops 63246336 | bytes 22620336 | solution.py:214
  37.7 0.1 copy.91
  37.8 0.6 copy.78
  38.4 0.1 broadcast_multiply_fusion
  38.6 0.1 slice_bitcast_fusion.5
  38.7 0.1 pad.16.clone
  38.7 0.1 pad.17.clone
  38.8 0.7 fusion.12
  39.6 0.6 fusion.15
  40.3 0.1 reduce_sum.33
  40.4 0.1 reduce_sum.32
  40.6 0.2 copy.93
  40.8 4.6 %collective-permute-start.5 = (f32[20,2,16,128]{3,1,2,0:T(2,128)S(1)}, f32[20,2,16,128]{3,1,2,0:T(2,128)S(1)}, u32[]{:S(2)}, u32[]{:S(2)}) collective-permute-start(f32[20,2,16,128]{3,1,2,0:T(2,128)S(1)} %copy.93), channel_id=1, source_target_pairs={{0,32},{32,64},{64,96},{96,128},{128,160},{160,192},{192,224},{224... | collective-permute-start | bytes 983048 | tf_op jit(solution)/shard_map/ppermute | solution.py:42
  45.3 1.9 %collective-permute-start.6 = (f32[20,2,16,128]{3,1,2,0:T(2,128)S(1)}, f32[20,2,16,128]{3,1,2,0:T(2,128)S(1)}, u32[]{:S(2)}, u32[]{:S(2)}) collective-permute-start(f32[20,2,16,128]{3,1,2,0:T(2,128)S(1)} %copy.93), channel_id=1, source_target_pairs={{32,0},{64,32},{96,64},{128,96},{160,128},{192,160},{224,192},{256... | collective-permute-start | bytes 983048 | tf_op jit(solution)/shard_map/ppermute | solution.py:43
  47.3 5.8 %collective-permute-start.4 = (f32[20,1,16,128]{3,1,2,0:T(1,128)S(1)}, f32[20,1,16,128]{3,1,2,0:T(1,128)S(1)}, u32[]{:S(2)}, u32[]{:S(2)}) collective-permute-start(f32[20,1,16,128]{3,1,2,0:T(1,128)S(1)} %bitcast.152), channel_id=1, source_target_pairs={{0,64},{32,96},{64,128},{96,160},{128,192},{160,224},{192,256},{22... | collective-permute-start | bytes 491528 | tf_op jit(solution)/shard_map/ppermute | solution.py:44
  53.1 1.9 %collective-permute-start.7 = (f32[20,1,16,128]{3,1,2,0:T(1,128)S(1)}, f32[20,1,16,128]{3,1,2,0:T(1,128)S(1)}, u32[]{:S(2)}, u32[]{:S(2)}) collective-permute-start(f32[20,1,16,128]{3,1,2,0:T(1,128)S(1)} %bitcast.151), channel_id=1, source_target_pairs={{64,0},{96,32},{128,64},{160,96},{192,128},{224,160},{256,192},{28... | collective-permute-start | bytes 491528 | tf_op jit(solution)/shard_map/ppermute | solution.py:45
  55.1 2.0 %collective-permute-done.4 = f32[20,1,16,128]{3,1,2,0:T(1,128)S(1)} collective-permute-done((f32[20,1,16,128]{3,1,2,0:T(1,128)S(1)}, f32[20,1,16,128]{3,1,2,0:T(1,128)S(1)}, u32[]{:S(2)}, u32[]{:S(2)}) %collective-permute-start.4) | collective-permute-done | bytes 163872 | tf_op jit(solution)/shard_map/ppermute | solution.py:44
  57.1 7.1 %collective-permute-done.7 = f32[20,1,16,128]{3,1,2,0:T(1,128)S(1)} collective-permute-done((f32[20,1,16,128]{3,1,2,0:T(1,128)S(1)}, f32[20,1,16,128]{3,1,2,0:T(1,128)S(1)}, u32[]{:S(2)}, u32[]{:S(2)}) %collective-permute-start.7) | collective-permute-done | bytes 163872 | tf_op jit(solution)/shard_map/ppermute | solution.py:45
  64.2 1.3 %concatenate.33 = f32[20,8,16,128]{3,1,2,0:T(8,128)S(1)} concatenate(f32[20,1,16,128]{3,1,2,0:T(1,128)S(1)} %collective-permute-done.4, f32[20,2,16,128]{3,1,2,0:T(2,128)S(1)} %collective-permute-done.5, f32[20,2,16,128]{3,1,2,0:T(2,128)S(1)} %copy.93, f32[20,2,16,128]{3,1,2,0:T(2,128)S(1)} %collective-permute-done.6, f32[20,1,16,128]{3,1,2,0:T(1,128)S(1)} %collective-permute-done.7), dimensions={1} | concatenate | bytes 2621440 | tf_op jit(solution)/shard_map/concatenate | solution.py:46
  65.6 5.5 %collective-permute-start.8 = (f32[20,8,3,128]{3,1,2,0:T(8,128)S(1)}, f32[20,8,3,128]{3,1,2,0:T(8,128)S(1)}, u32[]{:S(2)}, u32[]{:S(2)}) collective-permute-start(f32[20,8,3,128]{3,1,2,0:T(8,128)S(1)} %get-tuple-element.227), channel_id=1, source_target_pairs={{0,1},{1,2},{2,3},{3,4},{4,5},{5,6},{6,7},{7,8},{8,9},{9,10},{10,1... | collective-permute-start | bytes 737288 | tf_op jit(solution)/shard_map/ppermute | solution.py:48
  71.1 1.9 %collective-permute-start.9 = (f32[20,8,3,128]{3,1,2,0:T(8,128)S(1)}, f32[20,8,3,128]{3,1,2,0:T(8,128)S(1)}, u32[]{:S(2)}, u32[]{:S(2)}) collective-permute-start(f32[20,8,3,128]{3,1,2,0:T(8,128)S(1)} %get-tuple-element.228), channel_id=1, source_target_pairs={{1,0},{2,1},{3,2},{4,3},{5,4},{6,5},{7,6},{8,7},{9,8},{10,9},{11,1... | collective-permute-start | bytes 737288 | tf_op jit(solution)/shard_map/ppermute | solution.py:49
  73.0 0.6 fusion.55
  73.7 0.1 copy.99
  73.8 0.1 lt.47
  74.0 0.3 collective-permute-done.8
  74.3 6.5 %collective-permute-done.9 = f32[20,8,3,128]{3,1,2,0:T(8,128)S(1)} collective-permute-done((f32[20,8,3,128]{3,1,2,0:T(8,128)S(1)}, f32[20,8,3,128]{3,1,2,0:T(8,128)S(1)}, u32[]{:S(2)}, u32[]{:S(2)}) %collective-permute-start.9) | collective-permute-done | bytes 245792 | tf_op jit(solution)/shard_map/ppermute | solution.py:49
  80.7 1.4 %pad_maximum_fusion = f32[20,8,22,128]{3,1,2,0:T(8,128)S(1)} fusion(f32[20,8,3,128]{3,1,2,0:T(8,128)S(1)} %collective-permute-done.9, f32[20,8,16,128]{3,1,2,0:T(8,128)} %copy-done.2, f32[20,8,3,128]{3,1,2,0:T(8,128)S(1)} %collective-permute-done.8), kind=kLoop, calls=%fused_computation.109 | loop fusion | flops 901120 | bytes 3604480 | tf_op jit(solution)/shard_map/concatenate | solution.py:50
  82.2 5.0 %conditional.4 = (f32[20,4,18,128]{3,0,2,1:T(8,128)S(1)}, f32[5,6,34,128]{3,2,1,0:T(8,128)}, f32[2,2,16,128]{3,2,1,0:T(8,128)}) conditional(s32[]{:T(128)} %convert_element_type.36, (f32[6,20,128]{2,1,0:T(8,128)S(1)}, f32[20,8,22,128]{3,1,2,0:T(8,128)S(1)}, f32[2,6,20,128]{3,2,1,0:T(8,128)}, f32[19]{0:T(128)S(1)}, f32[19,19]{1,0:T(8,128)S(1)}, ...), branch_computations={%region_6.7_spmd, %region_7.10_spmd} | conditional | flops 122580992 | bytes 25361436 | solution.py:242
  82.4 1.4 %copy.80 = f32[5,8,2,22,2,128]{5,2,1,4,3,0:T(2,128)S(1)} copy(f32[5,8,2,22,2,128]{5,1,3,4,2,0:T(8,128)S(1)} %bitcast.134) | data formatting | bytes 3604480 | tf_op jit(solution)/shard_map/cond/branch_1_fun/transpose | solution.py:68
  83.9 0.1 pad.24.clone
  84.0 0.1 pad.25.clone
  84.0 0.6 fusion.45
  84.7 0.5 fusion.48
  85.2 0.1 reduce_sum.35
  85.4 0.1 reduce_sum.34
  85.5 0.6 copy.82
  86.2 0.9 copy.81
  87.1 8.8 %collective-permute-start.10 = (f32[2,2,16,128]{3,2,1,0:T(8,128)}, f32[2,2,16,128]{3,2,1,0:T(8,128)S(1)}, u32[]{:S(2)}, u32[]{:S(2)}) collective-permute-start(f32[2,2,16,128]{3,2,1,0:T(8,128)} %get-tuple-element.92), channel_id=1, source_target_pairs={{0,512},{512,0},{1,513},{513,1},{2,514},{514,2},{3,515},{515,3},{4... | collective-permute-start | bytes 98312 | tf_op jit(solution)/shard_map/ppermute | solution.py:243
  95.9 0.1 fusion.56
  96.0 1.4 %collective-permute-done.10 = f32[2,2,16,128]{3,2,1,0:T(8,128)S(1)} collective-permute-done((f32[2,2,16,128]{3,2,1,0:T(8,128)}, f32[2,2,16,128]{3,2,1,0:T(8,128)S(1)}, u32[]{:S(2)}, u32[]{:S(2)}) %collective-permute-start.10) | collective-permute-done | bytes 32800 | tf_op jit(solution)/shard_map/ppermute | solution.py:243
  97.4 4.0 %conditional.5 = (f32[1,20,2,16,128]{4,3,2,1,0:T(8,128)S(1)}) conditional(s32[]{:T(128)} %convert_element_type.36, (f32[2,16,128]{2,1,0:T(8,128)S(1)}, f32[20,4,18,128]{3,0,2,1:T(8,128)S(1)}, f32[2,2,16,128]{3,2,1,0:T(8,128)S(1)}, f32[19]{0:T(128)S(1)}, f32[19,19]{1,0:T(8,128)S(1)}) %tuple.103, (f32[4,32,128]{2,1,0:T(8,128)S(1)}, ...), branch_computations={%region_10.11_spmd, %region_11.12_spmd} | conditional | flops 19365888 | bytes 4157960 | solution.py:253
  97.4 0.9 slice_bitcast_fusion.19
  98.4 1.0 subtract_dynamic-update-slice_fusion
  99.4 2.0 %add_multiply_fusion.5 = f32[5,4,32,128]{3,2,1,0:T(8,128)S(1)} fusion(f32[5,4,32,128]{3,2,1,0:T(8,128)S(1)} %broadcast_dynamic-update-slice_fusion, f32[5,6,34,128]{3,2,1,0:T(8,128)} %get-tuple-element.82, f32[4,32,128]{2,1,0:T(8,128)S(1)} %get-tuple-element.226, f32[4,32,128]{2,1,0:T(8,128)S(1)} %get-tuple-element.224, f32[4,32,128]{2,1,0:T(8,128)S(1)} %get-tuple-element.81), kind=kLoop, calls=%fused_computation.100 | loop fusion | flops 1310720 | bytes 2490368 | tf_op jit(solution)/shard_map/cond/branch_1_fun/mul | solution.py:128
  101.5 0.7 copy-done.4
  (57 shorter events, 0.9 us)
Async XLA Ops:
  0.0 34.7 %copy-start.1 = (f32[1,20,2,16,128]{4,3,2,1,0:T(8,128)S(1)}, f32[1,20,2,16,128]{4,3,2,1,0:T(8,128)}, u32[]{:S(2)}) copy-start(f32[1,20,2,16,128]{4,3,2,1,0:T(8,128)} %param.11) | copy-start | bytes 983044
  0.0 34.7 %copy-start.3 = (f32[2,2,16,128]{3,2,1,0:T(8,128)S(1)}, f32[2,2,16,128]{3,2,1,0:T(8,128)}, u32[]{:S(2)}) copy-start(f32[2,2,16,128]{3,2,1,0:T(8,128)} %param.13) | copy-start | bytes 98308
  0.0 28.1 %copy-start.10 = (s32[19]{0:T(128)S(1)}, s32[19]{0:T(128)}, u32[]{:S(2)}) copy-start(s32[19]{0:T(128)} %param.14) | copy-start | bytes 232
  1.9 11.5 %collective-permute-start = (f32[23,2,16,128]{3,2,1,0:T(8,128)S(1)}, f32[23,2,16,128]{3,2,1,0:T(8,128)S(1)}, u32[]{:S(2)}, u32[]{:S(2)}) collective-permute-start(f32[23,2,16,128]{3,2,1,0:T(8,128)S(1)} %pad_maximum_fusion.2), channel_id=1, source_target_pairs={{0,32},{32,64},{64,96},{96,128},{128,160},{160,192},{192,224},{224... | collective-permute-start | bytes 1130504 | tf_op jit(solution)/shard_map/ppermute | solution.py:27
  5.9 13.4 %collective-permute-start.1 = (f32[23,2,16,128]{3,2,1,0:T(8,128)S(1)}, f32[23,2,16,128]{3,2,1,0:T(8,128)S(1)}, u32[]{:S(2)}, u32[]{:S(2)}) collective-permute-start(f32[23,2,16,128]{3,2,1,0:T(8,128)S(1)} %pad_maximum_fusion.2), channel_id=1, source_target_pairs={{32,0},{64,32},{96,64},{128,96},{160,128},{192,160},{224,192},{256... | collective-permute-start | bytes 1130504 | tf_op jit(solution)/shard_map/ppermute | solution.py:28
  20.4 7.8 %collective-permute-start.2 = (f32[23,6,2,128]{3,2,1,0:T(2,128)S(1)}, f32[23,6,2,128]{3,2,1,0:T(2,128)S(1)}, u32[]{:S(2)}, u32[]{:S(2)}) collective-permute-start(f32[23,6,2,128]{3,2,1,0:T(2,128)S(1)} %get-tuple-element.229), channel_id=1, source_target_pairs={{0,1},{1,2},{2,3},{3,4},{4,5},{5,6},{6,7},{7,8},{8,9},{9,10},{10,1... | collective-permute-start | bytes 423944 | tf_op jit(solution)/shard_map/ppermute | solution.py:32
  26.2 8.5 %collective-permute-start.3 = (f32[23,6,2,128]{3,2,1,0:T(2,128)S(1)}, f32[23,6,2,128]{3,2,1,0:T(2,128)S(1)}, u32[]{:S(2)}, u32[]{:S(2)}) collective-permute-start(f32[23,6,2,128]{3,2,1,0:T(2,128)S(1)} %get-tuple-element.230), channel_id=1, source_target_pairs={{1,0},{2,1},{3,2},{4,3},{5,4},{6,5},{7,6},{8,7},{9,8},{10,9},{11,1... | collective-permute-start | bytes 423944 | tf_op jit(solution)/shard_map/ppermute | solution.py:33
  35.0 1.2 %copy-start = (f32[23,6,20,128]{3,2,1,0:T(8,128)}, f32[23,6,20,128]{3,2,1,0:T(8,128)S(1)}, u32[]{:S(2)}) copy-start(f32[23,6,20,128]{3,2,1,0:T(8,128)S(1)} %pad_maximum_fusion.1) | copy-start | bytes 4239364
  36.3 1.4 %slice-start = ((f32[23,6,20,128]{3,2,1,0:T(8,128)}), f32[20,6,20,128]{3,2,1,0:T(8,128)S(1)}, s32[]{:S(2)}) async-start(f32[23,6,20,128]{3,2,1,0:T(8,128)} %copy-done), calls=%async_computation | async-start | bytes 2949120 | tf_op jit(solution)/shard_map/slice | solution.py:186
  36.3 1.4 %copy-start.9 = (f32[19]{0:T(128)S(1)}, f32[19]{0:T(128)}, u32[]{:S(2)}) copy-start(f32[19]{0:T(128)} %param.15) | copy-start | bytes 232
  40.6 4.8 %copy-start.5 = (f32[2,2,16,128]{3,2,1,0:T(8,128)}, f32[2,2,16,128]{3,2,1,0:T(8,128)S(1)}, u32[]{:S(2)}) copy-start(f32[2,2,16,128]{3,2,1,0:T(8,128)S(1)} %get-tuple-element.90) | copy-start | bytes 98308
  40.8 23.4 %collective-permute-start.5 = (f32[20,2,16,128]{3,1,2,0:T(2,128)S(1)}, f32[20,2,16,128]{3,1,2,0:T(2,128)S(1)}, u32[]{:S(2)}, u32[]{:S(2)}) collective-permute-start(f32[20,2,16,128]{3,1,2,0:T(2,128)S(1)} %copy.93), channel_id=1, source_target_pairs={{0,32},{32,64},{64,96},{96,128},{128,160},{160,192},{192,224},{224... | collective-permute-start | bytes 983048 | tf_op jit(solution)/shard_map/ppermute | solution.py:42
  45.3 18.9 %collective-permute-start.6 = (f32[20,2,16,128]{3,1,2,0:T(2,128)S(1)}, f32[20,2,16,128]{3,1,2,0:T(2,128)S(1)}, u32[]{:S(2)}, u32[]{:S(2)}) collective-permute-start(f32[20,2,16,128]{3,1,2,0:T(2,128)S(1)} %copy.93), channel_id=1, source_target_pairs={{32,0},{64,32},{96,64},{128,96},{160,128},{192,160},{224,192},{256... | collective-permute-start | bytes 983048 | tf_op jit(solution)/shard_map/ppermute | solution.py:43
  47.3 9.8 %collective-permute-start.4 = (f32[20,1,16,128]{3,1,2,0:T(1,128)S(1)}, f32[20,1,16,128]{3,1,2,0:T(1,128)S(1)}, u32[]{:S(2)}, u32[]{:S(2)}) collective-permute-start(f32[20,1,16,128]{3,1,2,0:T(1,128)S(1)} %bitcast.152), channel_id=1, source_target_pairs={{0,64},{32,96},{64,128},{96,160},{128,192},{160,224},{192,256},{22... | collective-permute-start | bytes 491528 | tf_op jit(solution)/shard_map/ppermute | solution.py:44
  53.1 20.6 %copy-start.8 = (s32[4,2,16]{2,1,0:T(2,128)S(1)}, s32[4,2,16]{2,1,0:T(2,128)}, u32[]{:S(2)}) copy-start(s32[4,2,16]{2,1,0:T(2,128)} %param.12) | copy-start | bytes 1540
  53.1 11.1 %collective-permute-start.7 = (f32[20,1,16,128]{3,1,2,0:T(1,128)S(1)}, f32[20,1,16,128]{3,1,2,0:T(1,128)S(1)}, u32[]{:S(2)}, u32[]{:S(2)}) collective-permute-start(f32[20,1,16,128]{3,1,2,0:T(1,128)S(1)} %bitcast.151), channel_id=1, source_target_pairs={{64,0},{96,32},{128,64},{160,96},{192,128},{224,160},{256,192},{28... | collective-permute-start | bytes 491528 | tf_op jit(solution)/shard_map/ppermute | solution.py:45
  65.5 8.7 %copy-start.2 = (f32[20,8,16,128]{3,1,2,0:T(8,128)}, f32[20,8,16,128]{3,1,2,0:T(8,128)S(1)}, u32[]{:S(2)}) copy-start(f32[20,8,16,128]{3,1,2,0:T(8,128)S(1)} %concatenate.33) | copy-start | bytes 3932164
  65.6 8.7 %collective-permute-start.8 = (f32[20,8,3,128]{3,1,2,0:T(8,128)S(1)}, f32[20,8,3,128]{3,1,2,0:T(8,128)S(1)}, u32[]{:S(2)}, u32[]{:S(2)}) collective-permute-start(f32[20,8,3,128]{3,1,2,0:T(8,128)S(1)} %get-tuple-element.227), channel_id=1, source_target_pairs={{0,1},{1,2},{2,3},{3,4},{4,5},{5,6},{6,7},{7,8},{8,9},{9,10},{10,1... | collective-permute-start | bytes 737288 | tf_op jit(solution)/shard_map/ppermute | solution.py:48
  71.1 9.6 %collective-permute-start.9 = (f32[20,8,3,128]{3,1,2,0:T(8,128)S(1)}, f32[20,8,3,128]{3,1,2,0:T(8,128)S(1)}, u32[]{:S(2)}, u32[]{:S(2)}) collective-permute-start(f32[20,8,3,128]{3,1,2,0:T(8,128)S(1)} %get-tuple-element.228), channel_id=1, source_target_pairs={{1,0},{2,1},{3,2},{4,3},{5,4},{6,5},{7,6},{8,7},{9,8},{10,9},{11,1... | collective-permute-start | bytes 737288 | tf_op jit(solution)/shard_map/ppermute | solution.py:49
  74.0 8.2 %copy-start.7 = (f32[128,128]{1,0:T(8,128)S(1)}, f32[128,128]{1,0:T(8,128)}, u32[]{:S(2)}) copy-start(f32[128,128]{1,0:T(8,128)} %fusion.55) | copy-start | bytes 196612
  84.7 0.8 copy-start.6
  87.1 10.3 %collective-permute-start.10 = (f32[2,2,16,128]{3,2,1,0:T(8,128)}, f32[2,2,16,128]{3,2,1,0:T(8,128)S(1)}, u32[]{:S(2)}, u32[]{:S(2)}) collective-permute-start(f32[2,2,16,128]{3,2,1,0:T(8,128)} %get-tuple-element.92), channel_id=1, source_target_pairs={{0,512},{512,0},{1,513},{513,1},{2,514},{514,2},{3,515},{515,3},{4... | collective-permute-start | bytes 98312 | tf_op jit(solution)/shard_map/ppermute | solution.py:243
  101.4 0.7 copy-start.4

commit v4 on v2

--- a/solution.py
+++ b/solution.py
@@ -24,10 +24,15 @@
 
 def halo_wide(block):
     up, down = shifts("gx")
-    before = lax.ppermute(block, "gx", up)
-    after = lax.ppermute(block, "gx", down)
-    wide = jnp.concatenate([before, block, after], axis=1)
-    rows = block.shape[1]
+    peers = lax.axis_size("gx")
+    up2 = [(i, i + 2) for i in range(peers - 2)]
+    down2 = [(j, i) for i, j in up2]
+    b1 = lax.ppermute(block, "gx", up)
+    a1 = lax.ppermute(block, "gx", down)
+    b2 = lax.ppermute(block, "gx", up2)
+    a2 = lax.ppermute(block, "gx", down2)
+    wide = jnp.concatenate([b2, b1, block, a1, a2], axis=1)
+    rows = 2 * block.shape[1]
     up, down = shifts("gy")
     below = lax.ppermute(wide[:, :, -rows:], "gy", up)
     above = lax.ppermute(wide[:, :, :rows], "gy", down)
@@ -183,14 +188,12 @@
     wet_fine_ext = wet_of_float(fine_levels(levels_ext), depth)
 
     def ocean_a():
-        fine = to_fine(state_ext)
-        reach = 2 * margin
+        fine = trim(to_fine(state_ext), 2 * margin - NSUB - 1)
         running = jnp.zeros((2, size_x, size_y, depth), jnp.float32)
         for substep in range(NSUB):
-            fine = ocean_substep(fine, trim(wet_fine_ext, substep + 1), 0.0)
-            left = reach - substep - 1
-            running = running + coarse_mean(trim(fine[0:2], left))
-        return to_coarse(fine), running
+            fine = ocean_substep(fine, trim(wet_fine_ext, 2 * margin - NSUB + substep), 0.0)
+            running = running + coarse_mean(trim(fine[0:2], NSUB - substep))
+        return jnp.zeros((channels, size_x, size_y, depth), jnp.float32), fine, running / NSUB
 
     def tracer_a():
         tracer = state_ext
@@ -202,36 +205,19 @@
                 onehot,
                 eco_rate,
             )
-        return tracer, jnp.zeros((2, size_x, size_y, depth), jnp.float32)
-
-    block_a, running = lax.cond(is_ocean, ocean_a, tracer_a)
-    ext2 = halo_wide(block_a)
-
-    def ocean_b():
-        return block_a, running / NSUB
-
-    def tracer_b():
-        tracer = ext2
-        for substep in range(margin):
-            tracer = tracer_substep(
-                tracer,
-                trim(wet_coarse_ext, substep + 1),
-                trim(flux_ext, substep + 1),
-                onehot,
-                eco_rate,
-            )
         absorbed = absorption(tracer, wet_coarse, above_table)
-        return tracer, jnp.broadcast_to(absorbed[None], (2, size_x, size_y, depth))
-
-    block_b, outgoing = lax.cond(is_ocean, ocean_b, tracer_b)
-    ext3 = halo_one(block_b)
+        outgoing = jnp.broadcast_to(absorbed[None], (2, size_x, size_y, depth))
+        fine_shape = (channels // 4, 2 * size_x + 2, 2 * size_y + 2, depth)
+        return tracer, jnp.zeros(fine_shape, jnp.float32), outgoing
+
+    tracer_blk, ocean_fine, outgoing = lax.cond(is_ocean, ocean_a, tracer_a)
+    ext3 = halo_one(tracer_blk)
     arrived = lax.ppermute(outgoing, "half", [(0, 1), (1, 0)])
 
     def ocean_c():
-        fine = trim(to_fine(ext3), 1)
         light = arrived[0:1]
         heating = HEATING * to_fine(jnp.broadcast_to(light, (4, size_x, size_y, depth)))[0]
-        return to_coarse(ocean_substep(fine, wet_fine, heating))
+        return to_coarse(ocean_substep(ocean_fine, wet_fine, heating))
 
     def tracer_c():
         return tracer_substep(ext3, wet_coarse, arrived, onehot, eco_rate)

time: 98.6 us -> 109 us (1.11)
  the two profiles are of different devices: /device:TPU:228 before, /device:TPU:219 now
where the time goes in v4:
time: 109 us; the launch traced here: 108 us
  starting transfers between devices  50.2 us (46%)
  waiting for transfers between devices  35.8 us (33%)
  other arithmetic  15.4 us (14%)
  local copies, waits for them, and re-layouts  5.93 us (5%)
    ppermute x1, starting transfers between devices, body(): arrived = lax.ppermute(outgoing, 'half', [(0, 1), (1, 0)])  11.7 us
    ppermute x1, waiting for transfers between devices, halo_wide(): b1 = lax.ppermute(block, 'gx', up)  10 us
    ppermute x1, starting transfers between devices, halo_one(): xb = lax.ppermute(block[:, -1:], 'gx', up)  8.82 us
    ppermute x1, starting transfers between devices, halo_wide(): b2 = lax.ppermute(block, 'gx', up2)  7.02 us
    ppermute x1, waiting for transfers between devices, halo_wide(): above = lax.ppermute(wide[:, :, :rows], 'gy', down)  6.57 us
    ppermute x1, starting transfers between devices, halo_wide(): below = lax.ppermute(wide[:, :, -rows:], 'gy', up)  6.24 us
    ppermute x1, waiting for transfers between devices, halo_wide(): a2 = lax.ppermute(block, 'gx', down2)  5.61 us
    mul x5, other arithmetic, ocean_substep(): return wet_mask * (centre + DT * (NU * spread - advect + forcing))  5.45 us
  transfers between devices with their start and end apart: 11, of which 7 were waited for; matrix products, arithmetic and copies ran while one was open for 1% of the time, Pallas kernels for 0%

profile of v4, /device:TPU:219, one launch (start us, length us, event | category | flops | bytes accessed | tf_op | source)
XLA Modules:
  0.0 108.2 jit_solution(16407098611326700365)
XLA Ops:
  0.0 0.8 fusion.54
  0.8 0.7 fusion.59
  1.5 0.7 reduce_max.18
  2.2 0.7 fusion.57
  2.9 0.1 copy.32
  2.9 1.0 conditional.3
  2.9 1.0 bitcast_multiply_fusion.1
  3.9 0.8 pad_maximum_fusion.1
  4.7 7.0 %collective-permute-start = (f32[23,2,16,128]{3,2,1,0:T(8,128)S(1)}, f32[23,2,16,128]{3,2,1,0:T(8,128)S(1)}, u32[]{:S(2)}, u32[]{:S(2)}) collective-permute-start(f32[23,2,16,128]{3,2,1,0:T(8,128)S(1)} %pad_maximum_fusion.1), channel_id=1, source_target_pairs={{0,64},{32,96},{64,128},{96,160},{128,192},{160,224},{192,256},{22... | collective-permute-start | bytes 1130504 | tf_op jit(solution)/shard_map/ppermute | solution.py:32
  11.8 4.0 %collective-permute-start.1 = (f32[23,2,16,128]{3,2,1,0:T(8,128)S(1)}, f32[23,2,16,128]{3,2,1,0:T(8,128)S(1)}, u32[]{:S(2)}, u32[]{:S(2)}) collective-permute-start(f32[23,2,16,128]{3,2,1,0:T(8,128)S(1)} %pad_maximum_fusion.1), channel_id=1, source_target_pairs={{0,32},{32,64},{64,96},{96,128},{128,160},{160,192},{192,224},{224... | collective-permute-start | bytes 1130504 | tf_op jit(solution)/shard_map/ppermute | solution.py:30
  15.8 1.9 %collective-permute-start.2 = (f32[23,2,16,128]{3,2,1,0:T(8,128)S(1)}, f32[23,2,16,128]{3,2,1,0:T(8,128)S(1)}, u32[]{:S(2)}, u32[]{:S(2)}) collective-permute-start(f32[23,2,16,128]{3,2,1,0:T(8,128)S(1)} %pad_maximum_fusion.1), channel_id=1, source_target_pairs={{32,0},{64,32},{96,64},{128,96},{160,128},{192,160},{224,192},{256... | collective-permute-start | bytes 1130504 | tf_op jit(solution)/shard_map/ppermute | solution.py:31
  17.7 1.9 %collective-permute-start.3 = (f32[23,2,16,128]{3,2,1,0:T(8,128)S(1)}, f32[23,2,16,128]{3,2,1,0:T(8,128)S(1)}, u32[]{:S(2)}, u32[]{:S(2)}) collective-permute-start(f32[23,2,16,128]{3,2,1,0:T(8,128)S(1)} %pad_maximum_fusion.1), channel_id=1, source_target_pairs={{64,0},{96,32},{128,64},{160,96},{192,128},{224,160},{256,192},{28... | collective-permute-start | bytes 1130504 | tf_op jit(solution)/shard_map/ppermute | solution.py:33
  19.6 0.6 fusion.55
  20.3 5.2 %collective-permute-done = f32[23,2,16,128]{3,2,1,0:T(8,128)S(1)} collective-permute-done((f32[23,2,16,128]{3,2,1,0:T(8,128)S(1)}, f32[23,2,16,128]{3,2,1,0:T(8,128)S(1)}, u32[]{:S(2)}, u32[]{:S(2)}) %collective-permute-start) | collective-permute-done | bytes 376864 | tf_op jit(solution)/shard_map/ppermute | solution.py:32
  25.5 10.0 %collective-permute-done.1 = f32[23,2,16,128]{3,2,1,0:T(8,128)S(1)} collective-permute-done((f32[23,2,16,128]{3,2,1,0:T(8,128)S(1)}, f32[23,2,16,128]{3,2,1,0:T(8,128)S(1)}, u32[]{:S(2)}, u32[]{:S(2)}) %collective-permute-start.1) | collective-permute-done | bytes 376864 | tf_op jit(solution)/shard_map/ppermute | solution.py:30
  35.5 0.0 copy-start.3
  35.6 5.6 %collective-permute-done.3 = f32[23,2,16,128]{3,2,1,0:T(8,128)S(1)} collective-permute-done((f32[23,2,16,128]{3,2,1,0:T(8,128)S(1)}, f32[23,2,16,128]{3,2,1,0:T(8,128)S(1)}, u32[]{:S(2)}, u32[]{:S(2)}) %collective-permute-start.3) | collective-permute-done | bytes 376864 | tf_op jit(solution)/shard_map/ppermute | solution.py:33
  41.3 0.2 fusion.61
  41.4 6.2 %collective-permute-start.4 = (f32[23,10,4,128]{3,2,1,0:T(4,128)S(1)}, f32[23,10,4,128]{3,2,1,0:T(4,128)S(1)}, u32[]{:S(2)}, u32[]{:S(2)}) collective-permute-start(f32[23,10,4,128]{3,2,1,0:T(4,128)S(1)} %get-tuple-element.151), channel_id=1, source_target_pairs={{0,1},{1,2},{2,3},{3,4},{4,5},{5,6},{6,7},{7,8},{8,9},{9,10},{10,1... | collective-permute-start | bytes 1413128 | tf_op jit(solution)/shard_map/ppermute | solution.py:37
  47.7 1.9 %collective-permute-start.5 = (f32[23,10,4,128]{3,2,1,0:T(4,128)S(1)}, f32[23,10,4,128]{3,2,1,0:T(4,128)}, u32[]{:S(2)}, u32[]{:S(2)}) collective-permute-start(f32[23,10,4,128]{3,2,1,0:T(4,128)S(1)} %get-tuple-element.152), channel_id=1, source_target_pairs={{1,0},{2,1},{3,2},{4,3},{5,4},{6,5},{7,6},{8,7},{9,8},{10,9},{11,1... | collective-permute-start | bytes 1413128 | tf_op jit(solution)/shard_map/ppermute | solution.py:38
  49.6 0.1 copy.36
  49.7 0.1 lt.57
  49.8 0.1 fusion.58
  49.9 0.1 fusion.56
  50.0 3.3 %collective-permute-done.4 = f32[23,10,4,128]{3,2,1,0:T(4,128)S(1)} collective-permute-done((f32[23,10,4,128]{3,2,1,0:T(4,128)S(1)}, f32[23,10,4,128]{3,2,1,0:T(4,128)S(1)}, u32[]{:S(2)}, u32[]{:S(2)}) %collective-permute-start.4) | collective-permute-done | bytes 471072 | tf_op jit(solution)/shard_map/ppermute | solution.py:37
  53.2 6.6 %collective-permute-done.5 = f32[23,10,4,128]{3,2,1,0:T(4,128)} collective-permute-done((f32[23,10,4,128]{3,2,1,0:T(4,128)S(1)}, f32[23,10,4,128]{3,2,1,0:T(4,128)}, u32[]{:S(2)}, u32[]{:S(2)}) %collective-permute-start.5) | collective-permute-done | bytes 471072 | tf_op jit(solution)/shard_map/ppermute | solution.py:38
  59.8 1.5 %pad_maximum_fusion = f32[23,10,24,128]{3,2,1,0:T(8,128)S(1)} fusion(f32[23,10,4,128]{3,2,1,0:T(4,128)} %collective-permute-done.5, f32[23,10,16,128]{3,2,1,0:T(8,128)S(1)} %constant_dynamic-update-slice_fusion.1, f32[23,10,4,128]{3,2,1,0:T(4,128)S(1)} %collective-permute-done.4), kind=kLoop, calls=%fused_computation.105 | loop fusion | flops 1413120 | bytes 5652480 | tf_op jit(solution)/shard_map/concatenate | solution.py:39
  61.3 0.2 slice.406
  61.5 1.3 %copy-done = f32[23,10,24,128]{3,2,1,0:T(8,128)} copy-done((f32[23,10,24,128]{3,2,1,0:T(8,128)}, f32[23,10,24,128]{3,2,1,0:T(8,128)S(1)}, u32[]{:S(2)}) %copy-start) | copy-done | bytes 2826264
  62.8 0.1 fusion.60
  63.0 0.1 copy.33
  63.1 0.2 copy.34
  63.3 0.1 lt.54
  63.4 0.2 compare_convert_fusion
  63.6 0.1 compare_convert_fusion.1
  63.8 7.0 %conditional.4 = (f32[20,2,16,128]{3,0,2,1:T(8,128)S(1)}, f32[5,6,34,128]{3,2,1,0:T(8,128)}, f32[2,2,16,128]{3,2,1,0:T(8,128)S(1)}) conditional(s32[]{:T(128)} %convert_element_type.42, (f32[10,24,128]{2,1,0:T(8,128)S(1)}, f32[20,10,24,128]{3,2,1,0:T(8,128)S(1)}, f32[23,10,24,128]{3,2,1,0:T(8,128)}, f32[19]{0:T(128)S(1)}, f32[19,19]{1,0:T(8,128)S(1)}, ...), branch_computations={%region_4.5_spmd, %region_5.10_spmd} | conditional | flops 248459264 | bytes 49717276 | solution.py:213
  64.0 1.3 %copy.28 = f32[5,10,2,24,2,128]{5,4,3,2,1,0:T(2,128)S(1)} copy(f32[5,10,2,24,2,128]{5,3,1,4,2,0:T(8,128)S(1)} %bitcast.125) | data formatting | bytes 4915200 | tf_op jit(solution)/shard_map/cond/branch_1_fun/transpose | solution.py:57
  65.3 0.1 slice_bitcast_fusion.9
  65.4 0.1 pad.33.clone
  65.5 0.1 pad.34.clone
  65.6 0.9 fusion.40
  66.5 0.1 slice_bitcast_fusion.11
  66.6 0.7 fusion.43
  67.3 0.1 slice_bitcast_fusion.13
  67.4 0.6 fusion.46
  68.1 1.3 %fusion.49 = f32[5,6,34,128]{3,2,1,0:T(8,128)} fusion(f32[1,6,34,128]{3,2,1,0:T(8,128)S(1)} %get-tuple-element.144, f32[1,6,34,128]{3,2,1,0:T(8,128)S(1)} %get-tuple-element.143, f32[5,8,36,128]{3,2,1,0:T(8,128)S(1)} %fusion.46, f32[5]{0:T(128)S(1)} %pad.34.clone, f32[5]{0:T(128)S(1)} %pad.33.clone, f32[6,34,128]{2,1,0:T(8,128)S(1)} %get-tuple-element.145, ...), kind=kLoop, calls=%fused_computation.70 | loop fusion | flops 2480640 | bytes 3655720 | tf_op jit(solution)/shard_map/cond/branch_1_fun/mul | solution.py:117
  69.4 0.9 slice.402
  70.3 0.1 reduce_sum.35
  70.4 0.1 reduce_sum.34
  70.5 0.1 reduce_sum.33
  70.7 0.1 reduce_sum.32
  70.8 11.7 %collective-permute-start.10 = (f32[2,2,16,128]{3,2,1,0:T(8,128)S(1)}, f32[2,2,16,128]{3,2,1,0:T(8,128)S(1)}, u32[]{:S(2)}, u32[]{:S(2)}) collective-permute-start(f32[2,2,16,128]{3,2,1,0:T(8,128)S(1)} %get-tuple-element.87), channel_id=1, source_target_pairs={{0,512},{512,0},{1,513},{513,1},{2,514},{514,2},{3,515},{515,3},{4... | collective-permute-start | bytes 98312 | tf_op jit(solution)/shard_map/ppermute | solution.py:215
  82.6 8.8 %collective-permute-start.6 = (f32[20,1,16,128]{3,0,2,1:T(8,128)S(1)}, f32[20,1,16,128]{3,0,2,1:T(8,128)S(1)}, u32[]{:S(2)}, u32[]{:S(2)}) collective-permute-start(f32[20,1,16,128]{3,0,2,1:T(8,128)S(1)} %get-tuple-element.156), channel_id=1, source_target_pairs={{0,32},{32,64},{64,96},{96,128},{128,160},{160,192},{192,224},{224... | collective-permute-start | bytes 491528 | tf_op jit(solution)/shard_map/ppermute | solution.py:44
  91.4 1.9 %collective-permute-start.7 = (f32[20,1,16,128]{3,0,2,1:T(8,128)S(1)}, f32[20,1,16,128]{3,0,2,1:T(8,128)S(1)}, u32[]{:S(2)}, u32[]{:S(2)}) collective-permute-start(f32[20,1,16,128]{3,0,2,1:T(8,128)S(1)} %get-tuple-element.155), channel_id=1, source_target_pairs={{32,0},{64,32},{96,64},{128,96},{160,128},{192,160},{224,192},{256... | collective-permute-start | bytes 491528 | tf_op jit(solution)/shard_map/ppermute | solution.py:45
  93.3 2.8 %collective-permute-start.8 = (f32[20,2,1,128]{3,0,2,1:T(8,128)S(1)}, f32[20,2,1,128]{3,0,2,1:T(8,128)S(1)}, u32[]{:S(2)}, u32[]{:S(2)}) collective-permute-start(f32[20,2,1,128]{3,0,2,1:T(8,128)S(1)} %get-tuple-element.153), channel_id=1, source_target_pairs={{0,1},{1,2},{2,3},{3,4},{4,5},{5,6},{6,7},{7,8},{8,9},{9,10},{10,1... | collective-permute-start | bytes 61448 | tf_op jit(solution)/shard_map/ppermute | solution.py:47
  96.2 1.9 %collective-permute-start.9 = (f32[20,2,1,128]{3,0,2,1:T(8,128)S(1)}, f32[20,2,1,128]{3,0,2,1:T(8,128)S(1)}, u32[]{:S(2)}, u32[]{:S(2)}) collective-permute-start(f32[20,2,1,128]{3,0,2,1:T(8,128)S(1)} %get-tuple-element.154), channel_id=1, source_target_pairs={{1,0},{2,1},{3,2},{4,3},{5,4},{6,5},{7,6},{8,7},{9,8},{10,9},{11,1... | collective-permute-start | bytes 61448 | tf_op jit(solution)/shard_map/ppermute | solution.py:48
  98.2 1.5 %collective-permute-done.7 = f32[20,1,16,128]{3,0,2,1:T(8,128)S(1)} collective-permute-done((f32[20,1,16,128]{3,0,2,1:T(8,128)S(1)}, f32[20,1,16,128]{3,0,2,1:T(8,128)S(1)}, u32[]{:S(2)}, u32[]{:S(2)}) %collective-permute-start.7) | collective-permute-done | bytes 163872 | tf_op jit(solution)/shard_map/ppermute | solution.py:45
  99.7 3.7 %collective-permute-done.9 = f32[20,2,1,128]{3,0,2,1:T(8,128)S(1)} collective-permute-done((f32[20,2,1,128]{3,0,2,1:T(8,128)S(1)}, f32[20,2,1,128]{3,0,2,1:T(8,128)S(1)}, u32[]{:S(2)}, u32[]{:S(2)}) %collective-permute-start.9) | collective-permute-done | bytes 20512 | tf_op jit(solution)/shard_map/ppermute | solution.py:48
  103.4 0.1 select_maximum_fusion
  103.5 4.0 %conditional.5 = (f32[1,20,2,16,128]{4,3,2,1,0:T(8,128)S(1)}) conditional(s32[]{:T(128)} %convert_element_type.42, (f32[2,16,128]{2,1,0:T(8,128)}, f32[20,4,16,128]{3,0,2,1:T(8,128)S(1)}, f32[20,4,18,128]{3,0,2,1:T(8,128)S(1)}, f32[20,2,16,128]{3,0,2,1:T(8,128)S(1)}, f32[2,2,16,128]{3,2,1,0:T(8,128)S(1)}, /*index=5*/f32[19]{0:T(128)S(1)}, ...), branch_computations={%region_10.11_spmd, %region_11.12_spmd} | conditional | flops 19365888 | bytes 4157960 | solution.py:225
  103.5 1.0 slice_bitcast_fusion.19
  104.5 1.0 subtract_dynamic-update-slice_fusion
  105.5 1.9 %add_multiply_fusion.5 = f32[5,4,32,128]{3,2,1,0:T(8,128)S(1)} fusion(f32[5,4,32,128]{3,2,1,0:T(8,128)S(1)} %broadcast_dynamic-update-slice_fusion, f32[5,6,34,128]{3,2,1,0:T(8,128)} %get-tuple-element.81, f32[4,32,128]{2,1,0:T(8,128)S(1)} %get-tuple-element.150, f32[4,32,128]{2,1,0:T(8,128)S(1)} %get-tuple-element.148, f32[4,32,128]{2,1,0:T(8,128)S(1)} %get-tuple-element.80), kind=kLoop, calls=%fused_computation.96 | loop fusion | flops 1310720 | bytes 2490368 | tf_op jit(solution)/shard_map/cond/branch_1_fun/mul | solution.py:117
  107.5 0.7 copy-done.1
  (45 shorter events, 0.6 us)
Async XLA Ops:
  2.9 32.6 %copy-start.2 = (f32[2,2,16,128]{3,2,1,0:T(8,128)S(1)}, f32[2,2,16,128]{3,2,1,0:T(8,128)}, u32[]{:S(2)}) copy-start(f32[2,2,16,128]{3,2,1,0:T(8,128)} %param.13) | copy-start | bytes 98308
  4.7 20.7 %collective-permute-start = (f32[23,2,16,128]{3,2,1,0:T(8,128)S(1)}, f32[23,2,16,128]{3,2,1,0:T(8,128)S(1)}, u32[]{:S(2)}, u32[]{:S(2)}) collective-permute-start(f32[23,2,16,128]{3,2,1,0:T(8,128)S(1)} %pad_maximum_fusion.1), channel_id=1, source_target_pairs={{0,64},{32,96},{64,128},{96,160},{128,192},{160,224},{192,256},{22... | collective-permute-start | bytes 1130504 | tf_op jit(solution)/shard_map/ppermute | solution.py:32
  11.8 23.7 %collective-permute-start.1 = (f32[23,2,16,128]{3,2,1,0:T(8,128)S(1)}, f32[23,2,16,128]{3,2,1,0:T(8,128)S(1)}, u32[]{:S(2)}, u32[]{:S(2)}) collective-permute-start(f32[23,2,16,128]{3,2,1,0:T(8,128)S(1)} %pad_maximum_fusion.1), channel_id=1, source_target_pairs={{0,32},{32,64},{64,96},{96,128},{128,160},{160,192},{192,224},{224... | collective-permute-start | bytes 1130504 | tf_op jit(solution)/shard_map/ppermute | solution.py:30
  15.8 19.8 %collective-permute-start.2 = (f32[23,2,16,128]{3,2,1,0:T(8,128)S(1)}, f32[23,2,16,128]{3,2,1,0:T(8,128)S(1)}, u32[]{:S(2)}, u32[]{:S(2)}) collective-permute-start(f32[23,2,16,128]{3,2,1,0:T(8,128)S(1)} %pad_maximum_fusion.1), channel_id=1, source_target_pairs={{32,0},{64,32},{96,64},{128,96},{160,128},{192,160},{224,192},{256... | collective-permute-start | bytes 1130504 | tf_op jit(solution)/shard_map/ppermute | solution.py:31
  17.7 23.5 %collective-permute-start.3 = (f32[23,2,16,128]{3,2,1,0:T(8,128)S(1)}, f32[23,2,16,128]{3,2,1,0:T(8,128)S(1)}, u32[]{:S(2)}, u32[]{:S(2)}) collective-permute-start(f32[23,2,16,128]{3,2,1,0:T(8,128)S(1)} %pad_maximum_fusion.1), channel_id=1, source_target_pairs={{64,0},{96,32},{128,64},{160,96},{192,128},{224,160},{256,192},{28... | collective-permute-start | bytes 1130504 | tf_op jit(solution)/shard_map/ppermute | solution.py:33
  35.5 14.1 %copy-start.3 = (s32[4,2,16]{2,1,0:T(2,128)S(1)}, s32[4,2,16]{2,1,0:T(2,128)}, u32[]{:S(2)}) copy-start(s32[4,2,16]{2,1,0:T(2,128)} %param.12) | copy-start | bytes 1540
  35.6 14.3 %copy-start.6 = (s32[19]{0:T(128)S(1)}, s32[19]{0:T(128)}, u32[]{:S(2)}) copy-start(s32[19]{0:T(128)} %param.14) | copy-start | bytes 232
  41.4 11.8 %collective-permute-start.4 = (f32[23,10,4,128]{3,2,1,0:T(4,128)S(1)}, f32[23,10,4,128]{3,2,1,0:T(4,128)S(1)}, u32[]{:S(2)}, u32[]{:S(2)}) collective-permute-start(f32[23,10,4,128]{3,2,1,0:T(4,128)S(1)} %get-tuple-element.151), channel_id=1, source_target_pairs={{0,1},{1,2},{2,3},{3,4},{4,5},{5,6},{6,7},{7,8},{8,9},{9,10},{10,1... | collective-permute-start | bytes 1413128 | tf_op jit(solution)/shard_map/ppermute | solution.py:37
  47.7 12.1 %collective-permute-start.5 = (f32[23,10,4,128]{3,2,1,0:T(4,128)S(1)}, f32[23,10,4,128]{3,2,1,0:T(4,128)}, u32[]{:S(2)}, u32[]{:S(2)}) collective-permute-start(f32[23,10,4,128]{3,2,1,0:T(4,128)S(1)} %get-tuple-element.152), channel_id=1, source_target_pairs={{1,0},{2,1},{3,2},{4,3},{5,4},{6,5},{7,6},{8,7},{9,8},{10,9},{11,1... | collective-permute-start | bytes 1413128 | tf_op jit(solution)/shard_map/ppermute | solution.py:38
  61.3 1.6 %copy-start = (f32[23,10,24,128]{3,2,1,0:T(8,128)}, f32[23,10,24,128]{3,2,1,0:T(8,128)S(1)}, u32[]{:S(2)}) copy-start(f32[23,10,24,128]{3,2,1,0:T(8,128)S(1)} %pad_maximum_fusion) | copy-start | bytes 8478724
  61.3 2.4 %copy-start.4 = (f32[128,128]{1,0:T(8,128)S(1)}, f32[128,128]{1,0:T(8,128)}, u32[]{:S(2)}) copy-start(f32[128,128]{1,0:T(8,128)} %fusion.55) | copy-start | bytes 196612
  61.3 2.4 %copy-start.5 = (f32[19]{0:T(128)S(1)}, f32[19]{0:T(128)}, u32[]{:S(2)}) copy-start(f32[19]{0:T(128)} %param.15) | copy-start | bytes 232
  70.8 27.3 %collective-permute-start.10 = (f32[2,2,16,128]{3,2,1,0:T(8,128)S(1)}, f32[2,2,16,128]{3,2,1,0:T(8,128)S(1)}, u32[]{:S(2)}, u32[]{:S(2)}) collective-permute-start(f32[2,2,16,128]{3,2,1,0:T(8,128)S(1)} %get-tuple-element.87), channel_id=1, source_target_pairs={{0,512},{512,0},{1,513},{513,1},{2,514},{514,2},{3,515},{515,3},{4... | collective-permute-start | bytes 98312 | tf_op jit(solution)/shard_map/ppermute | solution.py:215
  82.6 15.5 %collective-permute-start.6 = (f32[20,1,16,128]{3,0,2,1:T(8,128)S(1)}, f32[20,1,16,128]{3,0,2,1:T(8,128)S(1)}, u32[]{:S(2)}, u32[]{:S(2)}) collective-permute-start(f32[20,1,16,128]{3,0,2,1:T(8,128)S(1)} %get-tuple-element.156), channel_id=1, source_target_pairs={{0,32},{32,64},{64,96},{96,128},{128,160},{160,192},{192,224},{224... | collective-permute-start | bytes 491528 | tf_op jit(solution)/shard_map/ppermute | solution.py:44
  91.4 8.3 %collective-permute-start.7 = (f32[20,1,16,128]{3,0,2,1:T(8,128)S(1)}, f32[20,1,16,128]{3,0,2,1:T(8,128)S(1)}, u32[]{:S(2)}, u32[]{:S(2)}) collective-permute-start(f32[20,1,16,128]{3,0,2,1:T(8,128)S(1)} %get-tuple-element.155), channel_id=1, source_target_pairs={{32,0},{64,32},{96,64},{128,96},{160,128},{192,160},{224,192},{256... | collective-permute-start | bytes 491528 | tf_op jit(solution)/shard_map/ppermute | solution.py:45
  93.3 6.3 %collective-permute-start.8 = (f32[20,2,1,128]{3,0,2,1:T(8,128)S(1)}, f32[20,2,1,128]{3,0,2,1:T(8,128)S(1)}, u32[]{:S(2)}, u32[]{:S(2)}) collective-permute-start(f32[20,2,1,128]{3,0,2,1:T(8,128)S(1)} %get-tuple-element.153), channel_id=1, source_target_pairs={{0,1},{1,2},{2,3},{3,4},{4,5},{5,6},{6,7},{7,8},{8,9},{9,10},{10,1... | collective-permute-start | bytes 61448 | tf_op jit(solution)/shard_map/ppermute | solution.py:47
  96.2 7.3 %collective-permute-start.9 = (f32[20,2,1,128]{3,0,2,1:T(8,128)S(1)}, f32[20,2,1,128]{3,0,2,1:T(8,128)S(1)}, u32[]{:S(2)}, u32[]{:S(2)}) collective-permute-start(f32[20,2,1,128]{3,0,2,1:T(8,128)S(1)} %get-tuple-element.154), channel_id=1, source_target_pairs={{1,0},{2,1},{3,2},{4,3},{5,4},{6,5},{7,6},{8,7},{9,8},{10,9},{11,1... | collective-permute-start | bytes 61448 | tf_op jit(solution)/shard_map/ppermute | solution.py:48
  107.5 0.7 copy-start.1

commit v5 on v3

--- a/solution.py
+++ b/solution.py
@@ -22,44 +22,18 @@
     return up, down
 
 
-def halo_wide(block):
+def halo_x(block, cells):
     up, down = shifts("gx")
-    before = lax.ppermute(block, "gx", up)
-    after = lax.ppermute(block, "gx", down)
-    wide = jnp.concatenate([before, block, after], axis=1)
-    rows = block.shape[1]
+    before = lax.ppermute(block[:, block.shape[1] - cells :], "gx", up)
+    after = lax.ppermute(block[:, :cells], "gx", down)
+    return jnp.concatenate([before, block, after], axis=1)
+
+
+def halo_y(block, rows):
     up, down = shifts("gy")
-    below = lax.ppermute(wide[:, :, -rows:], "gy", up)
-    above = lax.ppermute(wide[:, :, :rows], "gy", down)
-    return jnp.concatenate([below, wide, above], axis=2)
-
-
-def halo_three(block):
-    up, down = shifts("gx")
-    peers = lax.axis_size("gx")
-    up2 = [(i, i + 2) for i in range(peers - 2)]
-    down2 = [(j, i) for i, j in up2]
-    b1 = lax.ppermute(block, "gx", up)
-    a1 = lax.ppermute(block, "gx", down)
-    b2 = lax.ppermute(block[:, -1:], "gx", up2)
-    a2 = lax.ppermute(block[:, :1], "gx", down2)
-    wide = jnp.concatenate([b2, b1, block, a1, a2], axis=1)
-    up, down = shifts("gy")
-    below = lax.ppermute(wide[:, :, -3:], "gy", up)
-    above = lax.ppermute(wide[:, :, :3], "gy", down)
-    return jnp.concatenate([below, wide, above], axis=2)
-
-
-def halo_one(block):
-    up, down = shifts("gx")
-    xb = lax.ppermute(block[:, -1:], "gx", up)
-    xa = lax.ppermute(block[:, :1], "gx", down)
-    up, down = shifts("gy")
-    yb = lax.ppermute(block[:, :, -1:], "gy", up)
-    ya = lax.ppermute(block[:, :, :1], "gy", down)
-    wide = jnp.concatenate([xb, block, xa], axis=1)
-    pad = ((0, 0), (1, 1), (0, 0), (0, 0))
-    return jnp.concatenate([jnp.pad(yb, pad), wide, jnp.pad(ya, pad)], axis=2)
+    below = lax.ppermute(block[:, :, block.shape[2] - rows :], "gy", up)
+    above = lax.ppermute(block[:, :, :rows], "gy", down)
+    return jnp.concatenate([below, block, above], axis=2)
 
 
 def to_fine(coarse):
@@ -99,10 +73,9 @@
     ).astype(jnp.float32)
 
 
-def trim(values, cut):
-    if cut == 0:
-        return values
-    return values[..., cut : values.shape[-3] - cut, cut : values.shape[-2] - cut, :]
+def trim(values, cut, cut_y=None):
+    cut_y = cut if cut_y is None else cut_y
+    return values[..., cut : values.shape[-3] - cut, cut_y : values.shape[-2] - cut_y, :]
 
 
 def ocean_substep(fields, wet_mask, heating):
@@ -172,8 +145,8 @@
         levels.astype(jnp.float32).transpose(1, 2, 0), ((0, 0), (0, 0), (0, depth - 4))
     )[None]
     packed = jnp.concatenate([state[0], old_flux, level_lanes], axis=0)
-    ext1 = halo_wide(packed)
-    margin = (ext1.shape[1] - size_x) // 2
+    reach_x, reach_y = size_x, NSUB + 1
+    ext1 = halo_y(halo_x(packed, reach_x), reach_y)
     onehot = (eco_prey[:, None] == lax.broadcasted_iota(jnp.int32, (species, species), 1)).astype(
         jnp.float32
     )
@@ -189,19 +162,26 @@
     wet_coarse_ext = wet_of_float(jnp.max(levels_ext, axis=0), depth)
     wet_fine_ext = wet_of_float(fine_levels(levels_ext), depth)
     zeros_flux = jnp.zeros((2, size_x, size_y, depth), jnp.float32)
+    mid_y, late_y = reach_y - 2, reach_y - 4
+    shape_mid = (channels, size_x, size_y + 2 * mid_y, depth)
+    shape_late = (channels, size_x, size_y + 2 * late_y, depth)
 
     def ocean_a():
-        fine = to_fine(raw_ext) * wet_fine_ext[None]
-        reach = 2 * margin
+        keep_y = NSUB + 2 * late_y
+        fine = trim(to_fine(raw_ext) * wet_fine_ext[None], 0, 2 * reach_y - keep_y)
         running = zeros_flux
-        for substep in range(2):
-            fine = ocean_substep(fine, trim(wet_fine_ext, substep + 1), 0.0)
-            running = running + coarse_mean(trim(fine[0:2], reach - substep - 1))
-        return to_coarse(trim(fine, reach - 2)), running
+        for substep in range(NSUB):
+            fine = ocean_substep(
+                fine, trim(wet_fine_ext, substep + 1, 2 * reach_y - keep_y + substep + 1), 0.0
+            )
+            running = running + coarse_mean(
+                trim(fine[0:2], 2 * reach_x - substep - 1, keep_y - substep - 1)
+            )
+        return jnp.zeros(shape_mid, jnp.float32), to_coarse(fine), running
 
     def tracer_a():
         tracer = raw_ext * wet_coarse_ext[None]
-        for substep in range(margin):
+        for substep in range(2):
             tracer = tracer_substep(
                 tracer,
                 trim(wet_coarse_ext, substep + 1),
@@ -209,46 +189,39 @@
                 onehot,
                 eco_rate,
             )
-        return tracer, zeros_flux
-
-    block_a, running = lax.cond(is_ocean, ocean_a, tracer_a)
-    ext2 = halo_three(block_a)
-    reach2 = (ext2.shape[1] - size_x) // 2
-    tracer_shape = (channels, size_x + 2, size_y + 2, depth)
-    ocean_shape = (channels // 4, 2 * size_x + 2, 2 * size_y + 2, depth)
+        return tracer, jnp.zeros(shape_late, jnp.float32), zeros_flux
+
+    block_mid, ocean_late, running = lax.cond(is_ocean, ocean_a, tracer_a)
+    ext2 = halo_x(block_mid, reach_x)
 
     def ocean_b():
-        fine = trim(to_fine(ext2), 2 * reach2 - 3)
-        summed = running
-        for substep in range(2):
-            fine = ocean_substep(fine, trim(wet_fine_ext, 2 * margin - 2 + substep), 0.0)
-            summed = summed + coarse_mean(trim(fine[0:2], 2 - substep))
-        return jnp.zeros(tracer_shape, jnp.float32), fine, summed / NSUB
+        return ocean_late, running / NSUB
 
     def tracer_b():
         tracer = ext2
         for substep in range(2):
             tracer = tracer_substep(
                 tracer,
-                trim(wet_coarse_ext, substep),
-                trim(flux_ext, substep),
+                trim(wet_coarse_ext, substep + 1, reach_y - mid_y + substep + 1),
+                trim(flux_ext, substep + 1, reach_y - mid_y + substep + 1),
                 onehot,
                 eco_rate,
             )
-        absorbed = absorption(trim(tracer, 1), wet_coarse, above_table)
-        outgoing = jnp.broadcast_to(absorbed[None], (2, size_x, size_y, depth))
-        return tracer, jnp.zeros(ocean_shape, jnp.float32), outgoing
-
-    tracer_b4, ocean_b4, outgoing = lax.cond(is_ocean, ocean_b, tracer_b)
+        absorbed = absorption(trim(tracer, 0, late_y), wet_coarse, above_table)
+        return tracer, jnp.broadcast_to(absorbed[None], (2, size_x, size_y, depth))
+
+    block_late, outgoing = lax.cond(is_ocean, ocean_b, tracer_b)
+    ext3 = halo_x(block_late, 1)
     arrived = lax.ppermute(outgoing, "half", [(0, 1), (1, 0)])
 
     def ocean_c():
+        fine = trim(to_fine(ext3), 1, 2 * late_y - 1)
         light = arrived[0:1]
         heating = HEATING * to_fine(jnp.broadcast_to(light, (4, size_x, size_y, depth)))[0]
-        return to_coarse(ocean_substep(ocean_b4, wet_fine, heating))
+        return to_coarse(ocean_substep(fine, wet_fine, heating))
 
     def tracer_c():
-        return tracer_substep(tracer_b4, wet_coarse, arrived, onehot, eco_rate)
+        return tracer_substep(trim(ext3, 0, late_y - 1), wet_coarse, arrived, onehot, eco_rate)
 
     return lax.cond(is_ocean, ocean_c, tracer_c)[None]
 

time: 103 us -> 88.5 us (0.86)
  the two profiles are of different devices: /device:TPU:155 before, /device:TPU:224 now
where the time goes in v5:
time: 88.5 us; the launch traced here: 87.9 us
  waiting for transfers between devices  37.3 us (42%)
  starting transfers between devices  29.3 us (33%)
  local copies, waits for them, and re-layouts  11.9 us (13%)
  other arithmetic  8.63 us (10%)
    ppermute x3, waiting for transfers between devices, halo_x(): before = lax.ppermute(block[:, block.shape[1] - cells:], 'gx', up)  16.5 us
    ppermute x3, waiting for transfers between devices, halo_x(): after = lax.ppermute(block[:, :cells], 'gx', down)  15.9 us
    ppermute x3, starting transfers between devices, halo_x(): before = lax.ppermute(block[:, block.shape[1] - cells:], 'gx', up)  13.5 us
    ppermute x3, starting transfers between devices, halo_x(): after = lax.ppermute(block[:, :cells], 'gx', down)  5.97 us
    ppermute x1, starting transfers between devices, halo_y(): above = lax.ppermute(block[:, :, :rows], 'gy', down)  5.75 us
    unnamed x16, local copies, waits for them, and re-layouts  3.33 us
    ppermute x1, waiting for transfers between devices, halo_y(): below = lax.ppermute(block[:, :, block.shape[2] - rows:], 'gy', up)  3.26 us
    mul x5, other arithmetic, ocean_substep(): return wet_mask * (centre + DT * (NU * spread - advect + forcing))  2.75 us
  transfers between devices with their start and end apart: 9, of which 8 were waited for; matrix products, arithmetic and copies ran while one was open for 1% of the time, Pallas kernels for 0%

profile of v5, /device:TPU:224, one launch (start us, length us, event | category | flops | bytes accessed | tf_op | source)
XLA Modules:
  0.0 87.9 jit_solution(12403359680516358135)
XLA Ops:
  0.0 1.2 %copy.174 = f32[1,20,2,16,128]{4,1,3,2,0:T(8,128)S(1)} copy(f32[1,20,2,16,128]{4,3,2,1,0:T(8,128)} %param.11) | data formatting | bytes 655360 | tf_op args[0]
  1.2 0.7 fusion.59
  1.9 0.1 copy.136
  1.9 0.8 copy.135
  2.8 5.5 %collective-permute-start = (f32[23,2,16,128]{3,0,2,1:T(8,128)S(1)}, f32[23,2,16,128]{3,0,2,1:T(8,128)S(1)}, u32[]{:S(2)}, u32[]{:S(2)}) collective-permute-start(f32[23,2,16,128]{3,0,2,1:T(8,128)S(1)} %pad_maximum_fusion.2), channel_id=1, source_target_pairs={{0,32},{32,64},{64,96},{96,128},{128,160},{160,192},{192,224},{224... | collective-permute-start | bytes 1130504 | tf_op jit(solution)/shard_map/ppermute | solution.py:27
  8.3 1.9 %collective-permute-start.1 = (f32[23,2,16,128]{3,0,2,1:T(8,128)S(1)}, f32[23,2,16,128]{3,0,2,1:T(8,128)S(1)}, u32[]{:S(2)}, u32[]{:S(2)}) collective-permute-start(f32[23,2,16,128]{3,0,2,1:T(8,128)S(1)} %pad_maximum_fusion.2), channel_id=1, source_target_pairs={{32,0},{64,32},{96,64},{128,96},{160,128},{192,160},{224,192},{256... | collective-permute-start | bytes 1130504 | tf_op jit(solution)/shard_map/ppermute | solution.py:28
  10.2 6.4 %collective-permute-done = f32[23,2,16,128]{3,0,2,1:T(8,128)S(1)} collective-permute-done((f32[23,2,16,128]{3,0,2,1:T(8,128)S(1)}, f32[23,2,16,128]{3,0,2,1:T(8,128)S(1)}, u32[]{:S(2)}, u32[]{:S(2)}) %collective-permute-start) | collective-permute-done | bytes 376864 | tf_op jit(solution)/shard_map/ppermute | solution.py:27
  16.7 5.3 %collective-permute-done.1 = f32[23,2,16,128]{3,0,2,1:T(8,128)S(1)} collective-permute-done((f32[23,2,16,128]{3,0,2,1:T(8,128)S(1)}, f32[23,2,16,128]{3,0,2,1:T(8,128)S(1)}, u32[]{:S(2)}, u32[]{:S(2)}) %collective-permute-start.1) | collective-permute-done | bytes 376864 | tf_op jit(solution)/shard_map/ppermute | solution.py:28
  22.1 1.9 %collective-permute-start.2 = (f32[23,6,5,128]{3,0,2,1:T(8,128)S(1)}, f32[23,6,5,128]{3,0,2,1:T(8,128)S(1)}, u32[]{:S(2)}, u32[]{:S(2)}) collective-permute-start(f32[23,6,5,128]{3,0,2,1:T(8,128)S(1)} %get-tuple-element.254), channel_id=1, source_target_pairs={{0,1},{1,2},{2,3},{3,4},{4,5},{5,6},{6,7},{7,8},{8,9},{9,10},{10,1... | collective-permute-start | bytes 1059848 | tf_op jit(solution)/shard_map/ppermute | solution.py:34
  24.0 5.8 %collective-permute-start.3 = (f32[23,6,5,128]{3,0,2,1:T(8,128)S(1)}, f32[23,6,5,128]{3,0,2,1:T(8,128)S(1)}, u32[]{:S(2)}, u32[]{:S(2)}) collective-permute-start(f32[23,6,5,128]{3,0,2,1:T(8,128)S(1)} %get-tuple-element.255), channel_id=1, source_target_pairs={{1,0},{2,1},{3,2},{4,3},{5,4},{6,5},{7,6},{8,7},{9,8},{10,9},{11,1... | collective-permute-start | bytes 1059848 | tf_op jit(solution)/shard_map/ppermute | solution.py:35
  29.8 0.1 fusion.58
  29.8 3.3 %collective-permute-done.2 = f32[23,6,5,128]{3,0,2,1:T(8,128)S(1)} collective-permute-done((f32[23,6,5,128]{3,0,2,1:T(8,128)S(1)}, f32[23,6,5,128]{3,0,2,1:T(8,128)S(1)}, u32[]{:S(2)}, u32[]{:S(2)}) %collective-permute-start.2) | collective-permute-done | bytes 353312 | tf_op jit(solution)/shard_map/ppermute | solution.py:34
  33.1 1.7 %collective-permute-done.3 = f32[23,6,5,128]{3,0,2,1:T(8,128)S(1)} collective-permute-done((f32[23,6,5,128]{3,0,2,1:T(8,128)S(1)}, f32[23,6,5,128]{3,0,2,1:T(8,128)S(1)}, u32[]{:S(2)}, u32[]{:S(2)}) %collective-permute-start.3) | collective-permute-done | bytes 353312 | tf_op jit(solution)/shard_map/ppermute | solution.py:35
  34.8 0.1 pad_maximum_fusion.9
  34.9 0.1 copy.137
  35.0 0.2 copy.138
  35.2 0.1 lt.43
  35.3 0.9 %compare_convert_fusion = f32[12,52,128]{2,1,0:T(8,128)} fusion(f32[12,52]{1,0:T(8,128)S(1)} %lt.43, f32[128]{0:T(128)S(1)} %iota_convert_fusion), kind=kLoop, calls=%fused_computation.119 | loop fusion | flops 159744 | bytes 322496 | tf_op jit(solution)/shard_map/convert_element_type | solution.py:73
  36.2 0.1 compare_convert_fusion.1
  36.3 0.1 pad_maximum_fusion
  36.5 0.1 pad_maximum_fusion.8
  36.6 0.5 copy-done.5
  37.1 10.1 %conditional.3 = (f32[20,2,18,128]{3,1,2,0:T(2,128)}, f32[2,2,16,128]{3,2,1,0:T(8,128)S(1)}, f32[20,2,22,128]{3,1,2,0:T(2,128)}) conditional(s32[]{:T(128)} %convert_element_type.36, (f32[6,26,128]{2,1,0:T(8,128)S(1)}, f32[20,6,26,128]{3,0,2,1:T(8,128)S(1)}, f32[2,6,26,128]{3,0,2,1:T(2,128)S(1)}, f32[19]{0:T(128)S(1)}, ...), branch_computations={%region_1.2_spmd, %region_2.7_spmd} | conditional | flops 85125120 | bytes 42651952 | solution.py:194
  37.1 0.3 copy.140
  37.5 1.4 %copy.173 = f32[5,2,2,6,26,128]{5,2,4,1,3,0:T(2,128)S(1)} copy(f32[5,2,2,6,26,128]{5,4,3,2,1,0:T(8,128)S(1)} %bitcast.141) | data formatting | bytes 3194880 | tf_op jit(solution)/shard_map/cond/branch_1_fun/reshape | solution.py:42
  38.9 1.1 %reshape.73 = f32[5,12,52,128]{3,2,1,0:T(8,128)S(1)} reshape(f32[5,6,2,26,2,128]{5,4,3,2,1,0:T(2,128)S(1)} %bitcast.142) | data formatting | bytes 3194880 | tf_op jit(solution)/shard_map/cond/branch_1_fun/reshape | solution.py:43
  40.1 1.1 %broadcast_multiply_fusion.1 = f32[5,12,52,128]{3,2,1,0:T(8,128)S(1)} fusion(f32[5,12,52,128]{3,2,1,0:T(8,128)S(1)} %reshape.73, f32[12,52,128]{2,1,0:T(8,128)} %get-tuple-element.64), kind=kLoop, calls=%fused_computation.24 | loop fusion | flops 399360 | bytes 3514368 | tf_op jit(solution)/shard_map/cond/branch_1_fun/mul | solution.py:171
  41.2 0.1 slice_bitcast_fusion.5
  41.3 0.9 copy-done
  42.2 0.1 pad.24.clone
  42.3 0.1 pad.25.clone
  42.3 0.9 %fusion.12 = f32[5,10,42,128]{3,2,1,0:T(8,128)S(1)} fusion(f32[1,10,42,128]{3,2,1,0:T(8,128)S(1)} %get-tuple-element.231, f32[1,10,42,128]{3,2,1,0:T(8,128)S(1)} %get-tuple-element.230, f32[5,12,52,128]{3,2,1,0:T(8,128)S(1)} %broadcast_multiply_fusion.1, f32[5]{0:T(128)S(1)} %pad.25.clone, f32[5]{0:T(128)S(1)} %pad.24.clone, ...), kind=kLoop, calls=%fused_computation.23 | loop fusion | flops 5107200 | bytes 7526440 | tf_op jit(solution)/shard_map/cond/branch_1_fun/mul | solution.py:101
  43.4 0.6 fusion.15
  44.0 0.4 fusion.18
  44.5 0.3 fusion.21
  44.9 0.1 reduce_sum.35
  45.0 0.1 reduce_sum.34
  45.1 0.1 reduce_sum.33
  45.2 0.1 reduce_sum.32
  45.3 0.1 copy.127
  45.4 0.9 %copy.128 = f32[5,2,2,2,18,128]{5,3,4,2,1,0:T(2,128)} copy(f32[5,2,2,2,18,128]{5,1,3,2,4,0:T(2,128)S(1)} %bitcast.144) | data formatting | bytes 737280 | tf_op jit(solution)/shard_map/cond/branch_1_fun/transpose | solution.py:48
  46.4 0.9 %broadcast.215.clone = f32[20,2,22,128]{3,1,2,0:T(2,128)} broadcast(f32[]{:T(128)} %constant.5.clone), dimensions={} | broadcast | bytes 450564 | tf_op jit(solution)/shard_map/broadcast.56
  47.3 3.7 %collective-permute-start.4 = (f32[20,2,22,128]{3,1,2,0:T(2,128)}, f32[20,2,22,128]{3,1,2,0:T(2,128)S(1)}, u32[]{:S(2)}, u32[]{:S(2)}) collective-permute-start(f32[20,2,22,128]{3,1,2,0:T(2,128)} %get-tuple-element.224), channel_id=1, source_target_pairs={{0,32},{32,64},{64,96},{96,128},{128,160},{160,192},{192,224},{224... | collective-permute-start | bytes 1351688 | tf_op jit(solution)/shard_map/ppermute | solution.py:27
  51.0 2.1 %collective-permute-start.5 = (f32[20,2,22,128]{3,1,2,0:T(2,128)}, f32[20,2,22,128]{3,1,2,0:T(2,128)S(1)}, u32[]{:S(2)}, u32[]{:S(2)}) collective-permute-start(f32[20,2,22,128]{3,1,2,0:T(2,128)} %get-tuple-element.224), channel_id=1, source_target_pairs={{32,0},{64,32},{96,64},{128,96},{160,128},{192,160},{224,192},{256... | collective-permute-start | bytes 1351688 | tf_op jit(solution)/shard_map/ppermute | solution.py:28
  53.1 0.1 copy.158
  53.3 0.1 reshape.91
  53.4 0.1 fusion.57
  53.4 8.1 %collective-permute-done.4 = f32[20,2,22,128]{3,1,2,0:T(2,128)S(1)} collective-permute-done((f32[20,2,22,128]{3,1,2,0:T(2,128)}, f32[20,2,22,128]{3,1,2,0:T(2,128)S(1)}, u32[]{:S(2)}, u32[]{:S(2)}) %collective-permute-start.4) | collective-permute-done | bytes 450592 | tf_op jit(solution)/shard_map/ppermute | solution.py:27
  61.5 5.2 %collective-permute-done.5 = f32[20,2,22,128]{3,1,2,0:T(2,128)S(1)} collective-permute-done((f32[20,2,22,128]{3,1,2,0:T(2,128)}, f32[20,2,22,128]{3,1,2,0:T(2,128)S(1)}, u32[]{:S(2)}, u32[]{:S(2)}) %collective-permute-start.5) | collective-permute-done | bytes 450592 | tf_op jit(solution)/shard_map/ppermute | solution.py:28
  66.8 1.6 %pad_maximum_fusion.1 = f32[20,6,22,128]{3,1,2,0:T(8,128)S(1)} fusion(f32[20,2,22,128]{3,1,2,0:T(2,128)S(1)} %collective-permute-done.5, f32[20,2,22,128]{3,1,2,0:T(2,128)} %get-tuple-element.224, f32[20,2,22,128]{3,1,2,0:T(2,128)S(1)} %collective-permute-done.4), kind=kLoop, calls=%fused_computation.111 | loop fusion | flops 675840 | bytes 2703360 | tf_op jit(solution)/shard_map/concatenate | solution.py:29
  68.4 1.1 %conditional.4 = (f32[20,2,18,128]{3,0,2,1:T(8,128)S(1)}, f32[2,2,16,128]{3,2,1,0:T(8,128)S(1)}) conditional(s32[]{:T(128)} %convert_element_type.36, (f32[6,26,128]{2,1,0:T(8,128)S(1)}, f32[20,6,22,128]{3,1,2,0:T(8,128)S(1)}, f32[2,6,26,128]{3,0,2,1:T(2,128)S(1)}, f32[19]{0:T(128)S(1)}, f32[19,19]{1,0:T(8,128)S(1)}, ...), branch_computations={%region_8.9_spmd, %region_9.10_spmd} | conditional | flops 76587008 | bytes 16014352 | solution.py:213
  68.4 1.0 %copy.146 = f32[20,2,18,128]{3,0,2,1:T(8,128)S(1)} copy(f32[20,2,18,128]{3,1,2,0:T(2,128)} %get-tuple-element.217) | data formatting | bytes 737280 | tf_op jit(solution)/shard_map
  69.4 0.1 copy.147
  69.6 4.3 %collective-permute-start.6 = (f32[20,1,18,128]{3,2,1,0:T(8,128)S(1)}, f32[20,1,18,128]{3,2,1,0:T(8,128)S(1)}, u32[]{:S(2)}, u32[]{:S(2)}) collective-permute-start(f32[20,1,18,128]{3,2,1,0:T(8,128)S(1)} %get-tuple-element.257), channel_id=1, source_target_pairs={{0,32},{32,64},{64,96},{96,128},{128,160},{160,192},{192,224},{224... | collective-permute-start | bytes 552968 | tf_op jit(solution)/shard_map/ppermute | solution.py:27
  73.9 0.1 fusion.56
  74.0 1.9 %collective-permute-start.7 = (f32[20,1,18,128]{3,2,1,0:T(8,128)S(1)}, f32[20,1,18,128]{3,2,1,0:T(8,128)S(1)}, u32[]{:S(2)}, u32[]{:S(2)}) collective-permute-start(f32[20,1,18,128]{3,2,1,0:T(8,128)S(1)} %get-tuple-element.256), channel_id=1, source_target_pairs={{32,0},{64,32},{96,64},{128,96},{160,128},{192,160},{224,192},{256... | collective-permute-start | bytes 552968 | tf_op jit(solution)/shard_map/ppermute | solution.py:28
  76.0 2.2 %collective-permute-start.8 = (f32[2,2,16,128]{3,1,2,0:T(2,128)S(1)}, f32[2,2,16,128]{3,1,2,0:T(2,128)S(1)}, u32[]{:S(2)}, u32[]{:S(2)}) collective-permute-start(f32[2,2,16,128]{3,1,2,0:T(2,128)S(1)} %copy.150), channel_id=1, source_target_pairs={{0,512},{512,0},{1,513},{513,1},{2,514},{514,2},{3,515},{515,3},{4... | collective-permute-start | bytes 98312 | tf_op jit(solution)/shard_map/ppermute | solution.py:215
  78.2 2.0 %collective-permute-done.6 = f32[20,1,18,128]{3,2,1,0:T(8,128)S(1)} collective-permute-done((f32[20,1,18,128]{3,2,1,0:T(8,128)S(1)}, f32[20,1,18,128]{3,2,1,0:T(8,128)S(1)}, u32[]{:S(2)}, u32[]{:S(2)}) %collective-permute-start.6) | collective-permute-done | bytes 184352 | tf_op jit(solution)/shard_map/ppermute | solution.py:27
  80.2 0.1 constant_dynamic-update-slice_fusion.2
  80.2 5.3 %collective-permute-done.7 = f32[20,1,18,128]{3,2,1,0:T(8,128)S(1)} collective-permute-done((f32[20,1,18,128]{3,2,1,0:T(8,128)S(1)}, f32[20,1,18,128]{3,2,1,0:T(8,128)S(1)}, u32[]{:S(2)}, u32[]{:S(2)}) %collective-permute-start.7) | collective-permute-done | bytes 184352 | tf_op jit(solution)/shard_map/ppermute | solution.py:28
  85.6 1.6 %conditional.5 = (f32[1,20,2,16,128]{4,3,2,1,0:T(8,128)S(1)}) conditional(s32[]{:T(128)} %convert_element_type.36, (f32[2,16,128]{2,1,0:T(8,128)S(1)}, f32[20,2,18,128]{3,0,2,1:T(8,128)S(1)}, f32[20,4,18,128]{3,2,1,0:T(8,128)S(1)}, f32[2,2,16,128]{3,1,2,0:T(2,128)S(1)}, f32[19]{0:T(128)S(1)}, /*index=5*/f32[19,19]{1,0:T(8,128)S(1)}) %tuple.108, ...), branch_computations={%region_10.11_spmd, %region_11.12_spmd} | conditional | flops 19365888 | bytes 6176776 | solution.py:226
  85.8 0.6 copy.130
  86.6 0.5 add_multiply_fusion.5
  87.2 0.7 copy-done.3
  (46 shorter events, 0.8 us)
Async XLA Ops:
  2.7 27.0 %copy-start.6 = (s32[19]{0:T(128)S(1)}, s32[19]{0:T(128)}, u32[]{:S(2)}) copy-start(s32[19]{0:T(128)} %param.14) | copy-start | bytes 232
  2.8 13.8 %collective-permute-start = (f32[23,2,16,128]{3,0,2,1:T(8,128)S(1)}, f32[23,2,16,128]{3,0,2,1:T(8,128)S(1)}, u32[]{:S(2)}, u32[]{:S(2)}) collective-permute-start(f32[23,2,16,128]{3,0,2,1:T(8,128)S(1)} %pad_maximum_fusion.2), channel_id=1, source_target_pairs={{0,32},{32,64},{64,96},{96,128},{128,160},{160,192},{192,224},{224... | collective-permute-start | bytes 1130504 | tf_op jit(solution)/shard_map/ppermute | solution.py:27
  8.3 13.7 %collective-permute-start.1 = (f32[23,2,16,128]{3,0,2,1:T(8,128)S(1)}, f32[23,2,16,128]{3,0,2,1:T(8,128)S(1)}, u32[]{:S(2)}, u32[]{:S(2)}) collective-permute-start(f32[23,2,16,128]{3,0,2,1:T(8,128)S(1)} %pad_maximum_fusion.2), channel_id=1, source_target_pairs={{32,0},{64,32},{96,64},{128,96},{160,128},{192,160},{224,192},{256... | collective-permute-start | bytes 1130504 | tf_op jit(solution)/shard_map/ppermute | solution.py:28
  22.1 11.0 %collective-permute-start.2 = (f32[23,6,5,128]{3,0,2,1:T(8,128)S(1)}, f32[23,6,5,128]{3,0,2,1:T(8,128)S(1)}, u32[]{:S(2)}, u32[]{:S(2)}) collective-permute-start(f32[23,6,5,128]{3,0,2,1:T(8,128)S(1)} %get-tuple-element.254), channel_id=1, source_target_pairs={{0,1},{1,2},{2,3},{3,4},{4,5},{5,6},{6,7},{7,8},{8,9},{9,10},{10,1... | collective-permute-start | bytes 1059848 | tf_op jit(solution)/shard_map/ppermute | solution.py:34
  24.0 10.8 %collective-permute-start.3 = (f32[23,6,5,128]{3,0,2,1:T(8,128)S(1)}, f32[23,6,5,128]{3,0,2,1:T(8,128)S(1)}, u32[]{:S(2)}, u32[]{:S(2)}) collective-permute-start(f32[23,6,5,128]{3,0,2,1:T(8,128)S(1)} %get-tuple-element.255), channel_id=1, source_target_pairs={{1,0},{2,1},{3,2},{4,3},{5,4},{6,5},{7,6},{8,7},{9,8},{10,9},{11,1... | collective-permute-start | bytes 1059848 | tf_op jit(solution)/shard_map/ppermute | solution.py:35
  36.3 0.8 copy-start.1
  36.5 0.7 copy-start.5
  37.1 16.0 %copy-start.4 = (s32[4,2,16]{2,1,0:T(2,128)S(1)}, s32[4,2,16]{2,1,0:T(2,128)}, u32[]{:S(2)}) copy-start(s32[4,2,16]{2,1,0:T(2,128)} %param.12) | copy-start | bytes 1540
  41.2 1.0 %copy-start = (f32[12,52,128]{2,1,0:T(8,128)S(1)}, f32[12,52,128]{2,1,0:T(8,128)}, u32[]{:S(2)}) copy-start(f32[12,52,128]{2,1,0:T(8,128)} %get-tuple-element.64) | copy-start | bytes 958468 | tf_op jit(solution)/shard_map/cond
  47.3 14.3 %collective-permute-start.4 = (f32[20,2,22,128]{3,1,2,0:T(2,128)}, f32[20,2,22,128]{3,1,2,0:T(2,128)S(1)}, u32[]{:S(2)}, u32[]{:S(2)}) collective-permute-start(f32[20,2,22,128]{3,1,2,0:T(2,128)} %get-tuple-element.224), channel_id=1, source_target_pairs={{0,32},{32,64},{64,96},{96,128},{128,160},{160,192},{192,224},{224... | collective-permute-start | bytes 1351688 | tf_op jit(solution)/shard_map/ppermute | solution.py:27
  51.0 15.8 %collective-permute-start.5 = (f32[20,2,22,128]{3,1,2,0:T(2,128)}, f32[20,2,22,128]{3,1,2,0:T(2,128)S(1)}, u32[]{:S(2)}, u32[]{:S(2)}) collective-permute-start(f32[20,2,22,128]{3,1,2,0:T(2,128)} %get-tuple-element.224), channel_id=1, source_target_pairs={{32,0},{64,32},{96,64},{128,96},{160,128},{192,160},{224,192},{256... | collective-permute-start | bytes 1351688 | tf_op jit(solution)/shard_map/ppermute | solution.py:28
  53.4 14.9 %copy-start.2 = (f32[6,26,128]{2,1,0:T(8,128)S(1)}, f32[6,26,128]{2,1,0:T(8,128)}, u32[]{:S(2)}) copy-start(f32[6,26,128]{2,1,0:T(8,128)} %copy-done.1) | copy-start | bytes 239620
  69.6 10.6 %collective-permute-start.6 = (f32[20,1,18,128]{3,2,1,0:T(8,128)S(1)}, f32[20,1,18,128]{3,2,1,0:T(8,128)S(1)}, u32[]{:S(2)}, u32[]{:S(2)}) collective-permute-start(f32[20,1,18,128]{3,2,1,0:T(8,128)S(1)} %get-tuple-element.257), channel_id=1, source_target_pairs={{0,32},{32,64},{64,96},{96,128},{128,160},{160,192},{192,224},{224... | collective-permute-start | bytes 552968 | tf_op jit(solution)/shard_map/ppermute | solution.py:27
  74.0 11.6 %collective-permute-start.7 = (f32[20,1,18,128]{3,2,1,0:T(8,128)S(1)}, f32[20,1,18,128]{3,2,1,0:T(8,128)S(1)}, u32[]{:S(2)}, u32[]{:S(2)}) collective-permute-start(f32[20,1,18,128]{3,2,1,0:T(8,128)S(1)} %get-tuple-element.256), channel_id=1, source_target_pairs={{32,0},{64,32},{96,64},{128,96},{160,128},{192,160},{224,192},{256... | collective-permute-start | bytes 552968 | tf_op jit(solution)/shard_map/ppermute | solution.py:28
  76.0 9.6 %collective-permute-start.8 = (f32[2,2,16,128]{3,1,2,0:T(2,128)S(1)}, f32[2,2,16,128]{3,1,2,0:T(2,128)S(1)}, u32[]{:S(2)}, u32[]{:S(2)}) collective-permute-start(f32[2,2,16,128]{3,1,2,0:T(2,128)S(1)} %copy.150), channel_id=1, source_target_pairs={{0,512},{512,0},{1,513},{513,1},{2,514},{514,2},{3,515},{515,3},{4... | collective-permute-start | bytes 98312 | tf_op jit(solution)/shard_map/ppermute | solution.py:215
  87.2 0.7 copy-start.3

commit v6 on v5

--- a/solution.py
+++ b/solution.py
@@ -26,6 +26,15 @@
     up, down = shifts("gx")
     before = lax.ppermute(block[:, block.shape[1] - cells :], "gx", up)
     after = lax.ppermute(block[:, :cells], "gx", down)
+    return jnp.concatenate([before, block, after], axis=1)
+
+
+def halo_x_tracer(block, cells):
+    peers = lax.axis_size("gx")
+    up = [(peers + i, peers + i + 1) for i in range(peers - 1)]
+    down = [(j, i) for i, j in up]
+    before = lax.ppermute(block[:, block.shape[1] - cells :], ("half", "gx"), up)
+    after = lax.ppermute(block[:, :cells], ("half", "gx"), down)
     return jnp.concatenate([before, block, after], axis=1)
 
 
@@ -167,17 +176,15 @@
     shape_late = (channels, size_x, size_y + 2 * late_y, depth)
 
     def ocean_a():
-        keep_y = NSUB + 2 * late_y
-        fine = trim(to_fine(raw_ext) * wet_fine_ext[None], 0, 2 * reach_y - keep_y)
+        cut = 2 * reach_y - 2 * mid_y - 2
+        fine = trim(to_fine(raw_ext) * wet_fine_ext[None], 2 * reach_x - 2, cut)
         running = zeros_flux
-        for substep in range(NSUB):
+        for substep in range(2):
             fine = ocean_substep(
-                fine, trim(wet_fine_ext, substep + 1, 2 * reach_y - keep_y + substep + 1), 0.0
-            )
-            running = running + coarse_mean(
-                trim(fine[0:2], 2 * reach_x - substep - 1, keep_y - substep - 1)
-            )
-        return jnp.zeros(shape_mid, jnp.float32), to_coarse(fine), running
+                fine, trim(wet_fine_ext, 2 * reach_x - 1 + substep, cut + substep + 1), 0.0
+            )
+            running = running + coarse_mean(trim(fine[0:2], 1 - substep, 2 * mid_y + 1 - substep))
+        return to_coarse(fine), running
 
     def tracer_a():
         tracer = raw_ext * wet_coarse_ext[None]
@@ -189,13 +196,21 @@
                 onehot,
                 eco_rate,
             )
-        return tracer, jnp.zeros(shape_late, jnp.float32), zeros_flux
-
-    block_mid, ocean_late, running = lax.cond(is_ocean, ocean_a, tracer_a)
+        return tracer, zeros_flux
+
+    block_mid, running = lax.cond(is_ocean, ocean_a, tracer_a)
     ext2 = halo_x(block_mid, reach_x)
+    fine_shape = (channels // 4, 2 * size_x + 2, 2 * size_y + 2, depth)
 
     def ocean_b():
-        return ocean_late, running / NSUB
+        fine = trim(to_fine(ext2), 2 * reach_x - 3, 2 * mid_y - 3)
+        summed = running
+        for substep in range(2):
+            fine = ocean_substep(
+                fine, trim(wet_fine_ext, 2 * reach_x - 2 + substep, 2 * reach_y - 2 + substep), 0.0
+            )
+            summed = summed + coarse_mean(trim(fine[0:2], 2 - substep))
+        return jnp.zeros(shape_late, jnp.float32), fine, summed / NSUB
 
     def tracer_b():
         tracer = ext2
@@ -208,17 +223,17 @@
                 eco_rate,
             )
         absorbed = absorption(trim(tracer, 0, late_y), wet_coarse, above_table)
-        return tracer, jnp.broadcast_to(absorbed[None], (2, size_x, size_y, depth))
-
-    block_late, outgoing = lax.cond(is_ocean, ocean_b, tracer_b)
-    ext3 = halo_x(block_late, 1)
+        outgoing = jnp.broadcast_to(absorbed[None], (2, size_x, size_y, depth))
+        return tracer, jnp.zeros(fine_shape, jnp.float32), outgoing
+
+    block_late, ocean_late, outgoing = lax.cond(is_ocean, ocean_b, tracer_b)
+    ext3 = halo_x_tracer(block_late, 1)
     arrived = lax.ppermute(outgoing, "half", [(0, 1), (1, 0)])
 
     def ocean_c():
-        fine = trim(to_fine(ext3), 1, 2 * late_y - 1)
         light = arrived[0:1]
         heating = HEATING * to_fine(jnp.broadcast_to(light, (4, size_x, size_y, depth)))[0]
-        return to_coarse(ocean_substep(fine, wet_fine, heating))
+        return to_coarse(ocean_substep(ocean_late, wet_fine, heating))
 
     def tracer_c():
         return tracer_substep(trim(ext3, 0, late_y - 1), wet_coarse, arrived, onehot, eco_rate)

time: 88.5 us -> 89.8 us (1.015)
  the two profiles are of different devices: /device:TPU:224 before, /device:TPU:228 now
where the time goes in v6:
time: 89.8 us; the launch traced here: 89.2 us
  waiting for transfers between devices  38.7 us (43%)
  starting transfers between devices  33.2 us (37%)
  local copies, waits for them, and re-layouts  7.5 us (8%)
  other arithmetic  4.8 us (5%)
  matrix products  4.28 us (5%)
    ppermute x2, waiting for transfers between devices, halo_x(): before = lax.ppermute(block[:, block.shape[1] - cells:], 'gx', up)  15.4 us
    ppermute x2, waiting for transfers between devices, halo_x(): after = lax.ppermute(block[:, :cells], 'gx', down)  9.7 us
    ppermute x2, starting transfers between devices, halo_x(): before = lax.ppermute(block[:, block.shape[1] - cells:], 'gx', up)  9.19 us
    ppermute x1, starting transfers between devices, body(): arrived = lax.ppermute(outgoing, 'half', [(0, 1), (1, 0)])  6.05 us
    ppermute x1, starting transfers between devices, halo_y(): above = lax.ppermute(block[:, :, :rows], 'gy', down)  5.75 us
    ppermute x1, waiting for transfers between devices, halo_x_tracer(): after = lax.ppermute(block[:, :cells], ('half', 'gx'), down)  5.33 us
    unnamed x18, local copies, waits for them, and re-layouts  4.35 us
    ppermute x1, starting transfers between devices, halo_x_tracer(): before = lax.ppermute(block[:, block.shape[1] - cells:], ('half', 'gx'), up)  4.32 us
  transfers between devices with their start and end apart: 9, of which 8 were waited for; matrix products, arithmetic and copies ran while one was open for 2% of the time, Pallas kernels for 0%

profile of v6, /device:TPU:228, one launch (start us, length us, event | category | flops | bytes accessed | tf_op | source)
XLA Modules:
  0.0 89.2 jit_solution(13951659173147716287)
XLA Ops:
  0.0 1.2 %copy.116 = f32[1,20,2,16,128]{4,1,3,2,0:T(8,128)S(1)} copy(f32[1,20,2,16,128]{4,3,2,1,0:T(8,128)} %param.11) | data formatting | bytes 655360 | tf_op args[0]
  1.2 0.7 fusion.59
  1.9 0.1 copy.93
  1.9 0.8 copy.92
  2.8 0.1 pad_maximum_fusion.2
  2.8 5.5 %collective-permute-start = (f32[23,2,16,128]{3,0,2,1:T(8,128)S(1)}, f32[23,2,16,128]{3,0,2,1:T(8,128)S(1)}, u32[]{:S(2)}, u32[]{:S(2)}) collective-permute-start(f32[23,2,16,128]{3,0,2,1:T(8,128)S(1)} %pad_maximum_fusion.2), channel_id=1, source_target_pairs={{0,32},{32,64},{64,96},{96,128},{128,160},{160,192},{192,224},{224... | collective-permute-start | bytes 1130504 | tf_op jit(solution)/shard_map/ppermute | solution.py:27
  8.3 1.9 %collective-permute-start.1 = (f32[23,2,16,128]{3,0,2,1:T(8,128)S(1)}, f32[23,2,16,128]{3,0,2,1:T(8,128)S(1)}, u32[]{:S(2)}, u32[]{:S(2)}) collective-permute-start(f32[23,2,16,128]{3,0,2,1:T(8,128)S(1)} %pad_maximum_fusion.2), channel_id=1, source_target_pairs={{32,0},{64,32},{96,64},{128,96},{160,128},{192,160},{224,192},{256... | collective-permute-start | bytes 1130504 | tf_op jit(solution)/shard_map/ppermute | solution.py:28
  10.2 6.4 %collective-permute-done = f32[23,2,16,128]{3,0,2,1:T(8,128)S(1)} collective-permute-done((f32[23,2,16,128]{3,0,2,1:T(8,128)S(1)}, f32[23,2,16,128]{3,0,2,1:T(8,128)S(1)}, u32[]{:S(2)}, u32[]{:S(2)}) %collective-permute-start) | collective-permute-done | bytes 376864 | tf_op jit(solution)/shard_map/ppermute | solution.py:27
  16.7 5.3 %collective-permute-done.1 = f32[23,2,16,128]{3,0,2,1:T(8,128)S(1)} collective-permute-done((f32[23,2,16,128]{3,0,2,1:T(8,128)S(1)}, f32[23,2,16,128]{3,0,2,1:T(8,128)S(1)}, u32[]{:S(2)}, u32[]{:S(2)}) %collective-permute-start.1) | collective-permute-done | bytes 376864 | tf_op jit(solution)/shard_map/ppermute | solution.py:28
  22.0 0.1 pad_maximum_fusion.7
  22.1 1.9 %collective-permute-start.2 = (f32[23,6,5,128]{3,0,2,1:T(8,128)S(1)}, f32[23,6,5,128]{3,0,2,1:T(8,128)S(1)}, u32[]{:S(2)}, u32[]{:S(2)}) collective-permute-start(f32[23,6,5,128]{3,0,2,1:T(8,128)S(1)} %get-tuple-element.224), channel_id=1, source_target_pairs={{0,1},{1,2},{2,3},{3,4},{4,5},{5,6},{6,7},{7,8},{8,9},{9,10},{10,1... | collective-permute-start | bytes 1059848 | tf_op jit(solution)/shard_map/ppermute | solution.py:43
  24.0 5.8 %collective-permute-start.3 = (f32[23,6,5,128]{3,0,2,1:T(8,128)S(1)}, f32[23,6,5,128]{3,0,2,1:T(8,128)S(1)}, u32[]{:S(2)}, u32[]{:S(2)}) collective-permute-start(f32[23,6,5,128]{3,0,2,1:T(8,128)S(1)} %get-tuple-element.225), channel_id=1, source_target_pairs={{1,0},{2,1},{3,2},{4,3},{5,4},{6,5},{7,6},{8,7},{9,8},{10,9},{11,1... | collective-permute-start | bytes 1059848 | tf_op jit(solution)/shard_map/ppermute | solution.py:44
  29.8 0.0 copy-done.7
  29.8 0.1 fusion.58
  29.8 3.3 %collective-permute-done.2 = f32[23,6,5,128]{3,0,2,1:T(8,128)S(1)} collective-permute-done((f32[23,6,5,128]{3,0,2,1:T(8,128)S(1)}, f32[23,6,5,128]{3,0,2,1:T(8,128)S(1)}, u32[]{:S(2)}, u32[]{:S(2)}) %collective-permute-start.2) | collective-permute-done | bytes 353312 | tf_op jit(solution)/shard_map/ppermute | solution.py:43
  33.1 1.7 %collective-permute-done.3 = f32[23,6,5,128]{3,0,2,1:T(8,128)S(1)} collective-permute-done((f32[23,6,5,128]{3,0,2,1:T(8,128)S(1)}, f32[23,6,5,128]{3,0,2,1:T(8,128)S(1)}, u32[]{:S(2)}, u32[]{:S(2)}) %collective-permute-start.3) | collective-permute-done | bytes 353312 | tf_op jit(solution)/shard_map/ppermute | solution.py:44
  34.8 0.1 pad_maximum_fusion.9
  34.9 0.1 copy.94
  35.0 0.2 copy.95
  35.2 0.1 lt.43
  35.3 0.9 %compare_convert_fusion = f32[12,52,128]{2,1,0:T(8,128)} fusion(f32[12,52]{1,0:T(8,128)S(1)} %lt.43, f32[128]{0:T(128)S(1)} %iota_convert_fusion), kind=kLoop, calls=%fused_computation.119 | loop fusion | flops 159744 | bytes 322496 | tf_op jit(solution)/shard_map/convert_element_type | solution.py:82
  36.2 0.1 compare_convert_fusion.1
  36.3 0.0 copy-start.2
  36.3 0.1 pad_maximum_fusion
  36.5 0.0 copy-start.6
  36.5 0.1 pad_maximum_fusion.8
  36.6 0.5 copy-done.6
  37.1 4.2 %conditional.3 = (f32[2,2,16,128]{3,2,1,0:T(8,128)S(1)}, f32[20,2,22,128]{3,2,1,0:T(8,128)}) conditional(s32[]{:T(128)} %convert_element_type.36, (f32[6,26,128]{2,1,0:T(8,128)S(1)}, f32[20,6,26,128]{3,0,2,1:T(8,128)S(1)}, f32[2,6,26,128]{3,0,2,1:T(2,128)S(1)}, f32[19]{0:T(128)S(1)}, f32[19,19]{1,0:T(8,128)S(1)}) %tuple.98, ...), branch_computations={%region_1.2_spmd, %region_2.5_spmd} | conditional | flops 85125120 | bytes 27982028 | solution.py:201
  37.1 0.3 broadcast_multiply_fusion
  37.4 1.3 %fusion.2 = f32[19,4,24,128]{3,0,2,1:T(8,128)S(1)} fusion(f32[20,6,26,128]{3,0,2,1:T(8,128)S(1)} %broadcast_multiply_fusion, f32[19]{0:T(128)S(1)} %get-tuple-element.64, f32[19,19]{1,0:T(8,128)S(1)} %get-tuple-element.65), kind=kOutput, calls=%fused_computation.3 | convolution fusion | flops 54165504 | bytes 3305984 | tf_op jit(solution)/shard_map/cond/branch_0_fun/ts,sxyk->txyk/dot_general | solution.py:125
  38.7 0.6 add_multiply_fusion
  39.4 0.7 fusion.5
  40.1 0.3 add_multiply_fusion.1
  40.4 0.9 copy.107
  41.3 3.7 %collective-permute-start.4 = (f32[20,2,22,128]{3,2,1,0:T(8,128)}, f32[20,2,22,128]{3,2,1,0:T(8,128)S(1)}, u32[]{:S(2)}, u32[]{:S(2)}) collective-permute-start(f32[20,2,22,128]{3,2,1,0:T(8,128)} %get-tuple-element.194), channel_id=1, source_target_pairs={{0,32},{32,64},{64,96},{96,128},{128,160},{160,192},{192,224},{224... | collective-permute-start | bytes 1351688 | tf_op jit(solution)/shard_map/ppermute | solution.py:27
  45.0 0.1 copy.103
  45.1 0.1 lt.47
  45.2 2.1 %collective-permute-start.5 = (f32[20,2,22,128]{3,2,1,0:T(8,128)}, f32[20,2,22,128]{3,2,1,0:T(8,128)S(1)}, u32[]{:S(2)}, u32[]{:S(2)}) collective-permute-start(f32[20,2,22,128]{3,2,1,0:T(8,128)} %get-tuple-element.194), channel_id=1, source_target_pairs={{32,0},{64,32},{96,64},{128,96},{160,128},{192,160},{224,192},{256... | collective-permute-start | bytes 1351688 | tf_op jit(solution)/shard_map/ppermute | solution.py:28
  47.4 0.1 fusion.57
  47.5 9.0 %collective-permute-done.4 = f32[20,2,22,128]{3,2,1,0:T(8,128)S(1)} collective-permute-done((f32[20,2,22,128]{3,2,1,0:T(8,128)}, f32[20,2,22,128]{3,2,1,0:T(8,128)S(1)}, u32[]{:S(2)}, u32[]{:S(2)}) %collective-permute-start.4) | collective-permute-done | bytes 450592 | tf_op jit(solution)/shard_map/ppermute | solution.py:27
  56.5 1.1 %constant_dynamic-update-slice_fusion.2 = f32[20,6,22,128]{3,2,1,0:T(8,128)S(1)} fusion(f32[20,6,22,128]{3,2,1,0:T(8,128)S(1)} %constant_dynamic-update-slice_fusion.3, f32[20,2,22,128]{3,2,1,0:T(8,128)} %get-tuple-element.194), kind=kLoop, calls=%fused_computation.134 | loop fusion | bytes 942080
  57.5 4.4 %collective-permute-done.5 = f32[20,2,22,128]{3,2,1,0:T(8,128)S(1)} collective-permute-done((f32[20,2,22,128]{3,2,1,0:T(8,128)}, f32[20,2,22,128]{3,2,1,0:T(8,128)S(1)}, u32[]{:S(2)}, u32[]{:S(2)}) %collective-permute-start.5) | collective-permute-done | bytes 450592 | tf_op jit(solution)/shard_map/ppermute | solution.py:28
  62.0 4.4 %conditional.4 = (f32[20,2,18,128]{3,0,2,1:T(8,128)S(1)}, f32[5,6,34,128]{3,2,1,0:T(8,128)}, f32[2,2,16,128]{3,2,1,0:T(8,128)S(1)}) conditional(s32[]{:T(128)} %convert_element_type.36, (f32[6,26,128]{2,1,0:T(8,128)S(1)}, f32[20,6,22,128]{3,2,1,0:T(8,128)S(1)}, f32[2,6,26,128]{3,0,2,1:T(2,128)S(1)}, f32[19]{0:T(128)S(1)}, f32[19,19]{1,0:T(8,128)S(1)}, ...), branch_computations={%region_6.7_spmd, %region_7.10_spmd} | conditional | flops 76587008 | bytes 17590460 | solution.py:229
  62.2 0.5 copy.101
  62.6 1.1 %fusion.17 = f32[19,4,20,128]{3,0,2,1:T(8,128)S(1)} fusion(f32[20,6,22,128]{3,0,2,1:T(8,128)S(1)} %copy.101, f32[19]{0:T(128)S(1)} %get-tuple-element.71, f32[19,19]{1,0:T(8,128)S(1)} %get-tuple-element.72), kind=kOutput, calls=%fused_computation.40 | convolution fusion | flops 45137920 | bytes 2757120 | tf_op jit(solution)/shard_map/cond/branch_0_fun/ts,sxyk->txyk/dot_general | solution.py:125
  63.8 0.6 add_multiply_fusion.3
  64.4 0.6 fusion.20
  65.0 0.3 add_multiply_fusion.4
  65.3 0.2 fusion.23
  65.5 0.9 broadcast.244
  66.3 6.1 %collective-permute-start.8 = (f32[2,2,16,128]{3,2,1,0:T(8,128)S(1)}, f32[2,2,16,128]{3,2,1,0:T(8,128)S(1)}, u32[]{:S(2)}, u32[]{:S(2)}) collective-permute-start(f32[2,2,16,128]{3,2,1,0:T(8,128)S(1)} %get-tuple-element.95), channel_id=1, source_target_pairs={{0,512},{512,0},{1,513},{513,1},{2,514},{514,2},{3,515},{515,3},{4... | collective-permute-start | bytes 98312 | tf_op jit(solution)/shard_map/ppermute | solution.py:231
  72.4 4.3 %collective-permute-start.6 = (f32[20,1,18,128]{3,0,2,1:T(8,128)S(1)}, f32[20,1,18,128]{3,0,2,1:T(8,128)S(1)}, u32[]{:S(2)}, u32[]{:S(2)}) collective-permute-start(f32[20,1,18,128]{3,0,2,1:T(8,128)S(1)} %get-tuple-element.226), channel_id=1, source_target_pairs={{512,544},{544,576},{576,608},{608,640},{640,672},{672,704},{704,7... | collective-permute-start | bytes 552968 | tf_op jit(solution)/shard_map/ppermute | solution.py:36
  76.8 1.9 %collective-permute-start.7 = (f32[20,1,18,128]{3,0,2,1:T(8,128)S(1)}, f32[20,1,18,128]{3,0,2,1:T(8,128)S(1)}, u32[]{:S(2)}, u32[]{:S(2)}) collective-permute-start(f32[20,1,18,128]{3,0,2,1:T(8,128)S(1)} %get-tuple-element.227), channel_id=1, source_target_pairs={{544,512},{576,544},{608,576},{640,608},{672,640},{704,672},{736,7... | collective-permute-start | bytes 552968 | tf_op jit(solution)/shard_map/ppermute | solution.py:37
  78.7 0.1 fusion.56
  78.8 0.0 collective-permute-done.8
  78.8 3.4 %collective-permute-done.6 = f32[20,1,18,128]{3,0,2,1:T(8,128)S(1)} collective-permute-done((f32[20,1,18,128]{3,0,2,1:T(8,128)S(1)}, f32[20,1,18,128]{3,0,2,1:T(8,128)S(1)}, u32[]{:S(2)}, u32[]{:S(2)}) %collective-permute-start.6) | collective-permute-done | bytes 184352 | tf_op jit(solution)/shard_map/ppermute | solution.py:36
  82.2 5.3 %collective-permute-done.7 = f32[20,1,18,128]{3,0,2,1:T(8,128)S(1)} collective-permute-done((f32[20,1,18,128]{3,0,2,1:T(8,128)S(1)}, f32[20,1,18,128]{3,0,2,1:T(8,128)S(1)}, u32[]{:S(2)}, u32[]{:S(2)}) %collective-permute-start.7) | collective-permute-done | bytes 184352 | tf_op jit(solution)/shard_map/ppermute | solution.py:37
  87.5 0.1 pad_maximum_fusion.1
  87.6 0.8 conditional.5
  87.6 0.5 fusion.52
  88.1 0.2 multiply_bitcast_fusion
  88.4 0.1 copy.88
  88.4 0.0 copy-start.4
  88.5 0.7 copy-done.4
  (30 shorter events, 0.3 us)
Async XLA Ops:
  1.9 27.8 %copy-start.7 = (s32[19]{0:T(128)S(1)}, s32[19]{0:T(128)}, u32[]{:S(2)}) copy-start(s32[19]{0:T(128)} %param.14) | copy-start | bytes 232
  2.8 13.8 %collective-permute-start = (f32[23,2,16,128]{3,0,2,1:T(8,128)S(1)}, f32[23,2,16,128]{3,0,2,1:T(8,128)S(1)}, u32[]{:S(2)}, u32[]{:S(2)}) collective-permute-start(f32[23,2,16,128]{3,0,2,1:T(8,128)S(1)} %pad_maximum_fusion.2), channel_id=1, source_target_pairs={{0,32},{32,64},{64,96},{96,128},{128,160},{160,192},{192,224},{224... | collective-permute-start | bytes 1130504 | tf_op jit(solution)/shard_map/ppermute | solution.py:27
  8.3 13.7 %collective-permute-start.1 = (f32[23,2,16,128]{3,0,2,1:T(8,128)S(1)}, f32[23,2,16,128]{3,0,2,1:T(8,128)S(1)}, u32[]{:S(2)}, u32[]{:S(2)}) collective-permute-start(f32[23,2,16,128]{3,0,2,1:T(8,128)S(1)} %pad_maximum_fusion.2), channel_id=1, source_target_pairs={{32,0},{64,32},{96,64},{128,96},{160,128},{192,160},{224,192},{256... | collective-permute-start | bytes 1130504 | tf_op jit(solution)/shard_map/ppermute | solution.py:28
  22.1 11.0 %collective-permute-start.2 = (f32[23,6,5,128]{3,0,2,1:T(8,128)S(1)}, f32[23,6,5,128]{3,0,2,1:T(8,128)S(1)}, u32[]{:S(2)}, u32[]{:S(2)}) collective-permute-start(f32[23,6,5,128]{3,0,2,1:T(8,128)S(1)} %get-tuple-element.224), channel_id=1, source_target_pairs={{0,1},{1,2},{2,3},{3,4},{4,5},{5,6},{6,7},{7,8},{8,9},{9,10},{10,1... | collective-permute-start | bytes 1059848 | tf_op jit(solution)/shard_map/ppermute | solution.py:43
  24.0 10.8 %collective-permute-start.3 = (f32[23,6,5,128]{3,0,2,1:T(8,128)S(1)}, f32[23,6,5,128]{3,0,2,1:T(8,128)S(1)}, u32[]{:S(2)}, u32[]{:S(2)}) collective-permute-start(f32[23,6,5,128]{3,0,2,1:T(8,128)S(1)} %get-tuple-element.225), channel_id=1, source_target_pairs={{1,0},{2,1},{3,2},{4,3},{5,4},{6,5},{7,6},{8,7},{9,8},{10,9},{11,1... | collective-permute-start | bytes 1059848 | tf_op jit(solution)/shard_map/ppermute | solution.py:44
  36.3 0.8 copy-start.2
  36.5 0.7 copy-start.6
  37.1 7.9 %copy-start.5 = (s32[4,2,16]{2,1,0:T(2,128)S(1)}, s32[4,2,16]{2,1,0:T(2,128)}, u32[]{:S(2)}) copy-start(s32[4,2,16]{2,1,0:T(2,128)} %param.12) | copy-start | bytes 1540
  41.3 15.1 %collective-permute-start.4 = (f32[20,2,22,128]{3,2,1,0:T(8,128)}, f32[20,2,22,128]{3,2,1,0:T(8,128)S(1)}, u32[]{:S(2)}, u32[]{:S(2)}) collective-permute-start(f32[20,2,22,128]{3,2,1,0:T(8,128)} %get-tuple-element.194), channel_id=1, source_target_pairs={{0,32},{32,64},{64,96},{96,128},{128,160},{160,192},{192,224},{224... | collective-permute-start | bytes 1351688 | tf_op jit(solution)/shard_map/ppermute | solution.py:27
  45.2 16.7 %collective-permute-start.5 = (f32[20,2,22,128]{3,2,1,0:T(8,128)}, f32[20,2,22,128]{3,2,1,0:T(8,128)S(1)}, u32[]{:S(2)}, u32[]{:S(2)}) collective-permute-start(f32[20,2,22,128]{3,2,1,0:T(8,128)} %get-tuple-element.194), channel_id=1, source_target_pairs={{32,0},{64,32},{96,64},{128,96},{160,128},{192,160},{224,192},{256... | collective-permute-start | bytes 1351688 | tf_op jit(solution)/shard_map/ppermute | solution.py:28
  47.5 14.5 %copy-start = (f32[12,52,128]{2,1,0:T(8,128)S(1)}, f32[12,52,128]{2,1,0:T(8,128)}, u32[]{:S(2)}) copy-start(f32[12,52,128]{2,1,0:T(8,128)} %compare_convert_fusion) | copy-start | bytes 958468
  47.5 14.5 %copy-start.3 = (f32[6,26,128]{2,1,0:T(8,128)S(1)}, f32[6,26,128]{2,1,0:T(8,128)}, u32[]{:S(2)}) copy-start(f32[6,26,128]{2,1,0:T(8,128)} %copy-done.2) | copy-start | bytes 239620
  66.3 12.4 %collective-permute-start.8 = (f32[2,2,16,128]{3,2,1,0:T(8,128)S(1)}, f32[2,2,16,128]{3,2,1,0:T(8,128)S(1)}, u32[]{:S(2)}, u32[]{:S(2)}) collective-permute-start(f32[2,2,16,128]{3,2,1,0:T(8,128)S(1)} %get-tuple-element.95), channel_id=1, source_target_pairs={{0,512},{512,0},{1,513},{513,1},{2,514},{514,2},{3,515},{515,3},{4... | collective-permute-start | bytes 98312 | tf_op jit(solution)/shard_map/ppermute | solution.py:231
  72.4 9.8 %collective-permute-start.6 = (f32[20,1,18,128]{3,0,2,1:T(8,128)S(1)}, f32[20,1,18,128]{3,0,2,1:T(8,128)S(1)}, u32[]{:S(2)}, u32[]{:S(2)}) collective-permute-start(f32[20,1,18,128]{3,0,2,1:T(8,128)S(1)} %get-tuple-element.226), channel_id=1, source_target_pairs={{512,544},{544,576},{576,608},{608,640},{640,672},{672,704},{704,7... | collective-permute-start | bytes 552968 | tf_op jit(solution)/shard_map/ppermute | solution.py:36
  76.8 10.8 %collective-permute-start.7 = (f32[20,1,18,128]{3,0,2,1:T(8,128)S(1)}, f32[20,1,18,128]{3,0,2,1:T(8,128)S(1)}, u32[]{:S(2)}, u32[]{:S(2)}) collective-permute-start(f32[20,1,18,128]{3,0,2,1:T(8,128)S(1)} %get-tuple-element.227), channel_id=1, source_target_pairs={{544,512},{576,544},{608,576},{640,608},{672,640},{704,672},{736,7... | collective-permute-start | bytes 552968 | tf_op jit(solution)/shard_map/ppermute | solution.py:37
  88.4 0.7 copy-start.4

commit v7 on v6

--- a/solution.py
+++ b/solution.py
@@ -210,7 +210,7 @@
                 fine, trim(wet_fine_ext, 2 * reach_x - 2 + substep, 2 * reach_y - 2 + substep), 0.0
             )
             summed = summed + coarse_mean(trim(fine[0:2], 2 - substep))
-        return jnp.zeros(shape_late, jnp.float32), fine, summed / NSUB
+        return jnp.zeros(shape_late, jnp.float32), fine, summed
 
     def tracer_b():
         tracer = ext2
@@ -222,12 +222,17 @@
                 onehot,
                 eco_rate,
             )
-        absorbed = absorption(trim(tracer, 0, late_y), wet_coarse, above_table)
-        outgoing = jnp.broadcast_to(absorbed[None], (2, size_x, size_y, depth))
-        return tracer, jnp.zeros(fine_shape, jnp.float32), outgoing
-
-    block_late, ocean_late, outgoing = lax.cond(is_ocean, ocean_b, tracer_b)
+        return tracer, jnp.zeros(fine_shape, jnp.float32), running
+
+    block_late, ocean_late, summed = lax.cond(is_ocean, ocean_b, tracer_b)
     ext3 = halo_x_tracer(block_late, 1)
+
+    def tracer_light():
+        absorbed = absorption(trim(block_late, 0, late_y), wet_coarse, above_table)
+        return jnp.broadcast_to(absorbed[None], (2, size_x, size_y, depth))
+
+    outgoing = lax.cond(is_ocean, lambda: summed / NSUB, tracer_light)
+    outgoing, ext3 = lax.optimization_barrier((outgoing, ext3))
     arrived = lax.ppermute(outgoing, "half", [(0, 1), (1, 0)])
 
     def ocean_c():

time: 89.8 us -> 93.9 us (1.046)
  the two profiles are of different devices: /device:TPU:228 before, /device:TPU:224 now
where the time goes in v7:
time: 93.9 us; the launch traced here: 93.3 us
  starting transfers between devices  37.3 us (40%)
  waiting for transfers between devices  31 us (33%)
  local copies, waits for them, and re-layouts  12.4 us (13%)
  other arithmetic  11.8 us (13%)
    ppermute x1, starting transfers between devices, body(): arrived = lax.ppermute(outgoing, 'half', [(0, 1), (1, 0)])  15 us
    ppermute x2, waiting for transfers between devices, halo_x(): before = lax.ppermute(block[:, block.shape[1] - cells:], 'gx', up)  14.8 us
    ppermute x2, waiting for transfers between devices, halo_x(): after = lax.ppermute(block[:, :cells], 'gx', down)  9.47 us
    ppermute x2, starting transfers between devices, halo_x(): before = lax.ppermute(block[:, block.shape[1] - cells:], 'gx', up)  9.2 us
    ppermute x1, starting transfers between devices, halo_y(): above = lax.ppermute(block[:, :, :rows], 'gy', down)  5.75 us
    mul x5, other arithmetic, ocean_substep(): return wet_mask * (centre + DT * (NU * spread - advect + forcing))  4.97 us
    unnamed x20, local copies, waits for them, and re-layouts  4.35 us
    ppermute x2, starting transfers between devices, halo_x(): after = lax.ppermute(block[:, :cells], 'gx', down)  4.05 us
  transfers between devices with their start and end apart: 9, of which 7 were waited for; matrix products, arithmetic and copies ran while one was open for 2% of the time, Pallas kernels for 0%

profile of v7, /device:TPU:224, one launch (start us, length us, event | category | flops | bytes accessed | tf_op | source)
XLA Modules:
  0.0 93.3 jit_solution(6747195249157523215)
XLA Ops:
  0.0 1.2 %copy.144 = f32[1,20,2,16,128]{4,1,3,2,0:T(8,128)S(1)} copy(f32[1,20,2,16,128]{4,3,2,1,0:T(8,128)} %param.13) | data formatting | bytes 655360 | tf_op args[0]
  1.2 0.7 fusion.58
  1.9 0.8 copy.115
  2.8 5.5 %collective-permute-start = (f32[23,2,16,128]{3,0,2,1:T(8,128)S(1)}, f32[23,2,16,128]{3,0,2,1:T(8,128)S(1)}, u32[]{:S(2)}, u32[]{:S(2)}) collective-permute-start(f32[23,2,16,128]{3,0,2,1:T(8,128)S(1)} %pad_maximum_fusion.2), channel_id=1, source_target_pairs={{0,32},{32,64},{64,96},{96,128},{128,160},{160,192},{192,224},{224... | collective-permute-start | bytes 1130504 | tf_op jit(solution)/shard_map/ppermute | solution.py:27
  8.3 1.9 %collective-permute-start.1 = (f32[23,2,16,128]{3,0,2,1:T(8,128)S(1)}, f32[23,2,16,128]{3,0,2,1:T(8,128)S(1)}, u32[]{:S(2)}, u32[]{:S(2)}) collective-permute-start(f32[23,2,16,128]{3,0,2,1:T(8,128)S(1)} %pad_maximum_fusion.2), channel_id=1, source_target_pairs={{32,0},{64,32},{96,64},{128,96},{160,128},{192,160},{224,192},{256... | collective-permute-start | bytes 1130504 | tf_op jit(solution)/shard_map/ppermute | solution.py:28
  10.2 6.4 %collective-permute-done = f32[23,2,16,128]{3,0,2,1:T(8,128)S(1)} collective-permute-done((f32[23,2,16,128]{3,0,2,1:T(8,128)S(1)}, f32[23,2,16,128]{3,0,2,1:T(8,128)S(1)}, u32[]{:S(2)}, u32[]{:S(2)}) %collective-permute-start) | collective-permute-done | bytes 376864 | tf_op jit(solution)/shard_map/ppermute | solution.py:27
  16.7 5.3 %collective-permute-done.1 = f32[23,2,16,128]{3,0,2,1:T(8,128)S(1)} collective-permute-done((f32[23,2,16,128]{3,0,2,1:T(8,128)S(1)}, f32[23,2,16,128]{3,0,2,1:T(8,128)S(1)}, u32[]{:S(2)}, u32[]{:S(2)}) %collective-permute-start.1) | collective-permute-done | bytes 376864 | tf_op jit(solution)/shard_map/ppermute | solution.py:28
  22.1 1.9 %collective-permute-start.2 = (f32[23,6,5,128]{3,0,2,1:T(8,128)S(1)}, f32[23,6,5,128]{3,0,2,1:T(8,128)S(1)}, u32[]{:S(2)}, u32[]{:S(2)}) collective-permute-start(f32[23,6,5,128]{3,0,2,1:T(8,128)S(1)} %get-tuple-element.247), channel_id=1, source_target_pairs={{0,1},{1,2},{2,3},{3,4},{4,5},{5,6},{6,7},{7,8},{8,9},{9,10},{10,1... | collective-permute-start | bytes 1059848 | tf_op jit(solution)/shard_map/ppermute | solution.py:43
  24.0 5.8 %collective-permute-start.3 = (f32[23,6,5,128]{3,0,2,1:T(8,128)S(1)}, f32[23,6,5,128]{3,0,2,1:T(8,128)S(1)}, u32[]{:S(2)}, u32[]{:S(2)}) collective-permute-start(f32[23,6,5,128]{3,0,2,1:T(8,128)S(1)} %get-tuple-element.248), channel_id=1, source_target_pairs={{1,0},{2,1},{3,2},{4,3},{5,4},{6,5},{7,6},{8,7},{9,8},{10,9},{11,1... | collective-permute-start | bytes 1059848 | tf_op jit(solution)/shard_map/ppermute | solution.py:44
  29.8 3.3 %collective-permute-done.2 = f32[23,6,5,128]{3,0,2,1:T(8,128)S(1)} collective-permute-done((f32[23,6,5,128]{3,0,2,1:T(8,128)S(1)}, f32[23,6,5,128]{3,0,2,1:T(8,128)S(1)}, u32[]{:S(2)}, u32[]{:S(2)}) %collective-permute-start.2) | collective-permute-done | bytes 353312 | tf_op jit(solution)/shard_map/ppermute | solution.py:43
  33.1 1.7 %collective-permute-done.3 = f32[23,6,5,128]{3,0,2,1:T(8,128)S(1)} collective-permute-done((f32[23,6,5,128]{3,0,2,1:T(8,128)S(1)}, f32[23,6,5,128]{3,0,2,1:T(8,128)S(1)}, u32[]{:S(2)}, u32[]{:S(2)}) %collective-permute-start.3) | collective-permute-done | bytes 353312 | tf_op jit(solution)/shard_map/ppermute | solution.py:44
  34.8 0.1 pad_maximum_fusion.9
  34.9 0.1 copy.117
  35.0 0.2 copy.118
  35.2 0.1 lt.43
  35.3 0.9 compare_convert_fusion
  36.2 0.1 compare_convert_fusion.1
  36.3 0.1 pad_maximum_fusion
  36.5 0.1 pad_maximum_fusion.8
  36.6 0.5 copy-done.7
  37.1 6.9 %conditional.4 = (f32[2,2,16,128]{3,2,1,0:T(8,128)S(1)}, f32[20,2,22,128]{3,2,1,0:T(8,128)}) conditional(s32[]{:T(128)} %convert_element_type.37, (f32[6,26,128]{2,1,0:T(8,128)S(1)}, f32[20,6,26,128]{3,0,2,1:T(8,128)S(1)}, f32[2,6,26,128]{3,0,2,1:T(2,128)S(1)}, f32[19]{0:T(128)S(1)}, f32[19,19]{1,0:T(8,128)S(1)}) %tuple.116, ...), branch_computations={%region_1.2_spmd, %region_2.5_spmd} | conditional | flops 85125120 | bytes 27982028 | solution.py:201
  37.1 0.3 copy.120
  37.5 1.4 %copy.142 = f32[5,2,2,6,26,128]{5,2,4,1,3,0:T(2,128)S(1)} copy(f32[5,2,2,6,26,128]{5,4,3,2,1,0:T(8,128)S(1)} %bitcast.158) | data formatting | bytes 3194880 | tf_op jit(solution)/shard_map/cond/branch_1_fun/reshape | solution.py:51
  38.9 1.1 %reshape.73 = f32[5,12,52,128]{3,2,1,0:T(8,128)S(1)} reshape(f32[5,6,2,26,2,128]{5,4,3,2,1,0:T(2,128)S(1)} %bitcast.159) | data formatting | bytes 3194880 | tf_op jit(solution)/shard_map/cond/branch_1_fun/reshape | solution.py:52
  40.0 1.2 %broadcast_multiply_fusion.1 = f32[5,12,52,128]{3,2,1,0:T(8,128)S(1)} fusion(f32[5,12,52,128]{3,2,1,0:T(8,128)S(1)} %reshape.73, f32[12,52,128]{2,1,0:T(8,128)} %get-tuple-element.72), kind=kLoop, calls=%fused_computation.20 | loop fusion | flops 399360 | bytes 3514368 | tf_op jit(solution)/shard_map/cond/branch_1_fun/mul | solution.py:180
  41.3 0.1 pad.16.clone
  41.4 0.1 pad.17.clone
  41.5 0.6 fusion.12
  42.1 0.4 fusion.15
  42.5 0.2 copy.107
  42.7 0.2 copy.108
  42.9 0.8 copy.134
  43.8 0.1 reduce_sum.33
  43.9 0.1 reduce_sum.32
  44.0 3.7 %collective-permute-start.4 = (f32[20,2,22,128]{3,2,1,0:T(8,128)}, f32[20,2,22,128]{3,2,1,0:T(8,128)S(1)}, u32[]{:S(2)}, u32[]{:S(2)}) collective-permute-start(f32[20,2,22,128]{3,2,1,0:T(8,128)} %get-tuple-element.217), channel_id=1, source_target_pairs={{0,32},{32,64},{64,96},{96,128},{128,160},{160,192},{192,224},{224... | collective-permute-start | bytes 1351688 | tf_op jit(solution)/shard_map/ppermute | solution.py:27
  47.7 2.1 %collective-permute-start.5 = (f32[20,2,22,128]{3,2,1,0:T(8,128)}, f32[20,2,22,128]{3,2,1,0:T(8,128)S(1)}, u32[]{:S(2)}, u32[]{:S(2)}) collective-permute-start(f32[20,2,22,128]{3,2,1,0:T(8,128)} %get-tuple-element.217), channel_id=1, source_target_pairs={{32,0},{64,32},{96,64},{128,96},{160,128},{192,160},{224,192},{256... | collective-permute-start | bytes 1351688 | tf_op jit(solution)/shard_map/ppermute | solution.py:28
  49.9 0.1 copy.129
  50.0 0.1 lt.47
  50.1 0.6 fusion.54
  50.7 8.4 %collective-permute-done.4 = f32[20,2,22,128]{3,2,1,0:T(8,128)S(1)} collective-permute-done((f32[20,2,22,128]{3,2,1,0:T(8,128)}, f32[20,2,22,128]{3,2,1,0:T(8,128)S(1)}, u32[]{:S(2)}, u32[]{:S(2)}) %collective-permute-start.4) | collective-permute-done | bytes 450592 | tf_op jit(solution)/shard_map/ppermute | solution.py:27
  59.2 1.1 %constant_dynamic-update-slice_fusion.2 = f32[20,6,22,128]{3,2,1,0:T(8,128)S(1)} fusion(f32[20,6,22,128]{3,2,1,0:T(8,128)S(1)} %constant_dynamic-update-slice_fusion.3, f32[20,2,22,128]{3,2,1,0:T(8,128)} %get-tuple-element.217), kind=kLoop, calls=%fused_computation.137 | loop fusion | bytes 942080
  60.3 4.1 %collective-permute-done.5 = f32[20,2,22,128]{3,2,1,0:T(8,128)S(1)} collective-permute-done((f32[20,2,22,128]{3,2,1,0:T(8,128)}, f32[20,2,22,128]{3,2,1,0:T(8,128)S(1)}, u32[]{:S(2)}, u32[]{:S(2)}) %collective-permute-start.5) | collective-permute-done | bytes 450592 | tf_op jit(solution)/shard_map/ppermute | solution.py:28
  64.5 5.3 %conditional.5 = (f32[20,2,18,128]{3,2,1,0:T(8,128)S(1)}, f32[5,6,34,128]{3,2,1,0:T(8,128)}, f32[2,2,16,128]{3,2,1,0:T(8,128)S(1)}) conditional(s32[]{:T(128)} %convert_element_type.37, (f32[6,26,128]{2,1,0:T(8,128)S(1)}, f32[20,6,22,128]{3,2,1,0:T(8,128)S(1)}, f32[2,6,26,128]{3,0,2,1:T(2,128)S(1)}, f32[19]{0:T(128)S(1)}, f32[19,19]{1,0:T(8,128)S(1)}, ...), branch_computations={%region_5.0_spmd, %region_6.9_spmd} | conditional | flops 70201344 | bytes 17590460 | solution.py:227
  64.7 0.7 copy.143
  65.4 0.9 reshape.79
  66.4 0.1 pad.24.clone
  66.5 0.1 pad.25.clone
  66.5 0.6 fusion.27
  67.2 1.3 %fusion.30 = f32[5,6,34,128]{3,2,1,0:T(8,128)} fusion(f32[1,6,34,128]{3,2,1,0:T(8,128)S(1)} %get-tuple-element.240, f32[1,6,34,128]{3,2,1,0:T(8,128)S(1)} %get-tuple-element.239, f32[5,8,36,128]{3,2,1,0:T(8,128)S(1)} %fusion.27, f32[5]{0:T(128)S(1)} %pad.25.clone, f32[5]{0:T(128)S(1)} %pad.24.clone, f32[6,34,128]{2,1,0:T(8,128)S(1)} %get-tuple-element.241, ...), kind=kLoop, calls=%fused_computation.63 | loop fusion | flops 2480640 | bytes 3655720 | tf_op jit(solution)/shard_map/cond/branch_1_fun/mul | solution.py:110
  68.5 0.9 slice.407
  69.5 0.1 reduce_sum.35
  69.6 0.1 reduce_sum.34
  69.7 0.1 copy.126
  69.9 0.7 collective-permute-start.6
  70.6 0.7 collective-permute-start.7
  71.4 0.1 pad_maximum_fusion.1
  71.5 15.0 %collective-permute-start.8 = (f32[2,2,16,128]{3,2,1,0:T(8,128)S(1)}, f32[2,2,16,128]{3,2,1,0:T(8,128)S(1)}, u32[]{:S(2)}, u32[]{:S(2)}) collective-permute-start(f32[2,2,16,128]{3,2,1,0:T(8,128)S(1)} %get-tuple-element.263), channel_id=1, source_target_pairs={{0,512},{512,0},{1,513},{513,1},{2,514},{514,2},{3,515},{515,3},{4... | collective-permute-start | bytes 98312 | tf_op jit(solution)/shard_map/ppermute | solution.py:236
  86.5 0.1 fusion.55
  86.6 1.8 %collective-permute-done.8 = f32[2,2,16,128]{3,2,1,0:T(8,128)S(1)} collective-permute-done((f32[2,2,16,128]{3,2,1,0:T(8,128)S(1)}, f32[2,2,16,128]{3,2,1,0:T(8,128)S(1)}, u32[]{:S(2)}, u32[]{:S(2)}) %collective-permute-start.8) | collective-permute-done | bytes 32800 | tf_op jit(solution)/shard_map/ppermute | solution.py:236
  88.4 4.1 %conditional.7 = (f32[1,20,2,16,128]{4,3,2,1,0:T(8,128)S(1)}) conditional(s32[]{:T(128)} %convert_element_type.37, (f32[2,16,128]{2,1,0:T(8,128)S(1)}, f32[20,4,18,128]{3,0,2,1:T(8,128)S(1)}, f32[2,2,16,128]{3,2,1,0:T(8,128)S(1)}, f32[19]{0:T(128)S(1)}, f32[19,19]{1,0:T(8,128)S(1)}) %tuple.118, (f32[4,32,128]{2,1,0:T(8,128)S(1)}, ...), branch_computations={%region_12.13_spmd, %region_13.14_spmd} | conditional | flops 19365888 | bytes 4157960 | solution.py:246
  88.4 0.9 %slice_bitcast_fusion.19 = (f32[4,32,128]{2,1,0:T(8,128)S(1)}, f32[5,4,32,128]{3,2,1,0:T(8,128)S(1)}, f32[4,32,128]{2,1,0:T(8,128)S(1)}) fusion(f32[5,6,34,128]{3,2,1,0:T(8,128)} %get-tuple-element.92), kind=kLoop, calls=%fused_computation.108 | loop fusion | flops 49151 | bytes 327680 | tf_op jit(solution)/shard_map/cond/branch_1_fun/mul | solution.py:98
  89.3 1.0 %subtract_dynamic-update-slice_fusion = f32[5,4,32,128]{3,2,1,0:T(8,128)S(1)} fusion(f32[5,4,32,128]{3,2,1,0:T(8,128)S(1)} %get-tuple-element.245, f32[5,6,34,128]{3,2,1,0:T(8,128)} %get-tuple-element.92), kind=kLoop, calls=%fused_computation.105 | loop fusion | flops 49152 | bytes 196608 | tf_op jit(solution)/shard_map/cond
  90.4 2.1 %add_multiply_fusion.5 = f32[5,4,32,128]{3,2,1,0:T(8,128)S(1)} fusion(f32[5,4,32,128]{3,2,1,0:T(8,128)S(1)} %broadcast_dynamic-update-slice_fusion, f32[5,6,34,128]{3,2,1,0:T(8,128)} %get-tuple-element.92, f32[4,32,128]{2,1,0:T(8,128)S(1)} %get-tuple-element.246, f32[4,32,128]{2,1,0:T(8,128)S(1)} %get-tuple-element.244, f32[4,32,128]{2,1,0:T(8,128)S(1)} %get-tuple-element.91), kind=kLoop, calls=%fused_computation.104 | loop fusion | flops 1310720 | bytes 2490368 | tf_op jit(solution)/shard_map/cond/branch_1_fun/mul | solution.py:110
  92.6 0.7 copy-done.4
  (54 shorter events, 0.9 us)
Async XLA Ops:
  1.9 27.8 %copy-start.8 = (s32[19]{0:T(128)S(1)}, s32[19]{0:T(128)}, u32[]{:S(2)}) copy-start(s32[19]{0:T(128)} %param.16) | copy-start | bytes 232
  2.8 13.8 %collective-permute-start = (f32[23,2,16,128]{3,0,2,1:T(8,128)S(1)}, f32[23,2,16,128]{3,0,2,1:T(8,128)S(1)}, u32[]{:S(2)}, u32[]{:S(2)}) collective-permute-start(f32[23,2,16,128]{3,0,2,1:T(8,128)S(1)} %pad_maximum_fusion.2), channel_id=1, source_target_pairs={{0,32},{32,64},{64,96},{96,128},{128,160},{160,192},{192,224},{224... | collective-permute-start | bytes 1130504 | tf_op jit(solution)/shard_map/ppermute | solution.py:27
  8.3 13.7 %collective-permute-start.1 = (f32[23,2,16,128]{3,0,2,1:T(8,128)S(1)}, f32[23,2,16,128]{3,0,2,1:T(8,128)S(1)}, u32[]{:S(2)}, u32[]{:S(2)}) collective-permute-start(f32[23,2,16,128]{3,0,2,1:T(8,128)S(1)} %pad_maximum_fusion.2), channel_id=1, source_target_pairs={{32,0},{64,32},{96,64},{128,96},{160,128},{192,160},{224,192},{256... | collective-permute-start | bytes 1130504 | tf_op jit(solution)/shard_map/ppermute | solution.py:28
  22.1 11.0 %collective-permute-start.2 = (f32[23,6,5,128]{3,0,2,1:T(8,128)S(1)}, f32[23,6,5,128]{3,0,2,1:T(8,128)S(1)}, u32[]{:S(2)}, u32[]{:S(2)}) collective-permute-start(f32[23,6,5,128]{3,0,2,1:T(8,128)S(1)} %get-tuple-element.247), channel_id=1, source_target_pairs={{0,1},{1,2},{2,3},{3,4},{4,5},{5,6},{6,7},{7,8},{8,9},{9,10},{10,1... | collective-permute-start | bytes 1059848 | tf_op jit(solution)/shard_map/ppermute | solution.py:43
  24.0 10.8 %collective-permute-start.3 = (f32[23,6,5,128]{3,0,2,1:T(8,128)S(1)}, f32[23,6,5,128]{3,0,2,1:T(8,128)S(1)}, u32[]{:S(2)}, u32[]{:S(2)}) collective-permute-start(f32[23,6,5,128]{3,0,2,1:T(8,128)S(1)} %get-tuple-element.248), channel_id=1, source_target_pairs={{1,0},{2,1},{3,2},{4,3},{5,4},{6,5},{7,6},{8,7},{9,8},{10,9},{11,1... | collective-permute-start | bytes 1059848 | tf_op jit(solution)/shard_map/ppermute | solution.py:44
  36.3 0.8 copy-start.2
  36.5 0.7 copy-start.7
  37.1 12.7 %copy-start.6 = (s32[4,2,16]{2,1,0:T(2,128)S(1)}, s32[4,2,16]{2,1,0:T(2,128)}, u32[]{:S(2)}) copy-start(s32[4,2,16]{2,1,0:T(2,128)} %param.14) | copy-start | bytes 1540
  40.0 1.3 %copy-start.1 = (f32[12,52,128]{2,1,0:T(8,128)S(1)}, f32[12,52,128]{2,1,0:T(8,128)}, u32[]{:S(2)}) copy-start(f32[12,52,128]{2,1,0:T(8,128)} %get-tuple-element.72) | copy-start | bytes 958468 | tf_op jit(solution)/shard_map/cond
  44.0 15.1 %collective-permute-start.4 = (f32[20,2,22,128]{3,2,1,0:T(8,128)}, f32[20,2,22,128]{3,2,1,0:T(8,128)S(1)}, u32[]{:S(2)}, u32[]{:S(2)}) collective-permute-start(f32[20,2,22,128]{3,2,1,0:T(8,128)} %get-tuple-element.217), channel_id=1, source_target_pairs={{0,32},{32,64},{64,96},{96,128},{128,160},{160,192},{192,224},{224... | collective-permute-start | bytes 1351688 | tf_op jit(solution)/shard_map/ppermute | solution.py:27
  47.7 16.7 %collective-permute-start.5 = (f32[20,2,22,128]{3,2,1,0:T(8,128)}, f32[20,2,22,128]{3,2,1,0:T(8,128)S(1)}, u32[]{:S(2)}, u32[]{:S(2)}) collective-permute-start(f32[20,2,22,128]{3,2,1,0:T(8,128)} %get-tuple-element.217), channel_id=1, source_target_pairs={{32,0},{64,32},{96,64},{128,96},{160,128},{192,160},{224,192},{256... | collective-permute-start | bytes 1351688 | tf_op jit(solution)/shard_map/ppermute | solution.py:28
  50.7 13.7 %copy-start = (f32[12,52,128]{2,1,0:T(8,128)S(1)}, f32[12,52,128]{2,1,0:T(8,128)}, u32[]{:S(2)}) copy-start(f32[12,52,128]{2,1,0:T(8,128)} %compare_convert_fusion) | copy-start | bytes 958468
  50.7 13.7 %copy-start.3 = (f32[6,26,128]{2,1,0:T(8,128)S(1)}, f32[6,26,128]{2,1,0:T(8,128)}, u32[]{:S(2)}) copy-start(f32[6,26,128]{2,1,0:T(8,128)} %copy-done.2) | copy-start | bytes 239620
  69.7 1.6 %copy-start.5 = (f32[128,128]{1,0:T(8,128)S(1)}, f32[128,128]{1,0:T(8,128)}, u32[]{:S(2)}) copy-start(f32[128,128]{1,0:T(8,128)} %fusion.54) | copy-start | bytes 196612
  69.9 1.5 %collective-permute-start.6 = (f32[20,1,18,128]{3,0,2,1:T(8,128)S(1)}, f32[20,1,18,128]{3,0,2,1:T(8,128)S(1)}, u32[]{:S(2)}, u32[]{:S(2)}) collective-permute-start(f32[20,1,18,128]{3,0,2,1:T(8,128)S(1)} %get-tuple-element.249), channel_id=1, source_target_pairs={{512,544},{544,576},{576,608},{608,640},{640,672},{672,704},{704,7... | collective-permute-start | bytes 552968 | tf_op jit(solution)/shard_map/ppermute | solution.py:36
  70.6 0.8 collective-permute-start.7
  71.5 16.9 %collective-permute-start.8 = (f32[2,2,16,128]{3,2,1,0:T(8,128)S(1)}, f32[2,2,16,128]{3,2,1,0:T(8,128)S(1)}, u32[]{:S(2)}, u32[]{:S(2)}) collective-permute-start(f32[2,2,16,128]{3,2,1,0:T(8,128)S(1)} %get-tuple-element.263), channel_id=1, source_target_pairs={{0,512},{512,0},{1,513},{513,1},{2,514},{514,2},{3,515},{515,3},{4... | collective-permute-start | bytes 98312 | tf_op jit(solution)/shard_map/ppermute | solution.py:236
  92.5 0.7 copy-start.4

commit v8 on v6

--- a/solution.py
+++ b/solution.py
@@ -110,6 +110,36 @@
     return wet_mask * (centre + DT * (NU * spread - advect + forcing))
 
 
+def ocean_substep_channels(fields, wet_mask, heating):
+    pad = ((0, 0), (0, 0), (0, 0), (1, 1), (1, 1), (0, 0))
+    wide = jnp.pad(fields, pad)
+    to_east = jnp.concatenate([fields[:, 1:2], wide[:, 0:1, :, 2:, 1:-1]], axis=1)
+    to_west = jnp.concatenate([wide[:, 1:2, :, :-2, 1:-1], fields[:, 0:1]], axis=1)
+    to_north = jnp.concatenate([fields[:, :, 1:2], wide[:, :, 0:1, 1:-1, 2:]], axis=2)
+    to_south = jnp.concatenate([wide[:, :, 1:2, 1:-1, :-2], fields[:, :, 0:1]], axis=2)
+    centre = fields
+    speed_east = centre[0]
+    speed_north = centre[1]
+    advect = speed_east * (to_east - to_west) * 0.5 + speed_north * (to_north - to_south) * 0.5
+    spread = to_east + to_west + to_north + to_south - 4.0 * centre
+    zeroes = jnp.zeros_like(speed_east)
+    forcing = jnp.stack(
+        [
+            CORIOLIS * speed_north - DRAG * speed_east,
+            -CORIOLIS * speed_east - DRAG * speed_north,
+            zeroes + heating,
+            zeroes,
+            zeroes + 1.0,
+        ]
+    )
+    return wet_mask * (centre + DT * (NU * spread - advect + forcing))
+
+
+def channel_mean(fields):
+    coarse = fields.reshape((fields.shape[0], 4) + fields.shape[3:])
+    return coarse.sum(axis=1) * 0.25
+
+
 def tracer_substep(fields, wet_mask, volume_flux, onehot, eco_rate):
     species = eco_rate.shape[0]
     centre = fields[:, 1:-1, 1:-1]
@@ -163,28 +193,33 @@
         lax.broadcasted_iota(jnp.int32, (depth, depth), 0)
         < lax.broadcasted_iota(jnp.int32, (depth, depth), 1)
     ).astype(jnp.float32)
-    wet_fine = wet_of(fine_levels(levels), depth)
     wet_coarse = wet_of(jnp.max(levels, axis=0), depth)
     raw_ext = ext1[:channels]
     flux_ext = ext1[channels : channels + 2]
     levels_ext = ext1[channels + 2, :, :, 0:4].transpose(2, 0, 1)
     wet_coarse_ext = wet_of_float(jnp.max(levels_ext, axis=0), depth)
-    wet_fine_ext = wet_of_float(fine_levels(levels_ext), depth)
     zeros_flux = jnp.zeros((2, size_x, size_y, depth), jnp.float32)
     mid_y, late_y = reach_y - 2, reach_y - 4
     shape_mid = (channels, size_x, size_y + 2 * mid_y, depth)
     shape_late = (channels, size_x, size_y + 2 * late_y, depth)
 
+    wet_ch_ext = wet_of_float(levels_ext, depth).reshape((2, 2) + levels_ext.shape[1:] + (depth,))
+
+    def as_fields(block):
+        return block.reshape((channels // 4, 2, 2) + block.shape[1:])
+
     def ocean_a():
-        cut = 2 * reach_y - 2 * mid_y - 2
-        fine = trim(to_fine(raw_ext) * wet_fine_ext[None], 2 * reach_x - 2, cut)
+        fields = as_fields(raw_ext)[..., 1:-1, 1:-1, :]
+        wet = wet_ch_ext[..., 1:-1, 1:-1, :]
+        fields = fields * wet[None]
         running = zeros_flux
         for substep in range(2):
-            fine = ocean_substep(
-                fine, trim(wet_fine_ext, 2 * reach_x - 1 + substep, cut + substep + 1), 0.0
+            fields = ocean_substep_channels(fields, wet, 0.0)
+            running = running + channel_mean(
+                fields[0:2, :, :, 1 : 1 + size_x, reach_y - 1 : reach_y - 1 + size_y]
             )
-            running = running + coarse_mean(trim(fine[0:2], 1 - substep, 2 * mid_y + 1 - substep))
-        return to_coarse(fine), running
+        keep = fields[..., 1 : 1 + size_x, reach_y - 1 - mid_y : reach_y - 1 + size_y + mid_y, :]
+        return keep.reshape(shape_mid), running
 
     def tracer_a():
         tracer = raw_ext * wet_coarse_ext[None]
@@ -202,15 +237,18 @@
     ext2 = halo_x(block_mid, reach_x)
     fine_shape = (channels // 4, 2 * size_x + 2, 2 * size_y + 2, depth)
 
+    fine_shape = (channels, size_x + 2, size_y + 2, depth)
+
     def ocean_b():
-        fine = trim(to_fine(ext2), 2 * reach_x - 3, 2 * mid_y - 3)
+        cut_y = mid_y - 2
+        fields = as_fields(ext2)[..., cut_y : ext2.shape[2] - cut_y, :]
+        wet = wet_ch_ext[..., reach_x - 2 : wet_ch_ext.shape[2] - reach_x + 2, reach_y - 2 : wet_ch_ext.shape[3] - reach_y + 2, :]
         summed = running
         for substep in range(2):
-            fine = ocean_substep(
-                fine, trim(wet_fine_ext, 2 * reach_x - 2 + substep, 2 * reach_y - 2 + substep), 0.0
-            )
-            summed = summed + coarse_mean(trim(fine[0:2], 2 - substep))
-        return jnp.zeros(shape_late, jnp.float32), fine, summed / NSUB
+            fields = ocean_substep_channels(fields, wet, 0.0)
+            summed = summed + channel_mean(fields[0:2, :, :, 2 : 2 + size_x, 2 : 2 + size_y])
+        keep = fields[..., 1:-1, 1:-1, :]
+        return jnp.zeros(shape_late, jnp.float32), keep.reshape(fine_shape), summed / NSUB
 
     def tracer_b():
         tracer = ext2
@@ -231,9 +269,11 @@
     arrived = lax.ppermute(outgoing, "half", [(0, 1), (1, 0)])
 
     def ocean_c():
-        light = arrived[0:1]
-        heating = HEATING * to_fine(jnp.broadcast_to(light, (4, size_x, size_y, depth)))[0]
-        return to_coarse(ocean_substep(ocean_late, wet_fine, heating))
+        light = jnp.pad(arrived[0], ((1, 1), (1, 1), (0, 0)))
+        heating = HEATING * jnp.broadcast_to(light, (2, 2) + light.shape)
+        wet = wet_ch_ext[..., reach_x - 1 : wet_ch_ext.shape[2] - reach_x + 1, reach_y - 1 : wet_ch_ext.shape[3] - reach_y + 1, :]
+        fields = ocean_substep_channels(as_fields(ocean_late), wet, heating)
+        return fields[..., 1 : 1 + size_x, 1 : 1 + size_y, :].reshape(channels, size_x, size_y, depth)
 
     def tracer_c():
         return tracer_substep(trim(ext3, 0, late_y - 1), wet_coarse, arrived, onehot, eco_rate)

time: 89.8 us -> 78.4 us (0.87)
  the two profiles are of different devices: /device:TPU:228 before, /device:TPU:100 now
where the time goes in v8:
time: 78.4 us; the launch traced here: 78 us
  waiting for transfers between devices  35.1 us (45%)
  starting transfers between devices  29.5 us (38%)
  local copies, waits for them, and re-layouts  4.39 us (6%)
  matrix products  4.28 us (5%)
  other arithmetic  4 us (5%)
    ppermute x2, waiting for transfers between devices, halo_x(): after = lax.ppermute(block[:, :cells], 'gx', down)  12.9 us
    ppermute x2, waiting for transfers between devices, halo_x(): before = lax.ppermute(block[:, block.shape[1] - cells:], 'gx', up)  9.89 us
    ppermute x2, starting transfers between devices, halo_x(): before = lax.ppermute(block[:, block.shape[1] - cells:], 'gx', up)  8.56 us
    ppermute x1, starting transfers between devices, halo_y(): above = lax.ppermute(block[:, :, :rows], 'gy', down)  5.75 us
    ppermute x1, starting transfers between devices, halo_x_tracer(): before = lax.ppermute(block[:, block.shape[1] - cells:], ('half', 'gx'), up)  5.6 us
    ppermute x1, waiting for transfers between devices, body(): arrived = lax.ppermute(outgoing, 'half', [(0, 1), (1, 0)])  5.38 us
    dot_general x5, matrix products, tracer_substep(): jnp.einsum('ts,sxyk->txyk', onehot, living, precision=lax.Precision.HIGHEST)  4.1 us
    ppermute x2, starting transfers between devices, halo_x(): after = lax.ppermute(block[:, :cells], 'gx', down)  3.84 us
  transfers between devices with their start and end apart: 9, of which 8 were waited for; matrix products, arithmetic and copies ran while one was open for 0% of the time, Pallas kernels for 0%

profile of v8, /device:TPU:100, one launch (start us, length us, event | category | flops | bytes accessed | tf_op | source)
XLA Modules:
  0.0 78.0 jit_solution(15528345421680130803)
XLA Ops:
  0.0 0.7 fusion.61
  0.7 0.8 %copy.47 = f32[2,2,16,128]{3,0,2,1:T(2,128)S(1)} copy(f32[2,2,16,128]{3,2,1,0:T(8,128)} %param.13) | data formatting | bytes 65536 | tf_op args[2]
  1.5 0.1 copy.48
  1.6 1.2 %copy.62 = f32[1,20,2,16,128]{4,1,3,2,0:T(8,128)S(1)} copy(f32[1,20,2,16,128]{4,3,2,1,0:T(8,128)} %param.11) | data formatting | bytes 655360 | tf_op args[0]
  2.7 0.0 copy-start.3
  2.8 0.1 pad_maximum_fusion.22
  2.8 1.9 %collective-permute-start.1 = (f32[23,2,16,128]{3,0,2,1:T(8,128)S(1)}, f32[23,2,16,128]{3,0,2,1:T(8,128)S(1)}, u32[]{:S(2)}, u32[]{:S(2)}) collective-permute-start(f32[23,2,16,128]{3,0,2,1:T(8,128)S(1)} %pad_maximum_fusion.22), channel_id=1, source_target_pairs={{32,0},{64,32},{96,64},{128,96},{160,128},{192,160},{224,192},{256... | collective-permute-start | bytes 1130504 | tf_op jit(solution)/shard_map/ppermute | solution.py:28
  4.7 4.3 %collective-permute-start = (f32[23,2,16,128]{3,0,2,1:T(8,128)S(1)}, f32[23,2,16,128]{3,0,2,1:T(8,128)S(1)}, u32[]{:S(2)}, u32[]{:S(2)}) collective-permute-start(f32[23,2,16,128]{3,0,2,1:T(8,128)S(1)} %pad_maximum_fusion.22), channel_id=1, source_target_pairs={{0,32},{32,64},{64,96},{96,128},{128,160},{160,192},{192,224},{224... | collective-permute-start | bytes 1130504 | tf_op jit(solution)/shard_map/ppermute | solution.py:27
  9.0 7.2 %collective-permute-done.1 = f32[23,2,16,128]{3,0,2,1:T(8,128)S(1)} collective-permute-done((f32[23,2,16,128]{3,0,2,1:T(8,128)S(1)}, f32[23,2,16,128]{3,0,2,1:T(8,128)S(1)}, u32[]{:S(2)}, u32[]{:S(2)}) %collective-permute-start.1) | collective-permute-done | bytes 376864 | tf_op jit(solution)/shard_map/ppermute | solution.py:28
  16.2 1.3 %collective-permute-done = f32[23,2,16,128]{3,0,2,1:T(8,128)S(1)} collective-permute-done((f32[23,2,16,128]{3,0,2,1:T(8,128)S(1)}, f32[23,2,16,128]{3,0,2,1:T(8,128)S(1)}, u32[]{:S(2)}, u32[]{:S(2)}) %collective-permute-start) | collective-permute-done | bytes 376864 | tf_op jit(solution)/shard_map/ppermute | solution.py:27
  17.5 0.1 pad_maximum_fusion.27
  17.6 1.9 %collective-permute-start.2 = (f32[23,6,5,128]{3,0,2,1:T(8,128)S(1)}, f32[23,6,5,128]{3,0,2,1:T(8,128)S(1)}, u32[]{:S(2)}, u32[]{:S(2)}) collective-permute-start(f32[23,6,5,128]{3,0,2,1:T(8,128)S(1)} %get-tuple-element.258), channel_id=1, source_target_pairs={{0,1},{1,2},{2,3},{3,4},{4,5},{5,6},{6,7},{7,8},{8,9},{9,10},{10,1... | collective-permute-start | bytes 1059848 | tf_op jit(solution)/shard_map/ppermute | solution.py:43
  19.5 5.8 %collective-permute-start.3 = (f32[23,6,5,128]{3,0,2,1:T(8,128)S(1)}, f32[23,6,5,128]{3,0,2,1:T(8,128)S(1)}, u32[]{:S(2)}, u32[]{:S(2)}) collective-permute-start(f32[23,6,5,128]{3,0,2,1:T(8,128)S(1)} %get-tuple-element.259), channel_id=1, source_target_pairs={{1,0},{2,1},{3,2},{4,3},{5,4},{6,5},{7,6},{8,7},{9,8},{10,9},{11,1... | collective-permute-start | bytes 1059848 | tf_op jit(solution)/shard_map/ppermute | solution.py:44
  25.3 0.0 copy-done.3
  25.3 0.1 fusion.60
  25.3 3.3 %collective-permute-done.2 = f32[23,6,5,128]{3,0,2,1:T(8,128)S(1)} collective-permute-done((f32[23,6,5,128]{3,0,2,1:T(8,128)S(1)}, f32[23,6,5,128]{3,0,2,1:T(8,128)S(1)}, u32[]{:S(2)}, u32[]{:S(2)}) %collective-permute-start.2) | collective-permute-done | bytes 353312 | tf_op jit(solution)/shard_map/ppermute | solution.py:43
  28.6 1.7 %collective-permute-done.3 = f32[23,6,5,128]{3,0,2,1:T(8,128)S(1)} collective-permute-done((f32[23,6,5,128]{3,0,2,1:T(8,128)S(1)}, f32[23,6,5,128]{3,0,2,1:T(8,128)S(1)}, u32[]{:S(2)}, u32[]{:S(2)}) %collective-permute-start.3) | collective-permute-done | bytes 353312 | tf_op jit(solution)/shard_map/ppermute | solution.py:44
  30.3 0.1 pad_maximum_fusion.29
  30.4 0.1 copy.49
  30.5 0.1 compare_convert_fusion.1
  30.6 0.2 compare_convert_fusion
  30.8 0.1 pad_maximum_fusion.20
  30.9 0.0 copy-start.2
  31.0 0.1 pad_maximum_fusion.28
  31.1 0.5 copy-done.2
  31.6 0.0 copy-start.1
  31.6 3.4 %conditional.3 = (f32[20,2,22,128]{3,2,1,0:T(8,128)S(1)}, f32[2,2,16,128]{3,2,1,0:T(8,128)S(1)}) conditional(s32[]{:T(128)} %convert_element_type.44, (f32[6,26,128]{2,1,0:T(8,128)S(1)}, f32[20,6,26,128]{3,0,2,1:T(8,128)S(1)}, f32[2,6,26,128]{3,0,2,1:T(2,128)S(1)}, f32[19]{0:T(128)S(1)}, f32[19,19]{1,0:T(8,128)S(1)}) %tuple.126, ...), branch_computations={%region_1.2_spmd, %region_2.5_spmd} | conditional | flops 85125120 | bytes 43647144 | solution.py:236
  31.7 0.3 broadcast_multiply_fusion
  31.9 1.3 %fusion.2 = f32[19,4,24,128]{3,0,2,1:T(8,128)S(1)} fusion(f32[20,6,26,128]{3,0,2,1:T(8,128)S(1)} %broadcast_multiply_fusion, f32[19]{0:T(128)S(1)} %get-tuple-element.64, f32[19,19]{1,0:T(8,128)S(1)} %get-tuple-element.65), kind=kOutput, calls=%fused_computation.3 | convolution fusion | flops 54165504 | bytes 3305984 | tf_op jit(solution)/shard_map/cond/branch_0_fun/ts,sxyk->txyk/dot_general | solution.py:155
  33.2 0.6 add_multiply_fusion
  33.9 0.7 fusion.5
  34.6 0.3 add_multiply_fusion.1
  34.9 0.1 copy.43
  35.0 4.3 %collective-permute-start.4 = (f32[20,2,22,128]{3,2,1,0:T(8,128)S(1)}, f32[20,2,22,128]{3,2,1,0:T(8,128)S(1)}, u32[]{:S(2)}, u32[]{:S(2)}) collective-permute-start(f32[20,2,22,128]{3,2,1,0:T(8,128)S(1)} %get-tuple-element.92), channel_id=1, source_target_pairs={{0,32},{32,64},{64,96},{96,128},{128,160},{160,192},{192,224},{224... | collective-permute-start | bytes 1351688 | tf_op jit(solution)/shard_map/ppermute | solution.py:27
  39.3 0.0 copy-done.1
  39.3 1.9 %collective-permute-start.5 = (f32[20,2,22,128]{3,2,1,0:T(8,128)S(1)}, f32[20,2,22,128]{3,2,1,0:T(8,128)S(1)}, u32[]{:S(2)}, u32[]{:S(2)}) collective-permute-start(f32[20,2,22,128]{3,2,1,0:T(8,128)S(1)} %get-tuple-element.92), channel_id=1, source_target_pairs={{32,0},{64,32},{96,64},{128,96},{160,128},{192,160},{224,192},{256... | collective-permute-start | bytes 1351688 | tf_op jit(solution)/shard_map/ppermute | solution.py:28
  41.3 0.1 fusion.59
  41.3 8.6 %collective-permute-done.4 = f32[20,2,22,128]{3,2,1,0:T(8,128)S(1)} collective-permute-done((f32[20,2,22,128]{3,2,1,0:T(8,128)S(1)}, f32[20,2,22,128]{3,2,1,0:T(8,128)S(1)}, u32[]{:S(2)}, u32[]{:S(2)}) %collective-permute-start.4) | collective-permute-done | bytes 450592 | tf_op jit(solution)/shard_map/ppermute | solution.py:27
  50.0 5.7 %collective-permute-done.5 = f32[20,2,22,128]{3,2,1,0:T(8,128)S(1)} collective-permute-done((f32[20,2,22,128]{3,2,1,0:T(8,128)S(1)}, f32[20,2,22,128]{3,2,1,0:T(8,128)S(1)}, u32[]{:S(2)}, u32[]{:S(2)}) %collective-permute-start.5) | collective-permute-done | bytes 450592 | tf_op jit(solution)/shard_map/ppermute | solution.py:28
  55.8 3.6 %conditional.4 = (f32[20,2,18,128]{3,0,2,1:T(8,128)S(1)}, f32[20,4,18,128]{3,2,1,0:T(8,128)S(1)}, f32[2,2,16,128]{3,2,1,0:T(8,128)S(1)}) conditional(s32[]{:T(128)} %convert_element_type.44, (f32[6,26,128]{2,1,0:T(8,128)S(1)}, f32[20,6,22,128]{3,2,1,0:T(8,128)S(1)}, f32[2,6,26,128]{3,0,2,1:T(2,128)S(1)}, f32[19]{0:T(128)S(1)}, ...), branch_computations={%region_6.7_spmd, %region_7.10_spmd} | conditional | flops 76587008 | bytes 51945652 | solution.py:267
  55.9 0.5 copy.53
  56.3 1.1 %fusion.17 = f32[19,4,20,128]{3,0,2,1:T(8,128)S(1)} fusion(f32[20,6,22,128]{3,0,2,1:T(8,128)S(1)} %copy.53, f32[19]{0:T(128)S(1)} %get-tuple-element.71, f32[19,19]{1,0:T(8,128)S(1)} %get-tuple-element.72), kind=kOutput, calls=%fused_computation.57 | convolution fusion | flops 45137920 | bytes 2757120 | tf_op jit(solution)/shard_map/cond/branch_0_fun/ts,sxyk->txyk/dot_general | solution.py:155
  57.4 0.6 add_multiply_fusion.3
  58.0 0.6 fusion.20
  58.6 0.3 add_multiply_fusion.4
  58.9 0.2 fusion.23
  59.1 0.1 broadcast.224
  59.4 5.6 %collective-permute-start.6 = (f32[20,1,18,128]{3,0,2,1:T(8,128)S(1)}, f32[20,1,18,128]{3,0,2,1:T(8,128)S(1)}, u32[]{:S(2)}, u32[]{:S(2)}) collective-permute-start(f32[20,1,18,128]{3,0,2,1:T(8,128)S(1)} %get-tuple-element.260), channel_id=1, source_target_pairs={{512,544},{544,576},{576,608},{608,640},{640,672},{672,704},{704,7... | collective-permute-start | bytes 552968 | tf_op jit(solution)/shard_map/ppermute | solution.py:36
  65.0 1.9 %collective-permute-start.7 = (f32[20,1,18,128]{3,0,2,1:T(8,128)S(1)}, f32[20,1,18,128]{3,0,2,1:T(8,128)S(1)}, u32[]{:S(2)}, u32[]{:S(2)}) collective-permute-start(f32[20,1,18,128]{3,0,2,1:T(8,128)S(1)} %get-tuple-element.261), channel_id=1, source_target_pairs={{544,512},{576,544},{608,576},{640,608},{672,640},{704,672},{736,7... | collective-permute-start | bytes 552968 | tf_op jit(solution)/shard_map/ppermute | solution.py:37
  67.0 1.9 %collective-permute-start.8 = (f32[2,2,16,128]{3,2,1,0:T(8,128)S(1)}, f32[2,2,16,128]{3,2,1,0:T(8,128)S(1)}, u32[]{:S(2)}, u32[]{:S(2)}) collective-permute-start(f32[2,2,16,128]{3,2,1,0:T(8,128)S(1)} %get-tuple-element.95), channel_id=1, source_target_pairs={{0,512},{512,0},{1,513},{513,1},{2,514},{514,2},{3,515},{515,3},{4... | collective-permute-start | bytes 98312 | tf_op jit(solution)/shard_map/ppermute | solution.py:269
  68.9 5.4 %collective-permute-done.8 = f32[2,2,16,128]{3,2,1,0:T(8,128)S(1)} collective-permute-done((f32[2,2,16,128]{3,2,1,0:T(8,128)S(1)}, f32[2,2,16,128]{3,2,1,0:T(8,128)S(1)}, u32[]{:S(2)}, u32[]{:S(2)}) %collective-permute-start.8) | collective-permute-done | bytes 32800 | tf_op jit(solution)/shard_map/ppermute | solution.py:269
  74.3 0.0 collective-permute-done.6
  74.3 2.1 %collective-permute-done.7 = f32[20,1,18,128]{3,0,2,1:T(8,128)S(1)} collective-permute-done((f32[20,1,18,128]{3,0,2,1:T(8,128)S(1)}, f32[20,1,18,128]{3,0,2,1:T(8,128)S(1)}, u32[]{:S(2)}, u32[]{:S(2)}) %collective-permute-start.7) | collective-permute-done | bytes 184352 | tf_op jit(solution)/shard_map/ppermute | solution.py:37
  76.3 0.1 pad_maximum_fusion.21
  76.4 0.8 %conditional.5 = (f32[1,20,2,16,128]{4,3,2,1,0:T(8,128)S(1)}) conditional(s32[]{:T(128)} %convert_element_type.44, (f32[2,16,128]{2,1,0:T(8,128)S(1)}, f32[20,2,18,128]{3,0,2,1:T(8,128)S(1)}, f32[20,4,18,128]{3,0,2,1:T(8,128)S(1)}, f32[2,2,16,128]{3,2,1,0:T(8,128)S(1)}, f32[19]{0:T(128)S(1)}, /*index=5*/f32[19,19]{1,0:T(8,128)S(1)}) %tuple.128, ...), branch_computations={%region_10.11_spmd, %region_11.12_spmd} | conditional | flops 19365888 | bytes 17584136 | solution.py:281
  76.4 0.5 fusion.52
  77.0 0.2 multiply_bitcast_fusion
  77.2 0.1 copy.44
  77.3 0.0 copy-start
  77.3 0.7 copy-done
  (24 shorter events, 0.3 us)
Async XLA Ops:
  2.7 22.5 %copy-start.3 = (s32[19]{0:T(128)S(1)}, s32[19]{0:T(128)}, u32[]{:S(2)}) copy-start(s32[19]{0:T(128)} %param.14) | copy-start | bytes 232
  2.8 13.4 %collective-permute-start.1 = (f32[23,2,16,128]{3,0,2,1:T(8,128)S(1)}, f32[23,2,16,128]{3,0,2,1:T(8,128)S(1)}, u32[]{:S(2)}, u32[]{:S(2)}) collective-permute-start(f32[23,2,16,128]{3,0,2,1:T(8,128)S(1)} %pad_maximum_fusion.22), channel_id=1, source_target_pairs={{32,0},{64,32},{96,64},{128,96},{160,128},{192,160},{224,192},{256... | collective-permute-start | bytes 1130504 | tf_op jit(solution)/shard_map/ppermute | solution.py:28
  4.7 12.7 %collective-permute-start = (f32[23,2,16,128]{3,0,2,1:T(8,128)S(1)}, f32[23,2,16,128]{3,0,2,1:T(8,128)S(1)}, u32[]{:S(2)}, u32[]{:S(2)}) collective-permute-start(f32[23,2,16,128]{3,0,2,1:T(8,128)S(1)} %pad_maximum_fusion.22), channel_id=1, source_target_pairs={{0,32},{32,64},{64,96},{96,128},{128,160},{160,192},{192,224},{224... | collective-permute-start | bytes 1130504 | tf_op jit(solution)/shard_map/ppermute | solution.py:27
  17.6 11.0 %collective-permute-start.2 = (f32[23,6,5,128]{3,0,2,1:T(8,128)S(1)}, f32[23,6,5,128]{3,0,2,1:T(8,128)S(1)}, u32[]{:S(2)}, u32[]{:S(2)}) collective-permute-start(f32[23,6,5,128]{3,0,2,1:T(8,128)S(1)} %get-tuple-element.258), channel_id=1, source_target_pairs={{0,1},{1,2},{2,3},{3,4},{4,5},{5,6},{6,7},{7,8},{8,9},{9,10},{10,1... | collective-permute-start | bytes 1059848 | tf_op jit(solution)/shard_map/ppermute | solution.py:43
  19.5 10.8 %collective-permute-start.3 = (f32[23,6,5,128]{3,0,2,1:T(8,128)S(1)}, f32[23,6,5,128]{3,0,2,1:T(8,128)S(1)}, u32[]{:S(2)}, u32[]{:S(2)}) collective-permute-start(f32[23,6,5,128]{3,0,2,1:T(8,128)S(1)} %get-tuple-element.259), channel_id=1, source_target_pairs={{1,0},{2,1},{3,2},{4,3},{5,4},{6,5},{7,6},{8,7},{9,8},{10,9},{11,1... | collective-permute-start | bytes 1059848 | tf_op jit(solution)/shard_map/ppermute | solution.py:44
  30.9 0.7 copy-start.2
  31.6 7.7 %copy-start.1 = (s32[4,2,16]{2,1,0:T(2,128)S(1)}, s32[4,2,16]{2,1,0:T(2,128)}, u32[]{:S(2)}) copy-start(s32[4,2,16]{2,1,0:T(2,128)} %param.12) | copy-start | bytes 1540
  35.0 14.9 %collective-permute-start.4 = (f32[20,2,22,128]{3,2,1,0:T(8,128)S(1)}, f32[20,2,22,128]{3,2,1,0:T(8,128)S(1)}, u32[]{:S(2)}, u32[]{:S(2)}) collective-permute-start(f32[20,2,22,128]{3,2,1,0:T(8,128)S(1)} %get-tuple-element.92), channel_id=1, source_target_pairs={{0,32},{32,64},{64,96},{96,128},{128,160},{160,192},{192,224},{224... | collective-permute-start | bytes 1351688 | tf_op jit(solution)/shard_map/ppermute | solution.py:27
  39.3 16.4 %collective-permute-start.5 = (f32[20,2,22,128]{3,2,1,0:T(8,128)S(1)}, f32[20,2,22,128]{3,2,1,0:T(8,128)S(1)}, u32[]{:S(2)}, u32[]{:S(2)}) collective-permute-start(f32[20,2,22,128]{3,2,1,0:T(8,128)S(1)} %get-tuple-element.92), channel_id=1, source_target_pairs={{32,0},{64,32},{96,64},{128,96},{160,128},{192,160},{224,192},{256... | collective-permute-start | bytes 1351688 | tf_op jit(solution)/shard_map/ppermute | solution.py:28
  59.4 14.9 %collective-permute-start.6 = (f32[20,1,18,128]{3,0,2,1:T(8,128)S(1)}, f32[20,1,18,128]{3,0,2,1:T(8,128)S(1)}, u32[]{:S(2)}, u32[]{:S(2)}) collective-permute-start(f32[20,1,18,128]{3,0,2,1:T(8,128)S(1)} %get-tuple-element.260), channel_id=1, source_target_pairs={{512,544},{544,576},{576,608},{608,640},{640,672},{672,704},{704,7... | collective-permute-start | bytes 552968 | tf_op jit(solution)/shard_map/ppermute | solution.py:36
  65.0 11.3 %collective-permute-start.7 = (f32[20,1,18,128]{3,0,2,1:T(8,128)S(1)}, f32[20,1,18,128]{3,0,2,1:T(8,128)S(1)}, u32[]{:S(2)}, u32[]{:S(2)}) collective-permute-start(f32[20,1,18,128]{3,0,2,1:T(8,128)S(1)} %get-tuple-element.261), channel_id=1, source_target_pairs={{544,512},{576,544},{608,576},{640,608},{672,640},{704,672},{736,7... | collective-permute-start | bytes 552968 | tf_op jit(solution)/shard_map/ppermute | solution.py:37
  67.0 7.3 %collective-permute-start.8 = (f32[2,2,16,128]{3,2,1,0:T(8,128)S(1)}, f32[2,2,16,128]{3,2,1,0:T(8,128)S(1)}, u32[]{:S(2)}, u32[]{:S(2)}) collective-permute-start(f32[2,2,16,128]{3,2,1,0:T(8,128)S(1)} %get-tuple-element.95), channel_id=1, source_target_pairs={{0,512},{512,0},{1,513},{513,1},{2,514},{514,2},{3,515},{515,3},{4... | collective-permute-start | bytes 98312 | tf_op jit(solution)/shard_map/ppermute | solution.py:269
  77.3 0.7 copy-start

commit v9 on v8

--- a/solution.py
+++ b/solution.py
@@ -152,7 +152,7 @@
     )
     spread = to_east + to_west + to_north + to_south - 4.0 * centre
     living = centre[:species]
-    prey_values = jnp.einsum("ts,sxyk->txyk", onehot, living, precision=lax.Precision.HIGHEST)
+    prey_values = jnp.take(living, onehot, axis=0)
     growth = eco_rate[:, None, None, None] * living * jnp.tanh(prey_values) - MORTALITY * living
     reaction = jnp.concatenate([growth, jnp.zeros_like(centre[species:])], axis=0)
     return wet_mask * (centre + DT * (NU * spread - advect + reaction))
@@ -186,9 +186,7 @@
     packed = jnp.concatenate([state[0], old_flux, level_lanes], axis=0)
     reach_x, reach_y = size_x, NSUB + 1
     ext1 = halo_y(halo_x(packed, reach_x), reach_y)
-    onehot = (eco_prey[:, None] == lax.broadcasted_iota(jnp.int32, (species, species), 1)).astype(
-        jnp.float32
-    )
+    onehot = jnp.clip(eco_prey, 0, species - 1)
     above_table = (
         lax.broadcasted_iota(jnp.int32, (depth, depth), 0)
         < lax.broadcasted_iota(jnp.int32, (depth, depth), 1)

time: 78.4 us -> 87.9 us (1.12)
  the two profiles are of different devices: /device:TPU:100 before, /device:TPU:356 now
where the time goes in v9:
time: 87.9 us; the launch traced here: 87.1 us
  waiting for transfers between devices  34.1 us (39%)
  starting transfers between devices  29.5 us (34%)
  local copies, waits for them, and re-layouts  14 us (16%)
  other arithmetic  8.26 us (9%)
    ppermute x2, waiting for transfers between devices, halo_x(): after = lax.ppermute(block[:, :cells], 'gx', down)  12.4 us
    ppermute x2, waiting for transfers between devices, halo_x(): before = lax.ppermute(block[:, block.shape[1] - cells:], 'gx', up)  8.77 us
    ppermute x2, starting transfers between devices, halo_x(): before = lax.ppermute(block[:, block.shape[1] - cells:], 'gx', up)  8.56 us
    ppermute x1, starting transfers between devices, halo_y(): above = lax.ppermute(block[:, :, :rows], 'gy', down)  5.75 us
    ppermute x1, starting transfers between devices, halo_x_tracer(): before = lax.ppermute(block[:, block.shape[1] - cells:], ('half', 'gx'), up)  5.6 us
    ppermute x1, waiting for transfers between devices, body(): arrived = lax.ppermute(outgoing, 'half', [(0, 1), (1, 0)])  5.38 us
    gather x5, local copies, waits for them, and re-layouts, tracer_substep(): prey_values = jnp.take(living, onehot, axis=0)  4.5 us
    unnamed x30, local copies, waits for them, and re-layouts  4.36 us
  transfers between devices with their start and end apart: 9, of which 8 were waited for; matrix products, arithmetic and copies ran while one was open for 3% of the time, Pallas kernels for 0%

profile of v9, /device:TPU:356, one launch (start us, length us, event | category | flops | bytes accessed | tf_op | source)
XLA Modules:
  0.0 87.1 jit_solution(17129487234874834547)
XLA Ops:
  0.0 0.7 fusion.37
  0.7 0.8 copy.33
  1.6 1.2 %copy.46 = f32[1,20,2,16,128]{4,1,3,2,0:T(8,128)S(1)} copy(f32[1,20,2,16,128]{4,3,2,1,0:T(8,128)} %param.11) | data formatting | bytes 655360 | tf_op args[0]
  2.8 1.9 %collective-permute-start.1 = (f32[23,2,16,128]{3,0,2,1:T(8,128)S(1)}, f32[23,2,16,128]{3,0,2,1:T(8,128)S(1)}, u32[]{:S(2)}, u32[]{:S(2)}) collective-permute-start(f32[23,2,16,128]{3,0,2,1:T(8,128)S(1)} %pad_maximum_fusion.22), channel_id=1, source_target_pairs={{32,0},{64,32},{96,64},{128,96},{160,128},{192,160},{224,192},{256... | collective-permute-start | bytes 1130504 | tf_op jit(solution)/shard_map/ppermute | solution.py:28
  4.7 4.3 %collective-permute-start = (f32[23,2,16,128]{3,0,2,1:T(8,128)S(1)}, f32[23,2,16,128]{3,0,2,1:T(8,128)S(1)}, u32[]{:S(2)}, u32[]{:S(2)}) collective-permute-start(f32[23,2,16,128]{3,0,2,1:T(8,128)S(1)} %pad_maximum_fusion.22), channel_id=1, source_target_pairs={{0,32},{32,64},{64,96},{96,128},{128,160},{160,192},{192,224},{224... | collective-permute-start | bytes 1130504 | tf_op jit(solution)/shard_map/ppermute | solution.py:27
  9.0 7.2 %collective-permute-done.1 = f32[23,2,16,128]{3,0,2,1:T(8,128)S(1)} collective-permute-done((f32[23,2,16,128]{3,0,2,1:T(8,128)S(1)}, f32[23,2,16,128]{3,0,2,1:T(8,128)S(1)}, u32[]{:S(2)}, u32[]{:S(2)}) %collective-permute-start.1) | collective-permute-done | bytes 376864 | tf_op jit(solution)/shard_map/ppermute | solution.py:28
  16.2 1.3 %collective-permute-done = f32[23,2,16,128]{3,0,2,1:T(8,128)S(1)} collective-permute-done((f32[23,2,16,128]{3,0,2,1:T(8,128)S(1)}, f32[23,2,16,128]{3,0,2,1:T(8,128)S(1)}, u32[]{:S(2)}, u32[]{:S(2)}) %collective-permute-start) | collective-permute-done | bytes 376864 | tf_op jit(solution)/shard_map/ppermute | solution.py:27
  17.6 1.9 %collective-permute-start.2 = (f32[23,6,5,128]{3,0,2,1:T(8,128)S(1)}, f32[23,6,5,128]{3,0,2,1:T(8,128)S(1)}, u32[]{:S(2)}, u32[]{:S(2)}) collective-permute-start(f32[23,6,5,128]{3,0,2,1:T(8,128)S(1)} %get-tuple-element.219), channel_id=1, source_target_pairs={{0,1},{1,2},{2,3},{3,4},{4,5},{5,6},{6,7},{7,8},{8,9},{9,10},{10,1... | collective-permute-start | bytes 1059848 | tf_op jit(solution)/shard_map/ppermute | solution.py:43
  19.5 5.8 %collective-permute-start.3 = (f32[23,6,5,128]{3,0,2,1:T(8,128)S(1)}, f32[23,6,5,128]{3,0,2,1:T(8,128)S(1)}, u32[]{:S(2)}, u32[]{:S(2)}) collective-permute-start(f32[23,6,5,128]{3,0,2,1:T(8,128)S(1)} %get-tuple-element.220), channel_id=1, source_target_pairs={{1,0},{2,1},{3,2},{4,3},{5,4},{6,5},{7,6},{8,7},{9,8},{10,9},{11,1... | collective-permute-start | bytes 1059848 | tf_op jit(solution)/shard_map/ppermute | solution.py:44
  25.3 3.3 %collective-permute-done.2 = f32[23,6,5,128]{3,0,2,1:T(8,128)S(1)} collective-permute-done((f32[23,6,5,128]{3,0,2,1:T(8,128)S(1)}, f32[23,6,5,128]{3,0,2,1:T(8,128)S(1)}, u32[]{:S(2)}, u32[]{:S(2)}) %collective-permute-start.2) | collective-permute-done | bytes 353312 | tf_op jit(solution)/shard_map/ppermute | solution.py:43
  28.6 1.7 %collective-permute-done.3 = f32[23,6,5,128]{3,0,2,1:T(8,128)S(1)} collective-permute-done((f32[23,6,5,128]{3,0,2,1:T(8,128)S(1)}, f32[23,6,5,128]{3,0,2,1:T(8,128)S(1)}, u32[]{:S(2)}, u32[]{:S(2)}) %collective-permute-start.3) | collective-permute-done | bytes 353312 | tf_op jit(solution)/shard_map/ppermute | solution.py:44
  30.3 0.1 pad_maximum_fusion.29
  30.4 0.1 copy.35
  30.5 0.1 compare_convert_fusion.1
  30.6 0.2 compare_convert_fusion
  30.8 0.1 pad_maximum_fusion.20
  31.0 0.1 pad_maximum_fusion.28
  31.1 0.5 copy-done.16
  31.6 8.3 %conditional.3 = (f32[20,2,22,128]{3,2,1,0:T(8,128)S(1)}, f32[2,2,16,128]{3,2,1,0:T(8,128)S(1)}) conditional(s32[]{:T(128)} %convert_element_type.41, (f32[6,26,128]{2,1,0:T(8,128)S(1)}, f32[20,6,26,128]{3,0,2,1:T(8,128)S(1)}, f32[2,6,26,128]{3,0,2,1:T(2,128)S(1)}, f32[19]{0:T(128)S(1)}, s32[19]{0:T(128)S(1)}) %tuple.116, ...), branch_computations={%region_1.2_spmd, %region_2.5_spmd} | conditional | flops 18350080 | bytes 43647144 | solution.py:234
  31.7 0.6 slice.257
  32.3 0.3 copy_multiply_fusion
  32.7 0.6 slice_bitcast_fusion.12
  33.3 0.6 slice_bitcast_fusion.10
  33.9 1.1 %slice.438 = f32[19,4,24,128]{3,2,1,0:T(8,128)} slice(f32[20,6,26,128]{3,2,1,0:T(8,128)S(1)} %copy_multiply_fusion), slice={[0:19], [1:5], [1:25], [0:128]} | slice | bytes 1867776 | tf_op jit(solution)/shard_map/cond/branch_0_fun/slice | solution.py:154
  35.0 1.8 %gather_fusion = f32[19,4,24,128]{3,2,1,0:T(8,128)S(1)} fusion(f32[19,4,24,128]{3,2,1,0:T(8,128)} %slice.438, s32[1024]{0:T(1024)S(1)} %pad_clamp_fusion), kind=kCustom, calls=%fused_computation | custom fusion | bytes 1867852 | tf_op jit(solution)/shard_map/cond/branch_0_fun/jit(_take)/gather | solution.py:155
  36.9 0.4 multiply_subtract_fusion.10
  37.3 0.4 copy-done.4
  37.7 0.8 add_multiply_fusion.2
  38.6 0.7 gather_fusion.1
  39.3 0.2 multiply_subtract_fusion.11
  39.5 0.4 add_multiply_fusion.3
  40.0 4.3 %collective-permute-start.4 = (f32[20,2,22,128]{3,2,1,0:T(8,128)S(1)}, f32[20,2,22,128]{3,2,1,0:T(8,128)}, u32[]{:S(2)}, u32[]{:S(2)}) collective-permute-start(f32[20,2,22,128]{3,2,1,0:T(8,128)S(1)} %get-tuple-element.92), channel_id=1, source_target_pairs={{0,32},{32,64},{64,96},{96,128},{128,160},{160,192},{192,224},{224... | collective-permute-start | bytes 1351688 | tf_op jit(solution)/shard_map/ppermute | solution.py:27
  44.3 0.6 fusion.35
  44.9 1.9 %collective-permute-start.5 = (f32[20,2,22,128]{3,2,1,0:T(8,128)S(1)}, f32[20,2,22,128]{3,2,1,0:T(8,128)S(1)}, u32[]{:S(2)}, u32[]{:S(2)}) collective-permute-start(f32[20,2,22,128]{3,2,1,0:T(8,128)S(1)} %get-tuple-element.92), channel_id=1, source_target_pairs={{32,0},{64,32},{96,64},{128,96},{160,128},{192,160},{224,192},{256... | collective-permute-start | bytes 1351688 | tf_op jit(solution)/shard_map/ppermute | solution.py:28
  46.9 0.7 fusion.36
  47.5 7.5 %collective-permute-done.4 = f32[20,2,22,128]{3,2,1,0:T(8,128)} collective-permute-done((f32[20,2,22,128]{3,2,1,0:T(8,128)S(1)}, f32[20,2,22,128]{3,2,1,0:T(8,128)}, u32[]{:S(2)}, u32[]{:S(2)}) %collective-permute-start.4) | collective-permute-done | bytes 450592 | tf_op jit(solution)/shard_map/ppermute | solution.py:27
  55.0 1.1 %constant_dynamic-update-slice_fusion.4 = f32[20,6,22,128]{3,2,1,0:T(8,128)S(1)} fusion(f32[20,2,22,128]{3,2,1,0:T(8,128)} %collective-permute-done.4), kind=kLoop, calls=%fused_computation.176 | loop fusion | bytes 942080
  56.1 5.2 %collective-permute-done.5 = f32[20,2,22,128]{3,2,1,0:T(8,128)S(1)} collective-permute-done((f32[20,2,22,128]{3,2,1,0:T(8,128)S(1)}, f32[20,2,22,128]{3,2,1,0:T(8,128)S(1)}, u32[]{:S(2)}, u32[]{:S(2)}) %collective-permute-start.5) | collective-permute-done | bytes 450592 | tf_op jit(solution)/shard_map/ppermute | solution.py:28
  61.4 6.2 %conditional.4 = (f32[20,2,18,128]{3,2,1,0:T(8,128)S(1)}, f32[20,4,18,128]{3,2,1,0:T(8,128)S(1)}, f32[2,2,16,128]{3,2,1,0:T(8,128)S(1)}) conditional(s32[]{:T(128)} %convert_element_type.41, (f32[6,26,128]{2,1,0:T(8,128)S(1)}, f32[20,6,22,128]{3,2,1,0:T(8,128)S(1)}, f32[2,6,26,128]{3,0,2,1:T(2,128)S(1)}, f32[19]{0:T(128)S(1)}, s32[19]{0:T(128)S(1)}, ...), branch_computations={%region_6.7_spmd, %region_7.10_spmd} | conditional | flops 22024192 | bytes 52076752 | solution.py:265
  61.4 0.5 compare_and_fusion.1
  61.9 0.6 pad_clamp_fusion.1
  62.5 0.6 slice.300
  63.2 0.1 slice.309
  63.3 0.7 gather_fusion.2
  64.1 0.4 multiply_subtract_fusion.12
  64.5 0.8 add_multiply_fusion.4
  65.3 0.7 gather_fusion.3
  66.0 0.2 multiply_subtract_fusion.13
  66.3 0.4 add_multiply_fusion.5
  66.7 0.3 copy-done.13
  67.0 0.1 copy-done.14
  67.1 0.2 fusion.17
  67.3 0.1 broadcast.272
  67.7 5.6 %collective-permute-start.6 = (f32[20,1,18,128]{3,2,1,0:T(8,128)S(1)}, f32[20,1,18,128]{3,2,1,0:T(8,128)S(1)}, u32[]{:S(2)}, u32[]{:S(2)}) collective-permute-start(f32[20,1,18,128]{3,2,1,0:T(8,128)S(1)} %get-tuple-element.221), channel_id=1, source_target_pairs={{512,544},{544,576},{576,608},{608,640},{640,672},{672,704},{704,7... | collective-permute-start | bytes 552968 | tf_op jit(solution)/shard_map/ppermute | solution.py:36
  73.3 1.9 %collective-permute-start.7 = (f32[20,1,18,128]{3,2,1,0:T(8,128)S(1)}, f32[20,1,18,128]{3,2,1,0:T(8,128)S(1)}, u32[]{:S(2)}, u32[]{:S(2)}) collective-permute-start(f32[20,1,18,128]{3,2,1,0:T(8,128)S(1)} %get-tuple-element.222), channel_id=1, source_target_pairs={{544,512},{576,544},{608,576},{640,608},{672,640},{704,672},{736,7... | collective-permute-start | bytes 552968 | tf_op jit(solution)/shard_map/ppermute | solution.py:37
  75.2 1.9 %collective-permute-start.8 = (f32[2,2,16,128]{3,2,1,0:T(8,128)S(1)}, f32[2,2,16,128]{3,2,1,0:T(8,128)S(1)}, u32[]{:S(2)}, u32[]{:S(2)}) collective-permute-start(f32[2,2,16,128]{3,2,1,0:T(8,128)S(1)} %get-tuple-element.95), channel_id=1, source_target_pairs={{0,512},{512,0},{1,513},{513,1},{2,514},{514,2},{3,515},{515,3},{4... | collective-permute-start | bytes 98312 | tf_op jit(solution)/shard_map/ppermute | solution.py:267
  77.1 5.4 %collective-permute-done.8 = f32[2,2,16,128]{3,2,1,0:T(8,128)S(1)} collective-permute-done((f32[2,2,16,128]{3,2,1,0:T(8,128)S(1)}, f32[2,2,16,128]{3,2,1,0:T(8,128)S(1)}, u32[]{:S(2)}, u32[]{:S(2)}) %collective-permute-start.8) | collective-permute-done | bytes 32800 | tf_op jit(solution)/shard_map/ppermute | solution.py:267
  82.5 2.6 %collective-permute-done.7 = f32[20,1,18,128]{3,2,1,0:T(8,128)S(1)} collective-permute-done((f32[20,1,18,128]{3,2,1,0:T(8,128)S(1)}, f32[20,1,18,128]{3,2,1,0:T(8,128)S(1)}, u32[]{:S(2)}, u32[]{:S(2)}) %collective-permute-start.7) | collective-permute-done | bytes 184352 | tf_op jit(solution)/shard_map/ppermute | solution.py:37
  85.1 0.1 pad_maximum_fusion.21
  85.2 1.1 %conditional.5 = (f32[1,20,2,16,128]{4,3,2,1,0:T(8,128)S(1)}) conditional(s32[]{:T(128)} %convert_element_type.41, (f32[2,16,128]{2,1,0:T(8,128)S(1)}, f32[20,2,18,128]{3,2,1,0:T(8,128)S(1)}, f32[20,4,18,128]{3,2,1,0:T(8,128)S(1)}, f32[2,2,16,128]{3,2,1,0:T(8,128)S(1)}, f32[19]{0:T(128)S(1)}, /*index=5*/s32[19]{0:T(128)S(1)}) %tuple.120, ...), branch_computations={%region_10.11_spmd, %region_11.12_spmd} | conditional | flops 3200000 | bytes 17584136 | solution.py:279
  85.3 0.6 gather_fusion.4
  85.9 0.1 multiply_subtract_fusion.14
  86.0 0.3 multiply_bitcast_fusion
  86.3 0.7 copy-done.3
  (81 shorter events, 0.7 us)
Async XLA Ops:
  2.7 22.5 %copy-start.24 = (s32[19]{0:T(128)S(1)}, s32[19]{0:T(128)}, u32[]{:S(2)}) copy-start(s32[19]{0:T(128)} %param.14) | copy-start | bytes 232
  2.8 13.4 %collective-permute-start.1 = (f32[23,2,16,128]{3,0,2,1:T(8,128)S(1)}, f32[23,2,16,128]{3,0,2,1:T(8,128)S(1)}, u32[]{:S(2)}, u32[]{:S(2)}) collective-permute-start(f32[23,2,16,128]{3,0,2,1:T(8,128)S(1)} %pad_maximum_fusion.22), channel_id=1, source_target_pairs={{32,0},{64,32},{96,64},{128,96},{160,128},{192,160},{224,192},{256... | collective-permute-start | bytes 1130504 | tf_op jit(solution)/shard_map/ppermute | solution.py:28
  4.7 12.7 %collective-permute-start = (f32[23,2,16,128]{3,0,2,1:T(8,128)S(1)}, f32[23,2,16,128]{3,0,2,1:T(8,128)S(1)}, u32[]{:S(2)}, u32[]{:S(2)}) collective-permute-start(f32[23,2,16,128]{3,0,2,1:T(8,128)S(1)} %pad_maximum_fusion.22), channel_id=1, source_target_pairs={{0,32},{32,64},{64,96},{96,128},{128,160},{160,192},{192,224},{224... | collective-permute-start | bytes 1130504 | tf_op jit(solution)/shard_map/ppermute | solution.py:27
  17.6 11.0 %collective-permute-start.2 = (f32[23,6,5,128]{3,0,2,1:T(8,128)S(1)}, f32[23,6,5,128]{3,0,2,1:T(8,128)S(1)}, u32[]{:S(2)}, u32[]{:S(2)}) collective-permute-start(f32[23,6,5,128]{3,0,2,1:T(8,128)S(1)} %get-tuple-element.219), channel_id=1, source_target_pairs={{0,1},{1,2},{2,3},{3,4},{4,5},{5,6},{6,7},{7,8},{8,9},{9,10},{10,1... | collective-permute-start | bytes 1059848 | tf_op jit(solution)/shard_map/ppermute | solution.py:43
  19.5 10.8 %collective-permute-start.3 = (f32[23,6,5,128]{3,0,2,1:T(8,128)S(1)}, f32[23,6,5,128]{3,0,2,1:T(8,128)S(1)}, u32[]{:S(2)}, u32[]{:S(2)}) collective-permute-start(f32[23,6,5,128]{3,0,2,1:T(8,128)S(1)} %get-tuple-element.220), channel_id=1, source_target_pairs={{1,0},{2,1},{3,2},{4,3},{5,4},{6,5},{7,6},{8,7},{9,8},{10,9},{11,1... | collective-permute-start | bytes 1059848 | tf_op jit(solution)/shard_map/ppermute | solution.py:44
  25.3 6.3 %copy-start.25 = (s32[19]{0:T(128)}, s32[19]{0:T(128)S(1)}, u32[]{:S(2)}) copy-start(s32[19]{0:T(128)S(1)} %broadcast_clamp_fusion) | copy-start | bytes 232
  30.6 1.0 %copy-start.1 = (f32[6,26,128]{2,1,0:T(8,128)}, f32[6,26,128]{2,1,0:T(8,128)S(1)}, u32[]{:S(2)}) copy-start(f32[6,26,128]{2,1,0:T(8,128)S(1)} %compare_convert_fusion.1) | copy-start | bytes 239620
  30.8 30.6 %copy-start = (f32[2,2,6,26,128]{4,3,2,1,0:T(8,128)}, f32[2,2,6,26,128]{4,3,2,1,0:T(8,128)S(1)}, u32[]{:S(2)}) copy-start(f32[2,2,6,26,128]{4,3,2,1,0:T(8,128)S(1)} %compare_convert_fusion) | copy-start | bytes 958468
  31.0 0.7 copy-start.16
  31.6 12.6 %copy-start.15 = (s32[4,2,16]{2,1,0:T(2,128)S(1)}, s32[4,2,16]{2,1,0:T(2,128)}, u32[]{:S(2)}) copy-start(s32[4,2,16]{2,1,0:T(2,128)} %param.12) | copy-start | bytes 1540
  31.6 5.2 %copy-start.18 = (f32[19]{0:T(128)}, f32[19]{0:T(128)S(1)}, u32[]{:S(2)}) copy-start(f32[19]{0:T(128)S(1)} %get-tuple-element.64) | copy-start | bytes 232 | tf_op jit(solution)/shard_map/cond
  31.6 5.2 %copy-start.21 = (pred[19]{0:T(512)(128)(4,1)}, pred[19]{0:T(512)(128)(4,1)S(1)}, u32[]{:S(2)}) copy-start(pred[19]{0:T(512)(128)(4,1)S(1)} %compare_and_fusion) | copy-start | bytes 61 | tf_op jit(solution)/shard_map/cond
  31.7 3.4 %copy-start.20 = (s32[1024]{0:T(1024)}, s32[1024]{0:T(1024)S(1)}, u32[]{:S(2)}) copy-start(s32[1024]{0:T(1024)S(1)} %pad_clamp_fusion) | copy-start | bytes 12292 | tf_op jit(solution)/shard_map/cond
  36.9 0.8 copy-start.4
  36.9 0.8 copy-start.5
  38.5 0.8 copy-start.19
  38.5 0.8 copy-start.22
  38.5 1.0 %copy-start.8 = (f32[2,22,128]{2,1,0:T(8,128)S(1)}, f32[2,22,128]{2,1,0:T(8,128)}, u32[]{:S(2)}) copy-start(f32[2,22,128]{2,1,0:T(8,128)} %slice.257) | copy-start | bytes 67588 | tf_op jit(solution)/shard_map/cond
  38.5 1.0 %copy-start.10 = (f32[2,22,128]{2,1,0:T(8,128)S(1)}, f32[2,22,128]{2,1,0:T(8,128)}, u32[]{:S(2)}) copy-start(f32[2,22,128]{2,1,0:T(8,128)} %get-tuple-element.209) | copy-start | bytes 67588 | tf_op jit(solution)/shard_map/cond
  38.5 1.0 %copy-start.11 = (f32[2,22,128]{2,1,0:T(8,128)S(1)}, f32[2,22,128]{2,1,0:T(8,128)}, u32[]{:S(2)}) copy-start(f32[2,22,128]{2,1,0:T(8,128)} %get-tuple-element.210) | copy-start | bytes 67588 | tf_op jit(solution)/shard_map/cond
  40.0 6.9 %copy-start.6 = (f32[2,2,16,128]{3,2,1,0:T(8,128)}, f32[2,2,16,128]{3,2,1,0:T(8,128)S(1)}, u32[]{:S(2)}) copy-start(f32[2,2,16,128]{3,2,1,0:T(8,128)S(1)} %get-tuple-element.93) | copy-start | bytes 98308
  40.0 15.0 %collective-permute-start.4 = (f32[20,2,22,128]{3,2,1,0:T(8,128)S(1)}, f32[20,2,22,128]{3,2,1,0:T(8,128)}, u32[]{:S(2)}, u32[]{:S(2)}) collective-permute-start(f32[20,2,22,128]{3,2,1,0:T(8,128)S(1)} %get-tuple-element.92), channel_id=1, source_target_pairs={{0,32},{32,64},{64,96},{96,128},{128,160},{160,192},{192,224},{224... | collective-permute-start | bytes 1351688 | tf_op jit(solution)/shard_map/ppermute | solution.py:27
  44.9 16.4 %collective-permute-start.5 = (f32[20,2,22,128]{3,2,1,0:T(8,128)S(1)}, f32[20,2,22,128]{3,2,1,0:T(8,128)S(1)}, u32[]{:S(2)}, u32[]{:S(2)}) collective-permute-start(f32[20,2,22,128]{3,2,1,0:T(8,128)S(1)} %get-tuple-element.92), channel_id=1, source_target_pairs={{32,0},{64,32},{96,64},{128,96},{160,128},{192,160},{224,192},{256... | collective-permute-start | bytes 1351688 | tf_op jit(solution)/shard_map/ppermute | solution.py:28
  47.5 13.8 %copy-start.2 = (f32[6,26,128]{2,1,0:T(8,128)S(1)}, f32[6,26,128]{2,1,0:T(8,128)}, u32[]{:S(2)}) copy-start(f32[6,26,128]{2,1,0:T(8,128)} %copy-done.1) | copy-start | bytes 239620
  47.5 13.8 %copy-start.17 = (f32[19]{0:T(128)S(1)}, f32[19]{0:T(128)}, u32[]{:S(2)}) copy-start(f32[19]{0:T(128)} %param.15) | copy-start | bytes 232
  47.5 13.8 %copy-start.26 = (s32[19]{0:T(128)S(1)}, s32[19]{0:T(128)}, u32[]{:S(2)}) copy-start(s32[19]{0:T(128)} %copy-done.25) | copy-start | bytes 232
  63.2 0.9 %copy-start.23 = (pred[19]{0:T(512)(128)(4,1)S(1)}, pred[19]{0:T(512)(128)(4,1)}, u32[]{:S(2)}) copy-start(pred[19]{0:T(512)(128)(4,1)} %compare_and_fusion.1) | copy-start | bytes 61 | tf_op jit(solution)/shard_map/cond
  65.3 1.0 %copy-start.9 = (f32[2,18,128]{2,1,0:T(8,128)S(1)}, f32[2,18,128]{2,1,0:T(8,128)}, u32[]{:S(2)}) copy-start(f32[2,18,128]{2,1,0:T(8,128)} %slice.300) | copy-start | bytes 55300 | tf_op jit(solution)/shard_map/cond
  66.2 0.7 copy-start.13
  66.2 0.8 copy-start.14
  67.6 17.6 %copy-start.12 = (f32[2,16,128]{2,1,0:T(8,128)S(1)}, f32[2,16,128]{2,1,0:T(8,128)}, u32[]{:S(2)}) copy-start(f32[2,16,128]{2,1,0:T(8,128)} %fusion.36) | copy-start | bytes 49156
  67.6 17.6 %copy-start.27 = (s32[19]{0:T(128)S(1)}, s32[19]{0:T(128)}, u32[]{:S(2)}) copy-start(s32[19]{0:T(128)} %copy-done.25) | copy-start | bytes 232
  67.7 14.9 %collective-permute-start.6 = (f32[20,1,18,128]{3,2,1,0:T(8,128)S(1)}, f32[20,1,18,128]{3,2,1,0:T(8,128)S(1)}, u32[]{:S(2)}, u32[]{:S(2)}) collective-permute-start(f32[20,1,18,128]{3,2,1,0:T(8,128)S(1)} %get-tuple-element.221), channel_id=1, source_target_pairs={{512,544},{544,576},{576,608},{608,640},{640,672},{672,704},{704,7... | collective-permute-start | bytes 552968 | tf_op jit(solution)/shard_map/ppermute | solution.py:36
  73.3 11.8 %collective-permute-start.7 = (f32[20,1,18,128]{3,2,1,0:T(8,128)S(1)}, f32[20,1,18,128]{3,2,1,0:T(8,128)S(1)}, u32[]{:S(2)}, u32[]{:S(2)}) collective-permute-start(f32[20,1,18,128]{3,2,1,0:T(8,128)S(1)} %get-tuple-element.222), channel_id=1, source_target_pairs={{544,512},{576,544},{608,576},{640,608},{672,640},{704,672},{736,7... | collective-permute-start | bytes 552968 | tf_op jit(solution)/shard_map/ppermute | solution.py:37
  75.2 7.3 %collective-permute-start.8 = (f32[2,2,16,128]{3,2,1,0:T(8,128)S(1)}, f32[2,2,16,128]{3,2,1,0:T(8,128)S(1)}, u32[]{:S(2)}, u32[]{:S(2)}) collective-permute-start(f32[2,2,16,128]{3,2,1,0:T(8,128)S(1)} %get-tuple-element.95), channel_id=1, source_target_pairs={{0,512},{512,0},{1,513},{513,1},{2,514},{514,2},{3,515},{515,3},{4... | collective-permute-start | bytes 98312 | tf_op jit(solution)/shard_map/ppermute | solution.py:267
  86.3 0.7 copy-start.3

commit v10 on v8

--- a/solution.py
+++ b/solution.py
@@ -36,6 +36,37 @@
     before = lax.ppermute(block[:, block.shape[1] - cells :], ("half", "gx"), up)
     after = lax.ppermute(block[:, :cells], ("half", "gx"), down)
     return jnp.concatenate([before, block, after], axis=1)
+
+
+def halo_cross(block, rows):
+    nx, ny = lax.axis_size("gx"), lax.axis_size("gy")
+    size_y = block.shape[2]
+    up, down = shifts("gx")
+    before = lax.ppermute(block, "gx", up)
+    after = lax.ppermute(block, "gx", down)
+    up, down = shifts("gy")
+    last_rows = block[:, :, size_y - rows :]
+    first_rows = block[:, :, :rows]
+    below = lax.ppermute(last_rows, "gy", up)
+    above = lax.ppermute(first_rows, "gy", down)
+
+    def diagonal(part, dx, dy):
+        pairs = [
+            (i * ny + j, (i + dx) * ny + j + dy)
+            for i in range(nx)
+            for j in range(ny)
+            if 0 <= i + dx < nx and 0 <= j + dy < ny
+        ]
+        return lax.ppermute(part, ("gx", "gy"), pairs)
+
+    below_before = diagonal(last_rows, 1, 1)
+    below_after = diagonal(last_rows, -1, 1)
+    above_before = diagonal(first_rows, 1, -1)
+    above_after = diagonal(first_rows, -1, -1)
+    middle = jnp.concatenate([before, block, after], axis=1)
+    low = jnp.concatenate([below_before, below, below_after], axis=1)
+    high = jnp.concatenate([above_before, above, above_after], axis=1)
+    return jnp.concatenate([low, middle, high], axis=2)
 
 
 def halo_y(block, rows):
@@ -185,7 +216,7 @@
     )[None]
     packed = jnp.concatenate([state[0], old_flux, level_lanes], axis=0)
     reach_x, reach_y = size_x, NSUB + 1
-    ext1 = halo_y(halo_x(packed, reach_x), reach_y)
+    ext1 = halo_cross(packed, reach_y)
     onehot = (eco_prey[:, None] == lax.broadcasted_iota(jnp.int32, (species, species), 1)).astype(
         jnp.float32
     )

time: 78.4 us -> 94.5 us (1.21)
  the two profiles are of different devices: /device:TPU:100 before, /device:TPU:152 now
where the time goes in v10:
time: 94.5 us; the launch traced here: 93.5 us
  starting transfers between devices  51.6 us (55%)
  waiting for transfers between devices  20.5 us (22%)
  other arithmetic  12.7 us (13%)
  local copies, waits for them, and re-layouts  7.68 us (8%)
    ppermute x1, starting transfers between devices, body(): arrived = lax.ppermute(outgoing, 'half', [(0, 1), (1, 0)])  16.3 us
    ppermute x4, starting transfers between devices, diagonal(): return lax.ppermute(part, ('gx', 'gy'), pairs)  13.5 us
    ppermute x1, waiting for transfers between devices, halo_x(): before = lax.ppermute(block[:, block.shape[1] - cells:], 'gx', up)  8.77 us
    mul x5, other arithmetic, ocean_substep_channels(): return wet_mask * (centre + DT * (NU * spread - advect + forcing))  5.59 us
    ppermute x1, starting transfers between devices, halo_cross(): before = lax.ppermute(block, 'gx', up)  5.49 us
    ppermute x1, starting transfers between devices, halo_x(): before = lax.ppermute(block[:, block.shape[1] - cells:], 'gx', up)  5.32 us
    ppermute x1, waiting for transfers between devices, halo_x(): after = lax.ppermute(block[:, :cells], 'gx', down)  5.22 us
    ppermute x4, waiting for transfers between devices, diagonal(): return lax.ppermute(part, ('gx', 'gy'), pairs)  4.44 us
  transfers between devices with their start and end apart: 13, of which 5 were waited for; matrix products, arithmetic and copies ran while one was open for 1% of the time, Pallas kernels for 0%

profile of v10, /device:TPU:152, one launch (start us, length us, event | category | flops | bytes accessed | tf_op | source)
XLA Modules:
  0.0 93.5 jit_solution(16365489176928877785)
XLA Ops:
  0.0 0.7 fusion.61
  0.8 0.1 copy.24
  0.8 1.0 %pad_maximum_fusion.21 = f32[23,2,16,128]{3,2,1,0:T(8,128)S(1)} fusion(f32[1,2,16,128]{3,2,1,0:T(8,128)S(1)} %copy.24, f32[2,2,16,128]{3,2,1,0:T(8,128)} %param.13, f32[20,2,16,128]{3,2,1,0:T(8,128)} %bitcast.118), kind=kLoop, calls=%fused_computation.166 | loop fusion | flops 188416 | bytes 753664 | tf_op jit(solution)/shard_map/concatenate | solution.py:217
  1.9 1.9 %collective-permute-start.2 = (f32[23,2,5,128]{3,2,1,0:T(8,128)S(1)}, f32[23,2,5,128]{3,2,1,0:T(8,128)S(1)}, u32[]{:S(2)}, u32[]{:S(2)}) collective-permute-start(f32[23,2,5,128]{3,2,1,0:T(8,128)S(1)} %get-tuple-element.226), channel_id=1, source_target_pairs={{32,1},{33,2},{34,3},{35,4},{36,5},{37,6},{38,7},{39,8},{40,9},{41... | collective-permute-start | bytes 353288 | tf_op jit(solution)/shard_map/ppermute | solution.py:60
  3.8 2.6 %collective-permute-start.1 = (f32[23,2,5,128]{3,2,1,0:T(8,128)S(1)}, f32[23,2,5,128]{3,2,1,0:T(8,128)S(1)}, u32[]{:S(2)}, u32[]{:S(2)}) collective-permute-start(f32[23,2,5,128]{3,2,1,0:T(8,128)S(1)} %get-tuple-element.226), channel_id=1, source_target_pairs={{0,1},{1,2},{2,3},{3,4},{4,5},{5,6},{6,7},{7,8},{8,9},{9,10},{10,1... | collective-permute-start | bytes 353288 | tf_op jit(solution)/shard_map/ppermute | solution.py:50
  6.4 4.8 %collective-permute-start = (f32[23,2,5,128]{3,2,1,0:T(8,128)S(1)}, f32[23,2,5,128]{3,2,1,0:T(8,128)S(1)}, u32[]{:S(2)}, u32[]{:S(2)}) collective-permute-start(f32[23,2,5,128]{3,2,1,0:T(8,128)S(1)} %get-tuple-element.226), channel_id=1, source_target_pairs={{0,33},{1,34},{2,35},{3,36},{4,37},{5,38},{6,39},{7,40},{8,41},{9,... | collective-permute-start | bytes 353288 | tf_op jit(solution)/shard_map/ppermute | solution.py:60
  11.3 1.9 %collective-permute-start.4 = (f32[23,2,16,128]{3,2,1,0:T(8,128)S(1)}, f32[23,2,16,128]{3,2,1,0:T(8,128)S(1)}, u32[]{:S(2)}, u32[]{:S(2)}) collective-permute-start(f32[23,2,16,128]{3,2,1,0:T(8,128)S(1)} %pad_maximum_fusion.21), channel_id=1, source_target_pairs={{32,0},{64,32},{96,64},{128,96},{160,128},{192,160},{224,192},{256... | collective-permute-start | bytes 1130504 | tf_op jit(solution)/shard_map/ppermute | solution.py:46
  13.2 5.5 %collective-permute-start.3 = (f32[23,2,16,128]{3,2,1,0:T(8,128)S(1)}, f32[23,2,16,128]{3,2,1,0:T(8,128)S(1)}, u32[]{:S(2)}, u32[]{:S(2)}) collective-permute-start(f32[23,2,16,128]{3,2,1,0:T(8,128)S(1)} %pad_maximum_fusion.21), channel_id=1, source_target_pairs={{0,32},{32,64},{64,96},{96,128},{128,160},{160,192},{192,224},{224... | collective-permute-start | bytes 1130504 | tf_op jit(solution)/shard_map/ppermute | solution.py:45
  18.7 1.9 %collective-permute-start.7 = (f32[23,2,5,128]{3,2,1,0:T(8,128)S(1)}, f32[23,2,5,128]{3,2,1,0:T(8,128)S(1)}, u32[]{:S(2)}, u32[]{:S(2)}) collective-permute-start(f32[23,2,5,128]{3,2,1,0:T(8,128)S(1)} %get-tuple-element.227), channel_id=1, source_target_pairs={{33,0},{34,1},{35,2},{36,3},{37,4},{38,5},{39,6},{40,7},{41,8},{42... | collective-permute-start | bytes 353288 | tf_op jit(solution)/shard_map/ppermute | solution.py:60
  20.6 3.2 %collective-permute-start.6 = (f32[23,2,5,128]{3,2,1,0:T(8,128)S(1)}, f32[23,2,5,128]{3,2,1,0:T(8,128)S(1)}, u32[]{:S(2)}, u32[]{:S(2)}) collective-permute-start(f32[23,2,5,128]{3,2,1,0:T(8,128)S(1)} %get-tuple-element.227), channel_id=1, source_target_pairs={{1,0},{2,1},{3,2},{4,3},{5,4},{6,5},{7,6},{8,7},{9,8},{10,9},{11,1... | collective-permute-start | bytes 353288 | tf_op jit(solution)/shard_map/ppermute | solution.py:51
  23.9 4.8 %collective-permute-start.5 = (f32[23,2,5,128]{3,2,1,0:T(8,128)S(1)}, f32[23,2,5,128]{3,2,1,0:T(8,128)S(1)}, u32[]{:S(2)}, u32[]{:S(2)}) collective-permute-start(f32[23,2,5,128]{3,2,1,0:T(8,128)S(1)} %get-tuple-element.227), channel_id=1, source_target_pairs={{1,32},{2,33},{3,34},{4,35},{5,36},{6,37},{7,38},{8,39},{9,40},{10... | collective-permute-start | bytes 353288 | tf_op jit(solution)/shard_map/ppermute | solution.py:60
  28.7 0.1 fusion.60
  28.8 1.6 %collective-permute-done.7 = f32[23,2,5,128]{3,2,1,0:T(8,128)S(1)} collective-permute-done((f32[23,2,5,128]{3,2,1,0:T(8,128)S(1)}, f32[23,2,5,128]{3,2,1,0:T(8,128)S(1)}, u32[]{:S(2)}, u32[]{:S(2)}) %collective-permute-start.7) | collective-permute-done | bytes 117792 | tf_op jit(solution)/shard_map/ppermute | solution.py:60
  30.4 2.8 %collective-permute-done.5 = f32[23,2,5,128]{3,2,1,0:T(8,128)S(1)} collective-permute-done((f32[23,2,5,128]{3,2,1,0:T(8,128)S(1)}, f32[23,2,5,128]{3,2,1,0:T(8,128)S(1)}, u32[]{:S(2)}, u32[]{:S(2)}) %collective-permute-start.5) | collective-permute-done | bytes 117792 | tf_op jit(solution)/shard_map/ppermute | solution.py:60
  33.3 0.1 fusion.62
  33.4 0.1 copy.25
  33.5 0.4 copy-done.12
  33.9 2.0 %maximum_maximum_fusion = f32[23,6,26,128]{3,2,1,0:T(8,128)S(1)} fusion(f32[23,2,5,128]{3,2,1,0:T(8,128)} %copy-done.8, f32[23,2,5,128]{3,2,1,0:T(8,128)} %copy-done.10, f32[23,2,5,128]{3,2,1,0:T(8,128)} %copy-done.12, f32[23,2,16,128]{3,2,1,0:T(8,128)S(1)} %collective-permute-done.4, f32[1,2,16,128]{3,2,1,0:T(8,128)} %copy-done.16, ...), kind=kLoop, calls=%fused_computation.163 | loop fusion | flops 4592640 | bytes 3674112 | tf_op jit(solution)/shard_map/concatenate | solution.py:69
  36.0 1.3 %copy-done = f32[23,6,26,128]{3,2,1,0:T(8,128)} copy-done((f32[23,6,26,128]{3,2,1,0:T(8,128)}, f32[23,6,26,128]{3,2,1,0:T(8,128)S(1)}, u32[]{:S(2)}) %copy-start) | copy-done | bytes 1837080
  37.3 0.7 compare_convert_fusion.1
  38.1 0.2 compare_convert_fusion
  38.3 0.7 maximum_maximum_fusion.1
  39.1 3.7 %conditional.3 = (f32[20,2,22,128]{3,2,1,0:T(8,128)S(1)}, f32[2,2,16,128]{3,2,1,0:T(8,128)S(1)}) conditional(s32[]{:T(128)} %convert_element_type.44, (f32[6,26,128]{2,1,0:T(8,128)}, f32[20,6,26,128]{3,2,1,0:T(8,128)S(1)}, f32[2,6,26,128]{3,2,1,0:T(8,128)}, f32[19]{0:T(128)S(1)}, f32[19,19]{1,0:T(8,128)S(1)}) %tuple.118, ...), branch_computations={%region_1.2_spmd, %region_2.5_spmd} | conditional | flops 85125120 | bytes 40452264 | solution.py:267
  39.1 0.1 pad.47.clone
  39.2 0.1 pad.46.clone
  39.3 0.2 slice_multiply_fusion
  39.5 0.2 fusion.66
  39.7 0.2 fusion.65
  39.9 0.8 fusion.12
  40.7 0.2 fusion.64
  41.0 0.2 fusion.63
  41.1 1.5 %fusion.15 = f32[5,2,2,4,24,128]{5,4,3,2,1,0:T(8,128)S(1)} fusion(f32[1,2,2,4,24,128]{5,4,3,2,1,0:T(8,128)S(1)} %get-tuple-element.151, f32[1,2,2,4,24,128]{5,4,3,2,1,0:T(8,128)S(1)} %get-tuple-element.150, f32[5,2,1,4,24,128]{5,4,3,2,1,0:T(8,128)S(1)} %get-tuple-element.160, f32[5,2,1,4,24,128]{5,4,3,2,1,0:T(8,128)S(1)} %get-tuple-element.159, ...), kind=kLoop, calls=%fused_computation.43 | loop fusion | flops 11550720 | bytes 11599912 | tf_op jit(solution)/shard_map/cond/branch_1_fun/mul | solution.py:166
  42.7 5.3 %collective-permute-start.8 = (f32[20,2,22,128]{3,2,1,0:T(8,128)S(1)}, f32[20,2,22,128]{3,2,1,0:T(8,128)}, u32[]{:S(2)}, u32[]{:S(2)}) collective-permute-start(f32[20,2,22,128]{3,2,1,0:T(8,128)S(1)} %get-tuple-element.92), channel_id=1, source_target_pairs={{0,32},{32,64},{64,96},{96,128},{128,160},{160,192},{192,224},{224... | collective-permute-start | bytes 1351688 | tf_op jit(solution)/shard_map/ppermute | solution.py:27
  48.1 1.9 %collective-permute-start.9 = (f32[20,2,22,128]{3,2,1,0:T(8,128)S(1)}, f32[20,2,22,128]{3,2,1,0:T(8,128)S(1)}, u32[]{:S(2)}, u32[]{:S(2)}) collective-permute-start(f32[20,2,22,128]{3,2,1,0:T(8,128)S(1)} %get-tuple-element.92), channel_id=1, source_target_pairs={{32,0},{64,32},{96,64},{128,96},{160,128},{192,160},{224,192},{256... | collective-permute-start | bytes 1351688 | tf_op jit(solution)/shard_map/ppermute | solution.py:28
  50.0 0.1 fusion.59
  50.1 8.8 %collective-permute-done.8 = f32[20,2,22,128]{3,2,1,0:T(8,128)} collective-permute-done((f32[20,2,22,128]{3,2,1,0:T(8,128)S(1)}, f32[20,2,22,128]{3,2,1,0:T(8,128)}, u32[]{:S(2)}, u32[]{:S(2)}) %collective-permute-start.8) | collective-permute-done | bytes 450592 | tf_op jit(solution)/shard_map/ppermute | solution.py:27
  58.9 1.1 %constant_dynamic-update-slice_fusion.4 = f32[20,6,22,128]{3,2,1,0:T(8,128)S(1)} fusion(f32[20,2,22,128]{3,2,1,0:T(8,128)} %collective-permute-done.8), kind=kLoop, calls=%fused_computation.179 | loop fusion | bytes 942080
  60.0 5.2 %collective-permute-done.9 = f32[20,2,22,128]{3,2,1,0:T(8,128)S(1)} collective-permute-done((f32[20,2,22,128]{3,2,1,0:T(8,128)S(1)}, f32[20,2,22,128]{3,2,1,0:T(8,128)S(1)}, u32[]{:S(2)}, u32[]{:S(2)}) %collective-permute-start.9) | collective-permute-done | bytes 450592 | tf_op jit(solution)/shard_map/ppermute | solution.py:28
  65.3 5.4 %conditional.4 = (f32[20,2,18,128]{3,0,2,1:T(8,128)S(1)}, f32[20,4,18,128]{3,2,1,0:T(8,128)S(1)}, f32[2,2,16,128]{3,2,1,0:T(8,128)S(1)}) conditional(s32[]{:T(128)} %convert_element_type.44, (f32[6,26,128]{2,1,0:T(8,128)}, f32[20,6,22,128]{3,2,1,0:T(8,128)S(1)}, f32[2,6,26,128]{3,2,1,0:T(8,128)}, f32[19]{0:T(128)S(1)}, f32[19,19]{1,0:T(8,128)S(1)}, ...), branch_computations={%region_6.7_spmd, %region_7.10_spmd} | conditional | flops 76587008 | bytes 51945652 | solution.py:298
  65.5 0.1 pad.71.clone
  65.6 0.1 pad.70.clone
  65.7 0.1 slice_bitcast_fusion.15
  65.8 0.2 slice.420
  65.9 0.4 pad_slice_fusion.13
  66.4 0.3 pad_slice_fusion.15
  66.7 1.1 %fusion.47 = f32[5,2,2,6,20,128]{5,4,3,2,1,0:T(8,128)S(1)} fusion(f32[1,2,2,6,20,128]{5,4,3,2,1,0:T(8,128)S(1)} %get-tuple-element.193, f32[1,2,2,6,20,128]{5,4,3,2,1,0:T(8,128)S(1)} %get-tuple-element.192, f32[5,2,1,6,20,128]{5,4,3,2,1,0:T(8,128)S(1)} %get-tuple-element.203, f32[5,2,1,6,20,128]{5,4,3,2,1,0:T(8,128)S(1)} %get-tuple-element.202, ...), kind=kLoop, calls=%fused_computation.108 | loop fusion | flops 7065600 | bytes 8601640 | tf_op jit(solution)/shard_map/cond/branch_1_fun/mul | solution.py:166
  67.8 0.1 slice_bitcast_fusion.13
  67.9 0.3 fusion.68
  68.1 0.2 fusion.67
  68.4 2.1 %fusion.50 = f32[5,2,2,6,20,128]{5,4,3,2,1,0:T(8,128)S(1)} fusion(f32[1,2,2,6,20,128]{5,4,3,2,1,0:T(8,128)S(1)} %get-tuple-element.181, f32[1,2,2,6,20,128]{5,4,3,2,1,0:T(8,128)S(1)} %get-tuple-element.180, f32[5,2,1,6,20,128]{5,4,3,2,1,0:T(8,128)S(1)} %get-tuple-element.190, f32[5,2,1,6,20,128]{5,4,3,2,1,0:T(8,128)S(1)} %get-tuple-element.189, ...), kind=kLoop, calls=%fused_computation.116 | loop fusion | flops 14131200 | bytes 14499880 | tf_op jit(solution)/shard_map/cond/branch_1_fun/mul | solution.py:166
  70.5 0.1 slice.433
  70.7 0.6 copy-done.19
  71.3 0.7 collective-permute-start.10
  72.0 0.7 collective-permute-start.11
  72.7 16.3 %collective-permute-start.12 = (f32[2,2,16,128]{3,2,1,0:T(8,128)}, f32[2,2,16,128]{3,2,1,0:T(8,128)S(1)}, u32[]{:S(2)}, u32[]{:S(2)}) collective-permute-start(f32[2,2,16,128]{3,2,1,0:T(8,128)} %copy-done.19), channel_id=1, source_target_pairs={{0,512},{512,0},{1,513},{513,1},{2,514},{514,2},{3,515},{515,3},{4... | collective-permute-start | bytes 98312 | tf_op jit(solution)/shard_map/ppermute | solution.py:300
  89.0 2.1 %collective-permute-done.12 = f32[2,2,16,128]{3,2,1,0:T(8,128)S(1)} collective-permute-done((f32[2,2,16,128]{3,2,1,0:T(8,128)}, f32[2,2,16,128]{3,2,1,0:T(8,128)S(1)}, u32[]{:S(2)}, u32[]{:S(2)}) %collective-permute-start.12) | collective-permute-done | bytes 32800 | tf_op jit(solution)/shard_map/ppermute | solution.py:300
  91.1 0.1 pad_maximum_fusion.20
  91.2 1.6 %conditional.5 = (f32[1,20,2,16,128]{4,3,2,1,0:T(8,128)S(1)}) conditional(s32[]{:T(128)} %convert_element_type.44, (f32[2,16,128]{2,1,0:T(8,128)S(1)}, f32[20,2,18,128]{3,0,2,1:T(8,128)S(1)}, f32[20,4,18,128]{3,0,2,1:T(8,128)S(1)}, f32[2,2,16,128]{3,2,1,0:T(8,128)S(1)}, f32[19]{0:T(128)S(1)}, /*index=5*/f32[19,19]{1,0:T(8,128)S(1)}) %tuple.120, ...), branch_computations={%region_10.11_spmd, %region_11.12_spmd} | conditional | flops 19365888 | bytes 17584136 | solution.py:312
  91.2 0.1 fusion.71
  91.4 0.2 fusion.73
  91.6 0.2 fusion.72
  91.8 0.7 add_add_fusion
  92.5 0.2 fusion.55
  92.8 0.7 copy-done.18
  (82 shorter events, 0.7 us)
Async XLA Ops:
  0.0 33.2 %copy-start.14 = (f32[2,2,16,128]{3,2,1,0:T(8,128)S(1)}, f32[2,2,16,128]{3,2,1,0:T(8,128)}, u32[]{:S(2)}) copy-start(f32[2,2,16,128]{3,2,1,0:T(8,128)} %param.13) | copy-start | bytes 98308
  0.0 33.3 %copy-start.1 = (f32[1,20,2,16,128]{4,3,2,1,0:T(8,128)S(1)}, f32[1,20,2,16,128]{4,3,2,1,0:T(8,128)}, u32[]{:S(2)}) copy-start(f32[1,20,2,16,128]{4,3,2,1,0:T(8,128)} %param.11) | copy-start | bytes 983044
  0.0 28.7 %copy-start.22 = (s32[19]{0:T(128)S(1)}, s32[19]{0:T(128)}, u32[]{:S(2)}) copy-start(s32[19]{0:T(128)} %param.14) | copy-start | bytes 232
  0.8 32.5 %copy-start.16 = (f32[1,2,16,128]{3,2,1,0:T(8,128)}, f32[1,2,16,128]{3,2,1,0:T(8,128)S(1)}, u32[]{:S(2)}) copy-start(f32[1,2,16,128]{3,2,1,0:T(8,128)S(1)} %copy.24) | copy-start | bytes 49156
  1.9 16.8 %collective-permute-start.2 = (f32[23,2,5,128]{3,2,1,0:T(8,128)S(1)}, f32[23,2,5,128]{3,2,1,0:T(8,128)S(1)}, u32[]{:S(2)}, u32[]{:S(2)}) collective-permute-start(f32[23,2,5,128]{3,2,1,0:T(8,128)S(1)} %get-tuple-element.226), channel_id=1, source_target_pairs={{32,1},{33,2},{34,3},{35,4},{36,5},{37,6},{38,7},{39,8},{40,9},{41... | collective-permute-start | bytes 353288 | tf_op jit(solution)/shard_map/ppermute | solution.py:60
  3.8 16.8 %collective-permute-start.1 = (f32[23,2,5,128]{3,2,1,0:T(8,128)S(1)}, f32[23,2,5,128]{3,2,1,0:T(8,128)S(1)}, u32[]{:S(2)}, u32[]{:S(2)}) collective-permute-start(f32[23,2,5,128]{3,2,1,0:T(8,128)S(1)} %get-tuple-element.226), channel_id=1, source_target_pairs={{0,1},{1,2},{2,3},{3,4},{4,5},{5,6},{6,7},{7,8},{8,9},{9,10},{10,1... | collective-permute-start | bytes 353288 | tf_op jit(solution)/shard_map/ppermute | solution.py:50
  6.4 17.4 %collective-permute-start = (f32[23,2,5,128]{3,2,1,0:T(8,128)S(1)}, f32[23,2,5,128]{3,2,1,0:T(8,128)S(1)}, u32[]{:S(2)}, u32[]{:S(2)}) collective-permute-start(f32[23,2,5,128]{3,2,1,0:T(8,128)S(1)} %get-tuple-element.226), channel_id=1, source_target_pairs={{0,33},{1,34},{2,35},{3,36},{4,37},{5,38},{6,39},{7,40},{8,41},{9,... | collective-permute-start | bytes 353288 | tf_op jit(solution)/shard_map/ppermute | solution.py:60
  11.3 22.0 %collective-permute-start.4 = (f32[23,2,16,128]{3,2,1,0:T(8,128)S(1)}, f32[23,2,16,128]{3,2,1,0:T(8,128)S(1)}, u32[]{:S(2)}, u32[]{:S(2)}) collective-permute-start(f32[23,2,16,128]{3,2,1,0:T(8,128)S(1)} %pad_maximum_fusion.21), channel_id=1, source_target_pairs={{32,0},{64,32},{96,64},{128,96},{160,128},{192,160},{224,192},{256... | collective-permute-start | bytes 1130504 | tf_op jit(solution)/shard_map/ppermute | solution.py:46
  13.2 20.1 %collective-permute-start.3 = (f32[23,2,16,128]{3,2,1,0:T(8,128)S(1)}, f32[23,2,16,128]{3,2,1,0:T(8,128)S(1)}, u32[]{:S(2)}, u32[]{:S(2)}) collective-permute-start(f32[23,2,16,128]{3,2,1,0:T(8,128)S(1)} %pad_maximum_fusion.21), channel_id=1, source_target_pairs={{0,32},{32,64},{64,96},{96,128},{128,160},{160,192},{192,224},{224... | collective-permute-start | bytes 1130504 | tf_op jit(solution)/shard_map/ppermute | solution.py:45
  18.7 11.7 %collective-permute-start.7 = (f32[23,2,5,128]{3,2,1,0:T(8,128)S(1)}, f32[23,2,5,128]{3,2,1,0:T(8,128)S(1)}, u32[]{:S(2)}, u32[]{:S(2)}) collective-permute-start(f32[23,2,5,128]{3,2,1,0:T(8,128)S(1)} %get-tuple-element.227), channel_id=1, source_target_pairs={{33,0},{34,1},{35,2},{36,3},{37,4},{38,5},{39,6},{40,7},{41,8},{42... | collective-permute-start | bytes 353288 | tf_op jit(solution)/shard_map/ppermute | solution.py:60
  20.6 12.9 %copy-start.4 = (f32[23,2,5,128]{3,2,1,0:T(8,128)}, f32[23,2,5,128]{3,2,1,0:T(8,128)S(1)}, u32[]{:S(2)}) copy-start(f32[23,2,5,128]{3,2,1,0:T(8,128)S(1)} %collective-permute-done.1) | copy-start | bytes 353284
  20.6 9.8 %collective-permute-start.6 = (f32[23,2,5,128]{3,2,1,0:T(8,128)S(1)}, f32[23,2,5,128]{3,2,1,0:T(8,128)S(1)}, u32[]{:S(2)}, u32[]{:S(2)}) collective-permute-start(f32[23,2,5,128]{3,2,1,0:T(8,128)S(1)} %get-tuple-element.227), channel_id=1, source_target_pairs={{1,0},{2,1},{3,2},{4,3},{5,4},{6,5},{7,6},{8,7},{9,8},{10,9},{11,1... | collective-permute-start | bytes 353288 | tf_op jit(solution)/shard_map/ppermute | solution.py:51
  23.8 9.7 %copy-start.6 = (f32[23,2,5,128]{3,2,1,0:T(8,128)}, f32[23,2,5,128]{3,2,1,0:T(8,128)S(1)}, u32[]{:S(2)}) copy-start(f32[23,2,5,128]{3,2,1,0:T(8,128)S(1)} %collective-permute-done) | copy-start | bytes 353284
  23.9 9.4 %collective-permute-start.5 = (f32[23,2,5,128]{3,2,1,0:T(8,128)S(1)}, f32[23,2,5,128]{3,2,1,0:T(8,128)S(1)}, u32[]{:S(2)}, u32[]{:S(2)}) collective-permute-start(f32[23,2,5,128]{3,2,1,0:T(8,128)S(1)} %get-tuple-element.227), channel_id=1, source_target_pairs={{1,32},{2,33},{3,34},{4,35},{5,36},{6,37},{7,38},{8,39},{9,40},{10... | collective-permute-start | bytes 353288 | tf_op jit(solution)/shard_map/ppermute | solution.py:60
  30.4 3.1 %copy-start.8 = (f32[23,2,5,128]{3,2,1,0:T(8,128)}, f32[23,2,5,128]{3,2,1,0:T(8,128)S(1)}, u32[]{:S(2)}) copy-start(f32[23,2,5,128]{3,2,1,0:T(8,128)S(1)} %collective-permute-done.7) | copy-start | bytes 353284
  30.4 3.1 %copy-start.10 = (f32[23,2,5,128]{3,2,1,0:T(8,128)}, f32[23,2,5,128]{3,2,1,0:T(8,128)S(1)}, u32[]{:S(2)}) copy-start(f32[23,2,5,128]{3,2,1,0:T(8,128)S(1)} %collective-permute-done.6) | copy-start | bytes 353284
  33.2 0.7 copy-start.12
  35.9 1.4 %copy-start = (f32[23,6,26,128]{3,2,1,0:T(8,128)}, f32[23,6,26,128]{3,2,1,0:T(8,128)S(1)}, u32[]{:S(2)}) copy-start(f32[23,6,26,128]{3,2,1,0:T(8,128)S(1)} %maximum_maximum_fusion) | copy-start | bytes 5511172
  36.0 2.3 %copy-start.5 = (f32[23,2,5,128]{3,2,1,0:T(8,128)S(1)}, f32[23,2,5,128]{3,2,1,0:T(8,128)}, u32[]{:S(2)}) copy-start(f32[23,2,5,128]{3,2,1,0:T(8,128)} %copy-done.4) | copy-start | bytes 353284
  36.0 2.3 %copy-start.7 = (f32[23,2,5,128]{3,2,1,0:T(8,128)S(1)}, f32[23,2,5,128]{3,2,1,0:T(8,128)}, u32[]{:S(2)}) copy-start(f32[23,2,5,128]{3,2,1,0:T(8,128)} %copy-done.6) | copy-start | bytes 353284
  36.0 2.3 %copy-start.9 = (f32[23,2,5,128]{3,2,1,0:T(8,128)S(1)}, f32[23,2,5,128]{3,2,1,0:T(8,128)}, u32[]{:S(2)}) copy-start(f32[23,2,5,128]{3,2,1,0:T(8,128)} %copy-done.8) | copy-start | bytes 353284
  36.0 2.3 %copy-start.11 = (f32[23,2,5,128]{3,2,1,0:T(8,128)S(1)}, f32[23,2,5,128]{3,2,1,0:T(8,128)}, u32[]{:S(2)}) copy-start(f32[23,2,5,128]{3,2,1,0:T(8,128)} %copy-done.10) | copy-start | bytes 353284
  36.0 2.3 %copy-start.13 = (f32[23,2,5,128]{3,2,1,0:T(8,128)S(1)}, f32[23,2,5,128]{3,2,1,0:T(8,128)}, u32[]{:S(2)}) copy-start(f32[23,2,5,128]{3,2,1,0:T(8,128)} %copy-done.12) | copy-start | bytes 353284
  36.0 2.3 %copy-start.15 = (f32[2,2,16,128]{3,2,1,0:T(8,128)S(1)}, f32[2,2,16,128]{3,2,1,0:T(8,128)}, u32[]{:S(2)}) copy-start(f32[2,2,16,128]{3,2,1,0:T(8,128)} %param.13) | copy-start | bytes 98308
  36.0 2.3 %copy-start.17 = (f32[1,2,16,128]{3,2,1,0:T(8,128)S(1)}, f32[1,2,16,128]{3,2,1,0:T(8,128)}, u32[]{:S(2)}) copy-start(f32[1,2,16,128]{3,2,1,0:T(8,128)} %copy-done.16) | copy-start | bytes 49156
  37.3 1.7 %slice-start = ((f32[23,6,26,128]{3,2,1,0:T(8,128)}), f32[20,6,26,128]{3,2,1,0:T(8,128)S(1)}, s32[]{:S(2)}) async-start(f32[23,6,26,128]{3,2,1,0:T(8,128)} %copy-done), calls=%async_computation | async-start | bytes 3932160 | tf_op jit(solution)/shard_map/slice | solution.py:228
  37.3 1.7 %copy-start.21 = (f32[19]{0:T(128)S(1)}, f32[19]{0:T(128)}, u32[]{:S(2)}) copy-start(f32[19]{0:T(128)} %param.15) | copy-start | bytes 232
  38.2 0.8 copy-start.2
  39.1 9.0 %copy-start.20 = (s32[4,2,16]{2,1,0:T(2,128)S(1)}, s32[4,2,16]{2,1,0:T(2,128)}, u32[]{:S(2)}) copy-start(s32[4,2,16]{2,1,0:T(2,128)} %param.12) | copy-start | bytes 1540
  42.7 16.1 %collective-permute-start.8 = (f32[20,2,22,128]{3,2,1,0:T(8,128)S(1)}, f32[20,2,22,128]{3,2,1,0:T(8,128)}, u32[]{:S(2)}, u32[]{:S(2)}) collective-permute-start(f32[20,2,22,128]{3,2,1,0:T(8,128)S(1)} %get-tuple-element.92), channel_id=1, source_target_pairs={{0,32},{32,64},{64,96},{96,128},{128,160},{160,192},{192,224},{224... | collective-permute-start | bytes 1351688 | tf_op jit(solution)/shard_map/ppermute | solution.py:27
  48.1 17.1 %collective-permute-start.9 = (f32[20,2,22,128]{3,2,1,0:T(8,128)S(1)}, f32[20,2,22,128]{3,2,1,0:T(8,128)S(1)}, u32[]{:S(2)}, u32[]{:S(2)}) collective-permute-start(f32[20,2,22,128]{3,2,1,0:T(8,128)S(1)} %get-tuple-element.92), channel_id=1, source_target_pairs={{32,0},{64,32},{96,64},{128,96},{160,128},{192,160},{224,192},{256... | collective-permute-start | bytes 1351688 | tf_op jit(solution)/shard_map/ppermute | solution.py:28
  50.1 15.1 %copy-start.3 = (f32[2,2,6,26,128]{4,3,2,1,0:T(8,128)S(1)}, f32[2,2,6,26,128]{4,3,2,1,0:T(8,128)}, u32[]{:S(2)}) copy-start(f32[2,2,6,26,128]{4,3,2,1,0:T(8,128)} %copy-done.2) | copy-start | bytes 958468
  70.7 0.6 copy-start.19
  71.3 19.8 %collective-permute-start.10 = (f32[20,1,18,128]{3,0,2,1:T(8,128)S(1)}, f32[20,1,18,128]{3,0,2,1:T(8,128)S(1)}, u32[]{:S(2)}, u32[]{:S(2)}) collective-permute-start(f32[20,1,18,128]{3,0,2,1:T(8,128)S(1)} %get-tuple-element.224), channel_id=1, source_target_pairs={{512,544},{544,576},{576,608},{608,640},{640,672},{672,704},{704,7... | collective-permute-start | bytes 552968 | tf_op jit(solution)/shard_map/ppermute | solution.py:36
  72.0 19.1 %collective-permute-start.11 = (f32[20,1,18,128]{3,0,2,1:T(8,128)S(1)}, f32[20,1,18,128]{3,0,2,1:T(8,128)S(1)}, u32[]{:S(2)}, u32[]{:S(2)}) collective-permute-start(f32[20,1,18,128]{3,0,2,1:T(8,128)S(1)} %get-tuple-element.225), channel_id=1, source_target_pairs={{544,512},{576,544},{608,576},{640,608},{672,640},{704,672},{736,7... | collective-permute-start | bytes 552968 | tf_op jit(solution)/shard_map/ppermute | solution.py:37
  72.7 18.4 %collective-permute-start.12 = (f32[2,2,16,128]{3,2,1,0:T(8,128)}, f32[2,2,16,128]{3,2,1,0:T(8,128)S(1)}, u32[]{:S(2)}, u32[]{:S(2)}) collective-permute-start(f32[2,2,16,128]{3,2,1,0:T(8,128)} %copy-done.19), channel_id=1, source_target_pairs={{0,512},{512,0},{1,513},{513,1},{2,514},{514,2},{3,515},{515,3},{4... | collective-permute-start | bytes 98312 | tf_op jit(solution)/shard_map/ppermute | solution.py:300
  92.8 0.7 copy-start.18

commit v11 on v8

--- a/solution.py
+++ b/solution.py
@@ -152,7 +152,7 @@
     )
     spread = to_east + to_west + to_north + to_south - 4.0 * centre
     living = centre[:species]
-    prey_values = jnp.einsum("ts,sxyk->txyk", onehot, living, precision=lax.Precision.HIGHEST)
+    prey_values = jnp.einsum("ts,sxyk->txyk", onehot, living, precision=lax.Precision.HIGH)
     growth = eco_rate[:, None, None, None] * living * jnp.tanh(prey_values) - MORTALITY * living
     reaction = jnp.concatenate([growth, jnp.zeros_like(centre[species:])], axis=0)
     return wet_mask * (centre + DT * (NU * spread - advect + reaction))

time: 78.4 us -> 77.1 us (0.983)
  matrix products: 4.28 us -> 2.88 us
    dot_general x5, matrix products: 4.1 us -> 2.69 us  [tracer_substep(): jnp.einsum('ts,sxyk->txyk', onehot, living, precision=lax.Precision.HIGH)]
where the time goes in v11:
time: 77.1 us; the launch traced here: 76.6 us
  waiting for transfers between devices  35.2 us (46%)
  starting transfers between devices  29.5 us (38%)
  local copies, waits for them, and re-layouts  4.39 us (6%)
  other arithmetic  4 us (5%)
  matrix products  2.88 us (4%)
    ppermute x2, waiting for transfers between devices, halo_x(): after = lax.ppermute(block[:, :cells], 'gx', down)  12.9 us
    ppermute x2, waiting for transfers between devices, halo_x(): before = lax.ppermute(block[:, block.shape[1] - cells:], 'gx', up)  9.89 us
    ppermute x2, starting transfers between devices, halo_x(): before = lax.ppermute(block[:, block.shape[1] - cells:], 'gx', up)  8.56 us
    ppermute x1, starting transfers between devices, halo_y(): above = lax.ppermute(block[:, :, :rows], 'gy', down)  5.75 us
    ppermute x1, starting transfers between devices, halo_x_tracer(): before = lax.ppermute(block[:, block.shape[1] - cells:], ('half', 'gx'), up)  5.59 us
    ppermute x1, waiting for transfers between devices, body(): arrived = lax.ppermute(outgoing, 'half', [(0, 1), (1, 0)])  5.38 us
    ppermute x2, starting transfers between devices, halo_x(): after = lax.ppermute(block[:, :cells], 'gx', down)  3.84 us
    unnamed x12, local copies, waits for them, and re-layouts  3.29 us
  transfers between devices with their start and end apart: 9, of which 8 were waited for; matrix products, arithmetic and copies ran while one was open for 0% of the time, Pallas kernels for 0%

profile of v11, /device:TPU:100, one launch (start us, length us, event | category | flops | bytes accessed | tf_op | source)
XLA Modules:
  0.0 76.6 jit_solution(8422378474780665592)
XLA Ops:
  0.0 0.7 fusion.61
  0.7 0.8 %copy.47 = f32[2,2,16,128]{3,0,2,1:T(2,128)S(1)} copy(f32[2,2,16,128]{3,2,1,0:T(8,128)} %param.13) | data formatting | bytes 65536 | tf_op args[2]
  1.5 0.1 copy.48
  1.6 1.2 %copy.62 = f32[1,20,2,16,128]{4,1,3,2,0:T(8,128)S(1)} copy(f32[1,20,2,16,128]{4,3,2,1,0:T(8,128)} %param.11) | data formatting | bytes 655360 | tf_op args[0]
  2.7 0.0 copy-start.3
  2.8 0.1 pad_maximum_fusion.22
  2.8 1.9 %collective-permute-start.1 = (f32[23,2,16,128]{3,0,2,1:T(8,128)S(1)}, f32[23,2,16,128]{3,0,2,1:T(8,128)S(1)}, u32[]{:S(2)}, u32[]{:S(2)}) collective-permute-start(f32[23,2,16,128]{3,0,2,1:T(8,128)S(1)} %pad_maximum_fusion.22), channel_id=1, source_target_pairs={{32,0},{64,32},{96,64},{128,96},{160,128},{192,160},{224,192},{256... | collective-permute-start | bytes 1130504 | tf_op jit(solution)/shard_map/ppermute | solution.py:28
  4.7 4.3 %collective-permute-start = (f32[23,2,16,128]{3,0,2,1:T(8,128)S(1)}, f32[23,2,16,128]{3,0,2,1:T(8,128)S(1)}, u32[]{:S(2)}, u32[]{:S(2)}) collective-permute-start(f32[23,2,16,128]{3,0,2,1:T(8,128)S(1)} %pad_maximum_fusion.22), channel_id=1, source_target_pairs={{0,32},{32,64},{64,96},{96,128},{128,160},{160,192},{192,224},{224... | collective-permute-start | bytes 1130504 | tf_op jit(solution)/shard_map/ppermute | solution.py:27
  9.0 7.2 %collective-permute-done.1 = f32[23,2,16,128]{3,0,2,1:T(8,128)S(1)} collective-permute-done((f32[23,2,16,128]{3,0,2,1:T(8,128)S(1)}, f32[23,2,16,128]{3,0,2,1:T(8,128)S(1)}, u32[]{:S(2)}, u32[]{:S(2)}) %collective-permute-start.1) | collective-permute-done | bytes 376864 | tf_op jit(solution)/shard_map/ppermute | solution.py:28
  16.2 1.3 %collective-permute-done = f32[23,2,16,128]{3,0,2,1:T(8,128)S(1)} collective-permute-done((f32[23,2,16,128]{3,0,2,1:T(8,128)S(1)}, f32[23,2,16,128]{3,0,2,1:T(8,128)S(1)}, u32[]{:S(2)}, u32[]{:S(2)}) %collective-permute-start) | collective-permute-done | bytes 376864 | tf_op jit(solution)/shard_map/ppermute | solution.py:27
  17.5 0.1 pad_maximum_fusion.27
  17.6 1.9 %collective-permute-start.2 = (f32[23,6,5,128]{3,0,2,1:T(8,128)S(1)}, f32[23,6,5,128]{3,0,2,1:T(8,128)S(1)}, u32[]{:S(2)}, u32[]{:S(2)}) collective-permute-start(f32[23,6,5,128]{3,0,2,1:T(8,128)S(1)} %get-tuple-element.258), channel_id=1, source_target_pairs={{0,1},{1,2},{2,3},{3,4},{4,5},{5,6},{6,7},{7,8},{8,9},{9,10},{10,1... | collective-permute-start | bytes 1059848 | tf_op jit(solution)/shard_map/ppermute | solution.py:43
  19.5 5.8 %collective-permute-start.3 = (f32[23,6,5,128]{3,0,2,1:T(8,128)S(1)}, f32[23,6,5,128]{3,0,2,1:T(8,128)S(1)}, u32[]{:S(2)}, u32[]{:S(2)}) collective-permute-start(f32[23,6,5,128]{3,0,2,1:T(8,128)S(1)} %get-tuple-element.259), channel_id=1, source_target_pairs={{1,0},{2,1},{3,2},{4,3},{5,4},{6,5},{7,6},{8,7},{9,8},{10,9},{11,1... | collective-permute-start | bytes 1059848 | tf_op jit(solution)/shard_map/ppermute | solution.py:44
  25.3 0.0 copy-done.3
  25.3 0.1 fusion.60
  25.3 3.3 %collective-permute-done.2 = f32[23,6,5,128]{3,0,2,1:T(8,128)S(1)} collective-permute-done((f32[23,6,5,128]{3,0,2,1:T(8,128)S(1)}, f32[23,6,5,128]{3,0,2,1:T(8,128)S(1)}, u32[]{:S(2)}, u32[]{:S(2)}) %collective-permute-start.2) | collective-permute-done | bytes 353312 | tf_op jit(solution)/shard_map/ppermute | solution.py:43
  28.6 1.7 %collective-permute-done.3 = f32[23,6,5,128]{3,0,2,1:T(8,128)S(1)} collective-permute-done((f32[23,6,5,128]{3,0,2,1:T(8,128)S(1)}, f32[23,6,5,128]{3,0,2,1:T(8,128)S(1)}, u32[]{:S(2)}, u32[]{:S(2)}) %collective-permute-start.3) | collective-permute-done | bytes 353312 | tf_op jit(solution)/shard_map/ppermute | solution.py:44
  30.3 0.1 pad_maximum_fusion.29
  30.4 0.1 copy.49
  30.5 0.1 compare_convert_fusion.1
  30.6 0.2 compare_convert_fusion
  30.8 0.1 pad_maximum_fusion.20
  30.9 0.0 copy-start.2
  31.0 0.1 pad_maximum_fusion.28
  31.1 0.5 copy-done.2
  31.6 0.0 copy-start.1
  31.6 2.7 %conditional.3 = (f32[20,2,22,128]{3,2,1,0:T(8,128)S(1)}, f32[2,2,16,128]{3,2,1,0:T(8,128)S(1)}) conditional(s32[]{:T(128)} %convert_element_type.44, (f32[6,26,128]{2,1,0:T(8,128)S(1)}, f32[20,6,26,128]{3,0,2,1:T(8,128)S(1)}, f32[2,6,26,128]{3,0,2,1:T(2,128)S(1)}, f32[19]{0:T(128)S(1)}, f32[19,19]{1,0:T(8,128)S(1)}) %tuple.126, ...), branch_computations={%region_1.2_spmd, %region_2.5_spmd} | conditional | flops 46310400 | bytes 43647144 | solution.py:236
  31.7 0.3 broadcast_multiply_fusion
  31.9 0.8 %fusion.2 = f32[19,4,24,128]{3,0,2,1:T(8,128)S(1)} fusion(f32[20,6,26,128]{3,0,2,1:T(8,128)S(1)} %broadcast_multiply_fusion, f32[19]{0:T(128)S(1)} %get-tuple-element.64, f32[19,19]{1,0:T(8,128)S(1)} %get-tuple-element.65), kind=kOutput, calls=%fused_computation.3 | convolution fusion | flops 27549696 | bytes 3305984 | tf_op jit(solution)/shard_map/cond/branch_0_fun/ts,sxyk->txyk/dot_general | solution.py:155
  32.8 0.6 add_multiply_fusion
  33.4 0.5 fusion.5
  33.9 0.3 add_multiply_fusion.1
  34.2 0.1 copy.43
  34.3 4.3 %collective-permute-start.4 = (f32[20,2,22,128]{3,2,1,0:T(8,128)S(1)}, f32[20,2,22,128]{3,2,1,0:T(8,128)S(1)}, u32[]{:S(2)}, u32[]{:S(2)}) collective-permute-start(f32[20,2,22,128]{3,2,1,0:T(8,128)S(1)} %get-tuple-element.92), channel_id=1, source_target_pairs={{0,32},{32,64},{64,96},{96,128},{128,160},{160,192},{192,224},{224... | collective-permute-start | bytes 1351688 | tf_op jit(solution)/shard_map/ppermute | solution.py:27
  38.6 0.0 copy-done.1
  38.7 1.9 %collective-permute-start.5 = (f32[20,2,22,128]{3,2,1,0:T(8,128)S(1)}, f32[20,2,22,128]{3,2,1,0:T(8,128)S(1)}, u32[]{:S(2)}, u32[]{:S(2)}) collective-permute-start(f32[20,2,22,128]{3,2,1,0:T(8,128)S(1)} %get-tuple-element.92), channel_id=1, source_target_pairs={{32,0},{64,32},{96,64},{128,96},{160,128},{192,160},{224,192},{256... | collective-permute-start | bytes 1351688 | tf_op jit(solution)/shard_map/ppermute | solution.py:28
  40.6 0.1 fusion.59
  40.7 8.6 %collective-permute-done.4 = f32[20,2,22,128]{3,2,1,0:T(8,128)S(1)} collective-permute-done((f32[20,2,22,128]{3,2,1,0:T(8,128)S(1)}, f32[20,2,22,128]{3,2,1,0:T(8,128)S(1)}, u32[]{:S(2)}, u32[]{:S(2)}) %collective-permute-start.4) | collective-permute-done | bytes 450592 | tf_op jit(solution)/shard_map/ppermute | solution.py:27
  49.3 5.7 %collective-permute-done.5 = f32[20,2,22,128]{3,2,1,0:T(8,128)S(1)} collective-permute-done((f32[20,2,22,128]{3,2,1,0:T(8,128)S(1)}, f32[20,2,22,128]{3,2,1,0:T(8,128)S(1)}, u32[]{:S(2)}, u32[]{:S(2)}) %collective-permute-start.5) | collective-permute-done | bytes 450592 | tf_op jit(solution)/shard_map/ppermute | solution.py:28
  55.1 3.0 %conditional.4 = (f32[20,2,18,128]{3,0,2,1:T(8,128)S(1)}, f32[20,4,18,128]{3,2,1,0:T(8,128)S(1)}, f32[2,2,16,128]{3,2,1,0:T(8,128)S(1)}) conditional(s32[]{:T(128)} %convert_element_type.44, (f32[6,26,128]{2,1,0:T(8,128)S(1)}, f32[20,6,22,128]{3,2,1,0:T(8,128)S(1)}, f32[2,6,26,128]{3,0,2,1:T(2,128)S(1)}, f32[19]{0:T(128)S(1)}, ...), branch_computations={%region_6.7_spmd, %region_7.10_spmd} | conditional | flops 44426240 | bytes 51945652 | solution.py:267
  55.2 0.5 copy.53
  55.7 0.7 fusion.17
  56.3 0.6 add_multiply_fusion.3
  56.9 0.4 fusion.20
  57.3 0.3 add_multiply_fusion.4
  57.6 0.2 fusion.23
  57.8 0.1 broadcast.224
  58.2 5.6 %collective-permute-start.6 = (f32[20,1,18,128]{3,0,2,1:T(8,128)S(1)}, f32[20,1,18,128]{3,0,2,1:T(8,128)S(1)}, u32[]{:S(2)}, u32[]{:S(2)}) collective-permute-start(f32[20,1,18,128]{3,0,2,1:T(8,128)S(1)} %get-tuple-element.260), channel_id=1, source_target_pairs={{512,544},{544,576},{576,608},{608,640},{640,672},{672,704},{704,7... | collective-permute-start | bytes 552968 | tf_op jit(solution)/shard_map/ppermute | solution.py:36
  63.8 1.9 %collective-permute-start.7 = (f32[20,1,18,128]{3,0,2,1:T(8,128)S(1)}, f32[20,1,18,128]{3,0,2,1:T(8,128)S(1)}, u32[]{:S(2)}, u32[]{:S(2)}) collective-permute-start(f32[20,1,18,128]{3,0,2,1:T(8,128)S(1)} %get-tuple-element.261), channel_id=1, source_target_pairs={{544,512},{576,544},{608,576},{640,608},{672,640},{704,672},{736,7... | collective-permute-start | bytes 552968 | tf_op jit(solution)/shard_map/ppermute | solution.py:37
  65.7 1.9 %collective-permute-start.8 = (f32[2,2,16,128]{3,2,1,0:T(8,128)S(1)}, f32[2,2,16,128]{3,2,1,0:T(8,128)S(1)}, u32[]{:S(2)}, u32[]{:S(2)}) collective-permute-start(f32[2,2,16,128]{3,2,1,0:T(8,128)S(1)} %get-tuple-element.95), channel_id=1, source_target_pairs={{0,512},{512,0},{1,513},{513,1},{2,514},{514,2},{3,515},{515,3},{4... | collective-permute-start | bytes 98312 | tf_op jit(solution)/shard_map/ppermute | solution.py:269
  67.6 5.4 %collective-permute-done.8 = f32[2,2,16,128]{3,2,1,0:T(8,128)S(1)} collective-permute-done((f32[2,2,16,128]{3,2,1,0:T(8,128)S(1)}, f32[2,2,16,128]{3,2,1,0:T(8,128)S(1)}, u32[]{:S(2)}, u32[]{:S(2)}) %collective-permute-start.8) | collective-permute-done | bytes 32800 | tf_op jit(solution)/shard_map/ppermute | solution.py:269
  73.0 0.0 collective-permute-done.6
  73.0 2.1 %collective-permute-done.7 = f32[20,1,18,128]{3,0,2,1:T(8,128)S(1)} collective-permute-done((f32[20,1,18,128]{3,0,2,1:T(8,128)S(1)}, f32[20,1,18,128]{3,0,2,1:T(8,128)S(1)}, u32[]{:S(2)}, u32[]{:S(2)}) %collective-permute-start.7) | collective-permute-done | bytes 184352 | tf_op jit(solution)/shard_map/ppermute | solution.py:37
  75.1 0.1 pad_maximum_fusion.21
  75.2 0.7 conditional.5
  75.2 0.3 fusion.52
  75.6 0.2 multiply_bitcast_fusion
  75.8 0.1 copy.44
  75.9 0.0 copy-start
  75.9 0.7 copy-done
  (24 shorter events, 0.3 us)
Async XLA Ops:
  2.7 22.5 %copy-start.3 = (s32[19]{0:T(128)S(1)}, s32[19]{0:T(128)}, u32[]{:S(2)}) copy-start(s32[19]{0:T(128)} %param.14) | copy-start | bytes 232
  2.8 13.4 %collective-permute-start.1 = (f32[23,2,16,128]{3,0,2,1:T(8,128)S(1)}, f32[23,2,16,128]{3,0,2,1:T(8,128)S(1)}, u32[]{:S(2)}, u32[]{:S(2)}) collective-permute-start(f32[23,2,16,128]{3,0,2,1:T(8,128)S(1)} %pad_maximum_fusion.22), channel_id=1, source_target_pairs={{32,0},{64,32},{96,64},{128,96},{160,128},{192,160},{224,192},{256... | collective-permute-start | bytes 1130504 | tf_op jit(solution)/shard_map/ppermute | solution.py:28
  4.7 12.7 %collective-permute-start = (f32[23,2,16,128]{3,0,2,1:T(8,128)S(1)}, f32[23,2,16,128]{3,0,2,1:T(8,128)S(1)}, u32[]{:S(2)}, u32[]{:S(2)}) collective-permute-start(f32[23,2,16,128]{3,0,2,1:T(8,128)S(1)} %pad_maximum_fusion.22), channel_id=1, source_target_pairs={{0,32},{32,64},{64,96},{96,128},{128,160},{160,192},{192,224},{224... | collective-permute-start | bytes 1130504 | tf_op jit(solution)/shard_map/ppermute | solution.py:27
  17.6 11.0 %collective-permute-start.2 = (f32[23,6,5,128]{3,0,2,1:T(8,128)S(1)}, f32[23,6,5,128]{3,0,2,1:T(8,128)S(1)}, u32[]{:S(2)}, u32[]{:S(2)}) collective-permute-start(f32[23,6,5,128]{3,0,2,1:T(8,128)S(1)} %get-tuple-element.258), channel_id=1, source_target_pairs={{0,1},{1,2},{2,3},{3,4},{4,5},{5,6},{6,7},{7,8},{8,9},{9,10},{10,1... | collective-permute-start | bytes 1059848 | tf_op jit(solution)/shard_map/ppermute | solution.py:43
  19.5 10.8 %collective-permute-start.3 = (f32[23,6,5,128]{3,0,2,1:T(8,128)S(1)}, f32[23,6,5,128]{3,0,2,1:T(8,128)S(1)}, u32[]{:S(2)}, u32[]{:S(2)}) collective-permute-start(f32[23,6,5,128]{3,0,2,1:T(8,128)S(1)} %get-tuple-element.259), channel_id=1, source_target_pairs={{1,0},{2,1},{3,2},{4,3},{5,4},{6,5},{7,6},{8,7},{9,8},{10,9},{11,1... | collective-permute-start | bytes 1059848 | tf_op jit(solution)/shard_map/ppermute | solution.py:44
  30.9 0.7 copy-start.2
  31.6 7.0 %copy-start.1 = (s32[4,2,16]{2,1,0:T(2,128)S(1)}, s32[4,2,16]{2,1,0:T(2,128)}, u32[]{:S(2)}) copy-start(s32[4,2,16]{2,1,0:T(2,128)} %param.12) | copy-start | bytes 1540
  34.3 14.9 %collective-permute-start.4 = (f32[20,2,22,128]{3,2,1,0:T(8,128)S(1)}, f32[20,2,22,128]{3,2,1,0:T(8,128)S(1)}, u32[]{:S(2)}, u32[]{:S(2)}) collective-permute-start(f32[20,2,22,128]{3,2,1,0:T(8,128)S(1)} %get-tuple-element.92), channel_id=1, source_target_pairs={{0,32},{32,64},{64,96},{96,128},{128,160},{160,192},{192,224},{224... | collective-permute-start | bytes 1351688 | tf_op jit(solution)/shard_map/ppermute | solution.py:27
  38.7 16.4 %collective-permute-start.5 = (f32[20,2,22,128]{3,2,1,0:T(8,128)S(1)}, f32[20,2,22,128]{3,2,1,0:T(8,128)S(1)}, u32[]{:S(2)}, u32[]{:S(2)}) collective-permute-start(f32[20,2,22,128]{3,2,1,0:T(8,128)S(1)} %get-tuple-element.92), channel_id=1, source_target_pairs={{32,0},{64,32},{96,64},{128,96},{160,128},{192,160},{224,192},{256... | collective-permute-start | bytes 1351688 | tf_op jit(solution)/shard_map/ppermute | solution.py:28
  58.2 14.8 %collective-permute-start.6 = (f32[20,1,18,128]{3,0,2,1:T(8,128)S(1)}, f32[20,1,18,128]{3,0,2,1:T(8,128)S(1)}, u32[]{:S(2)}, u32[]{:S(2)}) collective-permute-start(f32[20,1,18,128]{3,0,2,1:T(8,128)S(1)} %get-tuple-element.260), channel_id=1, source_target_pairs={{512,544},{544,576},{576,608},{608,640},{640,672},{672,704},{704,7... | collective-permute-start | bytes 552968 | tf_op jit(solution)/shard_map/ppermute | solution.py:36
  63.8 11.3 %collective-permute-start.7 = (f32[20,1,18,128]{3,0,2,1:T(8,128)S(1)}, f32[20,1,18,128]{3,0,2,1:T(8,128)S(1)}, u32[]{:S(2)}, u32[]{:S(2)}) collective-permute-start(f32[20,1,18,128]{3,0,2,1:T(8,128)S(1)} %get-tuple-element.261), channel_id=1, source_target_pairs={{544,512},{576,544},{608,576},{640,608},{672,640},{704,672},{736,7... | collective-permute-start | bytes 552968 | tf_op jit(solution)/shard_map/ppermute | solution.py:37
  65.7 7.3 %collective-permute-start.8 = (f32[2,2,16,128]{3,2,1,0:T(8,128)S(1)}, f32[2,2,16,128]{3,2,1,0:T(8,128)S(1)}, u32[]{:S(2)}, u32[]{:S(2)}) collective-permute-start(f32[2,2,16,128]{3,2,1,0:T(8,128)S(1)} %get-tuple-element.95), channel_id=1, source_target_pairs={{0,512},{512,0},{1,513},{513,1},{2,514},{514,2},{3,515},{515,3},{4... | collective-permute-start | bytes 98312 | tf_op jit(solution)/shard_map/ppermute | solution.py:269
  75.9 0.7 copy-start

commit v12 on v11

--- a/solution.py
+++ b/solution.py
@@ -170,7 +170,7 @@
 
 def absorption(tracer, wet_mask, above_table):
     attenuation = wet_mask * (0.03 + 0.05 * jax.nn.softplus(tracer[0]))
-    overhead = jnp.einsum("xyk,kl->xyl", attenuation, above_table, precision=lax.Precision.HIGHEST)
+    overhead = jnp.einsum("xyk,kl->xyl", attenuation, above_table, precision=lax.Precision.HIGH)
     return SURFACE * jnp.exp(-overhead) * (1.0 - jnp.exp(-attenuation))
 
 

time: 77.1 us -> 77 us (level)
  no operation moved by 1% of the time
where the time goes in v12:
time: 77 us; the launch traced here: 76.6 us
  waiting for transfers between devices  35.2 us (46%)
  starting transfers between devices  29.5 us (38%)
  local copies, waits for them, and re-layouts  4.39 us (6%)
  other arithmetic  4 us (5%)
  matrix products  2.86 us (4%)
    ppermute x2, waiting for transfers between devices, halo_x(): after = lax.ppermute(block[:, :cells], 'gx', down)  12.9 us
    ppermute x2, waiting for transfers between devices, halo_x(): before = lax.ppermute(block[:, block.shape[1] - cells:], 'gx', up)  9.89 us
    ppermute x2, starting transfers between devices, halo_x(): before = lax.ppermute(block[:, block.shape[1] - cells:], 'gx', up)  8.56 us
    ppermute x1, starting transfers between devices, halo_y(): above = lax.ppermute(block[:, :, :rows], 'gy', down)  5.75 us
    ppermute x1, starting transfers between devices, halo_x_tracer(): before = lax.ppermute(block[:, block.shape[1] - cells:], ('half', 'gx'), up)  5.59 us
    ppermute x1, waiting for transfers between devices, body(): arrived = lax.ppermute(outgoing, 'half', [(0, 1), (1, 0)])  5.38 us
    ppermute x2, starting transfers between devices, halo_x(): after = lax.ppermute(block[:, :cells], 'gx', down)  3.84 us
    unnamed x12, local copies, waits for them, and re-layouts  3.29 us
  transfers between devices with their start and end apart: 9, of which 8 were waited for; matrix products, arithmetic and copies ran while one was open for 0% of the time, Pallas kernels for 0%

profile of v12, /device:TPU:100, one launch (start us, length us, event | category | flops | bytes accessed | tf_op | source)
XLA Modules:
  0.0 76.6 jit_solution(6103990298858503895)
XLA Ops:
  0.0 0.7 fusion.61
  0.7 0.8 %copy.47 = f32[2,2,16,128]{3,0,2,1:T(2,128)S(1)} copy(f32[2,2,16,128]{3,2,1,0:T(8,128)} %param.13) | data formatting | bytes 65536 | tf_op args[2]
  1.5 0.1 copy.48
  1.6 1.2 %copy.62 = f32[1,20,2,16,128]{4,1,3,2,0:T(8,128)S(1)} copy(f32[1,20,2,16,128]{4,3,2,1,0:T(8,128)} %param.11) | data formatting | bytes 655360 | tf_op args[0]
  2.7 0.0 copy-start.3
  2.8 0.1 pad_maximum_fusion.22
  2.8 1.9 %collective-permute-start.1 = (f32[23,2,16,128]{3,0,2,1:T(8,128)S(1)}, f32[23,2,16,128]{3,0,2,1:T(8,128)S(1)}, u32[]{:S(2)}, u32[]{:S(2)}) collective-permute-start(f32[23,2,16,128]{3,0,2,1:T(8,128)S(1)} %pad_maximum_fusion.22), channel_id=1, source_target_pairs={{32,0},{64,32},{96,64},{128,96},{160,128},{192,160},{224,192},{256... | collective-permute-start | bytes 1130504 | tf_op jit(solution)/shard_map/ppermute | solution.py:28
  4.7 4.3 %collective-permute-start = (f32[23,2,16,128]{3,0,2,1:T(8,128)S(1)}, f32[23,2,16,128]{3,0,2,1:T(8,128)S(1)}, u32[]{:S(2)}, u32[]{:S(2)}) collective-permute-start(f32[23,2,16,128]{3,0,2,1:T(8,128)S(1)} %pad_maximum_fusion.22), channel_id=1, source_target_pairs={{0,32},{32,64},{64,96},{96,128},{128,160},{160,192},{192,224},{224... | collective-permute-start | bytes 1130504 | tf_op jit(solution)/shard_map/ppermute | solution.py:27
  9.0 7.2 %collective-permute-done.1 = f32[23,2,16,128]{3,0,2,1:T(8,128)S(1)} collective-permute-done((f32[23,2,16,128]{3,0,2,1:T(8,128)S(1)}, f32[23,2,16,128]{3,0,2,1:T(8,128)S(1)}, u32[]{:S(2)}, u32[]{:S(2)}) %collective-permute-start.1) | collective-permute-done | bytes 376864 | tf_op jit(solution)/shard_map/ppermute | solution.py:28
  16.2 1.3 %collective-permute-done = f32[23,2,16,128]{3,0,2,1:T(8,128)S(1)} collective-permute-done((f32[23,2,16,128]{3,0,2,1:T(8,128)S(1)}, f32[23,2,16,128]{3,0,2,1:T(8,128)S(1)}, u32[]{:S(2)}, u32[]{:S(2)}) %collective-permute-start) | collective-permute-done | bytes 376864 | tf_op jit(solution)/shard_map/ppermute | solution.py:27
  17.5 0.1 pad_maximum_fusion.27
  17.6 1.9 %collective-permute-start.2 = (f32[23,6,5,128]{3,0,2,1:T(8,128)S(1)}, f32[23,6,5,128]{3,0,2,1:T(8,128)S(1)}, u32[]{:S(2)}, u32[]{:S(2)}) collective-permute-start(f32[23,6,5,128]{3,0,2,1:T(8,128)S(1)} %get-tuple-element.258), channel_id=1, source_target_pairs={{0,1},{1,2},{2,3},{3,4},{4,5},{5,6},{6,7},{7,8},{8,9},{9,10},{10,1... | collective-permute-start | bytes 1059848 | tf_op jit(solution)/shard_map/ppermute | solution.py:43
  19.5 5.8 %collective-permute-start.3 = (f32[23,6,5,128]{3,0,2,1:T(8,128)S(1)}, f32[23,6,5,128]{3,0,2,1:T(8,128)S(1)}, u32[]{:S(2)}, u32[]{:S(2)}) collective-permute-start(f32[23,6,5,128]{3,0,2,1:T(8,128)S(1)} %get-tuple-element.259), channel_id=1, source_target_pairs={{1,0},{2,1},{3,2},{4,3},{5,4},{6,5},{7,6},{8,7},{9,8},{10,9},{11,1... | collective-permute-start | bytes 1059848 | tf_op jit(solution)/shard_map/ppermute | solution.py:44
  25.3 0.0 copy-done.3
  25.3 0.1 fusion.60
  25.3 3.3 %collective-permute-done.2 = f32[23,6,5,128]{3,0,2,1:T(8,128)S(1)} collective-permute-done((f32[23,6,5,128]{3,0,2,1:T(8,128)S(1)}, f32[23,6,5,128]{3,0,2,1:T(8,128)S(1)}, u32[]{:S(2)}, u32[]{:S(2)}) %collective-permute-start.2) | collective-permute-done | bytes 353312 | tf_op jit(solution)/shard_map/ppermute | solution.py:43
  28.6 1.7 %collective-permute-done.3 = f32[23,6,5,128]{3,0,2,1:T(8,128)S(1)} collective-permute-done((f32[23,6,5,128]{3,0,2,1:T(8,128)S(1)}, f32[23,6,5,128]{3,0,2,1:T(8,128)S(1)}, u32[]{:S(2)}, u32[]{:S(2)}) %collective-permute-start.3) | collective-permute-done | bytes 353312 | tf_op jit(solution)/shard_map/ppermute | solution.py:44
  30.3 0.1 pad_maximum_fusion.29
  30.4 0.1 copy.49
  30.5 0.1 compare_convert_fusion.1
  30.6 0.2 compare_convert_fusion
  30.8 0.1 pad_maximum_fusion.20
  30.9 0.0 copy-start.2
  31.0 0.1 pad_maximum_fusion.28
  31.1 0.5 copy-done.2
  31.6 0.0 copy-start.1
  31.6 2.7 %conditional.3 = (f32[20,2,22,128]{3,2,1,0:T(8,128)S(1)}, f32[2,2,16,128]{3,2,1,0:T(8,128)S(1)}) conditional(s32[]{:T(128)} %convert_element_type.44, (f32[6,26,128]{2,1,0:T(8,128)S(1)}, f32[20,6,26,128]{3,0,2,1:T(8,128)S(1)}, f32[2,6,26,128]{3,0,2,1:T(2,128)S(1)}, f32[19]{0:T(128)S(1)}, f32[19,19]{1,0:T(8,128)S(1)}) %tuple.126, ...), branch_computations={%region_1.2_spmd, %region_2.5_spmd} | conditional | flops 46310400 | bytes 43647144 | solution.py:236
  31.7 0.3 broadcast_multiply_fusion
  31.9 0.8 %fusion.2 = f32[19,4,24,128]{3,0,2,1:T(8,128)S(1)} fusion(f32[20,6,26,128]{3,0,2,1:T(8,128)S(1)} %broadcast_multiply_fusion, f32[19]{0:T(128)S(1)} %get-tuple-element.64, f32[19,19]{1,0:T(8,128)S(1)} %get-tuple-element.65), kind=kOutput, calls=%fused_computation.3 | convolution fusion | flops 27549696 | bytes 3305984 | tf_op jit(solution)/shard_map/cond/branch_0_fun/ts,sxyk->txyk/dot_general | solution.py:155
  32.8 0.6 add_multiply_fusion
  33.4 0.5 fusion.5
  33.9 0.3 add_multiply_fusion.1
  34.2 0.1 copy.43
  34.3 4.3 %collective-permute-start.4 = (f32[20,2,22,128]{3,2,1,0:T(8,128)S(1)}, f32[20,2,22,128]{3,2,1,0:T(8,128)S(1)}, u32[]{:S(2)}, u32[]{:S(2)}) collective-permute-start(f32[20,2,22,128]{3,2,1,0:T(8,128)S(1)} %get-tuple-element.92), channel_id=1, source_target_pairs={{0,32},{32,64},{64,96},{96,128},{128,160},{160,192},{192,224},{224... | collective-permute-start | bytes 1351688 | tf_op jit(solution)/shard_map/ppermute | solution.py:27
  38.6 0.0 copy-done.1
  38.7 1.9 %collective-permute-start.5 = (f32[20,2,22,128]{3,2,1,0:T(8,128)S(1)}, f32[20,2,22,128]{3,2,1,0:T(8,128)S(1)}, u32[]{:S(2)}, u32[]{:S(2)}) collective-permute-start(f32[20,2,22,128]{3,2,1,0:T(8,128)S(1)} %get-tuple-element.92), channel_id=1, source_target_pairs={{32,0},{64,32},{96,64},{128,96},{160,128},{192,160},{224,192},{256... | collective-permute-start | bytes 1351688 | tf_op jit(solution)/shard_map/ppermute | solution.py:28
  40.6 0.1 fusion.59
  40.7 8.6 %collective-permute-done.4 = f32[20,2,22,128]{3,2,1,0:T(8,128)S(1)} collective-permute-done((f32[20,2,22,128]{3,2,1,0:T(8,128)S(1)}, f32[20,2,22,128]{3,2,1,0:T(8,128)S(1)}, u32[]{:S(2)}, u32[]{:S(2)}) %collective-permute-start.4) | collective-permute-done | bytes 450592 | tf_op jit(solution)/shard_map/ppermute | solution.py:27
  49.3 5.7 %collective-permute-done.5 = f32[20,2,22,128]{3,2,1,0:T(8,128)S(1)} collective-permute-done((f32[20,2,22,128]{3,2,1,0:T(8,128)S(1)}, f32[20,2,22,128]{3,2,1,0:T(8,128)S(1)}, u32[]{:S(2)}, u32[]{:S(2)}) %collective-permute-start.5) | collective-permute-done | bytes 450592 | tf_op jit(solution)/shard_map/ppermute | solution.py:28
  55.1 3.0 %conditional.4 = (f32[20,2,18,128]{3,0,2,1:T(8,128)S(1)}, f32[20,4,18,128]{3,2,1,0:T(8,128)S(1)}, f32[2,2,16,128]{3,2,1,0:T(8,128)S(1)}) conditional(s32[]{:T(128)} %convert_element_type.44, (f32[6,26,128]{2,1,0:T(8,128)S(1)}, f32[20,6,22,128]{3,2,1,0:T(8,128)S(1)}, f32[2,6,26,128]{3,0,2,1:T(2,128)S(1)}, f32[19]{0:T(128)S(1)}, ...), branch_computations={%region_6.7_spmd, %region_7.10_spmd} | conditional | flops 41280512 | bytes 51945652 | solution.py:267
  55.2 0.5 copy.53
  55.7 0.7 fusion.17
  56.3 0.6 add_multiply_fusion.3
  56.9 0.4 fusion.20
  57.3 0.3 add_multiply_fusion.4
  57.6 0.2 fusion.23
  57.8 0.1 broadcast.224
  58.1 5.6 %collective-permute-start.6 = (f32[20,1,18,128]{3,0,2,1:T(8,128)S(1)}, f32[20,1,18,128]{3,0,2,1:T(8,128)S(1)}, u32[]{:S(2)}, u32[]{:S(2)}) collective-permute-start(f32[20,1,18,128]{3,0,2,1:T(8,128)S(1)} %get-tuple-element.260), channel_id=1, source_target_pairs={{512,544},{544,576},{576,608},{608,640},{640,672},{672,704},{704,7... | collective-permute-start | bytes 552968 | tf_op jit(solution)/shard_map/ppermute | solution.py:36
  63.7 1.9 %collective-permute-start.7 = (f32[20,1,18,128]{3,0,2,1:T(8,128)S(1)}, f32[20,1,18,128]{3,0,2,1:T(8,128)S(1)}, u32[]{:S(2)}, u32[]{:S(2)}) collective-permute-start(f32[20,1,18,128]{3,0,2,1:T(8,128)S(1)} %get-tuple-element.261), channel_id=1, source_target_pairs={{544,512},{576,544},{608,576},{640,608},{672,640},{704,672},{736,7... | collective-permute-start | bytes 552968 | tf_op jit(solution)/shard_map/ppermute | solution.py:37
  65.7 1.9 %collective-permute-start.8 = (f32[2,2,16,128]{3,2,1,0:T(8,128)S(1)}, f32[2,2,16,128]{3,2,1,0:T(8,128)S(1)}, u32[]{:S(2)}, u32[]{:S(2)}) collective-permute-start(f32[2,2,16,128]{3,2,1,0:T(8,128)S(1)} %get-tuple-element.95), channel_id=1, source_target_pairs={{0,512},{512,0},{1,513},{513,1},{2,514},{514,2},{3,515},{515,3},{4... | collective-permute-start | bytes 98312 | tf_op jit(solution)/shard_map/ppermute | solution.py:269
  67.6 5.4 %collective-permute-done.8 = f32[2,2,16,128]{3,2,1,0:T(8,128)S(1)} collective-permute-done((f32[2,2,16,128]{3,2,1,0:T(8,128)S(1)}, f32[2,2,16,128]{3,2,1,0:T(8,128)S(1)}, u32[]{:S(2)}, u32[]{:S(2)}) %collective-permute-start.8) | collective-permute-done | bytes 32800 | tf_op jit(solution)/shard_map/ppermute | solution.py:269
  73.0 0.0 collective-permute-done.6
  73.0 2.1 %collective-permute-done.7 = f32[20,1,18,128]{3,0,2,1:T(8,128)S(1)} collective-permute-done((f32[20,1,18,128]{3,0,2,1:T(8,128)S(1)}, f32[20,1,18,128]{3,0,2,1:T(8,128)S(1)}, u32[]{:S(2)}, u32[]{:S(2)}) %collective-permute-start.7) | collective-permute-done | bytes 184352 | tf_op jit(solution)/shard_map/ppermute | solution.py:37
  75.1 0.1 pad_maximum_fusion.21
  75.2 0.7 conditional.5
  75.2 0.3 fusion.52
  75.5 0.2 multiply_bitcast_fusion
  75.8 0.1 copy.44
  75.8 0.0 copy-start
  75.9 0.7 copy-done
  (24 shorter events, 0.3 us)
Async XLA Ops:
  2.7 22.5 %copy-start.3 = (s32[19]{0:T(128)S(1)}, s32[19]{0:T(128)}, u32[]{:S(2)}) copy-start(s32[19]{0:T(128)} %param.14) | copy-start | bytes 232
  2.8 13.4 %collective-permute-start.1 = (f32[23,2,16,128]{3,0,2,1:T(8,128)S(1)}, f32[23,2,16,128]{3,0,2,1:T(8,128)S(1)}, u32[]{:S(2)}, u32[]{:S(2)}) collective-permute-start(f32[23,2,16,128]{3,0,2,1:T(8,128)S(1)} %pad_maximum_fusion.22), channel_id=1, source_target_pairs={{32,0},{64,32},{96,64},{128,96},{160,128},{192,160},{224,192},{256... | collective-permute-start | bytes 1130504 | tf_op jit(solution)/shard_map/ppermute | solution.py:28
  4.7 12.7 %collective-permute-start = (f32[23,2,16,128]{3,0,2,1:T(8,128)S(1)}, f32[23,2,16,128]{3,0,2,1:T(8,128)S(1)}, u32[]{:S(2)}, u32[]{:S(2)}) collective-permute-start(f32[23,2,16,128]{3,0,2,1:T(8,128)S(1)} %pad_maximum_fusion.22), channel_id=1, source_target_pairs={{0,32},{32,64},{64,96},{96,128},{128,160},{160,192},{192,224},{224... | collective-permute-start | bytes 1130504 | tf_op jit(solution)/shard_map/ppermute | solution.py:27
  17.6 11.0 %collective-permute-start.2 = (f32[23,6,5,128]{3,0,2,1:T(8,128)S(1)}, f32[23,6,5,128]{3,0,2,1:T(8,128)S(1)}, u32[]{:S(2)}, u32[]{:S(2)}) collective-permute-start(f32[23,6,5,128]{3,0,2,1:T(8,128)S(1)} %get-tuple-element.258), channel_id=1, source_target_pairs={{0,1},{1,2},{2,3},{3,4},{4,5},{5,6},{6,7},{7,8},{8,9},{9,10},{10,1... | collective-permute-start | bytes 1059848 | tf_op jit(solution)/shard_map/ppermute | solution.py:43
  19.5 10.8 %collective-permute-start.3 = (f32[23,6,5,128]{3,0,2,1:T(8,128)S(1)}, f32[23,6,5,128]{3,0,2,1:T(8,128)S(1)}, u32[]{:S(2)}, u32[]{:S(2)}) collective-permute-start(f32[23,6,5,128]{3,0,2,1:T(8,128)S(1)} %get-tuple-element.259), channel_id=1, source_target_pairs={{1,0},{2,1},{3,2},{4,3},{5,4},{6,5},{7,6},{8,7},{9,8},{10,9},{11,1... | collective-permute-start | bytes 1059848 | tf_op jit(solution)/shard_map/ppermute | solution.py:44
  30.9 0.7 copy-start.2
  31.6 7.0 %copy-start.1 = (s32[4,2,16]{2,1,0:T(2,128)S(1)}, s32[4,2,16]{2,1,0:T(2,128)}, u32[]{:S(2)}) copy-start(s32[4,2,16]{2,1,0:T(2,128)} %param.12) | copy-start | bytes 1540
  34.3 14.9 %collective-permute-start.4 = (f32[20,2,22,128]{3,2,1,0:T(8,128)S(1)}, f32[20,2,22,128]{3,2,1,0:T(8,128)S(1)}, u32[]{:S(2)}, u32[]{:S(2)}) collective-permute-start(f32[20,2,22,128]{3,2,1,0:T(8,128)S(1)} %get-tuple-element.92), channel_id=1, source_target_pairs={{0,32},{32,64},{64,96},{96,128},{128,160},{160,192},{192,224},{224... | collective-permute-start | bytes 1351688 | tf_op jit(solution)/shard_map/ppermute | solution.py:27
  38.7 16.4 %collective-permute-start.5 = (f32[20,2,22,128]{3,2,1,0:T(8,128)S(1)}, f32[20,2,22,128]{3,2,1,0:T(8,128)S(1)}, u32[]{:S(2)}, u32[]{:S(2)}) collective-permute-start(f32[20,2,22,128]{3,2,1,0:T(8,128)S(1)} %get-tuple-element.92), channel_id=1, source_target_pairs={{32,0},{64,32},{96,64},{128,96},{160,128},{192,160},{224,192},{256... | collective-permute-start | bytes 1351688 | tf_op jit(solution)/shard_map/ppermute | solution.py:28
  58.1 14.8 %collective-permute-start.6 = (f32[20,1,18,128]{3,0,2,1:T(8,128)S(1)}, f32[20,1,18,128]{3,0,2,1:T(8,128)S(1)}, u32[]{:S(2)}, u32[]{:S(2)}) collective-permute-start(f32[20,1,18,128]{3,0,2,1:T(8,128)S(1)} %get-tuple-element.260), channel_id=1, source_target_pairs={{512,544},{544,576},{576,608},{608,640},{640,672},{672,704},{704,7... | collective-permute-start | bytes 552968 | tf_op jit(solution)/shard_map/ppermute | solution.py:36
  63.7 11.3 %collective-permute-start.7 = (f32[20,1,18,128]{3,0,2,1:T(8,128)S(1)}, f32[20,1,18,128]{3,0,2,1:T(8,128)S(1)}, u32[]{:S(2)}, u32[]{:S(2)}) collective-permute-start(f32[20,1,18,128]{3,0,2,1:T(8,128)S(1)} %get-tuple-element.261), channel_id=1, source_target_pairs={{544,512},{576,544},{608,576},{640,608},{672,640},{704,672},{736,7... | collective-permute-start | bytes 552968 | tf_op jit(solution)/shard_map/ppermute | solution.py:37
  65.7 7.3 %collective-permute-start.8 = (f32[2,2,16,128]{3,2,1,0:T(8,128)S(1)}, f32[2,2,16,128]{3,2,1,0:T(8,128)S(1)}, u32[]{:S(2)}, u32[]{:S(2)}) collective-permute-start(f32[2,2,16,128]{3,2,1,0:T(8,128)S(1)} %get-tuple-element.95), channel_id=1, source_target_pairs={{0,512},{512,0},{1,513},{513,1},{2,514},{514,2},{3,515},{515,3},{4... | collective-permute-start | bytes 98312 | tf_op jit(solution)/shard_map/ppermute | solution.py:269
  75.8 0.7 copy-start

commit v13 on v11

--- a/solution.py
+++ b/solution.py
@@ -180,8 +180,13 @@
     species = eco_rate.shape[0]
     channels = state.shape[1]
     is_ocean = lax.axis_index("half") == 0
-    level_lanes = jnp.pad(
-        levels.astype(jnp.float32).transpose(1, 2, 0), ((0, 0), (0, 0), (0, depth - 4))
+    lane_group = depth // 4
+    level_lanes = jnp.concatenate(
+        [
+            jnp.broadcast_to(levels[c].astype(jnp.float32)[:, :, None], (size_x, size_y, lane_group))
+            for c in range(4)
+        ],
+        axis=-1,
     )[None]
     packed = jnp.concatenate([state[0], old_flux, level_lanes], axis=0)
     reach_x, reach_y = size_x, NSUB + 1
@@ -196,7 +201,7 @@
     wet_coarse = wet_of(jnp.max(levels, axis=0), depth)
     raw_ext = ext1[:channels]
     flux_ext = ext1[channels : channels + 2]
-    levels_ext = ext1[channels + 2, :, :, 0:4].transpose(2, 0, 1)
+    levels_ext = ext1[channels + 2, :, :, ::lane_group].transpose(2, 0, 1)
     wet_coarse_ext = wet_of_float(jnp.max(levels_ext, axis=0), depth)
     zeros_flux = jnp.zeros((2, size_x, size_y, depth), jnp.float32)
     mid_y, late_y = reach_y - 2, reach_y - 4

time: 77.1 us -> 78.5 us (1.018)
  local copies, waits for them, and re-layouts: 4.39 us -> 6.64 us
  waiting for transfers between devices: 35.2 us -> 33 us
  other arithmetic: 4 us -> 4.96 us
    unnamed x12 -> x14, local copies, waits for them, and re-layouts: 3.29 us -> 4.53 us
    ppermute x2, waiting for transfers between devices: 12.9 us -> 11.8 us  [halo_x(): after = lax.ppermute(block[:, :cells], 'gx', down)]
    concatenate x1, other arithmetic: 0.15 us -> 1.26 us  [halo_y(): return jnp.concatenate([below, block, above], axis=2)]
    slice x1 -> x3, local copies, waits for them, and re-layouts: 0.12 us -> 0.92 us  [the longest x2 0.85 us: body(): levels_ext = ext1[channels + 2, :, :, ::lane_group].transpose(2, 0, 1)]
  transfers between devices with their start and end apart: 9 -> 9, of which waited for: 8 -> 8; matrix products, arithmetic and copies ran while one was open for 0% -> 2% of each run, Pallas kernels for 0% -> 0%
where the time goes in v13:
time: 78.5 us; the launch traced here: 78 us
  waiting for transfers between devices  33 us (42%)
  starting transfers between devices  29.9 us (38%)
  local copies, waits for them, and re-layouts  6.64 us (8%)
  other arithmetic  4.96 us (6%)
  matrix products  2.87 us (4%)
    ppermute x2, waiting for transfers between devices, halo_x(): after = lax.ppermute(block[:, :cells], 'gx', down)  11.8 us
    ppermute x2, waiting for transfers between devices, halo_x(): before = lax.ppermute(block[:, block.shape[1] - cells:], 'gx', up)  9.47 us
    ppermute x2, starting transfers between devices, halo_x(): before = lax.ppermute(block[:, block.shape[1] - cells:], 'gx', up)  8.56 us
    ppermute x1, starting transfers between devices, halo_y(): above = lax.ppermute(block[:, :, :rows], 'gy', down)  5.75 us
    ppermute x1, starting transfers between devices, halo_x_tracer(): before = lax.ppermute(block[:, block.shape[1] - cells:], ('half', 'gx'), up)  5.6 us
    ppermute x1, waiting for transfers between devices, body(): arrived = lax.ppermute(outgoing, 'half', [(0, 1), (1, 0)])  5.47 us
    unnamed x14, local copies, waits for them, and re-layouts  4.53 us
    ppermute x2, starting transfers between devices, halo_x(): after = lax.ppermute(block[:, :cells], 'gx', down)  4.26 us
  transfers between devices with their start and end apart: 9, of which 8 were waited for; matrix products, arithmetic and copies ran while one was open for 2% of the time, Pallas kernels for 0%

profile of v13, /device:TPU:100, one launch (start us, length us, event | category | flops | bytes accessed | tf_op | source)
XLA Modules:
  0.0 78.0 jit_solution(4132231614454436046)
XLA Ops:
  0.0 0.7 convert_bitcast_fusion.3
  0.7 0.8 %copy.32 = f32[2,2,16,128]{3,0,2,1:T(2,128)S(1)} copy(f32[2,2,16,128]{3,2,1,0:T(8,128)} %param.13) | data formatting | bytes 65536 | tf_op args[2]
  1.5 1.2 %copy.43 = f32[1,20,2,16,128]{4,1,3,2,0:T(8,128)S(1)} copy(f32[1,20,2,16,128]{4,3,2,1,0:T(8,128)} %param.11) | data formatting | bytes 655360 | tf_op args[0]
  2.7 0.1 broadcast_in_dim.20
  2.8 0.1 broadcast_in_dim.21
  2.8 0.1 broadcast_in_dim.23
  2.9 0.1 broadcast_in_dim.22
  3.0 0.1 pad_maximum_fusion.28
  3.1 0.1 pad_maximum_fusion.22
  3.1 1.9 %collective-permute-start.1 = (f32[23,2,16,128]{3,0,2,1:T(8,128)S(1)}, f32[23,2,16,128]{3,0,2,1:T(8,128)S(1)}, u32[]{:S(2)}, u32[]{:S(2)}) collective-permute-start(f32[23,2,16,128]{3,0,2,1:T(8,128)S(1)} %pad_maximum_fusion.22), channel_id=1, source_target_pairs={{32,0},{64,32},{96,64},{128,96},{160,128},{192,160},{224,192},{256... | collective-permute-start | bytes 1130504 | tf_op jit(solution)/shard_map/ppermute | solution.py:28
  5.1 4.3 %collective-permute-start = (f32[23,2,16,128]{3,0,2,1:T(8,128)S(1)}, f32[23,2,16,128]{3,0,2,1:T(8,128)S(1)}, u32[]{:S(2)}, u32[]{:S(2)}) collective-permute-start(f32[23,2,16,128]{3,0,2,1:T(8,128)S(1)} %pad_maximum_fusion.22), channel_id=1, source_target_pairs={{0,32},{32,64},{64,96},{96,128},{128,160},{160,192},{192,224},{224... | collective-permute-start | bytes 1130504 | tf_op jit(solution)/shard_map/ppermute | solution.py:27
  9.3 7.2 %collective-permute-done.1 = f32[23,2,16,128]{3,0,2,1:T(8,128)S(1)} collective-permute-done((f32[23,2,16,128]{3,0,2,1:T(8,128)S(1)}, f32[23,2,16,128]{3,0,2,1:T(8,128)S(1)}, u32[]{:S(2)}, u32[]{:S(2)}) %collective-permute-start.1) | collective-permute-done | bytes 376864 | tf_op jit(solution)/shard_map/ppermute | solution.py:28
  16.5 1.3 %collective-permute-done = f32[23,2,16,128]{3,0,2,1:T(8,128)S(1)} collective-permute-done((f32[23,2,16,128]{3,0,2,1:T(8,128)S(1)}, f32[23,2,16,128]{3,0,2,1:T(8,128)S(1)}, u32[]{:S(2)}, u32[]{:S(2)}) %collective-permute-start) | collective-permute-done | bytes 376864 | tf_op jit(solution)/shard_map/ppermute | solution.py:27
  17.8 0.1 pad_maximum_fusion.27
  17.9 1.9 %collective-permute-start.2 = (f32[23,6,5,128]{3,0,2,1:T(8,128)S(1)}, f32[23,6,5,128]{3,0,2,1:T(8,128)S(1)}, u32[]{:S(2)}, u32[]{:S(2)}) collective-permute-start(f32[23,6,5,128]{3,0,2,1:T(8,128)S(1)} %get-tuple-element.241), channel_id=1, source_target_pairs={{0,1},{1,2},{2,3},{3,4},{4,5},{5,6},{6,7},{7,8},{8,9},{9,10},{10,1... | collective-permute-start | bytes 1059848 | tf_op jit(solution)/shard_map/ppermute | solution.py:43
  19.8 5.8 %collective-permute-start.3 = (f32[23,6,5,128]{3,0,2,1:T(8,128)S(1)}, f32[23,6,5,128]{3,0,2,1:T(8,128)}, u32[]{:S(2)}, u32[]{:S(2)}) collective-permute-start(f32[23,6,5,128]{3,0,2,1:T(8,128)S(1)} %get-tuple-element.242), channel_id=1, source_target_pairs={{1,0},{2,1},{3,2},{4,3},{5,4},{6,5},{7,6},{8,7},{9,8},{10,9},{11,1... | collective-permute-start | bytes 1059848 | tf_op jit(solution)/shard_map/ppermute | solution.py:44
  25.6 0.0 copy-done.4
  25.6 0.1 fusion.60
  25.7 3.3 %collective-permute-done.2 = f32[23,6,5,128]{3,0,2,1:T(8,128)S(1)} collective-permute-done((f32[23,6,5,128]{3,0,2,1:T(8,128)S(1)}, f32[23,6,5,128]{3,0,2,1:T(8,128)S(1)}, u32[]{:S(2)}, u32[]{:S(2)}) %collective-permute-start.2) | collective-permute-done | bytes 353312 | tf_op jit(solution)/shard_map/ppermute | solution.py:43
  28.9 0.7 copy-done
  29.7 0.9 %collective-permute-done.3 = f32[23,6,5,128]{3,0,2,1:T(8,128)} collective-permute-done((f32[23,6,5,128]{3,0,2,1:T(8,128)S(1)}, f32[23,6,5,128]{3,0,2,1:T(8,128)}, u32[]{:S(2)}, u32[]{:S(2)}) %collective-permute-start.3) | collective-permute-done | bytes 353312 | tf_op jit(solution)/shard_map/ppermute | solution.py:44
  30.6 1.3 %pad_maximum_fusion.20 = f32[23,6,26,128]{3,0,2,1:T(8,128)S(1)} fusion(f32[23,6,5,128]{3,0,2,1:T(8,128)} %collective-permute-done.3, f32[23,2,16,128]{3,0,2,1:T(8,128)S(1)} %collective-permute-done.1, f32[1,2,16,128]{3,0,2,1:T(1,128)S(1)} %bitcast.139, f32[2,2,16,128]{3,0,2,1:T(2,128)S(1)} %copy.32, f32[20,2,16,128]{3,0,2,1:T(8,128)S(1)} %bitcast.130, ...), kind=kLoop, calls=%fused_computation.163 | loop fusion | flops 2755584 | bytes 3674112 | tf_op jit(solution)/shard_map/concatenate | solution.py:45
  31.8 0.7 slice.390
  32.6 0.1 slice.471
  32.7 0.1 copy.33
  32.8 0.1 compare_convert_fusion.1
  32.9 0.2 compare_convert_fusion
  33.1 0.0 copy-done.3
  33.1 0.0 copy-start.2
  33.1 2.7 %conditional.3 = (f32[20,2,22,128]{3,2,1,0:T(8,128)S(1)}, f32[2,2,16,128]{3,2,1,0:T(8,128)S(1)}) conditional(s32[]{:T(128)} %convert_element_type.79, (f32[6,26,128]{2,1,0:T(8,128)S(1)}, f32[20,6,26,128]{3,0,2,1:T(8,128)S(1)}, f32[2,6,26,128]{3,0,2,1:T(2,128)S(1)}, f32[19]{0:T(128)S(1)}, f32[19,19]{1,0:T(8,128)S(1)}) %tuple.124, ...), branch_computations={%region_1.0_spmd, %region_2.5_spmd} | conditional | flops 46310400 | bytes 43647144 | solution.py:241
  33.2 0.2 broadcast_multiply_fusion
  33.4 0.8 %fusion.2 = f32[19,4,24,128]{3,0,2,1:T(8,128)S(1)} fusion(f32[20,6,26,128]{3,0,2,1:T(8,128)S(1)} %broadcast_multiply_fusion, f32[19]{0:T(128)S(1)} %get-tuple-element.64, f32[19,19]{1,0:T(8,128)S(1)} %get-tuple-element.65), kind=kOutput, calls=%fused_computation.3 | convolution fusion | flops 27549696 | bytes 3305984 | tf_op jit(solution)/shard_map/cond/branch_0_fun/ts,sxyk->txyk/dot_general | solution.py:155
  34.3 0.6 add_multiply_fusion
  34.9 0.5 fusion.5
  35.4 0.3 add_multiply_fusion.1
  35.7 0.1 copy.29
  35.8 4.3 %collective-permute-start.4 = (f32[20,2,22,128]{3,2,1,0:T(8,128)S(1)}, f32[20,2,22,128]{3,2,1,0:T(8,128)}, u32[]{:S(2)}, u32[]{:S(2)}) collective-permute-start(f32[20,2,22,128]{3,2,1,0:T(8,128)S(1)} %get-tuple-element.92), channel_id=1, source_target_pairs={{0,32},{32,64},{64,96},{96,128},{128,160},{160,192},{192,224},{224... | collective-permute-start | bytes 1351688 | tf_op jit(solution)/shard_map/ppermute | solution.py:27
  40.1 0.0 copy-done.2
  40.1 2.3 %collective-permute-start.5 = (f32[20,2,22,128]{3,2,1,0:T(8,128)S(1)}, f32[20,2,22,128]{3,2,1,0:T(8,128)S(1)}, u32[]{:S(2)}, u32[]{:S(2)}) collective-permute-start(f32[20,2,22,128]{3,2,1,0:T(8,128)S(1)} %get-tuple-element.92), channel_id=1, source_target_pairs={{32,0},{64,32},{96,64},{128,96},{160,128},{192,160},{224,192},{256... | collective-permute-start | bytes 1351688 | tf_op jit(solution)/shard_map/ppermute | solution.py:28
  42.5 0.1 fusion.59
  42.6 8.2 %collective-permute-done.4 = f32[20,2,22,128]{3,2,1,0:T(8,128)} collective-permute-done((f32[20,2,22,128]{3,2,1,0:T(8,128)S(1)}, f32[20,2,22,128]{3,2,1,0:T(8,128)}, u32[]{:S(2)}, u32[]{:S(2)}) %collective-permute-start.4) | collective-permute-done | bytes 450592 | tf_op jit(solution)/shard_map/ppermute | solution.py:27
  50.7 1.1 %constant_dynamic-update-slice_fusion.4 = f32[20,6,22,128]{3,2,1,0:T(8,128)S(1)} fusion(f32[20,2,22,128]{3,2,1,0:T(8,128)} %collective-permute-done.4), kind=kLoop, calls=%fused_computation.184 | loop fusion | bytes 942080
  51.9 4.6 %collective-permute-done.5 = f32[20,2,22,128]{3,2,1,0:T(8,128)S(1)} collective-permute-done((f32[20,2,22,128]{3,2,1,0:T(8,128)S(1)}, f32[20,2,22,128]{3,2,1,0:T(8,128)S(1)}, u32[]{:S(2)}, u32[]{:S(2)}) %collective-permute-start.5) | collective-permute-done | bytes 450592 | tf_op jit(solution)/shard_map/ppermute | solution.py:28
  56.5 3.0 %conditional.4 = (f32[20,2,18,128]{3,0,2,1:T(8,128)S(1)}, f32[20,4,18,128]{3,2,1,0:T(8,128)S(1)}, f32[2,2,16,128]{3,2,1,0:T(8,128)S(1)}) conditional(s32[]{:T(128)} %convert_element_type.79, (f32[6,26,128]{2,1,0:T(8,128)S(1)}, f32[20,6,22,128]{3,2,1,0:T(8,128)S(1)}, f32[2,6,26,128]{3,0,2,1:T(2,128)S(1)}, f32[19]{0:T(128)S(1)}, ...), branch_computations={%region_6.7_spmd, %region_7.10_spmd} | conditional | flops 44426240 | bytes 51945652 | solution.py:272
  56.6 0.5 copy.37
  57.0 0.7 fusion.17
  57.7 0.5 add_multiply_fusion.3
  58.3 0.4 fusion.20
  58.7 0.3 add_multiply_fusion.4
  58.9 0.2 fusion.23
  59.1 0.1 broadcast.224
  59.5 5.6 %collective-permute-start.6 = (f32[20,1,18,128]{3,0,2,1:T(8,128)S(1)}, f32[20,1,18,128]{3,0,2,1:T(8,128)S(1)}, u32[]{:S(2)}, u32[]{:S(2)}) collective-permute-start(f32[20,1,18,128]{3,0,2,1:T(8,128)S(1)} %get-tuple-element.243), channel_id=1, source_target_pairs={{512,544},{544,576},{576,608},{608,640},{640,672},{672,704},{704,7... | collective-permute-start | bytes 552968 | tf_op jit(solution)/shard_map/ppermute | solution.py:36
  65.1 1.9 %collective-permute-start.7 = (f32[20,1,18,128]{3,0,2,1:T(8,128)S(1)}, f32[20,1,18,128]{3,0,2,1:T(8,128)S(1)}, u32[]{:S(2)}, u32[]{:S(2)}) collective-permute-start(f32[20,1,18,128]{3,0,2,1:T(8,128)S(1)} %get-tuple-element.244), channel_id=1, source_target_pairs={{544,512},{576,544},{608,576},{640,608},{672,640},{704,672},{736,7... | collective-permute-start | bytes 552968 | tf_op jit(solution)/shard_map/ppermute | solution.py:37
  67.0 1.9 %collective-permute-start.8 = (f32[2,2,16,128]{3,2,1,0:T(8,128)S(1)}, f32[2,2,16,128]{3,2,1,0:T(8,128)S(1)}, u32[]{:S(2)}, u32[]{:S(2)}) collective-permute-start(f32[2,2,16,128]{3,2,1,0:T(8,128)S(1)} %get-tuple-element.95), channel_id=1, source_target_pairs={{0,512},{512,0},{1,513},{513,1},{2,514},{514,2},{3,515},{515,3},{4... | collective-permute-start | bytes 98312 | tf_op jit(solution)/shard_map/ppermute | solution.py:274
  68.9 5.5 %collective-permute-done.8 = f32[2,2,16,128]{3,2,1,0:T(8,128)S(1)} collective-permute-done((f32[2,2,16,128]{3,2,1,0:T(8,128)S(1)}, f32[2,2,16,128]{3,2,1,0:T(8,128)S(1)}, u32[]{:S(2)}, u32[]{:S(2)}) %collective-permute-start.8) | collective-permute-done | bytes 32800 | tf_op jit(solution)/shard_map/ppermute | solution.py:274
  74.4 0.0 collective-permute-done.6
  74.4 2.1 %collective-permute-done.7 = f32[20,1,18,128]{3,0,2,1:T(8,128)S(1)} collective-permute-done((f32[20,1,18,128]{3,0,2,1:T(8,128)S(1)}, f32[20,1,18,128]{3,0,2,1:T(8,128)S(1)}, u32[]{:S(2)}, u32[]{:S(2)}) %collective-permute-start.7) | collective-permute-done | bytes 184352 | tf_op jit(solution)/shard_map/ppermute | solution.py:37
  76.5 0.1 pad_maximum_fusion.21
  76.6 0.7 conditional.5
  76.6 0.3 fusion.52
  77.0 0.2 multiply_bitcast_fusion
  77.2 0.1 copy.30
  77.3 0.0 copy-start.1
  77.3 0.7 copy-done.1
  (25 shorter events, 0.3 us)
Async XLA Ops:
  2.8 22.8 %copy-start.4 = (s32[19]{0:T(128)S(1)}, s32[19]{0:T(128)}, u32[]{:S(2)}) copy-start(s32[19]{0:T(128)} %param.14) | copy-start | bytes 232
  3.1 13.4 %collective-permute-start.1 = (f32[23,2,16,128]{3,0,2,1:T(8,128)S(1)}, f32[23,2,16,128]{3,0,2,1:T(8,128)S(1)}, u32[]{:S(2)}, u32[]{:S(2)}) collective-permute-start(f32[23,2,16,128]{3,0,2,1:T(8,128)S(1)} %pad_maximum_fusion.22), channel_id=1, source_target_pairs={{32,0},{64,32},{96,64},{128,96},{160,128},{192,160},{224,192},{256... | collective-permute-start | bytes 1130504 | tf_op jit(solution)/shard_map/ppermute | solution.py:28
  5.1 12.7 %collective-permute-start = (f32[23,2,16,128]{3,0,2,1:T(8,128)S(1)}, f32[23,2,16,128]{3,0,2,1:T(8,128)S(1)}, u32[]{:S(2)}, u32[]{:S(2)}) collective-permute-start(f32[23,2,16,128]{3,0,2,1:T(8,128)S(1)} %pad_maximum_fusion.22), channel_id=1, source_target_pairs={{0,32},{32,64},{64,96},{96,128},{128,160},{160,192},{192,224},{224... | collective-permute-start | bytes 1130504 | tf_op jit(solution)/shard_map/ppermute | solution.py:27
  17.9 11.0 %collective-permute-start.2 = (f32[23,6,5,128]{3,0,2,1:T(8,128)S(1)}, f32[23,6,5,128]{3,0,2,1:T(8,128)S(1)}, u32[]{:S(2)}, u32[]{:S(2)}) collective-permute-start(f32[23,6,5,128]{3,0,2,1:T(8,128)S(1)} %get-tuple-element.241), channel_id=1, source_target_pairs={{0,1},{1,2},{2,3},{3,4},{4,5},{5,6},{6,7},{7,8},{8,9},{9,10},{10,1... | collective-permute-start | bytes 1059848 | tf_op jit(solution)/shard_map/ppermute | solution.py:43
  19.8 10.8 %collective-permute-start.3 = (f32[23,6,5,128]{3,0,2,1:T(8,128)S(1)}, f32[23,6,5,128]{3,0,2,1:T(8,128)}, u32[]{:S(2)}, u32[]{:S(2)}) collective-permute-start(f32[23,6,5,128]{3,0,2,1:T(8,128)S(1)} %get-tuple-element.242), channel_id=1, source_target_pairs={{1,0},{2,1},{3,2},{4,3},{5,4},{6,5},{7,6},{8,7},{9,8},{10,9},{11,1... | collective-permute-start | bytes 1059848 | tf_op jit(solution)/shard_map/ppermute | solution.py:44
  25.7 7.4 %copy-start.3 = (f32[19]{0:T(128)S(1)}, f32[19]{0:T(128)}, u32[]{:S(2)}) copy-start(f32[19]{0:T(128)} %param.15) | copy-start | bytes 232
  28.9 0.8 copy-start
  33.1 7.0 %copy-start.2 = (s32[4,2,16]{2,1,0:T(2,128)S(1)}, s32[4,2,16]{2,1,0:T(2,128)}, u32[]{:S(2)}) copy-start(s32[4,2,16]{2,1,0:T(2,128)} %param.12) | copy-start | bytes 1540
  35.8 14.9 %collective-permute-start.4 = (f32[20,2,22,128]{3,2,1,0:T(8,128)S(1)}, f32[20,2,22,128]{3,2,1,0:T(8,128)}, u32[]{:S(2)}, u32[]{:S(2)}) collective-permute-start(f32[20,2,22,128]{3,2,1,0:T(8,128)S(1)} %get-tuple-element.92), channel_id=1, source_target_pairs={{0,32},{32,64},{64,96},{96,128},{128,160},{160,192},{192,224},{224... | collective-permute-start | bytes 1351688 | tf_op jit(solution)/shard_map/ppermute | solution.py:27
  40.1 16.3 %collective-permute-start.5 = (f32[20,2,22,128]{3,2,1,0:T(8,128)S(1)}, f32[20,2,22,128]{3,2,1,0:T(8,128)S(1)}, u32[]{:S(2)}, u32[]{:S(2)}) collective-permute-start(f32[20,2,22,128]{3,2,1,0:T(8,128)S(1)} %get-tuple-element.92), channel_id=1, source_target_pairs={{32,0},{64,32},{96,64},{128,96},{160,128},{192,160},{224,192},{256... | collective-permute-start | bytes 1351688 | tf_op jit(solution)/shard_map/ppermute | solution.py:28
  59.5 14.9 %collective-permute-start.6 = (f32[20,1,18,128]{3,0,2,1:T(8,128)S(1)}, f32[20,1,18,128]{3,0,2,1:T(8,128)S(1)}, u32[]{:S(2)}, u32[]{:S(2)}) collective-permute-start(f32[20,1,18,128]{3,0,2,1:T(8,128)S(1)} %get-tuple-element.243), channel_id=1, source_target_pairs={{512,544},{544,576},{576,608},{608,640},{640,672},{672,704},{704,7... | collective-permute-start | bytes 552968 | tf_op jit(solution)/shard_map/ppermute | solution.py:36
  65.1 11.4 %collective-permute-start.7 = (f32[20,1,18,128]{3,0,2,1:T(8,128)S(1)}, f32[20,1,18,128]{3,0,2,1:T(8,128)S(1)}, u32[]{:S(2)}, u32[]{:S(2)}) collective-permute-start(f32[20,1,18,128]{3,0,2,1:T(8,128)S(1)} %get-tuple-element.244), channel_id=1, source_target_pairs={{544,512},{576,544},{608,576},{640,608},{672,640},{704,672},{736,7... | collective-permute-start | bytes 552968 | tf_op jit(solution)/shard_map/ppermute | solution.py:37
  67.0 7.4 %collective-permute-start.8 = (f32[2,2,16,128]{3,2,1,0:T(8,128)S(1)}, f32[2,2,16,128]{3,2,1,0:T(8,128)S(1)}, u32[]{:S(2)}, u32[]{:S(2)}) collective-permute-start(f32[2,2,16,128]{3,2,1,0:T(8,128)S(1)} %get-tuple-element.95), channel_id=1, source_target_pairs={{0,512},{512,0},{1,513},{513,1},{2,514},{514,2},{3,515},{515,3},{4... | collective-permute-start | bytes 98312 | tf_op jit(solution)/shard_map/ppermute | solution.py:274
  77.3 0.7 copy-start.1

commit v14 on v11

--- a/solution.py
+++ b/solution.py
@@ -183,7 +183,12 @@
     level_lanes = jnp.pad(
         levels.astype(jnp.float32).transpose(1, 2, 0), ((0, 0), (0, 0), (0, depth - 4))
     )[None]
-    packed = jnp.concatenate([state[0], old_flux, level_lanes], axis=0)
+    own_wet = jnp.where(
+        is_ocean,
+        wet_of(levels, depth)[None].repeat(channels // 4, axis=0).reshape(channels, size_x, size_y, depth),
+        jnp.broadcast_to(wet_of(jnp.max(levels, axis=0), depth), (channels, size_x, size_y, depth)),
+    )
+    packed = jnp.concatenate([state[0] * own_wet, old_flux, level_lanes], axis=0)
     reach_x, reach_y = size_x, NSUB + 1
     ext1 = halo_y(halo_x(packed, reach_x), reach_y)
     onehot = (eco_prey[:, None] == lax.broadcasted_iota(jnp.int32, (species, species), 1)).astype(
@@ -211,7 +216,6 @@
     def ocean_a():
         fields = as_fields(raw_ext)[..., 1:-1, 1:-1, :]
         wet = wet_ch_ext[..., 1:-1, 1:-1, :]
-        fields = fields * wet[None]
         running = zeros_flux
         for substep in range(2):
             fields = ocean_substep_channels(fields, wet, 0.0)
@@ -222,7 +226,7 @@
         return keep.reshape(shape_mid), running
 
     def tracer_a():
-        tracer = raw_ext * wet_coarse_ext[None]
+        tracer = raw_ext
         for substep in range(2):
             tracer = tracer_substep(
                 tracer,

time: 77.1 us -> 90.5 us (1.17)
  the two profiles are of different devices: /device:TPU:100 before, /device:TPU:348 now
where the time goes in v14:
time: 90.5 us; the launch traced here: 89.4 us
  waiting for transfers between devices  36.7 us (41%)
  starting transfers between devices  26.2 us (29%)
  local copies, waits for them, and re-layouts  12.8 us (14%)
  other arithmetic  10.1 us (11%)
  matrix products  2.8 us (3%)
    ppermute x2, waiting for transfers between devices, halo_x(): after = lax.ppermute(block[:, :cells], 'gx', down)  12.5 us
    ppermute x2, waiting for transfers between devices, halo_x(): before = lax.ppermute(block[:, block.shape[1] - cells:], 'gx', up)  10.7 us
    ppermute x2, starting transfers between devices, halo_x(): before = lax.ppermute(block[:, block.shape[1] - cells:], 'gx', up)  8.56 us
    ppermute x1, starting transfers between devices, halo_x_tracer(): before = lax.ppermute(block[:, block.shape[1] - cells:], ('half', 'gx'), up)  5.6 us
    ppermute x1, waiting for transfers between devices, body(): arrived = lax.ppermute(outgoing, 'half', [(0, 1), (1, 0)])  5.38 us
    ppermute x1, waiting for transfers between devices, halo_y(): below = lax.ppermute(block[:, :, block.shape[2] - rows:], 'gy', up)  4.8 us
    ppermute x2, starting transfers between devices, halo_x(): after = lax.ppermute(block[:, :cells], 'gx', down)  3.84 us
    mul x5, local copies, waits for them, and re-layouts, tracer_substep(): volume_flux[0] * (to_east - to_west) * 0.5  3.33 us
  transfers between devices with their start and end apart: 9, of which 8 were waited for; matrix products, arithmetic and copies ran while one was open for 1% of the time, Pallas kernels for 0%

profile of v14, /device:TPU:348, one launch (start us, length us, event | category | flops | bytes accessed | tf_op | source)
XLA Modules:
  0.0 89.4 jit_solution(7954687469959144999)
XLA Ops:
  0.0 0.7 fusion.62
  0.7 0.8 fusion.58
  1.5 0.7 reduce_max.16
  2.3 1.0 %fusion.57 = f32[20,2,16,128]{3,2,1,0:T(8,128)S(1)} fusion(f32[1,20,2,16,128]{4,3,2,1,0:T(8,128)} %param.11, f32[2,16,128]{2,1,0:T(8,128)S(1)} %fusion.60, f32[4,2,16,128]{3,2,1,0:T(8,128)S(1)} %fusion.58, pred[]{:T(512)S(6)} %eq.11), kind=kLoop, calls=%fused_computation.166 | loop fusion | flops 163840 | bytes 737281 | tf_op jit(solution)/shard_map/mul | solution.py:191
  3.4 0.8 pad_maximum_fusion.23
  4.1 1.9 %collective-permute-start.1 = (f32[23,2,16,128]{3,2,1,0:T(8,128)S(1)}, f32[23,2,16,128]{3,2,1,0:T(8,128)S(1)}, u32[]{:S(2)}, u32[]{:S(2)}) collective-permute-start(f32[23,2,16,128]{3,2,1,0:T(8,128)S(1)} %pad_maximum_fusion.23), channel_id=1, source_target_pairs={{32,0},{64,32},{96,64},{128,96},{160,128},{192,160},{224,192},{256... | collective-permute-start | bytes 1130504 | tf_op jit(solution)/shard_map/ppermute | solution.py:28
  6.1 4.3 %collective-permute-start = (f32[23,2,16,128]{3,2,1,0:T(8,128)S(1)}, f32[23,2,16,128]{3,2,1,0:T(8,128)S(1)}, u32[]{:S(2)}, u32[]{:S(2)}) collective-permute-start(f32[23,2,16,128]{3,2,1,0:T(8,128)S(1)} %pad_maximum_fusion.23), channel_id=1, source_target_pairs={{0,32},{32,64},{64,96},{96,128},{128,160},{160,192},{192,224},{224... | collective-permute-start | bytes 1130504 | tf_op jit(solution)/shard_map/ppermute | solution.py:27
  10.4 6.8 %collective-permute-done.1 = f32[23,2,16,128]{3,2,1,0:T(8,128)S(1)} collective-permute-done((f32[23,2,16,128]{3,2,1,0:T(8,128)S(1)}, f32[23,2,16,128]{3,2,1,0:T(8,128)S(1)}, u32[]{:S(2)}, u32[]{:S(2)}) %collective-permute-start.1) | collective-permute-done | bytes 376864 | tf_op jit(solution)/shard_map/ppermute | solution.py:28
  17.2 1.3 %collective-permute-done = f32[23,2,16,128]{3,2,1,0:T(8,128)S(1)} collective-permute-done((f32[23,2,16,128]{3,2,1,0:T(8,128)S(1)}, f32[23,2,16,128]{3,2,1,0:T(8,128)S(1)}, u32[]{:S(2)}, u32[]{:S(2)}) %collective-permute-start) | collective-permute-done | bytes 376864 | tf_op jit(solution)/shard_map/ppermute | solution.py:27
  18.6 0.1 fusion.74
  18.7 0.1 copy.49
  18.8 1.9 %collective-permute-start.3 = (f32[23,6,5,128]{3,0,2,1:T(8,128)S(1)}, f32[23,6,5,128]{3,0,2,1:T(8,128)S(1)}, u32[]{:S(2)}, u32[]{:S(2)}) collective-permute-start(f32[23,6,5,128]{3,0,2,1:T(8,128)S(1)} %copy.49), channel_id=1, source_target_pairs={{1,0},{2,1},{3,2},{4,3},{5,4},{6,5},{7,6},{8,7},{9,8},{10,9},{11,1... | collective-permute-start | bytes 1059848 | tf_op jit(solution)/shard_map/ppermute | solution.py:44
  20.7 0.1 copy.48
  20.9 2.4 %collective-permute-start.2 = (f32[23,6,5,128]{3,0,2,1:T(8,128)S(1)}, f32[23,6,5,128]{3,0,2,1:T(8,128)S(1)}, u32[]{:S(2)}, u32[]{:S(2)}) collective-permute-start(f32[23,6,5,128]{3,0,2,1:T(8,128)S(1)} %copy.48), channel_id=1, source_target_pairs={{0,1},{1,2},{2,3},{3,4},{4,5},{5,6},{6,7},{7,8},{8,9},{9,10},{10,1... | collective-permute-start | bytes 1059848 | tf_op jit(solution)/shard_map/ppermute | solution.py:43
  23.3 0.7 fusion.61
  24.0 1.8 %collective-permute-done.3 = f32[23,6,5,128]{3,0,2,1:T(8,128)S(1)} collective-permute-done((f32[23,6,5,128]{3,0,2,1:T(8,128)S(1)}, f32[23,6,5,128]{3,0,2,1:T(8,128)S(1)}, u32[]{:S(2)}, u32[]{:S(2)}) %collective-permute-start.3) | collective-permute-done | bytes 353312 | tf_op jit(solution)/shard_map/ppermute | solution.py:44
  25.8 0.1 copy.51
  25.9 4.8 %collective-permute-done.2 = f32[23,6,5,128]{3,0,2,1:T(8,128)S(1)} collective-permute-done((f32[23,6,5,128]{3,0,2,1:T(8,128)S(1)}, f32[23,6,5,128]{3,0,2,1:T(8,128)S(1)}, u32[]{:S(2)}, u32[]{:S(2)}) %collective-permute-start.2) | collective-permute-done | bytes 353312 | tf_op jit(solution)/shard_map/ppermute | solution.py:43
  30.7 0.1 copy.50
  30.8 0.8 copy-done.1
  31.6 0.1 copy.52
  31.8 1.6 %pad_maximum_fusion.20 = f32[23,6,26,128]{3,2,1,0:T(8,128)S(1)} fusion(f32[23,6,5,128]{3,2,1,0:T(8,128)S(1)} %copy.51, f32[23,2,16,128]{3,2,1,0:T(8,128)S(1)} %collective-permute-done.1, f32[1,2,16,128]{3,2,1,0:T(8,128)S(1)} %copy.47, f32[2,2,16,128]{3,2,1,0:T(8,128)} %param.13, f32[20,2,16,128]{3,2,1,0:T(8,128)S(1)} %fusion.57, ...), kind=kLoop, calls=%fused_computation.160 | loop fusion | flops 2755584 | bytes 3674112 | tf_op jit(solution)/shard_map/concatenate | solution.py:45
  33.4 1.4 %copy-done = f32[23,6,26,128]{3,2,1,0:T(8,128)} copy-done((f32[23,6,26,128]{3,2,1,0:T(8,128)}, f32[23,6,26,128]{3,2,1,0:T(8,128)S(1)}, u32[]{:S(2)}) %copy-start) | copy-done | bytes 1837080
  34.8 0.7 compare_convert_fusion.1
  35.5 0.2 compare_convert_fusion
  35.7 0.7 pad_maximum_fusion.24
  36.4 0.8 slice-done
  37.3 6.5 %conditional.3 = (f32[20,2,22,128]{3,2,1,0:T(8,128)S(1)}, f32[2,2,16,128]{3,2,1,0:T(8,128)S(1)}) conditional(s32[]{:T(128)} %convert_element_type.48, (f32[6,26,128]{2,1,0:T(8,128)}, f32[20,6,26,128]{3,2,1,0:T(8,128)S(1)}, f32[2,6,26,128]{3,2,1,0:T(8,128)}, f32[19]{0:T(128)S(1)}, f32[19,19]{1,0:T(8,128)S(1)}) %tuple.132, ...), branch_computations={%region_2.3_spmd, %region_3.0_spmd} | conditional | flops 45911040 | bytes 40255656 | solution.py:240
  37.3 0.9 %copy.54 = f32[20,6,26,128]{3,0,2,1:T(8,128)S(1)} copy(f32[20,6,26,128]{3,2,1,0:T(8,128)S(1)} %get-tuple-element.164) | data formatting | bytes 3194880 | tf_op jit(solution)/shard_map
  38.2 0.8 slice.263
  39.0 0.8 slice.264
  39.8 0.8 slice_bitcast_fusion.3
  40.6 0.9 slice_bitcast_fusion.1
  41.5 0.7 fusion.1
  42.2 0.6 add_multiply_fusion
  42.9 0.5 fusion.4
  43.3 0.3 add_multiply_fusion.1
  43.7 0.1 copy.44
  43.8 4.3 %collective-permute-start.4 = (f32[20,2,22,128]{3,2,1,0:T(8,128)S(1)}, f32[20,2,22,128]{3,2,1,0:T(8,128)S(1)}, u32[]{:S(2)}, u32[]{:S(2)}) collective-permute-start(f32[20,2,22,128]{3,2,1,0:T(8,128)S(1)} %get-tuple-element.92), channel_id=1, source_target_pairs={{0,32},{32,64},{64,96},{96,128},{128,160},{160,192},{192,224},{224... | collective-permute-start | bytes 1351688 | tf_op jit(solution)/shard_map/ppermute | solution.py:27
  48.1 1.9 %collective-permute-start.5 = (f32[20,2,22,128]{3,2,1,0:T(8,128)S(1)}, f32[20,2,22,128]{3,2,1,0:T(8,128)S(1)}, u32[]{:S(2)}, u32[]{:S(2)}) collective-permute-start(f32[20,2,22,128]{3,2,1,0:T(8,128)S(1)} %get-tuple-element.92), channel_id=1, source_target_pairs={{32,0},{64,32},{96,64},{128,96},{160,128},{192,160},{224,192},{256... | collective-permute-start | bytes 1351688 | tf_op jit(solution)/shard_map/ppermute | solution.py:28
  50.1 9.5 %collective-permute-done.4 = f32[20,2,22,128]{3,2,1,0:T(8,128)S(1)} collective-permute-done((f32[20,2,22,128]{3,2,1,0:T(8,128)S(1)}, f32[20,2,22,128]{3,2,1,0:T(8,128)S(1)}, u32[]{:S(2)}, u32[]{:S(2)}) %collective-permute-start.4) | collective-permute-done | bytes 450592 | tf_op jit(solution)/shard_map/ppermute | solution.py:27
  59.6 5.7 %collective-permute-done.5 = f32[20,2,22,128]{3,2,1,0:T(8,128)S(1)} collective-permute-done((f32[20,2,22,128]{3,2,1,0:T(8,128)S(1)}, f32[20,2,22,128]{3,2,1,0:T(8,128)S(1)}, u32[]{:S(2)}, u32[]{:S(2)}) %collective-permute-start.5) | collective-permute-done | bytes 450592 | tf_op jit(solution)/shard_map/ppermute | solution.py:28
  65.3 6.2 %conditional.4 = (f32[20,2,18,128]{3,0,2,1:T(8,128)S(1)}, f32[20,4,18,128]{3,2,1,0:T(8,128)S(1)}, f32[2,2,16,128]{3,2,1,0:T(8,128)S(1)}) conditional(s32[]{:T(128)} %convert_element_type.48, (f32[6,26,128]{2,1,0:T(8,128)}, f32[20,6,22,128]{3,2,1,0:T(8,128)S(1)}, f32[2,6,26,128]{3,2,1,0:T(8,128)}, f32[19]{0:T(128)S(1)}, f32[19,19]{1,0:T(8,128)S(1)}, ...), branch_computations={%region_6.7_spmd, %region_7.10_spmd} | conditional | flops 44426240 | bytes 51945652 | solution.py:271
  65.3 0.8 slice.306
  66.1 0.8 slice.307
  67.0 0.8 slice_bitcast_fusion.11
  67.7 0.9 slice_bitcast_fusion.9
  68.6 0.5 copy.55
  69.1 0.7 fusion.16
  69.8 0.6 add_multiply_fusion.3
  70.4 0.4 fusion.19
  70.8 0.3 add_multiply_fusion.4
  71.1 0.2 fusion.22
  71.3 0.1 broadcast.226
  71.6 5.6 %collective-permute-start.6 = (f32[20,1,18,128]{3,0,2,1:T(8,128)S(1)}, f32[20,1,18,128]{3,0,2,1:T(8,128)S(1)}, u32[]{:S(2)}, u32[]{:S(2)}) collective-permute-start(f32[20,1,18,128]{3,0,2,1:T(8,128)S(1)} %get-tuple-element.258), channel_id=1, source_target_pairs={{512,544},{544,576},{576,608},{608,640},{640,672},{672,704},{704,7... | collective-permute-start | bytes 552968 | tf_op jit(solution)/shard_map/ppermute | solution.py:36
  77.2 1.9 %collective-permute-start.7 = (f32[20,1,18,128]{3,0,2,1:T(8,128)S(1)}, f32[20,1,18,128]{3,0,2,1:T(8,128)S(1)}, u32[]{:S(2)}, u32[]{:S(2)}) collective-permute-start(f32[20,1,18,128]{3,0,2,1:T(8,128)S(1)} %get-tuple-element.259), channel_id=1, source_target_pairs={{544,512},{576,544},{608,576},{640,608},{672,640},{704,672},{736,7... | collective-permute-start | bytes 552968 | tf_op jit(solution)/shard_map/ppermute | solution.py:37
  79.1 1.9 %collective-permute-start.8 = (f32[2,2,16,128]{3,2,1,0:T(8,128)S(1)}, f32[2,2,16,128]{3,2,1,0:T(8,128)S(1)}, u32[]{:S(2)}, u32[]{:S(2)}) collective-permute-start(f32[2,2,16,128]{3,2,1,0:T(8,128)S(1)} %get-tuple-element.95), channel_id=1, source_target_pairs={{0,512},{512,0},{1,513},{513,1},{2,514},{514,2},{3,515},{515,3},{4... | collective-permute-start | bytes 98312 | tf_op jit(solution)/shard_map/ppermute | solution.py:273
  81.1 5.4 %collective-permute-done.8 = f32[2,2,16,128]{3,2,1,0:T(8,128)S(1)} collective-permute-done((f32[2,2,16,128]{3,2,1,0:T(8,128)S(1)}, f32[2,2,16,128]{3,2,1,0:T(8,128)S(1)}, u32[]{:S(2)}, u32[]{:S(2)}) %collective-permute-start.8) | collective-permute-done | bytes 32800 | tf_op jit(solution)/shard_map/ppermute | solution.py:273
  86.4 1.5 %collective-permute-done.7 = f32[20,1,18,128]{3,0,2,1:T(8,128)S(1)} collective-permute-done((f32[20,1,18,128]{3,0,2,1:T(8,128)S(1)}, f32[20,1,18,128]{3,0,2,1:T(8,128)S(1)}, u32[]{:S(2)}, u32[]{:S(2)}) %collective-permute-start.7) | collective-permute-done | bytes 184352 | tf_op jit(solution)/shard_map/ppermute | solution.py:37
  87.9 0.1 pad_maximum_fusion.22
  88.0 0.7 conditional.5
  88.0 0.3 fusion.51
  88.4 0.2 multiply_bitcast_fusion
  88.7 0.7 copy-done.11
  (49 shorter events, 0.6 us)
Async XLA Ops:
  0.0 18.5 %copy-start.7 = (f32[2,2,16,128]{3,2,1,0:T(8,128)S(1)}, f32[2,2,16,128]{3,2,1,0:T(8,128)}, u32[]{:S(2)}) copy-start(f32[2,2,16,128]{3,2,1,0:T(8,128)} %param.13) | copy-start | bytes 98308
  2.3 16.3 %copy-start.12 = (f32[2,16,128]{2,1,0:T(8,128)}, f32[2,16,128]{2,1,0:T(8,128)S(1)}, u32[]{:S(2)}) copy-start(f32[2,16,128]{2,1,0:T(8,128)S(1)} %fusion.60) | copy-start | bytes 49156
  4.1 13.0 %collective-permute-start.1 = (f32[23,2,16,128]{3,2,1,0:T(8,128)S(1)}, f32[23,2,16,128]{3,2,1,0:T(8,128)S(1)}, u32[]{:S(2)}, u32[]{:S(2)}) collective-permute-start(f32[23,2,16,128]{3,2,1,0:T(8,128)S(1)} %pad_maximum_fusion.23), channel_id=1, source_target_pairs={{32,0},{64,32},{96,64},{128,96},{160,128},{192,160},{224,192},{256... | collective-permute-start | bytes 1130504 | tf_op jit(solution)/shard_map/ppermute | solution.py:28
  6.1 12.4 %collective-permute-start = (f32[23,2,16,128]{3,2,1,0:T(8,128)S(1)}, f32[23,2,16,128]{3,2,1,0:T(8,128)S(1)}, u32[]{:S(2)}, u32[]{:S(2)}) collective-permute-start(f32[23,2,16,128]{3,2,1,0:T(8,128)S(1)} %pad_maximum_fusion.23), channel_id=1, source_target_pairs={{0,32},{32,64},{64,96},{96,128},{128,160},{160,192},{192,224},{224... | collective-permute-start | bytes 1130504 | tf_op jit(solution)/shard_map/ppermute | solution.py:27
  18.5 12.3 %copy-start.3 = (f32[23,2,16,128]{3,2,1,0:T(8,128)}, f32[23,2,16,128]{3,2,1,0:T(8,128)S(1)}, u32[]{:S(2)}) copy-start(f32[23,2,16,128]{3,2,1,0:T(8,128)S(1)} %collective-permute-done) | copy-start | bytes 1130500
  18.7 4.6 %copy-start.15 = (s32[19]{0:T(128)S(1)}, s32[19]{0:T(128)}, u32[]{:S(2)}) copy-start(s32[19]{0:T(128)} %param.14) | copy-start | bytes 232
  18.8 7.0 %collective-permute-start.3 = (f32[23,6,5,128]{3,0,2,1:T(8,128)S(1)}, f32[23,6,5,128]{3,0,2,1:T(8,128)S(1)}, u32[]{:S(2)}, u32[]{:S(2)}) collective-permute-start(f32[23,6,5,128]{3,0,2,1:T(8,128)S(1)} %copy.49), channel_id=1, source_target_pairs={{1,0},{2,1},{3,2},{4,3},{5,4},{6,5},{7,6},{8,7},{9,8},{10,9},{11,1... | collective-permute-start | bytes 1059848 | tf_op jit(solution)/shard_map/ppermute | solution.py:44
  20.9 9.8 %collective-permute-start.2 = (f32[23,6,5,128]{3,0,2,1:T(8,128)S(1)}, f32[23,6,5,128]{3,0,2,1:T(8,128)S(1)}, u32[]{:S(2)}, u32[]{:S(2)}) collective-permute-start(f32[23,6,5,128]{3,0,2,1:T(8,128)S(1)} %copy.48), channel_id=1, source_target_pairs={{0,1},{1,2},{2,3},{3,4},{4,5},{5,6},{6,7},{7,8},{8,9},{9,10},{10,1... | collective-permute-start | bytes 1059848 | tf_op jit(solution)/shard_map/ppermute | solution.py:43
  30.8 0.8 copy-start.1
  33.4 1.4 %copy-start = (f32[23,6,26,128]{3,2,1,0:T(8,128)}, f32[23,6,26,128]{3,2,1,0:T(8,128)S(1)}, u32[]{:S(2)}) copy-start(f32[23,6,26,128]{3,2,1,0:T(8,128)S(1)} %pad_maximum_fusion.20) | copy-start | bytes 5511172
  33.4 2.3 %copy-start.2 = (f32[23,6,5,128]{3,2,1,0:T(8,128)S(1)}, f32[23,6,5,128]{3,2,1,0:T(8,128)}, u32[]{:S(2)}) copy-start(f32[23,6,5,128]{3,2,1,0:T(8,128)} %copy-done.1) | copy-start | bytes 1059844
  33.4 2.3 %copy-start.4 = (f32[23,2,16,128]{3,2,1,0:T(8,128)S(1)}, f32[23,2,16,128]{3,2,1,0:T(8,128)}, u32[]{:S(2)}) copy-start(f32[23,2,16,128]{3,2,1,0:T(8,128)} %copy-done.3) | copy-start | bytes 1130500
  33.4 2.3 %copy-start.8 = (f32[2,2,16,128]{3,2,1,0:T(8,128)S(1)}, f32[2,2,16,128]{3,2,1,0:T(8,128)}, u32[]{:S(2)}) copy-start(f32[2,2,16,128]{3,2,1,0:T(8,128)} %param.13) | copy-start | bytes 98308
  34.8 1.7 %copy-start.9 = (f32[19,19]{1,0:T(8,128)S(1)}, f32[19,19]{1,0:T(8,128)}, u32[]{:S(2)}) copy-start(f32[19,19]{1,0:T(8,128)} %fusion.61) | copy-start | bytes 4336
  34.8 1.7 %copy-start.14 = (f32[19]{0:T(128)S(1)}, f32[19]{0:T(128)}, u32[]{:S(2)}) copy-start(f32[19]{0:T(128)} %param.15) | copy-start | bytes 232
  35.5 1.8 %slice-start = ((f32[23,6,26,128]{3,2,1,0:T(8,128)}), f32[20,6,26,128]{3,2,1,0:T(8,128)S(1)}, s32[]{:S(2)}) async-start(f32[23,6,26,128]{3,2,1,0:T(8,128)} %copy-done), calls=%async_computation | async-start | bytes 3932160 | tf_op jit(solution)/shard_map/slice | solution.py:202
  35.7 1.6 %copy-start.5 = (f32[2,2,6,26,128]{4,3,2,1,0:T(8,128)}, f32[2,2,6,26,128]{4,3,2,1,0:T(8,128)S(1)}, u32[]{:S(2)}) copy-start(f32[2,2,6,26,128]{4,3,2,1,0:T(8,128)S(1)} %compare_convert_fusion) | copy-start | bytes 958468
  43.8 15.7 %collective-permute-start.4 = (f32[20,2,22,128]{3,2,1,0:T(8,128)S(1)}, f32[20,2,22,128]{3,2,1,0:T(8,128)S(1)}, u32[]{:S(2)}, u32[]{:S(2)}) collective-permute-start(f32[20,2,22,128]{3,2,1,0:T(8,128)S(1)} %get-tuple-element.92), channel_id=1, source_target_pairs={{0,32},{32,64},{64,96},{96,128},{128,160},{160,192},{192,224},{224... | collective-permute-start | bytes 1351688 | tf_op jit(solution)/shard_map/ppermute | solution.py:27
  48.1 17.2 %collective-permute-start.5 = (f32[20,2,22,128]{3,2,1,0:T(8,128)S(1)}, f32[20,2,22,128]{3,2,1,0:T(8,128)S(1)}, u32[]{:S(2)}, u32[]{:S(2)}) collective-permute-start(f32[20,2,22,128]{3,2,1,0:T(8,128)S(1)} %get-tuple-element.92), channel_id=1, source_target_pairs={{32,0},{64,32},{96,64},{128,96},{160,128},{192,160},{224,192},{256... | collective-permute-start | bytes 1351688 | tf_op jit(solution)/shard_map/ppermute | solution.py:28
  50.0 15.3 %copy-start.6 = (f32[2,2,6,26,128]{4,3,2,1,0:T(8,128)S(1)}, f32[2,2,6,26,128]{4,3,2,1,0:T(8,128)}, u32[]{:S(2)}) copy-start(f32[2,2,6,26,128]{4,3,2,1,0:T(8,128)} %copy-done.5) | copy-start | bytes 958468
  50.0 15.3 %copy-start.10 = (f32[19,19]{1,0:T(8,128)S(1)}, f32[19,19]{1,0:T(8,128)}, u32[]{:S(2)}) copy-start(f32[19,19]{1,0:T(8,128)} %fusion.61) | copy-start | bytes 4336
  50.0 15.3 %copy-start.13 = (f32[2,16,128]{2,1,0:T(8,128)S(1)}, f32[2,16,128]{2,1,0:T(8,128)}, u32[]{:S(2)}) copy-start(f32[2,16,128]{2,1,0:T(8,128)} %copy-done.12) | copy-start | bytes 49156
  71.6 14.8 %collective-permute-start.6 = (f32[20,1,18,128]{3,0,2,1:T(8,128)S(1)}, f32[20,1,18,128]{3,0,2,1:T(8,128)S(1)}, u32[]{:S(2)}, u32[]{:S(2)}) collective-permute-start(f32[20,1,18,128]{3,0,2,1:T(8,128)S(1)} %get-tuple-element.258), channel_id=1, source_target_pairs={{512,544},{544,576},{576,608},{608,640},{640,672},{672,704},{704,7... | collective-permute-start | bytes 552968 | tf_op jit(solution)/shard_map/ppermute | solution.py:36
  77.2 10.7 %collective-permute-start.7 = (f32[20,1,18,128]{3,0,2,1:T(8,128)S(1)}, f32[20,1,18,128]{3,0,2,1:T(8,128)S(1)}, u32[]{:S(2)}, u32[]{:S(2)}) collective-permute-start(f32[20,1,18,128]{3,0,2,1:T(8,128)S(1)} %get-tuple-element.259), channel_id=1, source_target_pairs={{544,512},{576,544},{608,576},{640,608},{672,640},{704,672},{736,7... | collective-permute-start | bytes 552968 | tf_op jit(solution)/shard_map/ppermute | solution.py:37
  79.1 7.3 %collective-permute-start.8 = (f32[2,2,16,128]{3,2,1,0:T(8,128)S(1)}, f32[2,2,16,128]{3,2,1,0:T(8,128)S(1)}, u32[]{:S(2)}, u32[]{:S(2)}) collective-permute-start(f32[2,2,16,128]{3,2,1,0:T(8,128)S(1)} %get-tuple-element.95), channel_id=1, source_target_pairs={{0,512},{512,0},{1,513},{513,1},{2,514},{514,2},{3,515},{515,3},{4... | collective-permute-start | bytes 98312 | tf_op jit(solution)/shard_map/ppermute | solution.py:273
  88.7 0.7 copy-start.11

commit v15 on v11

--- a/solution.py
+++ b/solution.py
@@ -260,8 +260,8 @@
                 onehot,
                 eco_rate,
             )
-        absorbed = absorption(trim(tracer, 0, late_y), wet_coarse, above_table)
-        outgoing = jnp.broadcast_to(absorbed[None], (2, size_x, size_y, depth))
+        chlorophyll = trim(tracer, 0, late_y)[0]
+        outgoing = jnp.broadcast_to(chlorophyll[None], (2, size_x, size_y, depth))
         return tracer, jnp.zeros(fine_shape, jnp.float32), outgoing
 
     block_late, ocean_late, outgoing = lax.cond(is_ocean, ocean_b, tracer_b)
@@ -269,7 +269,7 @@
     arrived = lax.ppermute(outgoing, "half", [(0, 1), (1, 0)])
 
     def ocean_c():
-        light = jnp.pad(arrived[0], ((1, 1), (1, 1), (0, 0)))
+        light = jnp.pad(absorption(arrived, wet_coarse, above_table), ((1, 1), (1, 1), (0, 0)))
         heating = HEATING * jnp.broadcast_to(light, (2, 2) + light.shape)
         wet = wet_ch_ext[..., reach_x - 1 : wet_ch_ext.shape[2] - reach_x + 1, reach_y - 1 : wet_ch_ext.shape[3] - reach_y + 1, :]
         fields = ocean_substep_channels(as_fields(ocean_late), wet, heating)

time: 77.1 us -> 77.2 us (level)
  no operation moved by 1% of the time
where the time goes in v15:
time: 77.2 us; the launch traced here: 76.7 us
  waiting for transfers between devices  35.1 us (45%)
  starting transfers between devices  29.5 us (38%)
  local copies, waits for them, and re-layouts  4.72 us (6%)
  other arithmetic  4.01 us (5%)
  matrix products  2.69 us (3%)
    ppermute x2, waiting for transfers between devices, halo_x(): after = lax.ppermute(block[:, :cells], 'gx', down)  12.8 us
    ppermute x2, waiting for transfers between devices, halo_x(): before = lax.ppermute(block[:, block.shape[1] - cells:], 'gx', up)  9.98 us
    ppermute x2, starting transfers between devices, halo_x(): before = lax.ppermute(block[:, block.shape[1] - cells:], 'gx', up)  8.56 us
    ppermute x1, starting transfers between devices, halo_y(): above = lax.ppermute(block[:, :, :rows], 'gy', down)  5.75 us
    ppermute x1, starting transfers between devices, halo_x_tracer(): before = lax.ppermute(block[:, block.shape[1] - cells:], ('half', 'gx'), up)  5.61 us
    ppermute x1, waiting for transfers between devices, body(): arrived = lax.ppermute(outgoing, 'half', [(0, 1), (1, 0)])  5.37 us
    ppermute x2, starting transfers between devices, halo_x(): after = lax.ppermute(block[:, :cells], 'gx', down)  3.84 us
    unnamed x12, local copies, waits for them, and re-layouts  3.29 us
  transfers between devices with their start and end apart: 9, of which 8 were waited for; matrix products, arithmetic and copies ran while one was open for 0% of the time, Pallas kernels for 0%

profile of v15, /device:TPU:100, one launch (start us, length us, event | category | flops | bytes accessed | tf_op | source)
XLA Modules:
  0.0 76.7 jit_solution(14821741143948386410)
XLA Ops:
  0.0 0.7 fusion.60
  0.7 0.8 %copy.68 = f32[2,2,16,128]{3,0,2,1:T(2,128)S(1)} copy(f32[2,2,16,128]{3,2,1,0:T(8,128)} %param.13) | data formatting | bytes 65536 | tf_op args[2]
  1.5 0.1 copy.69
  1.6 1.2 %copy.87 = f32[1,20,2,16,128]{4,1,3,2,0:T(8,128)S(1)} copy(f32[1,20,2,16,128]{4,3,2,1,0:T(8,128)} %param.11) | data formatting | bytes 655360 | tf_op args[0]
  2.7 0.0 copy-start.3
  2.8 0.1 pad_maximum_fusion.22
  2.8 1.9 %collective-permute-start.1 = (f32[23,2,16,128]{3,0,2,1:T(8,128)S(1)}, f32[23,2,16,128]{3,0,2,1:T(8,128)S(1)}, u32[]{:S(2)}, u32[]{:S(2)}) collective-permute-start(f32[23,2,16,128]{3,0,2,1:T(8,128)S(1)} %pad_maximum_fusion.22), channel_id=1, source_target_pairs={{32,0},{64,32},{96,64},{128,96},{160,128},{192,160},{224,192},{256... | collective-permute-start | bytes 1130504 | tf_op jit(solution)/shard_map/ppermute | solution.py:28
  4.7 4.3 %collective-permute-start = (f32[23,2,16,128]{3,0,2,1:T(8,128)S(1)}, f32[23,2,16,128]{3,0,2,1:T(8,128)S(1)}, u32[]{:S(2)}, u32[]{:S(2)}) collective-permute-start(f32[23,2,16,128]{3,0,2,1:T(8,128)S(1)} %pad_maximum_fusion.22), channel_id=1, source_target_pairs={{0,32},{32,64},{64,96},{96,128},{128,160},{160,192},{192,224},{224... | collective-permute-start | bytes 1130504 | tf_op jit(solution)/shard_map/ppermute | solution.py:27
  9.0 7.2 %collective-permute-done.1 = f32[23,2,16,128]{3,0,2,1:T(8,128)S(1)} collective-permute-done((f32[23,2,16,128]{3,0,2,1:T(8,128)S(1)}, f32[23,2,16,128]{3,0,2,1:T(8,128)S(1)}, u32[]{:S(2)}, u32[]{:S(2)}) %collective-permute-start.1) | collective-permute-done | bytes 376864 | tf_op jit(solution)/shard_map/ppermute | solution.py:28
  16.2 1.3 %collective-permute-done = f32[23,2,16,128]{3,0,2,1:T(8,128)S(1)} collective-permute-done((f32[23,2,16,128]{3,0,2,1:T(8,128)S(1)}, f32[23,2,16,128]{3,0,2,1:T(8,128)S(1)}, u32[]{:S(2)}, u32[]{:S(2)}) %collective-permute-start) | collective-permute-done | bytes 376864 | tf_op jit(solution)/shard_map/ppermute | solution.py:27
  17.5 0.1 pad_maximum_fusion.27
  17.6 1.9 %collective-permute-start.2 = (f32[23,6,5,128]{3,0,2,1:T(8,128)S(1)}, f32[23,6,5,128]{3,0,2,1:T(8,128)S(1)}, u32[]{:S(2)}, u32[]{:S(2)}) collective-permute-start(f32[23,6,5,128]{3,0,2,1:T(8,128)S(1)} %get-tuple-element.293), channel_id=1, source_target_pairs={{0,1},{1,2},{2,3},{3,4},{4,5},{5,6},{6,7},{7,8},{8,9},{9,10},{10,1... | collective-permute-start | bytes 1059848 | tf_op jit(solution)/shard_map/ppermute | solution.py:43
  19.5 5.8 %collective-permute-start.3 = (f32[23,6,5,128]{3,0,2,1:T(8,128)S(1)}, f32[23,6,5,128]{3,0,2,1:T(8,128)S(1)}, u32[]{:S(2)}, u32[]{:S(2)}) collective-permute-start(f32[23,6,5,128]{3,0,2,1:T(8,128)S(1)} %get-tuple-element.294), channel_id=1, source_target_pairs={{1,0},{2,1},{3,2},{4,3},{5,4},{6,5},{7,6},{8,7},{9,8},{10,9},{11,1... | collective-permute-start | bytes 1059848 | tf_op jit(solution)/shard_map/ppermute | solution.py:44
  25.3 0.0 copy-done.3
  25.3 0.1 fusion.59
  25.3 3.3 %collective-permute-done.2 = f32[23,6,5,128]{3,0,2,1:T(8,128)S(1)} collective-permute-done((f32[23,6,5,128]{3,0,2,1:T(8,128)S(1)}, f32[23,6,5,128]{3,0,2,1:T(8,128)S(1)}, u32[]{:S(2)}, u32[]{:S(2)}) %collective-permute-start.2) | collective-permute-done | bytes 353312 | tf_op jit(solution)/shard_map/ppermute | solution.py:43
  28.6 1.7 %collective-permute-done.3 = f32[23,6,5,128]{3,0,2,1:T(8,128)S(1)} collective-permute-done((f32[23,6,5,128]{3,0,2,1:T(8,128)S(1)}, f32[23,6,5,128]{3,0,2,1:T(8,128)S(1)}, u32[]{:S(2)}, u32[]{:S(2)}) %collective-permute-start.3) | collective-permute-done | bytes 353312 | tf_op jit(solution)/shard_map/ppermute | solution.py:44
  30.3 0.1 pad_maximum_fusion.29
  30.4 0.1 copy.70
  30.5 0.1 compare_convert_fusion.1
  30.6 0.2 compare_convert_fusion
  30.8 0.1 pad_maximum_fusion.20
  30.9 0.0 copy-start.2
  31.0 0.1 pad_maximum_fusion.28
  31.1 0.5 copy-done.2
  31.6 0.0 copy-start.1
  31.6 2.7 %conditional.3 = (f32[20,2,22,128]{3,2,1,0:T(8,128)S(1)}, f32[2,2,16,128]{3,2,1,0:T(8,128)S(1)}) conditional(s32[]{:T(128)} %convert_element_type.44, (f32[6,26,128]{2,1,0:T(8,128)S(1)}, f32[20,6,26,128]{3,0,2,1:T(8,128)S(1)}, f32[2,6,26,128]{3,0,2,1:T(2,128)S(1)}, f32[19]{0:T(128)S(1)}, f32[19,19]{1,0:T(8,128)S(1)}) %tuple.136, ...), branch_computations={%region_1.2_spmd, %region_2.5_spmd} | conditional | flops 46310400 | bytes 43647144 | solution.py:236
  31.7 0.2 broadcast_multiply_fusion
  31.9 0.8 %fusion.2 = f32[19,4,24,128]{3,0,2,1:T(8,128)S(1)} fusion(f32[20,6,26,128]{3,0,2,1:T(8,128)S(1)} %broadcast_multiply_fusion, f32[19]{0:T(128)S(1)} %get-tuple-element.64, f32[19,19]{1,0:T(8,128)S(1)} %get-tuple-element.65), kind=kOutput, calls=%fused_computation.3 | convolution fusion | flops 27549696 | bytes 3305984 | tf_op jit(solution)/shard_map/cond/branch_0_fun/ts,sxyk->txyk/dot_general | solution.py:155
  32.8 0.6 add_multiply_fusion
  33.4 0.5 fusion.5
  33.9 0.3 add_multiply_fusion.1
  34.2 0.1 copy.63
  34.3 4.3 %collective-permute-start.4 = (f32[20,2,22,128]{3,2,1,0:T(8,128)S(1)}, f32[20,2,22,128]{3,2,1,0:T(8,128)S(1)}, u32[]{:S(2)}, u32[]{:S(2)}) collective-permute-start(f32[20,2,22,128]{3,2,1,0:T(8,128)S(1)} %get-tuple-element.92), channel_id=1, source_target_pairs={{0,32},{32,64},{64,96},{96,128},{128,160},{160,192},{192,224},{224... | collective-permute-start | bytes 1351688 | tf_op jit(solution)/shard_map/ppermute | solution.py:27
  38.6 1.9 %collective-permute-start.5 = (f32[20,2,22,128]{3,2,1,0:T(8,128)S(1)}, f32[20,2,22,128]{3,2,1,0:T(8,128)S(1)}, u32[]{:S(2)}, u32[]{:S(2)}) collective-permute-start(f32[20,2,22,128]{3,2,1,0:T(8,128)S(1)} %get-tuple-element.92), channel_id=1, source_target_pairs={{32,0},{64,32},{96,64},{128,96},{160,128},{192,160},{224,192},{256... | collective-permute-start | bytes 1351688 | tf_op jit(solution)/shard_map/ppermute | solution.py:28
  40.5 0.0 copy-done.1
  40.6 8.7 %collective-permute-done.4 = f32[20,2,22,128]{3,2,1,0:T(8,128)S(1)} collective-permute-done((f32[20,2,22,128]{3,2,1,0:T(8,128)S(1)}, f32[20,2,22,128]{3,2,1,0:T(8,128)S(1)}, u32[]{:S(2)}, u32[]{:S(2)}) %collective-permute-start.4) | collective-permute-done | bytes 450592 | tf_op jit(solution)/shard_map/ppermute | solution.py:27
  49.3 5.7 %collective-permute-done.5 = f32[20,2,22,128]{3,2,1,0:T(8,128)S(1)} collective-permute-done((f32[20,2,22,128]{3,2,1,0:T(8,128)S(1)}, f32[20,2,22,128]{3,2,1,0:T(8,128)S(1)}, u32[]{:S(2)}, u32[]{:S(2)}) %collective-permute-start.5) | collective-permute-done | bytes 450592 | tf_op jit(solution)/shard_map/ppermute | solution.py:28
  55.0 2.9 %conditional.4 = (f32[20,2,18,128]{3,2,1,0:T(8,128)S(1)}, f32[20,4,18,128]{3,2,1,0:T(8,128)S(1)}, f32[2,2,16,128]{3,2,1,0:T(8,128)S(1)}) conditional(s32[]{:T(128)} %convert_element_type.44, (f32[6,26,128]{2,1,0:T(8,128)S(1)}, f32[20,6,22,128]{3,2,1,0:T(8,128)S(1)}, f32[2,6,26,128]{3,0,2,1:T(2,128)S(1)}, f32[19]{0:T(128)S(1)}, ...), branch_computations={%region_5.6_spmd, %region_6.0_spmd} | conditional | flops 38040576 | bytes 51945652 | solution.py:267
  55.1 0.5 copy.74
  55.6 0.7 fusion.17
  56.3 0.6 add_multiply_fusion.3
  56.9 0.4 fusion.20
  57.3 0.3 add_multiply_fusion.4
  57.6 0.1 copy.64
  57.7 0.1 broadcast.223
  58.0 0.1 copy.76
  58.1 5.6 %collective-permute-start.6 = (f32[20,1,18,128]{3,0,2,1:T(8,128)S(1)}, f32[20,1,18,128]{3,0,2,1:T(8,128)S(1)}, u32[]{:S(2)}, u32[]{:S(2)}) collective-permute-start(f32[20,1,18,128]{3,0,2,1:T(8,128)S(1)} %get-tuple-element.295), channel_id=1, source_target_pairs={{512,544},{544,576},{576,608},{608,640},{640,672},{672,704},{704,7... | collective-permute-start | bytes 552968 | tf_op jit(solution)/shard_map/ppermute | solution.py:36
  63.8 1.9 %collective-permute-start.7 = (f32[20,1,18,128]{3,0,2,1:T(8,128)S(1)}, f32[20,1,18,128]{3,0,2,1:T(8,128)S(1)}, u32[]{:S(2)}, u32[]{:S(2)}) collective-permute-start(f32[20,1,18,128]{3,0,2,1:T(8,128)S(1)} %get-tuple-element.296), channel_id=1, source_target_pairs={{544,512},{576,544},{608,576},{640,608},{672,640},{704,672},{736,7... | collective-permute-start | bytes 552968 | tf_op jit(solution)/shard_map/ppermute | solution.py:37
  65.7 0.1 fusion.58
  65.8 1.9 %collective-permute-start.8 = (f32[2,2,16,128]{3,2,1,0:T(8,128)S(1)}, f32[2,2,16,128]{3,2,1,0:T(8,128)S(1)}, u32[]{:S(2)}, u32[]{:S(2)}) collective-permute-start(f32[2,2,16,128]{3,2,1,0:T(8,128)S(1)} %get-tuple-element.95), channel_id=1, source_target_pairs={{0,512},{512,0},{1,513},{513,1},{2,514},{514,2},{3,515},{515,3},{4... | collective-permute-start | bytes 98312 | tf_op jit(solution)/shard_map/ppermute | solution.py:269
  67.7 5.4 %collective-permute-done.8 = f32[2,2,16,128]{3,2,1,0:T(8,128)S(1)} collective-permute-done((f32[2,2,16,128]{3,2,1,0:T(8,128)S(1)}, f32[2,2,16,128]{3,2,1,0:T(8,128)S(1)}, u32[]{:S(2)}, u32[]{:S(2)}) %collective-permute-start.8) | collective-permute-done | bytes 32800 | tf_op jit(solution)/shard_map/ppermute | solution.py:269
  73.1 0.0 collective-permute-done.6
  73.1 2.0 %collective-permute-done.7 = f32[20,1,18,128]{3,0,2,1:T(8,128)S(1)} collective-permute-done((f32[20,1,18,128]{3,0,2,1:T(8,128)S(1)}, f32[20,1,18,128]{3,0,2,1:T(8,128)S(1)}, u32[]{:S(2)}, u32[]{:S(2)}) %collective-permute-start.7) | collective-permute-done | bytes 184352 | tf_op jit(solution)/shard_map/ppermute | solution.py:37
  75.1 0.1 pad_maximum_fusion.21
  75.2 0.8 %conditional.5 = (f32[1,20,2,16,128]{4,3,2,1,0:T(8,128)S(1)}) conditional(s32[]{:T(128)} %convert_element_type.44, (f32[2,16,128]{2,1,0:T(8,128)S(1)}, f32[20,2,18,128]{3,2,1,0:T(8,128)S(1)}, f32[20,4,18,128]{3,0,2,1:T(8,128)S(1)}, f32[2,2,16,128]{3,2,1,0:T(8,128)S(1)}, f32[19]{0:T(128)S(1)}, /*index=5*/f32[19,19]{1,0:T(8,128)S(1)}) %tuple.138, ...), branch_computations={%region_10.11_spmd, %region_11.12_spmd} | conditional | flops 10493952 | bytes 17698824 | solution.py:281
  75.2 0.1 copy.79
  75.3 0.3 fusion.32
  75.7 0.2 multiply_bitcast_fusion
  75.9 0.1 copy.65
  76.0 0.0 copy-start
  76.0 0.7 copy-done
  (24 shorter events, 0.3 us)
Async XLA Ops:
  2.7 22.5 %copy-start.3 = (s32[19]{0:T(128)S(1)}, s32[19]{0:T(128)}, u32[]{:S(2)}) copy-start(s32[19]{0:T(128)} %param.14) | copy-start | bytes 232
  2.8 13.4 %collective-permute-start.1 = (f32[23,2,16,128]{3,0,2,1:T(8,128)S(1)}, f32[23,2,16,128]{3,0,2,1:T(8,128)S(1)}, u32[]{:S(2)}, u32[]{:S(2)}) collective-permute-start(f32[23,2,16,128]{3,0,2,1:T(8,128)S(1)} %pad_maximum_fusion.22), channel_id=1, source_target_pairs={{32,0},{64,32},{96,64},{128,96},{160,128},{192,160},{224,192},{256... | collective-permute-start | bytes 1130504 | tf_op jit(solution)/shard_map/ppermute | solution.py:28
  4.7 12.7 %collective-permute-start = (f32[23,2,16,128]{3,0,2,1:T(8,128)S(1)}, f32[23,2,16,128]{3,0,2,1:T(8,128)S(1)}, u32[]{:S(2)}, u32[]{:S(2)}) collective-permute-start(f32[23,2,16,128]{3,0,2,1:T(8,128)S(1)} %pad_maximum_fusion.22), channel_id=1, source_target_pairs={{0,32},{32,64},{64,96},{96,128},{128,160},{160,192},{192,224},{224... | collective-permute-start | bytes 1130504 | tf_op jit(solution)/shard_map/ppermute | solution.py:27
  17.6 11.0 %collective-permute-start.2 = (f32[23,6,5,128]{3,0,2,1:T(8,128)S(1)}, f32[23,6,5,128]{3,0,2,1:T(8,128)S(1)}, u32[]{:S(2)}, u32[]{:S(2)}) collective-permute-start(f32[23,6,5,128]{3,0,2,1:T(8,128)S(1)} %get-tuple-element.293), channel_id=1, source_target_pairs={{0,1},{1,2},{2,3},{3,4},{4,5},{5,6},{6,7},{7,8},{8,9},{9,10},{10,1... | collective-permute-start | bytes 1059848 | tf_op jit(solution)/shard_map/ppermute | solution.py:43
  19.5 10.8 %collective-permute-start.3 = (f32[23,6,5,128]{3,0,2,1:T(8,128)S(1)}, f32[23,6,5,128]{3,0,2,1:T(8,128)S(1)}, u32[]{:S(2)}, u32[]{:S(2)}) collective-permute-start(f32[23,6,5,128]{3,0,2,1:T(8,128)S(1)} %get-tuple-element.294), channel_id=1, source_target_pairs={{1,0},{2,1},{3,2},{4,3},{5,4},{6,5},{7,6},{8,7},{9,8},{10,9},{11,1... | collective-permute-start | bytes 1059848 | tf_op jit(solution)/shard_map/ppermute | solution.py:44
  30.9 0.7 copy-start.2
  31.6 8.9 %copy-start.1 = (s32[4,2,16]{2,1,0:T(2,128)S(1)}, s32[4,2,16]{2,1,0:T(2,128)}, u32[]{:S(2)}) copy-start(s32[4,2,16]{2,1,0:T(2,128)} %param.12) | copy-start | bytes 1540
  34.3 14.9 %collective-permute-start.4 = (f32[20,2,22,128]{3,2,1,0:T(8,128)S(1)}, f32[20,2,22,128]{3,2,1,0:T(8,128)S(1)}, u32[]{:S(2)}, u32[]{:S(2)}) collective-permute-start(f32[20,2,22,128]{3,2,1,0:T(8,128)S(1)} %get-tuple-element.92), channel_id=1, source_target_pairs={{0,32},{32,64},{64,96},{96,128},{128,160},{160,192},{192,224},{224... | collective-permute-start | bytes 1351688 | tf_op jit(solution)/shard_map/ppermute | solution.py:27
  38.6 16.4 %collective-permute-start.5 = (f32[20,2,22,128]{3,2,1,0:T(8,128)S(1)}, f32[20,2,22,128]{3,2,1,0:T(8,128)S(1)}, u32[]{:S(2)}, u32[]{:S(2)}) collective-permute-start(f32[20,2,22,128]{3,2,1,0:T(8,128)S(1)} %get-tuple-element.92), channel_id=1, source_target_pairs={{32,0},{64,32},{96,64},{128,96},{160,128},{192,160},{224,192},{256... | collective-permute-start | bytes 1351688 | tf_op jit(solution)/shard_map/ppermute | solution.py:28
  58.1 14.9 %collective-permute-start.6 = (f32[20,1,18,128]{3,0,2,1:T(8,128)S(1)}, f32[20,1,18,128]{3,0,2,1:T(8,128)S(1)}, u32[]{:S(2)}, u32[]{:S(2)}) collective-permute-start(f32[20,1,18,128]{3,0,2,1:T(8,128)S(1)} %get-tuple-element.295), channel_id=1, source_target_pairs={{512,544},{544,576},{576,608},{608,640},{640,672},{672,704},{704,7... | collective-permute-start | bytes 552968 | tf_op jit(solution)/shard_map/ppermute | solution.py:36
  63.8 11.3 %collective-permute-start.7 = (f32[20,1,18,128]{3,0,2,1:T(8,128)S(1)}, f32[20,1,18,128]{3,0,2,1:T(8,128)S(1)}, u32[]{:S(2)}, u32[]{:S(2)}) collective-permute-start(f32[20,1,18,128]{3,0,2,1:T(8,128)S(1)} %get-tuple-element.296), channel_id=1, source_target_pairs={{544,512},{576,544},{608,576},{640,608},{672,640},{704,672},{736,7... | collective-permute-start | bytes 552968 | tf_op jit(solution)/shard_map/ppermute | solution.py:37
  65.8 7.3 %collective-permute-start.8 = (f32[2,2,16,128]{3,2,1,0:T(8,128)S(1)}, f32[2,2,16,128]{3,2,1,0:T(8,128)S(1)}, u32[]{:S(2)}, u32[]{:S(2)}) collective-permute-start(f32[2,2,16,128]{3,2,1,0:T(8,128)S(1)} %get-tuple-element.95), channel_id=1, source_target_pairs={{0,512},{512,0},{1,513},{513,1},{2,514},{514,2},{3,515},{515,3},{4... | collective-permute-start | bytes 98312 | tf_op jit(solution)/shard_map/ppermute | solution.py:269
  76.0 0.7 copy-start
